TPU v7x, 128 devices: a whole 4x4x4 slice. The times are simulated.
128 devices in a mesh: face: 4 (over y), col: 32 (over z, x, core).
Axes of the slice: x: 4, y: 4, z: 4, core: 2. Of those that a mesh axis runs over, the one named last changes fastest.
Arguments:
- dyn_state: float32 [16, 256, 16, 720], P('face', 'col'), may hold values from -6 to 6
- edge_links: int32 [16, 256, 4], P('face', 'col'), may hold values from 0 to 32767, as said below
- phys_slot: int32 [16, 256, 4], P('face', 'col'), may hold values from 0 to 16383, as said below
- crm_active: int32 [16384], P(('face', 'col')), may hold values 0 or 1
- crm_state: bfloat16 [10, 32, 64, 16384], P(None, None, None, ('face', 'col')), may hold values from -4 to 4
Outputs:
- dyn_new: float32 [16, 256, 16, 720], P('face', 'col')
- column_tend: float32 [16, 256, 4, 320], P('face', 'col')
- crm_new: bfloat16 [10, 32, 64, 16384], P(None, None, None, ('face', 'col'))
Inputs may be any that keep to these rules, and one draw needn't show every extreme that they name: `edge_links`: each entry is 8 n + 2 k' + r: element n (id row * 256 + column in a grid of 16 x 256 elements), its edge k' (0 to 3) and a reversal bit r. For edge 0 of element (row, column) n lies in row - 1, for edge 2 in row + 1, for edge 1 in column + 1, for edge 3 in column - 1, rows modulo 16 and columns modulo 256; the other coordinate differs by at most one. `phys_slot`: A permutation of the physics columns. The physics column p lives on device p // 128 of face+col; of the quadrants on one device of the element layout exactly 1 go to each device.
All inputs are finite; a program needn't handle non-finite values. No bound on the sum of `crm_active` on one device may be relied on, other than what follows from the above.
Results may differ from a plain program's by a relative error of at most 0.001.
Values sent between devices are 32-bit elements; how exact they have to be, the bound alone decides.
No kernel may reach another device: no remote copies, remote signals or barrier semaphores. Data moves between devices by JAX's collectives and lax.ppermute only.
A program may use at most 192 MiB of HBM per device.

v0:
```python
import jax
import jax.numpy as jnp
import numpy as np
from jax import lax
from jax.experimental import pallas as pl
from jax.experimental.pallas import tpu as pltpu
from jax.sharding import PartitionSpec as P

NFLD = 10
LEV = 72
CLEV = 32
DSTEPS = 2
CSTEPS = 2


KAPPA = 0.1
ADVECT = 0.1
DIFF_X = 0.2
DIFF_Z = 0.1
RELAX = 0.2
CONVERT = 0.5


def extended_2(cells, sides, width):
    for axis, dim in sides:
        count = lax.axis_size(axis)
        head = lax.slice_in_dim(cells, 0, width, axis=dim)
        tail = lax.slice_in_dim(cells, cells.shape[dim] - width, cells.shape[dim], axis=dim)
        cells = jnp.concatenate(
            [
                lax.ppermute(tail, axis, [(i, (i + 1) % count) for i in range(count)]),
                cells,
                lax.ppermute(head, axis, [((i + 1) % count, i) for i in range(count)]),
            ],
            axis=dim,
        )
    return cells


def node_tables():
    laplace = np.zeros((16, 16), np.float32)
    for row_a in range(4):
        for row_b in range(4):
            here = row_a * 4 + row_b
            for step_a, step_b in ((1, 0), (-1, 0), (0, 1), (0, -1)):
                near_a, near_b = (row_a + step_a, row_b + step_b)
                if 0 <= near_a < 4 and 0 <= near_b < 4:
                    laplace[here, near_a * 4 + near_b] += 1.0
                    laplace[here, here] -= 1.0
    edge_nodes = np.array([[0, 1, 2, 3], [3, 7, 11, 15], [12, 13, 14, 15], [0, 4, 8, 12]])
    spread = np.zeros((16, 16), np.float32)
    for edge in range(4):
        for point in range(4):
            spread[edge_nodes[edge, point], edge * 4 + point] = 1.0
    denom = 1.0 + spread.sum(axis=1)
    quarter = np.zeros((4, 16), np.float32)
    for row_a in range(4):
        for row_b in range(4):
            quarter[row_a // 2 * 2 + row_b // 2, row_a * 4 + row_b] = 0.25
    return (laplace, spread, denom, quarter)


def matched_points(links):
    other_edge = links // 2 % 4
    reversal = links % 2
    points = jnp.arange(4, dtype=jnp.int32)
    along = jnp.where(reversal[..., None] == 1, 3 - points, points)
    base = jnp.where(other_edge == 1, 3, jnp.where(other_edge == 2, 12, 0))
    stride = jnp.where((other_edge == 1) | (other_edge == 3), 4, 1)
    return base[..., None] + stride[..., None] * along


ZCHUNK = 4


def crm_kernel(force_ref, live_ref, state_hbm, new_hbm, tend_ref, held, mid, out, in_sem, out_sem):
    nfld, nlev, nx, _ = held.shape
    chunks = nlev // ZCHUNK

    def in_copy(c):
        part = pl.ds(c * ZCHUNK, ZCHUNK)
        return pltpu.make_async_copy(state_hbm.at[:, part], held.at[:, part], in_sem.at[c])

    def out_copy(c):
        part = pl.ds(c * ZCHUNK, ZCHUNK)
        return pltpu.make_async_copy(out.at[:, part], new_hbm.at[:, part], out_sem.at[c])

    for c in range(chunks):
        in_copy(c).start()
    live = live_ref[...] == 1

    def sweep(src, z, last):
        upper_z = jnp.minimum(z + 1, nlev - 1)
        lower_z = jnp.maximum(z - 1, 0)
        lead = src[0, z].astype(jnp.float32)
        kept = {}

        def finish(f, fresh, state):
            new = jnp.where(live, fresh, state)
            if last:
                out[f, z] = new.astype(out.dtype)
                tend_ref[f, pl.ds(z, 1)] = (jnp.mean(new, axis=0, keepdims=True) - tend_ref[f, pl.ds(z, 1)]) / CSTEPS
            else:
                mid[f, z] = new

        for f in range(nfld):
            state = src[f, z].astype(jnp.float32)
            upper = src[f, upper_z].astype(jnp.float32)
            lower = src[f, lower_z].astype(jnp.float32)
            east = pltpu.roll(state, nx - 1, 0)
            west = pltpu.roll(state, 1, 0)
            mean_x = jnp.mean(state, axis=0, keepdims=True)
            if not last:
                tend_ref[f, pl.ds(z, 1)] = mean_x
            fresh = (
                state
                - ADVECT * lead * (east - west)
                + DIFF_X * (east + west - 2.0 * state)
                + DIFF_Z * (upper + lower - 2.0 * state)
                + RELAX * (force_ref[f, pl.ds(z, 1)] - mean_x)
            )
            if f in (2, 3):
                kept[f] = (fresh, state)
                if f == 3:
                    cond = CONVERT * jnp.maximum(kept[3][0] - kept[2][0], 0.0)
                    finish(2, *kept[2])
                    finish(3, kept[3][0] - cond, kept[3][1])
                continue
            if f == 4:
                fresh = fresh + cond
            finish(f, fresh, state)

    for c in range(chunks):
        if c == 0:
            in_copy(0).wait()
        if c + 1 < chunks:
            in_copy(c + 1).wait()

        def first(z, carry):
            sweep(held, z, False)
            return carry

        lax.fori_loop(c * ZCHUNK, (c + 1) * ZCHUNK, first, 0)
    for c in range(chunks):

        def second(z, carry):
            sweep(mid, z, True)
            return carry

        lax.fori_loop(c * ZCHUNK, (c + 1) * ZCHUNK, second, 0)
        out_copy(c).start()
    for c in range(chunks):
        out_copy(c).wait()


def crm_run(state, forcing, active):
    nfld, nlev, nx, ncol = state.shape
    return pl.pallas_call(
        crm_kernel,
        out_shape=(
            jax.ShapeDtypeStruct(state.shape, jnp.bfloat16),
            jax.ShapeDtypeStruct((nfld, nlev, ncol), jnp.float32),
        ),
        in_specs=[
            pl.BlockSpec(memory_space=pltpu.VMEM),
            pl.BlockSpec(memory_space=pltpu.VMEM),
            pl.BlockSpec(memory_space=pl.ANY),
        ],
        out_specs=(
            pl.BlockSpec(memory_space=pl.ANY),
            pl.BlockSpec(memory_space=pltpu.VMEM),
        ),
        scratch_shapes=[
            pltpu.VMEM(state.shape, jnp.bfloat16),
            pltpu.VMEM(state.shape, jnp.float32),
            pltpu.VMEM(state.shape, jnp.bfloat16),
            pltpu.SemaphoreType.DMA((nlev // ZCHUNK,)),
            pltpu.SemaphoreType.DMA((nlev // ZCHUNK,)),
        ],
        compiler_params=pltpu.CompilerParams(vmem_limit_bytes=48 * 1024 * 1024),
    )(forcing, active.reshape(1, ncol), state)


def per_device(dyn_state, edge_links, phys_slot, crm_active, crm_state):
    laplace, spread, denom, quarter = [jnp.asarray(table) for table in node_tables()]
    rows_dev, cols_dev, nodes, width = dyn_state.shape
    nface = lax.axis_size("face")
    ncol = lax.axis_size("col")
    ndev = nface * ncol
    total_rows = rows_dev * nface
    total_cols = cols_dev * ncol
    neighbour = edge_links // 8
    pick = matched_points(edge_links)
    near_row = neighbour // total_cols
    near_col = neighbour % total_cols
    local_row = lax.broadcasted_iota(jnp.int32, (rows_dev, cols_dev, 4), 0)
    local_col = lax.broadcasted_iota(jnp.int32, (rows_dev, cols_dev, 4), 1)
    drow = (near_row - (lax.axis_index("face") * rows_dev + local_row) + 1) % total_rows - 1
    dcol = (near_col - (lax.axis_index("col") * cols_dev + local_col) + 1) % total_cols - 1
    place = (local_row + drow + 1) * (cols_dev + 2) + (local_col + dcol + 1)
    index_flat = place[..., None] * 16 + pick
    index_flat = index_flat.reshape(-1)
    state = dyn_state
    for step in range(DSTEPS):
        state = state + KAPPA * jnp.einsum(
            "nm,rcmw->rcnw", laplace, state, precision=lax.Precision.HIGHEST
        )
        extended = extended_2(state, (("face", 0), ("col", 1)), 1)
        matched = jnp.take(extended.reshape(-1, width), index_flat, axis=0).reshape(
            rows_dev, cols_dev, 16, width
        )
        summed = jnp.einsum("nm,rcmw->rcnw", spread, matched, precision=lax.Precision.HIGHEST)
        state = (state + summed) / denom[None, None, :, None]
    columns = jnp.einsum("qn,rcnw->rcqw", quarter, state, precision=lax.Precision.HIGHEST).reshape(
        -1, width
    )
    per_dev = columns.shape[0]
    count = per_dev // ndev
    keys_local = phys_slot.reshape(-1)
    order = jnp.argsort(keys_local, stable=True)
    outgoing = columns[order]
    out_keys = keys_local[order]
    arrived, arrived_keys = (
        lax.all_to_all(
            outgoing.reshape(ndev, count, width),
            ("face", "col"),
            split_axis=0,
            concat_axis=0,
            tiled=True,
        ),
        lax.all_to_all(
            out_keys.reshape(ndev, count), ("face", "col"), split_axis=0, concat_axis=0, tiled=True
        ),
    )
    slots = arrived_keys.reshape(-1) % per_dev
    physics = jnp.zeros((per_dev, width), jnp.float32).at[slots].set(arrived.reshape(-1, width))
    forcing = physics.reshape(per_dev, NFLD, LEV)[:, :, :CLEV].transpose(1, 2, 0)
    crm_new, tend = crm_run(crm_state, forcing, crm_active)
    tend_rows = tend.reshape(NFLD * CLEV, per_dev).T[slots]
    returned = lax.all_to_all(
        tend_rows.reshape(ndev, count, NFLD * CLEV),
        ("face", "col"),
        split_axis=0,
        concat_axis=0,
        tiled=True,
    )
    placed = (
        jnp.zeros((per_dev, NFLD * CLEV), jnp.float32)
        .at[order]
        .set(returned.reshape(per_dev, NFLD * CLEV))
    )
    column_tend = placed.reshape(rows_dev, cols_dev, 4, NFLD * CLEV)
    return (state, column_tend, crm_new)


def solution(mesh):
    return jax.shard_map(
        per_device,
        mesh=mesh,
        in_specs=(
            P("face", "col", None, None),
            P("face", "col", None),
            P("face", "col", None),
            P(("face", "col")),
            P(None, None, None, ("face", "col")),
        ),
        out_specs=(
            P("face", "col", None, None),
            P("face", "col", None, None),
            P(None, None, None, ("face", "col")),
        ),
        check_vma=False,
    )
```

profile of v0, /device:TPU:1, one launch (start us, length us, event | category | flops | bytes accessed | tf_op | source)
XLA Modules:
  0.0 135.1 jit_solution(15058313201695603467)
XLA Ops:
  0.6 3.4 %bitcast_add_fusion.3 = f32[4,8,16,720]{3,2,1,0:T(8,128)S(1)} fusion(f32[4,8,16,720]{3,2,1,0:T(8,128)} %param.11, f32[16,16,1,1]{1,0,3,2:T(8,128)} %constant.155), kind=kOutput, calls=%fused_computation.14 | convolution fusion | flops 71516160 | bytes 2950144 | tf_op jit(solution)/shard_map/nm,rcmw->rcnw/dot_general | solution.py:205
  4.1 2.2 %collective-permute-start = (f32[1,8,16,720]{3,2,1,0:T(8,128)S(1)}, f32[1,8,16,720]{3,2,1,0:T(8,128)S(1)}, u32[]{:S(2)}, u32[]{:S(2)}) collective-permute-start(f32[1,8,16,720]{3,2,1,0:T(8,128)S(1)} %get-tuple-element.18), channel_id=1, source_target_pairs={{0,32},{32,64},{64,96},{96,0},{1,33},{33,65},{65,97},{97,1},{2,34}... | collective-permute-start | bytes 1105928 | tf_op jit(solution)/shard_map/ppermute | solution.py:31
  8.7 7.7 %collective-permute-done = f32[1,8,16,720]{3,2,1,0:T(8,128)S(1)} collective-permute-done((f32[1,8,16,720]{3,2,1,0:T(8,128)S(1)}, f32[1,8,16,720]{3,2,1,0:T(8,128)S(1)}, u32[]{:S(2)}, u32[]{:S(2)}) %collective-permute-start) | collective-permute-done | bytes 368672 | tf_op jit(solution)/shard_map/ppermute | solution.py:31
  16.5 2.5 %collective-permute-start.2 = (f32[6,1,16,720]{3,2,1,0:T(8,128)S(1)}, f32[6,1,16,720]{3,2,1,0:T(8,128)S(1)}, u32[]{:S(2)}, u32[]{:S(2)}) collective-permute-start(f32[6,1,16,720]{3,2,1,0:T(8,128)S(1)} %get-tuple-element.14), channel_id=1, source_target_pairs={{0,1},{1,2},{2,3},{3,4},{4,5},{5,6},{6,7},{7,8},{8,9},{9,10},{10,1... | collective-permute-start | bytes 829448 | tf_op jit(solution)/shard_map/ppermute | solution.py:31
  19.1 3.6 %collective-permute-done.2 = f32[6,1,16,720]{3,2,1,0:T(8,128)S(1)} collective-permute-done((f32[6,1,16,720]{3,2,1,0:T(8,128)S(1)}, f32[6,1,16,720]{3,2,1,0:T(8,128)S(1)}, u32[]{:S(2)}, u32[]{:S(2)}) %collective-permute-start.2) | collective-permute-done | bytes 276512 | tf_op jit(solution)/shard_map/ppermute | solution.py:31
  22.7 2.8 %collective-permute-done.3 = f32[6,1,16,720]{3,2,1,0:T(8,128)S(1)} collective-permute-done((f32[6,1,16,720]{3,2,1,0:T(8,128)S(1)}, f32[6,1,16,720]{3,2,1,0:T(8,128)S(1)}, u32[]{:S(2)}, u32[]{:S(2)}) %collective-permute-start.3) | collective-permute-done | bytes 276512 | tf_op jit(solution)/shard_map/ppermute | solution.py:33
  25.5 1.8 %pad_maximum_fusion = f32[6,10,16,720]{3,2,1,0:T(8,128)S(1)} fusion(f32[6,1,16,720]{3,2,1,0:T(8,128)S(1)} %collective-permute-done.3, f32[1,8,16,720]{3,2,1,0:T(8,128)} %copy-done.7, f32[4,8,16,720]{3,2,1,0:T(8,128)} %copy-done.2, f32[1,8,16,720]{3,2,1,0:T(8,128)S(1)} %collective-permute-done, f32[6,1,16,720]{3,2,1,0:T(8,128)S(1)} %collective-permute-done.2), kind=kLoop, calls=%fused_computation.7 | loop fusion | flops 2764800 | bytes 5529600 | tf_op jit(solution)/shard_map/concatenate | solution.py:29
  27.3 2.6 %gather_fusion.3 = f32[512,720]{1,0:T(8,128)} fusion(f32[960,720]{1,0:T(8,128)S(1)} %bitcast.66, s32[1024]{0:T(1024)S(1)} %pad_clamp_fusion.2), kind=kCustom, calls=%fused_computation.clone | custom fusion | bytes 2951168 | tf_op jit(solution)/shard_map/jit(_take)/gather | solution.py:209
  29.9 1.6 %broadcast_select_fusion.1 = f32[512,720]{1,0:T(8,128)S(1)} fusion(f32[512,720]{1,0:T(8,128)} %gather_fusion.3, pred[512]{0:T(512)(128)(4,1)S(1)} %compare_and_fusion), kind=kLoop, calls=%fused_computation.17 | loop fusion | flops 368640 | bytes 2949632 | tf_op jit(solution)/shard_map/jit(_take)/select_n | solution.py:209
  33.0 1.8 %bitcast_add_fusion.1 = f32[4,8,16,720]{3,2,1,0:T(8,128)S(1)} fusion(f32[16,16,1,1]{1,0,3,2:T(8,128)S(1)} %copy-done.11, f32[4,8,16,720]{3,2,1,0:T(8,128)S(1)} %copy-done.3, f32[4,8,720,16]{2,3,1,0:T(8,128)S(1)} %fusion.35, f32[16]{0:T(128)S(1)} %copy-done.15), kind=kOutput, calls=%fused_computation.11 | convolution fusion | flops 72990720 | bytes 4424768 | tf_op jit(solution)/shard_map/nm,rcmw->rcnw/dot_general | solution.py:205
  38.0 2.5 %sort.17 = (s32[128]{0:T(128)}, s32[128]{0:T(128)S(1)}) sort(s32[128]{0:T(128)S(1)} %reshape.140, s32[128]{0:T(128)S(1)} %iota.35), dimensions={0}, to_apply=%region_0.2 | sort | flops 896 | bytes 2048 | tf_op jit(solution)/shard_map/jit(argsort)/sort | solution.py:220
  40.6 4.5 %collective-permute-done.4 = f32[1,8,16,720]{3,2,1,0:T(8,128)S(1)} collective-permute-done((f32[1,8,16,720]{3,2,1,0:T(8,128)S(1)}, f32[1,8,16,720]{3,2,1,0:T(8,128)S(1)}, u32[]{:S(2)}, u32[]{:S(2)}) %collective-permute-start.4) | collective-permute-done | bytes 368672 | tf_op jit(solution)/shard_map/ppermute | solution.py:31
  45.1 2.9 %collective-permute-start.6 = (f32[6,1,16,720]{3,2,1,0:T(8,128)S(1)}, f32[6,1,16,720]{3,2,1,0:T(8,128)S(1)}, u32[]{:S(2)}, u32[]{:S(2)}) collective-permute-start(f32[6,1,16,720]{3,2,1,0:T(8,128)S(1)} %get-tuple-element.12), channel_id=1, source_target_pairs={{0,1},{1,2},{2,3},{3,4},{4,5},{5,6},{6,7},{7,8},{8,9},{9,10},{10,1... | collective-permute-start | bytes 829448 | tf_op jit(solution)/shard_map/ppermute | solution.py:31
  50.0 11.1 %all-to-all-start = ((s32[128,1,1]{2,1,0:T(1,128)}), s32[128,1,1]{2,1,0:T(1,128)S(1)}, u32[]{:S(2)}, u32[]{:S(2)}) async-start(s32[128,1,1]{2,1,0:T(1,128)} %copy.53), calls=%async_computation | async-start | bytes 131072 | tf_op jit(solution)/shard_map/all_to_all | solution.py:231
  61.9 1.9 %pad_maximum_fusion.1 = f32[6,10,16,720]{3,2,1,0:T(8,128)S(1)} fusion(f32[6,1,16,720]{3,2,1,0:T(8,128)} %collective-permute-done.7, f32[1,8,16,720]{3,2,1,0:T(8,128)} %copy-done.8, f32[4,8,16,720]{3,2,1,0:T(8,128)} %copy-done.4, f32[1,8,16,720]{3,2,1,0:T(8,128)S(1)} %collective-permute-done.4, f32[6,1,16,720]{3,2,1,0:T(8,128)} %copy-done.9), kind=kLoop, calls=%fused_computation.8 | loop fusion | flops 2764800 | bytes 5529600 | tf_op jit(solution)/shard_map/concatenate | solution.py:29
  63.8 2.6 %gather_fusion.4 = f32[512,720]{1,0:T(8,128)} fusion(f32[960,720]{1,0:T(8,128)S(1)} %bitcast.65, s32[1024]{0:T(1024)S(1)} %pad_clamp_fusion.2), kind=kCustom, calls=%fused_computation.1.clone | custom fusion | bytes 2951168 | tf_op jit(solution)/shard_map/jit(_take)/gather | solution.py:209
  66.4 1.7 %broadcast_select_fusion = f32[512,720]{1,0:T(8,128)S(1)} fusion(f32[512,720]{1,0:T(8,128)} %gather_fusion.4, pred[512]{0:T(512)(128)(4,1)S(1)} %compare_and_fusion), kind=kLoop, calls=%fused_computation.16 | loop fusion | flops 368640 | bytes 2949632 | tf_op jit(solution)/shard_map/jit(_take)/select_n | solution.py:209
  68.3 1.5 %fusion = f32[4,8,16,720]{3,2,1,0:T(8,128)S(1)} fusion(f32[4,8,16,720]{3,2,1,0:T(8,128)S(1)} %copy-done.5, f32[4,8,16,720]{3,2,1,0:T(8,128)S(1)} %bitcast.68, f32[16,16,1,1]{1,0,3,2:T(8,128)S(1)} %copy-done.10, f32[16]{0:T(128)S(1)} %copy-done.15), kind=kOutput, calls=%fused_computation.10 | convolution fusion | flops 71516160 | bytes 4424768 | tf_op jit(solution)/shard_map/nm,rcmw->rcnw/dot_general | solution.py:212
  72.9 9.8 %all-to-all-start.1 = ((f32[128,1,720]{2,1,0:T(1,128)}), f32[128,1,720]{2,1,0:T(1,128)S(1)}, u32[]{:S(2)}, u32[]{:S(2)}) async-start(f32[128,1,720]{2,1,0:T(1,128)} %copy.54), calls=%async_computation.1 | async-start | bytes 786432 | tf_op jit(solution)/shard_map/all_to_all | solution.py:224
  82.7 2.4 %reduce = s32[128]{0:T(128)S(1)} reduce(s32[128,1,1]{2,1,0:T(1,128)S(1)} %all-to-all-done, s32[]{:T(128)} %constant.127.clone.1), dimensions={1,2}, to_apply=%all_to_all.15.reduce_sub_computation | reduce | bytes 1028 | tf_op jit(solution)/shard_map/all_to_all | solution.py:231
  85.1 9.8 %all-to-all-done.1 = f32[128,1,720]{2,1,0:T(1,128)S(1)} async-done(((f32[128,1,720]{2,1,0:T(1,128)}), f32[128,1,720]{2,1,0:T(1,128)S(1)}, u32[]{:S(2)}, u32[]{:S(2)}) %all-to-all-start.1) | async-done | bytes 368672 | tf_op jit(solution)/shard_map/all_to_all | solution.py:224
  96.5 2.5 %copy-done = bf16[10,32,64,128]{3,2,1,0:T(8,128)(2,1)S(1)} copy-done((bf16[10,32,64,128]{3,2,1,0:T(8,128)(2,1)S(1)}, bf16[10,32,64,128]{3,2,1,0:T(8,128)(2,1)}, u32[]{:S(2)}) %copy-start) | copy-done | bytes 5242904
  98.9 18.4 %shard_map.112 = (bf16[10,32,64,128]{3,2,1,0:T(8,128)(2,1)}, f32[10,32,128]{2,1,0:T(8,128)S(1)}) custom-call(f32[10,32,128]{2,1,0:T(8,128)S(1)} %slice_bitcast_fusion.force_ref, s32[1,128]{1,0:T(1,128)S(1)} %bitcast.64, bf16[10,32,64,128]{3,2,1,0:T(8,128)(2,1)S(1)} %copy-done), custom_call_target="tpu_custom_call" | custom-call | tf_op jit(solution)/shard_map/pallas_call | solution.py:158
  118.5 14.9 %all_to_all.22 = f32[128,1,320]{2,1,0:T(1,128)S(1)} all-to-all(f32[128,1,320]{2,1,0:T(1,128)S(1)} %copy.59), channel_id=1, replica_groups=mesh['face'=4,'col'=32] {'face','col'}, dimensions={0} | all-to-all | bytes 327680 | tf_op jit(solution)/shard_map/all_to_all | solution.py:240
  (82 shorter events, 17.6 us)
Async XLA Ops:
  4.0 12.5 %copy-start.2 = (f32[4,8,16,720]{3,2,1,0:T(8,128)}, f32[4,8,16,720]{3,2,1,0:T(8,128)S(1)}, u32[]{:S(2)}) copy-start(f32[4,8,16,720]{3,2,1,0:T(8,128)S(1)} %bitcast_add_fusion.3) | copy-start | bytes 4423684
  4.0 3.8 %copy-start.12 = (s32[4,8,4]{1,2,0:T(4,128)S(1)}, s32[4,8,4]{1,2,0:T(4,128)}, u32[]{:S(2)}) copy-start(s32[4,8,4]{1,2,0:T(4,128)} %param.12) | copy-start | bytes 1540
  4.1 12.3 %collective-permute-start = (f32[1,8,16,720]{3,2,1,0:T(8,128)S(1)}, f32[1,8,16,720]{3,2,1,0:T(8,128)S(1)}, u32[]{:S(2)}, u32[]{:S(2)}) collective-permute-start(f32[1,8,16,720]{3,2,1,0:T(8,128)S(1)} %get-tuple-element.18), channel_id=1, source_target_pairs={{0,32},{32,64},{64,96},{96,0},{1,33},{33,65},{65,97},{97,1},{2,34}... | collective-permute-start | bytes 1105928 | tf_op jit(solution)/shard_map/ppermute | solution.py:31
  6.3 10.1 %collective-permute-start.1 = (f32[1,8,16,720]{3,2,1,0:T(8,128)S(1)}, f32[1,8,16,720]{3,2,1,0:T(8,128)S(1)}, u32[]{:S(2)}, u32[]{:S(2)}) collective-permute-start(f32[1,8,16,720]{3,2,1,0:T(8,128)S(1)} %get-tuple-element.19), channel_id=1, source_target_pairs={{32,0},{64,32},{96,64},{0,96},{33,1},{65,33},{97,65},{1,97},{34,2}... | collective-permute-start | bytes 1105928 | tf_op jit(solution)/shard_map/ppermute | solution.py:33
  16.4 6.3 %copy-start.7 = (f32[1,8,16,720]{3,2,1,0:T(8,128)}, f32[1,8,16,720]{3,2,1,0:T(8,128)S(1)}, u32[]{:S(2)}) copy-start(f32[1,8,16,720]{3,2,1,0:T(8,128)S(1)} %collective-permute-done.1) | copy-start | bytes 1105924
  16.5 6.2 %collective-permute-start.2 = (f32[6,1,16,720]{3,2,1,0:T(8,128)S(1)}, f32[6,1,16,720]{3,2,1,0:T(8,128)S(1)}, u32[]{:S(2)}, u32[]{:S(2)}) collective-permute-start(f32[6,1,16,720]{3,2,1,0:T(8,128)S(1)} %get-tuple-element.14), channel_id=1, source_target_pairs={{0,1},{1,2},{2,3},{3,4},{4,5},{5,6},{6,7},{7,8},{8,9},{9,10},{10,1... | collective-permute-start | bytes 829448 | tf_op jit(solution)/shard_map/ppermute | solution.py:31
  19.0 6.4 %collective-permute-start.3 = (f32[6,1,16,720]{3,2,1,0:T(8,128)S(1)}, f32[6,1,16,720]{3,2,1,0:T(8,128)S(1)}, u32[]{:S(2)}, u32[]{:S(2)}) collective-permute-start(f32[6,1,16,720]{3,2,1,0:T(8,128)S(1)} %get-tuple-element.15), channel_id=1, source_target_pairs={{1,0},{2,1},{3,2},{4,3},{5,4},{6,5},{7,6},{8,7},{9,8},{10,9},{11,1... | collective-permute-start | bytes 829448 | tf_op jit(solution)/shard_map/ppermute | solution.py:33
  29.9 1.6 %copy-start.10 = (f32[16,16,1,1]{1,0,3,2:T(8,128)S(1)}, f32[16,16,1,1]{1,0,3,2:T(8,128)}, u32[]{:S(2)}) copy-start(f32[16,16,1,1]{1,0,3,2:T(8,128)} %constant.156) | copy-start | bytes 3076
  31.5 1.5 %copy-start.3 = (f32[4,8,16,720]{3,2,1,0:T(8,128)S(1)}, f32[4,8,16,720]{3,2,1,0:T(8,128)}, u32[]{:S(2)}) copy-start(f32[4,8,16,720]{3,2,1,0:T(8,128)} %copy-done.2) | copy-start | bytes 4423684
  31.5 1.5 %copy-start.11 = (f32[16,16,1,1]{1,0,3,2:T(8,128)S(1)}, f32[16,16,1,1]{1,0,3,2:T(8,128)}, u32[]{:S(2)}) copy-start(f32[16,16,1,1]{1,0,3,2:T(8,128)} %constant.155) | copy-start | bytes 3076
  34.8 10.3 %copy-start.4 = (f32[4,8,16,720]{3,2,1,0:T(8,128)}, f32[4,8,16,720]{3,2,1,0:T(8,128)S(1)}, u32[]{:S(2)}) copy-start(f32[4,8,16,720]{3,2,1,0:T(8,128)S(1)} %bitcast_add_fusion.1) | copy-start | bytes 4423684
  34.9 3.0 %copy-start.13 = (s32[4,8,4]{1,2,0:T(4,128)S(1)}, s32[4,8,4]{1,2,0:T(4,128)}, u32[]{:S(2)}) copy-start(s32[4,8,4]{1,2,0:T(4,128)} %param.13) | copy-start | bytes 1540
  34.9 10.1 %collective-permute-start.4 = (f32[1,8,16,720]{3,2,1,0:T(8,128)S(1)}, f32[1,8,16,720]{3,2,1,0:T(8,128)S(1)}, u32[]{:S(2)}, u32[]{:S(2)}) collective-permute-start(f32[1,8,16,720]{3,2,1,0:T(8,128)S(1)} %get-tuple-element.16), channel_id=1, source_target_pairs={{0,32},{32,64},{64,96},{96,0},{1,33},{33,65},{65,97},{97,1},{2,34}... | collective-permute-start | bytes 1105928 | tf_op jit(solution)/shard_map/ppermute | solution.py:31
  36.3 8.8 %collective-permute-start.5 = (f32[1,8,16,720]{3,2,1,0:T(8,128)S(1)}, f32[1,8,16,720]{3,2,1,0:T(8,128)S(1)}, u32[]{:S(2)}, u32[]{:S(2)}) collective-permute-start(f32[1,8,16,720]{3,2,1,0:T(8,128)S(1)} %get-tuple-element.17), channel_id=1, source_target_pairs={{32,0},{64,32},{96,64},{0,96},{33,1},{65,33},{97,65},{1,97},{34,2}... | collective-permute-start | bytes 1105928 | tf_op jit(solution)/shard_map/ppermute | solution.py:33
  45.1 4.2 %copy-start.8 = (f32[1,8,16,720]{3,2,1,0:T(8,128)}, f32[1,8,16,720]{3,2,1,0:T(8,128)S(1)}, u32[]{:S(2)}) copy-start(f32[1,8,16,720]{3,2,1,0:T(8,128)S(1)} %collective-permute-done.5) | copy-start | bytes 1105924
  45.1 16.0 %collective-permute-start.6 = (f32[6,1,16,720]{3,2,1,0:T(8,128)S(1)}, f32[6,1,16,720]{3,2,1,0:T(8,128)S(1)}, u32[]{:S(2)}, u32[]{:S(2)}) collective-permute-start(f32[6,1,16,720]{3,2,1,0:T(8,128)S(1)} %get-tuple-element.12), channel_id=1, source_target_pairs={{0,1},{1,2},{2,3},{3,4},{4,5},{5,6},{6,7},{7,8},{8,9},{9,10},{10,1... | collective-permute-start | bytes 829448 | tf_op jit(solution)/shard_map/ppermute | solution.py:31
  48.0 13.8 %collective-permute-start.7 = (f32[6,1,16,720]{3,2,1,0:T(8,128)S(1)}, f32[6,1,16,720]{3,2,1,0:T(8,128)}, u32[]{:S(2)}, u32[]{:S(2)}) collective-permute-start(f32[6,1,16,720]{3,2,1,0:T(8,128)S(1)} %get-tuple-element.13), channel_id=1, source_target_pairs={{1,0},{2,1},{3,2},{4,3},{5,4},{6,5},{7,6},{8,7},{9,8},{10,9},{11,1... | collective-permute-start | bytes 829448 | tf_op jit(solution)/shard_map/ppermute | solution.py:33
  50.0 22.9 %all-to-all-start = ((s32[128,1,1]{2,1,0:T(1,128)}), s32[128,1,1]{2,1,0:T(1,128)S(1)}, u32[]{:S(2)}, u32[]{:S(2)}) async-start(s32[128,1,1]{2,1,0:T(1,128)} %copy.53), calls=%async_computation | async-start | bytes 131072 | tf_op jit(solution)/shard_map/all_to_all | solution.py:231
  66.4 1.9 %copy-start.5 = (f32[4,8,16,720]{3,2,1,0:T(8,128)S(1)}, f32[4,8,16,720]{3,2,1,0:T(8,128)}, u32[]{:S(2)}) copy-start(f32[4,8,16,720]{3,2,1,0:T(8,128)} %copy-done.4) | copy-start | bytes 4423684
  68.3 1.5 %copy-start.14 = (f32[4,16,1,1]{1,0,3,2:T(4,128)S(1)}, f32[4,16,1,1]{1,0,3,2:T(4,128)}, u32[]{:S(2)}) copy-start(f32[4,16,1,1]{1,0,3,2:T(4,128)} %constant.157) | copy-start | bytes 772
  69.8 1.9 %copy-start.6 = (f32[4,8,16,720]{3,2,1,0:T(8,128)}, f32[4,8,16,720]{3,2,1,0:T(8,128)S(1)}, u32[]{:S(2)}) copy-start(f32[4,8,16,720]{3,2,1,0:T(8,128)S(1)} %fusion) | copy-start | bytes 4423684
  71.8 24.7 %copy-start.1 = (s32[128]{0:T(128)S(1)}, s32[128]{0:T(128)}, u32[]{:S(2)}) copy-start(s32[128]{0:T(128)} %param.14) | copy-start | bytes 1540
  72.9 22.0 %all-to-all-start.1 = ((f32[128,1,720]{2,1,0:T(1,128)}), f32[128,1,720]{2,1,0:T(1,128)S(1)}, u32[]{:S(2)}, u32[]{:S(2)}) async-start(f32[128,1,720]{2,1,0:T(1,128)} %copy.54), calls=%async_computation.1 | async-start | bytes 786432 | tf_op jit(solution)/shard_map/all_to_all | solution.py:224
  96.4 2.5 %copy-start = (bf16[10,32,64,128]{3,2,1,0:T(8,128)(2,1)S(1)}, bf16[10,32,64,128]{3,2,1,0:T(8,128)(2,1)}, u32[]{:S(2)}) copy-start(bf16[10,32,64,128]{3,2,1,0:T(8,128)(2,1)} %state_hbm.1) | copy-start | bytes 15728644
  (2 other events, 2.2 us)
where the time goes:
time: 135 us
  starting transfers between devices  32.9 us (24%)
  waiting for transfers between devices  28.5 us (21%)
  Pallas kernels  18.4 us (14%)
  local copies, waits for them, and re-layouts  18 us (13%)
  blocking collectives  14.9 us (11%)
  other arithmetic  12.3 us (9%)
  matrix products  9.12 us (7%)
    pallas_call x1, Pallas kernels, crm_run(): pl.pallas_call(crm_kernel, out_shape=(jax.ShapeDtypeStruct(state.shape, j...  18.4 us
    ppermute x4, waiting for transfers between devices, extended_2(): lax.ppermute(tail, axis, [(i, (i + 1) % count) for i in range(count)])  15.9 us
    all_to_all x1, blocking collectives, per_device(): lax.all_to_all(tend_rows.reshape(ndev, count, NFLD * CLEV), ('face', 'col...  14.9 us
    all_to_all x1, starting transfers between devices, per_device(): lax.all_to_all(out_keys.reshape(ndev, count), ('face', 'col'), split_axis...  11.1 us
    all_to_all x1, waiting for transfers between devices, per_device(): lax.all_to_all(outgoing.reshape(ndev, count, width), ('face', 'col'), spl...  9.82 us
    all_to_all x1, starting transfers between devices, per_device(): lax.all_to_all(outgoing.reshape(ndev, count, width), ('face', 'col'), spl...  9.76 us
    ppermute x4, starting transfers between devices, extended_2(): lax.ppermute(tail, axis, [(i, (i + 1) % count) for i in range(count)])  9.01 us
    gather x2, local copies, waits for them, and re-layouts, per_device(): jnp.take(extended.reshape(-1, width), index_flat, axis=0)  5.19 us
  transfers between devices with their start and end apart: 10, of which 5 were waited for; matrix products, arithmetic and copies ran while one was open for 14% of the time, Pallas kernels for 0%

commit v1 on v0

--- a/solution.py
+++ b/solution.py
@@ -179,6 +179,20 @@
         ],
         compiler_params=pltpu.CompilerParams(vmem_limit_bytes=48 * 1024 * 1024),
     )(forcing, active.reshape(1, ncol), state)
+
+
+TWO_STAGE = False
+
+
+def exchange(chunks):
+    if not TWO_STAGE:
+        return lax.all_to_all(chunks, ("face", "col"), split_axis=0, concat_axis=0, tiled=True)
+    nface = lax.axis_size("face")
+    ncol = lax.axis_size("col")
+    grid = chunks.reshape((nface, ncol) + chunks.shape[1:])
+    grid = lax.all_to_all(grid, "col", split_axis=1, concat_axis=1, tiled=True)
+    grid = lax.all_to_all(grid, "face", split_axis=0, concat_axis=0, tiled=True)
+    return grid.reshape(chunks.shape)
 
 
 def per_device(dyn_state, edge_links, phys_slot, crm_active, crm_state):
@@ -211,39 +225,27 @@
         )
         summed = jnp.einsum("nm,rcmw->rcnw", spread, matched, precision=lax.Precision.HIGHEST)
         state = (state + summed) / denom[None, None, :, None]
-    columns = jnp.einsum("qn,rcnw->rcqw", quarter, state, precision=lax.Precision.HIGHEST).reshape(
-        -1, width
+    cut = state.reshape(rows_dev, cols_dev, nodes, NFLD, LEV)[..., :CLEV].reshape(
+        rows_dev, cols_dev, nodes, NFLD * CLEV
+    )
+    columns = jnp.einsum("qn,rcnw->rcqw", quarter, cut, precision=lax.Precision.HIGHEST).reshape(
+        -1, NFLD * CLEV
     )
     per_dev = columns.shape[0]
     count = per_dev // ndev
     keys_local = phys_slot.reshape(-1)
     order = jnp.argsort(keys_local, stable=True)
-    outgoing = columns[order]
     out_keys = keys_local[order]
-    arrived, arrived_keys = (
-        lax.all_to_all(
-            outgoing.reshape(ndev, count, width),
-            ("face", "col"),
-            split_axis=0,
-            concat_axis=0,
-            tiled=True,
-        ),
-        lax.all_to_all(
-            out_keys.reshape(ndev, count), ("face", "col"), split_axis=0, concat_axis=0, tiled=True
-        ),
-    )
-    slots = arrived_keys.reshape(-1) % per_dev
-    physics = jnp.zeros((per_dev, width), jnp.float32).at[slots].set(arrived.reshape(-1, width))
-    forcing = physics.reshape(per_dev, NFLD, LEV)[:, :, :CLEV].transpose(1, 2, 0)
+    outgoing = jnp.concatenate(
+        [columns[order], out_keys.astype(jnp.float32)[:, None]], axis=1
+    )
+    arrived = exchange(outgoing.reshape(ndev, count, NFLD * CLEV + 1)).reshape(per_dev, -1)
+    slots = arrived[:, NFLD * CLEV].astype(jnp.int32) % per_dev
+    physics = jnp.zeros((per_dev, NFLD * CLEV), jnp.float32).at[slots].set(arrived[:, : NFLD * CLEV])
+    forcing = physics.reshape(per_dev, NFLD, CLEV).transpose(1, 2, 0)
     crm_new, tend = crm_run(crm_state, forcing, crm_active)
     tend_rows = tend.reshape(NFLD * CLEV, per_dev).T[slots]
-    returned = lax.all_to_all(
-        tend_rows.reshape(ndev, count, NFLD * CLEV),
-        ("face", "col"),
-        split_axis=0,
-        concat_axis=0,
-        tiled=True,
-    )
+    returned = exchange(tend_rows.reshape(ndev, count, NFLD * CLEV))
     placed = (
         jnp.zeros((per_dev, NFLD * CLEV), jnp.float32)
         .at[order]

time: 135 us -> 134 us (level)
  blocking collectives: 14.9 us -> 37.3 us
  starting transfers between devices: 32.9 us -> 12.2 us
  waiting for transfers between devices: 28.5 us -> 22.8 us
  local copies, waits for them, and re-layouts: 18 us -> 23.2 us
  other arithmetic: 12.3 us -> 10 us
    all_to_all x1 -> x2, blocking collectives: 14.9 us -> 37.3 us  [exchange(): lax.all_to_all(chunks, ('face', 'col'), split_axis=0, concat_axis=0, tile...]
    all_to_all x2 -> x0, starting transfers between devices: 20.9 us -> none  [the longest x1 11.1 us: per_device(): lax.all_to_all(out_keys.reshape(ndev, count), ('face', 'col'), split_axis...]
    all_to_all x2 -> x0, waiting for transfers between devices: 9.82 us -> none  [the longest x1 9.82 us: per_device(): lax.all_to_all(outgoing.reshape(ndev, count, width), ('face', 'col'), spl...]
    reshape x3 -> x5, local copies, waits for them, and re-layouts: 1.49 us -> 7.24 us  [the longest x2 6.76 us: per_device(): state.reshape(rows_dev, cols_dev, nodes, NFLD, LEV)[..., :CLEV]]
    all_to_all x1 -> x0, other arithmetic: 2.35 us -> none  [per_device(): lax.all_to_all(out_keys.reshape(ndev, count), ('face', 'col'), split_axis...]
    ppermute x4, waiting for transfers between devices: 15.9 us -> 18 us  [extended_2(): lax.ppermute(tail, axis, [(i, (i + 1) % count) for i in range(count)])]
    ppermute x4, waiting for transfers between devices: 2.78 us -> 4.83 us  [extended_2(): lax.ppermute(head, axis, [((i + 1) % count, i) for i in range(count)])]
  transfers between devices with their start and end apart: 10 -> 8, of which waited for: 5 -> 6; matrix products, arithmetic and copies ran while one was open for 14% -> 4% of each run, Pallas kernels for 0% -> 0%
where the time goes in v1:
time: 134 us
  blocking collectives  37.3 us (28%)
  local copies, waits for them, and re-layouts  23.2 us (17%)
  waiting for transfers between devices  22.8 us (17%)
  Pallas kernels  18.4 us (14%)
  starting transfers between devices  12.2 us (9%)
  other arithmetic  10 us (7%)
  matrix products  8.71 us (7%)
    all_to_all x2, blocking collectives, exchange(): lax.all_to_all(chunks, ('face', 'col'), split_axis=0, concat_axis=0, tile...  37.3 us
    pallas_call x1, Pallas kernels, crm_run(): pl.pallas_call(crm_kernel, out_shape=(jax.ShapeDtypeStruct(state.shape, j...  18.4 us
    ppermute x4, waiting for transfers between devices, extended_2(): lax.ppermute(tail, axis, [(i, (i + 1) % count) for i in range(count)])  18 us
    ppermute x4, starting transfers between devices, extended_2(): lax.ppermute(tail, axis, [(i, (i + 1) % count) for i in range(count)])  9.01 us
    reshape x2, local copies, waits for them, and re-layouts, per_device(): state.reshape(rows_dev, cols_dev, nodes, NFLD, LEV)[..., :CLEV]  6.76 us
    gather x2, local copies, waits for them, and re-layouts, per_device(): jnp.take(extended.reshape(-1, width), index_flat, axis=0)  5.19 us
    dot_general x2, matrix products, per_device(): jnp.einsum('nm,rcmw->rcnw', laplace, state, precision=lax.Precision.HIGHEST)  5.18 us
    ppermute x4, waiting for transfers between devices, extended_2(): lax.ppermute(head, axis, [((i + 1) % count, i) for i in range(count)])  4.83 us
  transfers between devices with their start and end apart: 8, of which 6 were waited for; matrix products, arithmetic and copies ran while one was open for 4% of the time, Pallas kernels for 0%

profile of v1, /device:TPU:1, one launch (start us, length us, event | category | flops | bytes accessed | tf_op | source)
XLA Modules:
  0.0 133.8 jit_solution(12105279047208052384)
XLA Ops:
  0.6 3.4 %bitcast_add_fusion.3 = f32[4,8,16,720]{3,2,1,0:T(8,128)S(1)} fusion(f32[4,8,16,720]{3,2,1,0:T(8,128)} %param.11, f32[16,16,1,1]{1,0,3,2:T(8,128)} %constant.154), kind=kOutput, calls=%fused_computation.14 | convolution fusion | flops 71516160 | bytes 2950144 | tf_op jit(solution)/shard_map/nm,rcmw->rcnw/dot_general | solution.py:219
  4.1 2.2 %collective-permute-start = (f32[1,8,16,720]{3,2,1,0:T(8,128)S(1)}, f32[1,8,16,720]{3,2,1,0:T(8,128)S(1)}, u32[]{:S(2)}, u32[]{:S(2)}) collective-permute-start(f32[1,8,16,720]{3,2,1,0:T(8,128)S(1)} %get-tuple-element.18), channel_id=1, source_target_pairs={{0,32},{32,64},{64,96},{96,0},{1,33},{33,65},{65,97},{97,1},{2,34}... | collective-permute-start | bytes 1105928 | tf_op jit(solution)/shard_map/ppermute | solution.py:31
  8.7 7.7 %collective-permute-done = f32[1,8,16,720]{3,2,1,0:T(8,128)S(1)} collective-permute-done((f32[1,8,16,720]{3,2,1,0:T(8,128)S(1)}, f32[1,8,16,720]{3,2,1,0:T(8,128)S(1)}, u32[]{:S(2)}, u32[]{:S(2)}) %collective-permute-start) | collective-permute-done | bytes 368672 | tf_op jit(solution)/shard_map/ppermute | solution.py:31
  16.5 2.5 %collective-permute-start.2 = (f32[6,1,16,720]{3,2,1,0:T(8,128)S(1)}, f32[6,1,16,720]{3,2,1,0:T(8,128)S(1)}, u32[]{:S(2)}, u32[]{:S(2)}) collective-permute-start(f32[6,1,16,720]{3,2,1,0:T(8,128)S(1)} %get-tuple-element.14), channel_id=1, source_target_pairs={{0,1},{1,2},{2,3},{3,4},{4,5},{5,6},{6,7},{7,8},{8,9},{9,10},{10,1... | collective-permute-start | bytes 829448 | tf_op jit(solution)/shard_map/ppermute | solution.py:31
  19.1 3.6 %collective-permute-done.2 = f32[6,1,16,720]{3,2,1,0:T(8,128)S(1)} collective-permute-done((f32[6,1,16,720]{3,2,1,0:T(8,128)S(1)}, f32[6,1,16,720]{3,2,1,0:T(8,128)S(1)}, u32[]{:S(2)}, u32[]{:S(2)}) %collective-permute-start.2) | collective-permute-done | bytes 276512 | tf_op jit(solution)/shard_map/ppermute | solution.py:31
  22.7 2.8 %collective-permute-done.3 = f32[6,1,16,720]{3,2,1,0:T(8,128)S(1)} collective-permute-done((f32[6,1,16,720]{3,2,1,0:T(8,128)S(1)}, f32[6,1,16,720]{3,2,1,0:T(8,128)S(1)}, u32[]{:S(2)}, u32[]{:S(2)}) %collective-permute-start.3) | collective-permute-done | bytes 276512 | tf_op jit(solution)/shard_map/ppermute | solution.py:33
  25.5 1.8 %pad_maximum_fusion = f32[6,10,16,720]{3,2,1,0:T(8,128)S(1)} fusion(f32[6,1,16,720]{3,2,1,0:T(8,128)S(1)} %collective-permute-done.3, f32[1,8,16,720]{3,2,1,0:T(8,128)} %copy-done.7, f32[4,8,16,720]{3,2,1,0:T(8,128)} %copy-done.2, f32[1,8,16,720]{3,2,1,0:T(8,128)S(1)} %collective-permute-done, f32[6,1,16,720]{3,2,1,0:T(8,128)S(1)} %collective-permute-done.2), kind=kLoop, calls=%fused_computation.7 | loop fusion | flops 2764800 | bytes 5529600 | tf_op jit(solution)/shard_map/concatenate | solution.py:29
  27.3 2.6 %gather_fusion.3 = f32[512,720]{1,0:T(8,128)} fusion(f32[960,720]{1,0:T(8,128)S(1)} %bitcast.67, s32[1024]{0:T(1024)S(1)} %pad_clamp_fusion.2), kind=kCustom, calls=%fused_computation.clone | custom fusion | bytes 2951168 | tf_op jit(solution)/shard_map/jit(_take)/gather | solution.py:223
  29.9 1.6 %broadcast_select_fusion.1 = f32[512,720]{1,0:T(8,128)S(1)} fusion(f32[512,720]{1,0:T(8,128)} %gather_fusion.3, pred[512]{0:T(512)(128)(4,1)S(1)} %compare_and_fusion), kind=kLoop, calls=%fused_computation.17 | loop fusion | flops 368640 | bytes 2949632 | tf_op jit(solution)/shard_map/jit(_take)/select_n | solution.py:223
  33.0 1.8 %bitcast_add_fusion.1 = f32[4,8,16,720]{3,2,1,0:T(8,128)S(1)} fusion(f32[16,16,1,1]{1,0,3,2:T(8,128)S(1)} %copy-done.11, f32[4,8,16,720]{3,2,1,0:T(8,128)S(1)} %copy-done.3, f32[4,8,720,16]{2,3,1,0:T(8,128)S(1)} %fusion.33, f32[16]{0:T(128)S(1)} %copy-done.15), kind=kOutput, calls=%fused_computation.11 | convolution fusion | flops 72990720 | bytes 4424768 | tf_op jit(solution)/shard_map/nm,rcmw->rcnw/dot_general | solution.py:219
  38.0 2.5 %sort.17 = (s32[128]{0:T(128)}, s32[128]{0:T(128)S(1)}) sort(s32[128]{0:T(128)S(1)} %reshape.89, s32[128]{0:T(128)S(1)} %iota.35), dimensions={0}, to_apply=%region_0.2 | sort | flops 896 | bytes 2048 | tf_op jit(solution)/shard_map/jit(argsort)/sort | solution.py:237
  40.6 4.5 %collective-permute-done.4 = f32[1,8,16,720]{3,2,1,0:T(8,128)S(1)} collective-permute-done((f32[1,8,16,720]{3,2,1,0:T(8,128)S(1)}, f32[1,8,16,720]{3,2,1,0:T(8,128)S(1)}, u32[]{:S(2)}, u32[]{:S(2)}) %collective-permute-start.4) | collective-permute-done | bytes 368672 | tf_op jit(solution)/shard_map/ppermute | solution.py:31
  45.1 2.9 %collective-permute-start.6 = (f32[6,1,16,720]{3,2,1,0:T(8,128)S(1)}, f32[6,1,16,720]{3,2,1,0:T(8,128)S(1)}, u32[]{:S(2)}, u32[]{:S(2)}) collective-permute-start(f32[6,1,16,720]{3,2,1,0:T(8,128)S(1)} %get-tuple-element.12), channel_id=1, source_target_pairs={{0,1},{1,2},{2,3},{3,4},{4,5},{5,6},{6,7},{7,8},{8,9},{9,10},{10,1... | collective-permute-start | bytes 829448 | tf_op jit(solution)/shard_map/ppermute | solution.py:31
  49.6 2.1 %collective-permute-done.6 = f32[6,1,16,720]{3,2,1,0:T(8,128)S(1)} collective-permute-done((f32[6,1,16,720]{3,2,1,0:T(8,128)S(1)}, f32[6,1,16,720]{3,2,1,0:T(8,128)S(1)}, u32[]{:S(2)}, u32[]{:S(2)}) %collective-permute-start.6) | collective-permute-done | bytes 276512 | tf_op jit(solution)/shard_map/ppermute | solution.py:31
  52.4 2.0 %collective-permute-done.7 = f32[6,1,16,720]{3,2,1,0:T(8,128)} collective-permute-done((f32[6,1,16,720]{3,2,1,0:T(8,128)S(1)}, f32[6,1,16,720]{3,2,1,0:T(8,128)}, u32[]{:S(2)}, u32[]{:S(2)}) %collective-permute-start.7) | collective-permute-done | bytes 276512 | tf_op jit(solution)/shard_map/ppermute | solution.py:33
  54.5 1.9 %pad_maximum_fusion.1 = f32[6,10,16,720]{3,2,1,0:T(8,128)S(1)} fusion(f32[6,1,16,720]{3,2,1,0:T(8,128)} %collective-permute-done.7, f32[1,8,16,720]{3,2,1,0:T(8,128)} %copy-done.8, f32[4,8,16,720]{3,2,1,0:T(8,128)} %copy-done.4, f32[1,8,16,720]{3,2,1,0:T(8,128)S(1)} %collective-permute-done.4, f32[6,1,16,720]{3,2,1,0:T(8,128)} %copy-done.9), kind=kLoop, calls=%fused_computation.8 | loop fusion | flops 2764800 | bytes 5529600 | tf_op jit(solution)/shard_map/concatenate | solution.py:29
  56.4 2.6 %gather_fusion.4 = f32[512,720]{1,0:T(8,128)} fusion(f32[960,720]{1,0:T(8,128)S(1)} %bitcast.66, s32[1024]{0:T(1024)S(1)} %pad_clamp_fusion.2), kind=kCustom, calls=%fused_computation.1.clone | custom fusion | bytes 2951168 | tf_op jit(solution)/shard_map/jit(_take)/gather | solution.py:223
  59.0 1.7 %broadcast_select_fusion = f32[512,720]{1,0:T(8,128)S(1)} fusion(f32[512,720]{1,0:T(8,128)} %gather_fusion.4, pred[512]{0:T(512)(128)(4,1)S(1)} %compare_and_fusion), kind=kLoop, calls=%fused_computation.16 | loop fusion | flops 368640 | bytes 2949632 | tf_op jit(solution)/shard_map/jit(_take)/select_n | solution.py:223
  62.4 3.5 %reshape.90 = f32[4,8,16,10,72]{4,3,2,1,0:T(8,128)} reshape(f32[4,8,16,720]{3,2,1,0:T(8,128)S(1)} %fusion) | data formatting | bytes 2949120 | tf_op jit(solution)/shard_map/reshape | solution.py:228
  66.0 3.2 %reshape.91 = f32[4,8,16,320]{3,2,1,0:T(8,128)S(1)} reshape(f32[4,8,16,10,32]{4,3,2,1,0:T(8,128)} %bitcast.68) | data formatting | bytes 1310720 | tf_op jit(solution)/shard_map/reshape | solution.py:228
  70.9 22.7 %all_to_all.10 = f32[128,1,321]{2,1,0:T(1,128)S(1)} all-to-all(f32[128,1,321]{2,1,0:T(1,128)S(1)} %copy.44), channel_id=1, replica_groups=mesh['face'=4,'col'=32] {'face','col'}, dimensions={0} | all-to-all | bytes 328704 | tf_op jit(solution)/shard_map/all_to_all | solution.py:189
  95.3 2.5 %copy-done = bf16[10,32,64,128]{3,2,1,0:T(8,128)(2,1)S(1)} copy-done((bf16[10,32,64,128]{3,2,1,0:T(8,128)(2,1)S(1)}, bf16[10,32,64,128]{3,2,1,0:T(8,128)(2,1)}, u32[]{:S(2)}) %copy-start) | copy-done | bytes 5242904
  97.8 18.4 %shard_map.112 = (bf16[10,32,64,128]{3,2,1,0:T(8,128)(2,1)}, f32[10,32,128]{2,1,0:T(8,128)S(1)}) custom-call(f32[10,32,128]{2,1,0:T(8,128)S(1)} %bitcast.63, s32[1,128]{1,0:T(1,128)S(1)} %bitcast.65, bf16[10,32,64,128]{3,2,1,0:T(8,128)(2,1)S(1)} %copy-done), custom_call_target="tpu_custom_call" | custom-call | tf_op jit(solution)/shard_map/pallas_call | solution.py:158
  117.3 14.6 %all_to_all.11 = f32[128,1,320]{2,1,0:T(1,128)S(1)} all-to-all(f32[128,1,320]{2,1,0:T(1,128)S(1)} %copy.49), channel_id=1, replica_groups=mesh['face'=4,'col'=32] {'face','col'}, dimensions={0} | all-to-all | bytes 327680 | tf_op jit(solution)/shard_map/all_to_all | solution.py:189
  (84 shorter events, 17.4 us)
Async XLA Ops:
  4.0 12.5 %copy-start.2 = (f32[4,8,16,720]{3,2,1,0:T(8,128)}, f32[4,8,16,720]{3,2,1,0:T(8,128)S(1)}, u32[]{:S(2)}) copy-start(f32[4,8,16,720]{3,2,1,0:T(8,128)S(1)} %bitcast_add_fusion.3) | copy-start | bytes 4423684
  4.0 3.8 %copy-start.12 = (s32[4,8,4]{1,2,0:T(4,128)S(1)}, s32[4,8,4]{1,2,0:T(4,128)}, u32[]{:S(2)}) copy-start(s32[4,8,4]{1,2,0:T(4,128)} %param.12) | copy-start | bytes 1540
  4.1 12.3 %collective-permute-start = (f32[1,8,16,720]{3,2,1,0:T(8,128)S(1)}, f32[1,8,16,720]{3,2,1,0:T(8,128)S(1)}, u32[]{:S(2)}, u32[]{:S(2)}) collective-permute-start(f32[1,8,16,720]{3,2,1,0:T(8,128)S(1)} %get-tuple-element.18), channel_id=1, source_target_pairs={{0,32},{32,64},{64,96},{96,0},{1,33},{33,65},{65,97},{97,1},{2,34}... | collective-permute-start | bytes 1105928 | tf_op jit(solution)/shard_map/ppermute | solution.py:31
  6.3 10.1 %collective-permute-start.1 = (f32[1,8,16,720]{3,2,1,0:T(8,128)S(1)}, f32[1,8,16,720]{3,2,1,0:T(8,128)S(1)}, u32[]{:S(2)}, u32[]{:S(2)}) collective-permute-start(f32[1,8,16,720]{3,2,1,0:T(8,128)S(1)} %get-tuple-element.19), channel_id=1, source_target_pairs={{32,0},{64,32},{96,64},{0,96},{33,1},{65,33},{97,65},{1,97},{34,2}... | collective-permute-start | bytes 1105928 | tf_op jit(solution)/shard_map/ppermute | solution.py:33
  16.4 6.3 %copy-start.7 = (f32[1,8,16,720]{3,2,1,0:T(8,128)}, f32[1,8,16,720]{3,2,1,0:T(8,128)S(1)}, u32[]{:S(2)}) copy-start(f32[1,8,16,720]{3,2,1,0:T(8,128)S(1)} %collective-permute-done.1) | copy-start | bytes 1105924
  16.5 6.2 %collective-permute-start.2 = (f32[6,1,16,720]{3,2,1,0:T(8,128)S(1)}, f32[6,1,16,720]{3,2,1,0:T(8,128)S(1)}, u32[]{:S(2)}, u32[]{:S(2)}) collective-permute-start(f32[6,1,16,720]{3,2,1,0:T(8,128)S(1)} %get-tuple-element.14), channel_id=1, source_target_pairs={{0,1},{1,2},{2,3},{3,4},{4,5},{5,6},{6,7},{7,8},{8,9},{9,10},{10,1... | collective-permute-start | bytes 829448 | tf_op jit(solution)/shard_map/ppermute | solution.py:31
  19.0 6.4 %collective-permute-start.3 = (f32[6,1,16,720]{3,2,1,0:T(8,128)S(1)}, f32[6,1,16,720]{3,2,1,0:T(8,128)S(1)}, u32[]{:S(2)}, u32[]{:S(2)}) collective-permute-start(f32[6,1,16,720]{3,2,1,0:T(8,128)S(1)} %get-tuple-element.15), channel_id=1, source_target_pairs={{1,0},{2,1},{3,2},{4,3},{5,4},{6,5},{7,6},{8,7},{9,8},{10,9},{11,1... | collective-permute-start | bytes 829448 | tf_op jit(solution)/shard_map/ppermute | solution.py:33
  29.9 1.6 %copy-start.10 = (f32[16,16,1,1]{1,0,3,2:T(8,128)S(1)}, f32[16,16,1,1]{1,0,3,2:T(8,128)}, u32[]{:S(2)}) copy-start(f32[16,16,1,1]{1,0,3,2:T(8,128)} %constant.155) | copy-start | bytes 3076
  31.5 1.5 %copy-start.3 = (f32[4,8,16,720]{3,2,1,0:T(8,128)S(1)}, f32[4,8,16,720]{3,2,1,0:T(8,128)}, u32[]{:S(2)}) copy-start(f32[4,8,16,720]{3,2,1,0:T(8,128)} %copy-done.2) | copy-start | bytes 4423684
  31.5 1.5 %copy-start.11 = (f32[16,16,1,1]{1,0,3,2:T(8,128)S(1)}, f32[16,16,1,1]{1,0,3,2:T(8,128)}, u32[]{:S(2)}) copy-start(f32[16,16,1,1]{1,0,3,2:T(8,128)} %constant.154) | copy-start | bytes 3076
  31.5 1.5 %copy-start.15 = (f32[16]{0:T(128)S(1)}, f32[16]{0:T(128)}, u32[]{:S(2)}) copy-start(f32[16]{0:T(128)} %constant.152) | copy-start | bytes 196
  34.8 10.3 %copy-start.4 = (f32[4,8,16,720]{3,2,1,0:T(8,128)}, f32[4,8,16,720]{3,2,1,0:T(8,128)S(1)}, u32[]{:S(2)}) copy-start(f32[4,8,16,720]{3,2,1,0:T(8,128)S(1)} %bitcast_add_fusion.1) | copy-start | bytes 4423684
  34.9 3.0 %copy-start.13 = (s32[4,8,4]{1,2,0:T(4,128)S(1)}, s32[4,8,4]{1,2,0:T(4,128)}, u32[]{:S(2)}) copy-start(s32[4,8,4]{1,2,0:T(4,128)} %param.13) | copy-start | bytes 1540
  34.9 10.1 %collective-permute-start.4 = (f32[1,8,16,720]{3,2,1,0:T(8,128)S(1)}, f32[1,8,16,720]{3,2,1,0:T(8,128)S(1)}, u32[]{:S(2)}, u32[]{:S(2)}) collective-permute-start(f32[1,8,16,720]{3,2,1,0:T(8,128)S(1)} %get-tuple-element.16), channel_id=1, source_target_pairs={{0,32},{32,64},{64,96},{96,0},{1,33},{33,65},{65,97},{97,1},{2,34}... | collective-permute-start | bytes 1105928 | tf_op jit(solution)/shard_map/ppermute | solution.py:31
  36.3 8.8 %collective-permute-start.5 = (f32[1,8,16,720]{3,2,1,0:T(8,128)S(1)}, f32[1,8,16,720]{3,2,1,0:T(8,128)S(1)}, u32[]{:S(2)}, u32[]{:S(2)}) collective-permute-start(f32[1,8,16,720]{3,2,1,0:T(8,128)S(1)} %get-tuple-element.17), channel_id=1, source_target_pairs={{32,0},{64,32},{96,64},{0,96},{33,1},{65,33},{97,65},{1,97},{34,2}... | collective-permute-start | bytes 1105928 | tf_op jit(solution)/shard_map/ppermute | solution.py:33
  45.1 4.4 %copy-start.8 = (f32[1,8,16,720]{3,2,1,0:T(8,128)}, f32[1,8,16,720]{3,2,1,0:T(8,128)S(1)}, u32[]{:S(2)}) copy-start(f32[1,8,16,720]{3,2,1,0:T(8,128)S(1)} %collective-permute-done.5) | copy-start | bytes 1105924
  45.1 6.6 %collective-permute-start.6 = (f32[6,1,16,720]{3,2,1,0:T(8,128)S(1)}, f32[6,1,16,720]{3,2,1,0:T(8,128)S(1)}, u32[]{:S(2)}, u32[]{:S(2)}) collective-permute-start(f32[6,1,16,720]{3,2,1,0:T(8,128)S(1)} %get-tuple-element.12), channel_id=1, source_target_pairs={{0,1},{1,2},{2,3},{3,4},{4,5},{5,6},{6,7},{7,8},{8,9},{9,10},{10,1... | collective-permute-start | bytes 829448 | tf_op jit(solution)/shard_map/ppermute | solution.py:31
  48.0 6.4 %collective-permute-start.7 = (f32[6,1,16,720]{3,2,1,0:T(8,128)S(1)}, f32[6,1,16,720]{3,2,1,0:T(8,128)}, u32[]{:S(2)}, u32[]{:S(2)}) collective-permute-start(f32[6,1,16,720]{3,2,1,0:T(8,128)S(1)} %get-tuple-element.13), channel_id=1, source_target_pairs={{1,0},{2,1},{3,2},{4,3},{5,4},{6,5},{7,6},{8,7},{9,8},{10,9},{11,1... | collective-permute-start | bytes 829448 | tf_op jit(solution)/shard_map/ppermute | solution.py:33
  51.7 0.7 copy-start.9
  59.0 1.9 %copy-start.5 = (f32[4,8,16,720]{3,2,1,0:T(8,128)S(1)}, f32[4,8,16,720]{3,2,1,0:T(8,128)}, u32[]{:S(2)}) copy-start(f32[4,8,16,720]{3,2,1,0:T(8,128)} %copy-done.4) | copy-start | bytes 4423684
  62.4 3.6 %copy-start.6 = (f32[4,8,16,720]{3,2,1,0:T(8,128)}, f32[4,8,16,720]{3,2,1,0:T(8,128)S(1)}, u32[]{:S(2)}) copy-start(f32[4,8,16,720]{3,2,1,0:T(8,128)S(1)} %fusion) | copy-start | bytes 4423684
  66.0 3.2 %copy-start.14 = (f32[4,16,1,1]{1,0,3,2:T(4,128)S(1)}, f32[4,16,1,1]{1,0,3,2:T(4,128)}, u32[]{:S(2)}) copy-start(f32[4,16,1,1]{1,0,3,2:T(4,128)} %constant.156) | copy-start | bytes 772
  70.6 24.7 %copy-start.1 = (s32[128]{0:T(128)S(1)}, s32[128]{0:T(128)}, u32[]{:S(2)}) copy-start(s32[128]{0:T(128)} %param.14) | copy-start | bytes 1540
  95.3 2.5 %copy-start = (bf16[10,32,64,128]{3,2,1,0:T(8,128)(2,1)S(1)}, bf16[10,32,64,128]{3,2,1,0:T(8,128)(2,1)}, u32[]{:S(2)}) copy-start(bf16[10,32,64,128]{3,2,1,0:T(8,128)(2,1)} %state_hbm.1) | copy-start | bytes 15728644

commit v2 on v1

--- a/solution.py
+++ b/solution.py
@@ -181,7 +181,7 @@
     )(forcing, active.reshape(1, ncol), state)
 
 
-TWO_STAGE = False
+TWO_STAGE = True
 
 
 def exchange(chunks):
@@ -225,12 +225,9 @@
         )
         summed = jnp.einsum("nm,rcmw->rcnw", spread, matched, precision=lax.Precision.HIGHEST)
         state = (state + summed) / denom[None, None, :, None]
-    cut = state.reshape(rows_dev, cols_dev, nodes, NFLD, LEV)[..., :CLEV].reshape(
-        rows_dev, cols_dev, nodes, NFLD * CLEV
-    )
-    columns = jnp.einsum("qn,rcnw->rcqw", quarter, cut, precision=lax.Precision.HIGHEST).reshape(
-        -1, NFLD * CLEV
-    )
+    columns = jnp.einsum("qn,rcnw->rcqw", quarter, state, precision=lax.Precision.HIGHEST).reshape(
+        -1, NFLD, LEV
+    )[:, :, :CLEV].reshape(-1, NFLD * CLEV)
     per_dev = columns.shape[0]
     count = per_dev // ndev
     keys_local = phys_slot.reshape(-1)

time: 134 us -> 140 us (1.045)
  blocking collectives: 37.3 us -> 49.1 us
  local copies, waits for them, and re-layouts: 23.2 us -> 16.8 us
    all_to_all x2 -> x4, blocking collectives: 37.3 us -> 49.1 us  [the longest x2 31.7 us: exchange(): grid = lax.all_to_all(grid, 'col', split_axis=1, concat_axis=1, tiled=True)]
    reshape x5 -> x2, local copies, waits for them, and re-layouts: 7.24 us -> 0.71 us  [the longest x1 0.59 us: per_device(): jnp.einsum('qn,rcnw->rcqw', quarter, state, precision=lax.Precision.HIGHEST)]
where the time goes in v2:
time: 140 us
  blocking collectives  49.1 us (35%)
  waiting for transfers between devices  22.8 us (16%)
  Pallas kernels  18.4 us (13%)
  local copies, waits for them, and re-layouts  16.8 us (12%)
  starting transfers between devices  12.2 us (9%)
  other arithmetic  10.2 us (7%)
  matrix products  9.12 us (7%)
    all_to_all x2, blocking collectives, exchange(): grid = lax.all_to_all(grid, 'col', split_axis=1, concat_axis=1, tiled=True)  31.7 us
    pallas_call x1, Pallas kernels, crm_run(): pl.pallas_call(crm_kernel, out_shape=(jax.ShapeDtypeStruct(state.shape, j...  18.4 us
    ppermute x4, waiting for transfers between devices, extended_2(): lax.ppermute(tail, axis, [(i, (i + 1) % count) for i in range(count)])  17.9 us
    all_to_all x2, blocking collectives, exchange(): grid = lax.all_to_all(grid, 'face', split_axis=0, concat_axis=0, tiled=True)  17.4 us
    ppermute x4, starting transfers between devices, extended_2(): lax.ppermute(tail, axis, [(i, (i + 1) % count) for i in range(count)])  9.01 us
    gather x2, local copies, waits for them, and re-layouts, per_device(): jnp.take(extended.reshape(-1, width), index_flat, axis=0)  5.19 us
    dot_general x2, matrix products, per_device(): jnp.einsum('nm,rcmw->rcnw', laplace, state, precision=lax.Precision.HIGHEST)  5.18 us
    ppermute x4, waiting for transfers between devices, extended_2(): lax.ppermute(head, axis, [((i + 1) % count, i) for i in range(count)])  4.85 us
  transfers between devices with their start and end apart: 8, of which 6 were waited for; matrix products, arithmetic and copies ran while one was open for 4% of the time, Pallas kernels for 0%

profile of v2, /device:TPU:1, one launch (start us, length us, event | category | flops | bytes accessed | tf_op | source)
XLA Modules:
  0.0 139.8 jit_solution(6045069537554495009)
XLA Ops:
  0.6 3.4 %bitcast_add_fusion.3 = f32[4,8,16,720]{3,2,1,0:T(8,128)S(1)} fusion(f32[4,8,16,720]{3,2,1,0:T(8,128)} %param.11, f32[16,16,1,1]{1,0,3,2:T(8,128)} %constant.154), kind=kOutput, calls=%fused_computation.14 | convolution fusion | flops 71516160 | bytes 2950144 | tf_op jit(solution)/shard_map/nm,rcmw->rcnw/dot_general | solution.py:219
  4.1 2.2 %collective-permute-start = (f32[1,8,16,720]{3,2,1,0:T(8,128)S(1)}, f32[1,8,16,720]{3,2,1,0:T(8,128)S(1)}, u32[]{:S(2)}, u32[]{:S(2)}) collective-permute-start(f32[1,8,16,720]{3,2,1,0:T(8,128)S(1)} %get-tuple-element.18), channel_id=1, source_target_pairs={{0,32},{32,64},{64,96},{96,0},{1,33},{33,65},{65,97},{97,1},{2,34}... | collective-permute-start | bytes 1105928 | tf_op jit(solution)/shard_map/ppermute | solution.py:31
  8.7 7.7 %collective-permute-done = f32[1,8,16,720]{3,2,1,0:T(8,128)S(1)} collective-permute-done((f32[1,8,16,720]{3,2,1,0:T(8,128)S(1)}, f32[1,8,16,720]{3,2,1,0:T(8,128)S(1)}, u32[]{:S(2)}, u32[]{:S(2)}) %collective-permute-start) | collective-permute-done | bytes 368672 | tf_op jit(solution)/shard_map/ppermute | solution.py:31
  16.5 2.5 %collective-permute-start.2 = (f32[6,1,16,720]{3,2,1,0:T(8,128)S(1)}, f32[6,1,16,720]{3,2,1,0:T(8,128)S(1)}, u32[]{:S(2)}, u32[]{:S(2)}) collective-permute-start(f32[6,1,16,720]{3,2,1,0:T(8,128)S(1)} %get-tuple-element.14), channel_id=1, source_target_pairs={{0,1},{1,2},{2,3},{3,4},{4,5},{5,6},{6,7},{7,8},{8,9},{9,10},{10,1... | collective-permute-start | bytes 829448 | tf_op jit(solution)/shard_map/ppermute | solution.py:31
  19.1 3.6 %collective-permute-done.2 = f32[6,1,16,720]{3,2,1,0:T(8,128)S(1)} collective-permute-done((f32[6,1,16,720]{3,2,1,0:T(8,128)S(1)}, f32[6,1,16,720]{3,2,1,0:T(8,128)S(1)}, u32[]{:S(2)}, u32[]{:S(2)}) %collective-permute-start.2) | collective-permute-done | bytes 276512 | tf_op jit(solution)/shard_map/ppermute | solution.py:31
  22.7 2.8 %collective-permute-done.3 = f32[6,1,16,720]{3,2,1,0:T(8,128)S(1)} collective-permute-done((f32[6,1,16,720]{3,2,1,0:T(8,128)S(1)}, f32[6,1,16,720]{3,2,1,0:T(8,128)S(1)}, u32[]{:S(2)}, u32[]{:S(2)}) %collective-permute-start.3) | collective-permute-done | bytes 276512 | tf_op jit(solution)/shard_map/ppermute | solution.py:33
  25.5 1.8 %pad_maximum_fusion = f32[6,10,16,720]{3,2,1,0:T(8,128)S(1)} fusion(f32[6,1,16,720]{3,2,1,0:T(8,128)S(1)} %collective-permute-done.3, f32[1,8,16,720]{3,2,1,0:T(8,128)} %copy-done.7, f32[4,8,16,720]{3,2,1,0:T(8,128)} %copy-done.2, f32[1,8,16,720]{3,2,1,0:T(8,128)S(1)} %collective-permute-done, f32[6,1,16,720]{3,2,1,0:T(8,128)S(1)} %collective-permute-done.2), kind=kLoop, calls=%fused_computation.7 | loop fusion | flops 2764800 | bytes 5529600 | tf_op jit(solution)/shard_map/concatenate | solution.py:29
  27.3 2.6 %gather_fusion.3 = f32[512,720]{1,0:T(8,128)} fusion(f32[960,720]{1,0:T(8,128)S(1)} %bitcast.58, s32[1024]{0:T(1024)S(1)} %pad_clamp_fusion.2), kind=kCustom, calls=%fused_computation.clone | custom fusion | bytes 2951168 | tf_op jit(solution)/shard_map/jit(_take)/gather | solution.py:223
  29.9 1.6 %broadcast_select_fusion.1 = f32[512,720]{1,0:T(8,128)S(1)} fusion(f32[512,720]{1,0:T(8,128)} %gather_fusion.3, pred[512]{0:T(512)(128)(4,1)S(1)} %compare_and_fusion), kind=kLoop, calls=%fused_computation.17 | loop fusion | flops 368640 | bytes 2949632 | tf_op jit(solution)/shard_map/jit(_take)/select_n | solution.py:223
  33.0 1.8 %bitcast_add_fusion.1 = f32[4,8,16,720]{3,2,1,0:T(8,128)S(1)} fusion(f32[16,16,1,1]{1,0,3,2:T(8,128)S(1)} %copy-done.11, f32[4,8,16,720]{3,2,1,0:T(8,128)S(1)} %copy-done.3, f32[4,8,720,16]{2,3,1,0:T(8,128)S(1)} %fusion.32, f32[16]{0:T(128)S(1)} %copy-done.15), kind=kOutput, calls=%fused_computation.11 | convolution fusion | flops 72990720 | bytes 4424768 | tf_op jit(solution)/shard_map/nm,rcmw->rcnw/dot_general | solution.py:219
  38.0 2.5 %sort.17 = (s32[128]{0:T(128)}, s32[128]{0:T(128)S(1)}) sort(s32[128]{0:T(128)S(1)} %reshape.80, s32[128]{0:T(128)S(1)} %iota.35), dimensions={0}, to_apply=%region_0.2 | sort | flops 896 | bytes 2048 | tf_op jit(solution)/shard_map/jit(argsort)/sort | solution.py:234
  40.6 4.5 %collective-permute-done.4 = f32[1,8,16,720]{3,2,1,0:T(8,128)S(1)} collective-permute-done((f32[1,8,16,720]{3,2,1,0:T(8,128)S(1)}, f32[1,8,16,720]{3,2,1,0:T(8,128)S(1)}, u32[]{:S(2)}, u32[]{:S(2)}) %collective-permute-start.4) | collective-permute-done | bytes 368672 | tf_op jit(solution)/shard_map/ppermute | solution.py:31
  45.1 2.9 %collective-permute-start.6 = (f32[6,1,16,720]{3,2,1,0:T(8,128)S(1)}, f32[6,1,16,720]{3,2,1,0:T(8,128)S(1)}, u32[]{:S(2)}, u32[]{:S(2)}) collective-permute-start(f32[6,1,16,720]{3,2,1,0:T(8,128)S(1)} %get-tuple-element.12), channel_id=1, source_target_pairs={{0,1},{1,2},{2,3},{3,4},{4,5},{5,6},{6,7},{7,8},{8,9},{9,10},{10,1... | collective-permute-start | bytes 829448 | tf_op jit(solution)/shard_map/ppermute | solution.py:31
  49.7 2.0 %collective-permute-done.6 = f32[6,1,16,720]{3,2,1,0:T(8,128)S(1)} collective-permute-done((f32[6,1,16,720]{3,2,1,0:T(8,128)S(1)}, f32[6,1,16,720]{3,2,1,0:T(8,128)S(1)}, u32[]{:S(2)}, u32[]{:S(2)}) %collective-permute-start.6) | collective-permute-done | bytes 276512 | tf_op jit(solution)/shard_map/ppermute | solution.py:31
  52.4 2.1 %collective-permute-done.7 = f32[6,1,16,720]{3,2,1,0:T(8,128)} collective-permute-done((f32[6,1,16,720]{3,2,1,0:T(8,128)S(1)}, f32[6,1,16,720]{3,2,1,0:T(8,128)}, u32[]{:S(2)}, u32[]{:S(2)}) %collective-permute-start.7) | collective-permute-done | bytes 276512 | tf_op jit(solution)/shard_map/ppermute | solution.py:33
  54.5 1.9 %pad_maximum_fusion.1 = f32[6,10,16,720]{3,2,1,0:T(8,128)S(1)} fusion(f32[6,1,16,720]{3,2,1,0:T(8,128)} %collective-permute-done.7, f32[1,8,16,720]{3,2,1,0:T(8,128)} %copy-done.8, f32[4,8,16,720]{3,2,1,0:T(8,128)} %copy-done.4, f32[1,8,16,720]{3,2,1,0:T(8,128)S(1)} %collective-permute-done.4, f32[6,1,16,720]{3,2,1,0:T(8,128)} %copy-done.9), kind=kLoop, calls=%fused_computation.8 | loop fusion | flops 2764800 | bytes 5529600 | tf_op jit(solution)/shard_map/concatenate | solution.py:29
  56.4 2.6 %gather_fusion.4 = f32[512,720]{1,0:T(8,128)} fusion(f32[960,720]{1,0:T(8,128)S(1)} %bitcast.57, s32[1024]{0:T(1024)S(1)} %pad_clamp_fusion.2), kind=kCustom, calls=%fused_computation.1.clone | custom fusion | bytes 2951168 | tf_op jit(solution)/shard_map/jit(_take)/gather | solution.py:223
  59.0 1.7 %broadcast_select_fusion = f32[512,720]{1,0:T(8,128)S(1)} fusion(f32[512,720]{1,0:T(8,128)} %gather_fusion.4, pred[512]{0:T(512)(128)(4,1)S(1)} %compare_and_fusion), kind=kLoop, calls=%fused_computation.16 | loop fusion | flops 368640 | bytes 2949632 | tf_op jit(solution)/shard_map/jit(_take)/select_n | solution.py:223
  65.4 18.6 %all_to_all.20 = f32[4,32,1,321]{3,0,2,1:T(4,128)S(1)} all-to-all(f32[4,32,1,321]{3,0,2,1:T(4,128)S(1)} %pad_maximum_fusion.8), channel_id=1, replica_groups=mesh['face'=4,'col'=32] {'col'}, dimensions={1} | all-to-all | bytes 328704 | tf_op jit(solution)/shard_map/all_to_all | solution.py:193
  84.1 9.1 %all_to_all.21 = f32[4,32,1,321]{3,1,2,0:T(8,128)S(1)} all-to-all(f32[4,32,1,321]{3,1,2,0:T(8,128)S(1)} %copy.51), channel_id=1, replica_groups=mesh['face'=4,'col'=32] {'face'}, dimensions={0} | all-to-all | bytes 328704 | tf_op jit(solution)/shard_map/all_to_all | solution.py:194
  94.6 2.5 %copy-done = bf16[10,32,64,128]{3,2,1,0:T(8,128)(2,1)S(1)} copy-done((bf16[10,32,64,128]{3,2,1,0:T(8,128)(2,1)S(1)}, bf16[10,32,64,128]{3,2,1,0:T(8,128)(2,1)}, u32[]{:S(2)}) %copy-start) | copy-done | bytes 5242904
  97.1 18.4 %shard_map.112 = (bf16[10,32,64,128]{3,2,1,0:T(8,128)(2,1)}, f32[10,32,128]{2,1,0:T(8,128)S(1)}) custom-call(f32[10,32,128]{2,1,0:T(8,128)S(1)} %bitcast.54, s32[1,128]{1,0:T(1,128)S(1)} %bitcast.56, bf16[10,32,64,128]{3,2,1,0:T(8,128)(2,1)S(1)} %copy-done), custom_call_target="tpu_custom_call" | custom-call | tf_op jit(solution)/shard_map/pallas_call | solution.py:158
  116.6 13.1 %all_to_all.22 = f32[4,32,1,320]{3,0,2,1:T(4,128)S(1)} all-to-all(f32[4,32,1,320]{3,0,2,1:T(4,128)S(1)} %copy.54), channel_id=1, replica_groups=mesh['face'=4,'col'=32] {'col'}, dimensions={1} | all-to-all | bytes 327680 | tf_op jit(solution)/shard_map/all_to_all | solution.py:193
  129.7 8.3 %all_to_all.23 = f32[4,32,1,320]{3,1,2,0:T(8,128)S(1)} all-to-all(f32[4,32,1,320]{3,1,2,0:T(8,128)S(1)} %copy.55), channel_id=1, replica_groups=mesh['face'=4,'col'=32] {'face'}, dimensions={0} | all-to-all | bytes 327680 | tf_op jit(solution)/shard_map/all_to_all | solution.py:194
  (86 shorter events, 18.4 us)
Async XLA Ops:
  4.0 12.5 %copy-start.2 = (f32[4,8,16,720]{3,2,1,0:T(8,128)}, f32[4,8,16,720]{3,2,1,0:T(8,128)S(1)}, u32[]{:S(2)}) copy-start(f32[4,8,16,720]{3,2,1,0:T(8,128)S(1)} %bitcast_add_fusion.3) | copy-start | bytes 4423684
  4.0 3.8 %copy-start.12 = (s32[4,8,4]{1,2,0:T(4,128)S(1)}, s32[4,8,4]{1,2,0:T(4,128)}, u32[]{:S(2)}) copy-start(s32[4,8,4]{1,2,0:T(4,128)} %param.12) | copy-start | bytes 1540
  4.1 12.3 %collective-permute-start = (f32[1,8,16,720]{3,2,1,0:T(8,128)S(1)}, f32[1,8,16,720]{3,2,1,0:T(8,128)S(1)}, u32[]{:S(2)}, u32[]{:S(2)}) collective-permute-start(f32[1,8,16,720]{3,2,1,0:T(8,128)S(1)} %get-tuple-element.18), channel_id=1, source_target_pairs={{0,32},{32,64},{64,96},{96,0},{1,33},{33,65},{65,97},{97,1},{2,34}... | collective-permute-start | bytes 1105928 | tf_op jit(solution)/shard_map/ppermute | solution.py:31
  6.3 10.1 %collective-permute-start.1 = (f32[1,8,16,720]{3,2,1,0:T(8,128)S(1)}, f32[1,8,16,720]{3,2,1,0:T(8,128)S(1)}, u32[]{:S(2)}, u32[]{:S(2)}) collective-permute-start(f32[1,8,16,720]{3,2,1,0:T(8,128)S(1)} %get-tuple-element.19), channel_id=1, source_target_pairs={{32,0},{64,32},{96,64},{0,96},{33,1},{65,33},{97,65},{1,97},{34,2}... | collective-permute-start | bytes 1105928 | tf_op jit(solution)/shard_map/ppermute | solution.py:33
  16.4 6.3 %copy-start.7 = (f32[1,8,16,720]{3,2,1,0:T(8,128)}, f32[1,8,16,720]{3,2,1,0:T(8,128)S(1)}, u32[]{:S(2)}) copy-start(f32[1,8,16,720]{3,2,1,0:T(8,128)S(1)} %collective-permute-done.1) | copy-start | bytes 1105924
  16.5 6.2 %collective-permute-start.2 = (f32[6,1,16,720]{3,2,1,0:T(8,128)S(1)}, f32[6,1,16,720]{3,2,1,0:T(8,128)S(1)}, u32[]{:S(2)}, u32[]{:S(2)}) collective-permute-start(f32[6,1,16,720]{3,2,1,0:T(8,128)S(1)} %get-tuple-element.14), channel_id=1, source_target_pairs={{0,1},{1,2},{2,3},{3,4},{4,5},{5,6},{6,7},{7,8},{8,9},{9,10},{10,1... | collective-permute-start | bytes 829448 | tf_op jit(solution)/shard_map/ppermute | solution.py:31
  19.0 6.4 %collective-permute-start.3 = (f32[6,1,16,720]{3,2,1,0:T(8,128)S(1)}, f32[6,1,16,720]{3,2,1,0:T(8,128)S(1)}, u32[]{:S(2)}, u32[]{:S(2)}) collective-permute-start(f32[6,1,16,720]{3,2,1,0:T(8,128)S(1)} %get-tuple-element.15), channel_id=1, source_target_pairs={{1,0},{2,1},{3,2},{4,3},{5,4},{6,5},{7,6},{8,7},{9,8},{10,9},{11,1... | collective-permute-start | bytes 829448 | tf_op jit(solution)/shard_map/ppermute | solution.py:33
  29.9 1.6 %copy-start.10 = (f32[16,16,1,1]{1,0,3,2:T(8,128)S(1)}, f32[16,16,1,1]{1,0,3,2:T(8,128)}, u32[]{:S(2)}) copy-start(f32[16,16,1,1]{1,0,3,2:T(8,128)} %constant.155) | copy-start | bytes 3076
  31.5 1.5 %copy-start.3 = (f32[4,8,16,720]{3,2,1,0:T(8,128)S(1)}, f32[4,8,16,720]{3,2,1,0:T(8,128)}, u32[]{:S(2)}) copy-start(f32[4,8,16,720]{3,2,1,0:T(8,128)} %copy-done.2) | copy-start | bytes 4423684
  31.5 1.5 %copy-start.11 = (f32[16,16,1,1]{1,0,3,2:T(8,128)S(1)}, f32[16,16,1,1]{1,0,3,2:T(8,128)}, u32[]{:S(2)}) copy-start(f32[16,16,1,1]{1,0,3,2:T(8,128)} %constant.154) | copy-start | bytes 3076
  31.5 1.5 %copy-start.15 = (f32[16]{0:T(128)S(1)}, f32[16]{0:T(128)}, u32[]{:S(2)}) copy-start(f32[16]{0:T(128)} %constant.152) | copy-start | bytes 196
  34.8 10.3 %copy-start.4 = (f32[4,8,16,720]{3,2,1,0:T(8,128)}, f32[4,8,16,720]{3,2,1,0:T(8,128)S(1)}, u32[]{:S(2)}) copy-start(f32[4,8,16,720]{3,2,1,0:T(8,128)S(1)} %bitcast_add_fusion.1) | copy-start | bytes 4423684
  34.9 3.0 %copy-start.13 = (s32[4,8,4]{1,2,0:T(4,128)S(1)}, s32[4,8,4]{1,2,0:T(4,128)}, u32[]{:S(2)}) copy-start(s32[4,8,4]{1,2,0:T(4,128)} %param.13) | copy-start | bytes 1540
  34.9 10.1 %collective-permute-start.4 = (f32[1,8,16,720]{3,2,1,0:T(8,128)S(1)}, f32[1,8,16,720]{3,2,1,0:T(8,128)S(1)}, u32[]{:S(2)}, u32[]{:S(2)}) collective-permute-start(f32[1,8,16,720]{3,2,1,0:T(8,128)S(1)} %get-tuple-element.16), channel_id=1, source_target_pairs={{0,32},{32,64},{64,96},{96,0},{1,33},{33,65},{65,97},{97,1},{2,34}... | collective-permute-start | bytes 1105928 | tf_op jit(solution)/shard_map/ppermute | solution.py:31
  36.3 8.8 %collective-permute-start.5 = (f32[1,8,16,720]{3,2,1,0:T(8,128)S(1)}, f32[1,8,16,720]{3,2,1,0:T(8,128)S(1)}, u32[]{:S(2)}, u32[]{:S(2)}) collective-permute-start(f32[1,8,16,720]{3,2,1,0:T(8,128)S(1)} %get-tuple-element.17), channel_id=1, source_target_pairs={{32,0},{64,32},{96,64},{0,96},{33,1},{65,33},{97,65},{1,97},{34,2}... | collective-permute-start | bytes 1105928 | tf_op jit(solution)/shard_map/ppermute | solution.py:33
  45.1 4.4 %copy-start.8 = (f32[1,8,16,720]{3,2,1,0:T(8,128)}, f32[1,8,16,720]{3,2,1,0:T(8,128)S(1)}, u32[]{:S(2)}) copy-start(f32[1,8,16,720]{3,2,1,0:T(8,128)S(1)} %collective-permute-done.5) | copy-start | bytes 1105924
  45.1 6.6 %collective-permute-start.6 = (f32[6,1,16,720]{3,2,1,0:T(8,128)S(1)}, f32[6,1,16,720]{3,2,1,0:T(8,128)S(1)}, u32[]{:S(2)}, u32[]{:S(2)}) collective-permute-start(f32[6,1,16,720]{3,2,1,0:T(8,128)S(1)} %get-tuple-element.12), channel_id=1, source_target_pairs={{0,1},{1,2},{2,3},{3,4},{4,5},{5,6},{6,7},{7,8},{8,9},{9,10},{10,1... | collective-permute-start | bytes 829448 | tf_op jit(solution)/shard_map/ppermute | solution.py:31
  48.0 6.4 %collective-permute-start.7 = (f32[6,1,16,720]{3,2,1,0:T(8,128)S(1)}, f32[6,1,16,720]{3,2,1,0:T(8,128)}, u32[]{:S(2)}, u32[]{:S(2)}) collective-permute-start(f32[6,1,16,720]{3,2,1,0:T(8,128)S(1)} %get-tuple-element.13), channel_id=1, source_target_pairs={{1,0},{2,1},{3,2},{4,3},{5,4},{6,5},{7,6},{8,7},{9,8},{10,9},{11,1... | collective-permute-start | bytes 829448 | tf_op jit(solution)/shard_map/ppermute | solution.py:33
  51.7 0.7 copy-start.9
  59.0 1.9 %copy-start.5 = (f32[4,8,16,720]{3,2,1,0:T(8,128)S(1)}, f32[4,8,16,720]{3,2,1,0:T(8,128)}, u32[]{:S(2)}) copy-start(f32[4,8,16,720]{3,2,1,0:T(8,128)} %copy-done.4) | copy-start | bytes 4423684
  60.9 1.5 %copy-start.14 = (f32[4,16,1,1]{1,0,3,2:T(4,128)S(1)}, f32[4,16,1,1]{1,0,3,2:T(4,128)}, u32[]{:S(2)}) copy-start(f32[4,16,1,1]{1,0,3,2:T(4,128)} %constant.156) | copy-start | bytes 772
  62.4 1.6 %copy-start.6 = (f32[4,8,16,720]{3,2,1,0:T(8,128)}, f32[4,8,16,720]{3,2,1,0:T(8,128)S(1)}, u32[]{:S(2)}) copy-start(f32[4,8,16,720]{3,2,1,0:T(8,128)S(1)} %fusion) | copy-start | bytes 4423684
  65.2 29.4 %copy-start.1 = (s32[128]{0:T(128)S(1)}, s32[128]{0:T(128)}, u32[]{:S(2)}) copy-start(s32[128]{0:T(128)} %param.14) | copy-start | bytes 1540
  94.6 2.5 %copy-start = (bf16[10,32,64,128]{3,2,1,0:T(8,128)(2,1)S(1)}, bf16[10,32,64,128]{3,2,1,0:T(8,128)(2,1)}, u32[]{:S(2)}) copy-start(bf16[10,32,64,128]{3,2,1,0:T(8,128)(2,1)} %state_hbm.1) | copy-start | bytes 15728644

commit v3 on v2

--- a/solution.py
+++ b/solution.py
@@ -21,20 +21,38 @@
 CONVERT = 0.5
 
 
-def extended_2(cells, sides, width):
-    for axis, dim in sides:
-        count = lax.axis_size(axis)
-        head = lax.slice_in_dim(cells, 0, width, axis=dim)
-        tail = lax.slice_in_dim(cells, cells.shape[dim] - width, cells.shape[dim], axis=dim)
-        cells = jnp.concatenate(
-            [
-                lax.ppermute(tail, axis, [(i, (i + 1) % count) for i in range(count)]),
-                cells,
-                lax.ppermute(head, axis, [((i + 1) % count, i) for i in range(count)]),
-            ],
-            axis=dim,
-        )
-    return cells
+def rim_points(cells):
+    return jnp.concatenate([cells[:, :, 0:5], cells[:, :, 7:9], cells[:, :, 11:16]], axis=2)
+
+
+def halo_table(rim):
+    nface = lax.axis_size("face")
+    ncol = lax.axis_size("col")
+    rows, cols = rim.shape[:2]
+
+    def along(piece, axis, count, step):
+        return lax.ppermute(piece, axis, [(i, (i + step) % count) for i in range(count)])
+
+    def corner(piece, df, dc):
+        pairs = [
+            (f * ncol + c, ((f + df) % nface) * ncol + (c + dc) % ncol)
+            for f in range(nface)
+            for c in range(ncol)
+        ]
+        return lax.ppermute(piece, ("face", "col"), pairs)
+
+    up = along(rim[rows - 1 : rows], "face", nface, 1)
+    down = along(rim[0:1], "face", nface, -1)
+    left = along(rim[:, cols - 1 : cols], "col", ncol, 1)
+    right = along(rim[:, 0:1], "col", ncol, -1)
+    up_left = corner(rim[rows - 1 : rows, cols - 1 : cols], 1, 1)
+    up_right = corner(rim[rows - 1 : rows, 0:1], 1, -1)
+    down_left = corner(rim[0:1, cols - 1 : cols], -1, 1)
+    down_right = corner(rim[0:1, 0:1], -1, -1)
+    top = jnp.concatenate([up_left, up, up_right], axis=1)
+    middle = jnp.concatenate([left, rim, right], axis=1)
+    bottom = jnp.concatenate([down_left, down, down_right], axis=1)
+    return jnp.concatenate([top, middle, bottom], axis=0)
 
 
 def node_tables():
@@ -164,10 +182,10 @@
         in_specs=[
             pl.BlockSpec(memory_space=pltpu.VMEM),
             pl.BlockSpec(memory_space=pltpu.VMEM),
-            pl.BlockSpec(memory_space=pl.ANY),
+            pl.BlockSpec(memory_space=pltpu.HBM),
         ],
         out_specs=(
-            pl.BlockSpec(memory_space=pl.ANY),
+            pl.BlockSpec(memory_space=pltpu.HBM),
             pl.BlockSpec(memory_space=pltpu.VMEM),
         ),
         scratch_shapes=[
@@ -181,7 +199,7 @@
     )(forcing, active.reshape(1, ncol), state)
 
 
-TWO_STAGE = True
+TWO_STAGE = False
 
 
 def exchange(chunks):
@@ -212,14 +230,16 @@
     drow = (near_row - (lax.axis_index("face") * rows_dev + local_row) + 1) % total_rows - 1
     dcol = (near_col - (lax.axis_index("col") * cols_dev + local_col) + 1) % total_cols - 1
     place = (local_row + drow + 1) * (cols_dev + 2) + (local_col + dcol + 1)
-    index_flat = place[..., None] * 16 + pick
+    rim_slot = np.full(16, 0, np.int32)
+    rim_slot[[0, 1, 2, 3, 4, 7, 8, 11, 12, 13, 14, 15]] = np.arange(12, dtype=np.int32)
+    index_flat = place[..., None] * 12 + jnp.asarray(rim_slot)[pick]
     index_flat = index_flat.reshape(-1)
     state = dyn_state
     for step in range(DSTEPS):
         state = state + KAPPA * jnp.einsum(
             "nm,rcmw->rcnw", laplace, state, precision=lax.Precision.HIGHEST
         )
-        extended = extended_2(state, (("face", 0), ("col", 1)), 1)
+        extended = halo_table(rim_points(state))
         matched = jnp.take(extended.reshape(-1, width), index_flat, axis=0).reshape(
             rows_dev, cols_dev, 16, width
         )

time: 140 us -> 152 us (1.086)
  starting transfers between devices: 12.2 us -> 33.1 us
  waiting for transfers between devices: 22.8 us -> 7.86 us
  blocking collectives: 49.1 us -> 34.6 us
  local copies, waits for them, and re-layouts: 16.8 us -> 30.2 us
  other arithmetic: 10.2 us -> 17.2 us
    ppermute x8 -> x16, starting transfers between devices: 12.2 us -> 33.1 us  [the longest x8 22.8 us: corner(): return lax.ppermute(piece, ('face', 'col'), pairs)]
    ppermute x8 -> x16, waiting for transfers between devices: 22.8 us -> 7.86 us  [the longest x8 7.84 us: corner(): return lax.ppermute(piece, ('face', 'col'), pairs)]
    all_to_all x4 -> x2, blocking collectives: 49.1 us -> 34.6 us  [exchange(): lax.all_to_all(chunks, ('face', 'col'), split_axis=0, concat_axis=0, tile...]
    reshape x0 -> x4, local copies, waits for them, and re-layouts: none -> 5.48 us  [the longest x2 5.07 us: per_device(): extended.reshape(-1, width)]
    gather x0 -> x2, local copies, waits for them, and re-layouts: none -> 3.48 us  [per_device(): index_flat = place[..., None] * 12 + jnp.asarray(rim_slot)[pick]]
    slice x2 -> x6, other arithmetic: 0.08 us -> 3.25 us  [the longest x2 1.68 us: halo_table(): left = along(rim[:, cols - 1:cols], 'col', ncol, 1)]
    concatenate x3 -> x4, other arithmetic: 3.79 us -> 6.44 us  [the longest x2 5.66 us: halo_table(): return jnp.concatenate([top, middle, bottom], axis=0)]
    unnamed x33 -> x47, local copies, waits for them, and re-layouts: 3.53 us -> 6.17 us
  transfers between devices with their start and end apart: 8 -> 16, of which waited for: 6 -> 2; matrix products, arithmetic and copies ran while one was open for 4% -> 9% of each run, Pallas kernels for 0% -> 0%
where the time goes in v3:
time: 152 us
  blocking collectives  34.6 us (23%)
  starting transfers between devices  33.1 us (22%)
  local copies, waits for them, and re-layouts  30.2 us (20%)
  Pallas kernels  18.4 us (12%)
  other arithmetic  17.2 us (11%)
  matrix products  9.14 us (6%)
  waiting for transfers between devices  7.86 us (5%)
    all_to_all x2, blocking collectives, exchange(): lax.all_to_all(chunks, ('face', 'col'), split_axis=0, concat_axis=0, tile...  34.6 us
    ppermute x8, starting transfers between devices, corner(): return lax.ppermute(piece, ('face', 'col'), pairs)  22.8 us
    pallas_call x1, Pallas kernels, crm_run(): pl.pallas_call(crm_kernel, out_shape=(jax.ShapeDtypeStruct(state.shape, j...  18.4 us
    ppermute x8, starting transfers between devices, along(): lax.ppermute(piece, axis, [(i, (i + step) % count) for i in range(count)])  10.3 us
    ppermute x8, waiting for transfers between devices, corner(): return lax.ppermute(piece, ('face', 'col'), pairs)  7.84 us
    unnamed x47, local copies, waits for them, and re-layouts  6.17 us
    concatenate x2, other arithmetic, halo_table(): return jnp.concatenate([top, middle, bottom], axis=0)  5.66 us
    dot_general x2, matrix products, per_device(): jnp.einsum('nm,rcmw->rcnw', laplace, state, precision=lax.Precision.HIGHEST)  5.2 us
  transfers between devices with their start and end apart: 16, of which 2 were waited for; matrix products, arithmetic and copies ran while one was open for 9% of the time, Pallas kernels for 0%

profile of v3, /device:TPU:1, one launch (start us, length us, event | category | flops | bytes accessed | tf_op | source)
XLA Modules:
  0.0 151.8 jit_solution(915399069160183264)
XLA Ops:
  0.6 3.4 %bitcast_add_fusion.3 = f32[4,8,16,720]{3,2,1,0:T(8,128)S(1)} fusion(f32[4,8,16,720]{3,2,1,0:T(8,128)} %param.12, f32[16,16,1,1]{1,0,3,2:T(8,128)} %constant.159), kind=kOutput, calls=%fused_computation.17 | convolution fusion | flops 71516160 | bytes 2950144 | tf_op jit(solution)/shard_map/nm,rcmw->rcnw/dot_general | solution.py:239
  6.0 3.6 %collective-permute-start = (f32[1,1,12,720]{3,2,1,0:T(8,128)}, f32[1,1,12,720]{3,2,1,0:T(8,128)S(1)}, u32[]{:S(2)}, u32[]{:S(2)}) collective-permute-start(f32[1,1,12,720]{3,2,1,0:T(8,128)} %get-tuple-element.18), channel_id=1, source_target_pairs={{0,33},{1,34},{2,35},{3,36},{4,37},{5,38},{6,39},{7,40},{8,41},{9,... | collective-permute-start | bytes 103688 | tf_op jit(solution)/shard_map/ppermute | solution.py:42
  9.7 3.8 %collective-permute-start.5 = (f32[1,1,12,720]{3,2,1,0:T(8,128)}, f32[1,1,12,720]{3,2,1,0:T(8,128)}, u32[]{:S(2)}, u32[]{:S(2)}) collective-permute-start(f32[1,1,12,720]{3,2,1,0:T(8,128)} %get-tuple-element.20), channel_id=1, source_target_pairs={{0,97},{1,98},{2,99},{3,100},{4,101},{5,102},{6,103},{7,104},{8,10... | collective-permute-start | bytes 103688 | tf_op jit(solution)/shard_map/ppermute | solution.py:42
  14.1 2.7 %collective-permute-start.6 = (f32[1,8,12,720]{3,2,1,0:T(8,128)S(1)}, f32[1,8,12,720]{3,2,1,0:T(8,128)S(1)}, u32[]{:S(2)}, u32[]{:S(2)}) collective-permute-start(f32[1,8,12,720]{3,2,1,0:T(8,128)S(1)} %pad_maximum_fusion.3), channel_id=1, source_target_pairs={{0,96},{32,0},{64,32},{96,64},{1,97},{33,1},{65,33},{97,65},{2,98}... | collective-permute-start | bytes 829448 | tf_op jit(solution)/shard_map/ppermute | solution.py:34
  17.6 3.3 %gather_fusion = s32[512]{0:T(512)S(1)} fusion(s32[16]{0:T(128)S(1)} %copy-done.2, s32[1024]{0:T(1024)S(1)} %pad_clamp_fusion.3), kind=kCustom, calls=%fused_computation.2 | custom fusion | bytes 6144 | tf_op jit(solution)/shard_map/gather | solution.py:235
  22.9 2.5 %sort.17 = (s32[128]{0:T(128)}, s32[128]{0:T(128)S(1)}) sort(s32[128]{0:T(128)S(1)} %reshape.101, s32[128]{0:T(128)S(1)} %iota.34), dimensions={0}, to_apply=%region_0.2 | sort | flops 896 | bytes 2048 | tf_op jit(solution)/shard_map/jit(argsort)/sort | solution.py:254
  28.6 5.8 %collective-permute-start.7 = (f32[1,1,12,720]{3,2,1,0:T(8,128)}, f32[1,1,12,720]{3,2,1,0:T(8,128)}, u32[]{:S(2)}, u32[]{:S(2)}) collective-permute-start(f32[1,1,12,720]{3,2,1,0:T(8,128)} %get-tuple-element.19), channel_id=1, source_target_pairs={{0,127},{1,96},{2,97},{3,98},{4,99},{5,100},{6,101},{7,102},{8,103... | collective-permute-start | bytes 103688 | tf_op jit(solution)/shard_map/ppermute | solution.py:42
  34.4 1.8 %gather_fusion.2 = s32[128]{0:T(128)} fusion(s32[128]{0:T(128)S(1)} %reshape.101, s32[1024]{0:T(1024)S(1)} %pad_clamp_fusion.1), kind=kCustom, calls=%fused_computation.4 | custom fusion | bytes 1536 | tf_op jit(solution)/shard_map/gather | solution.py:255
  36.2 2.8 %maximum_maximum_fusion = f32[6,10,12,720]{3,2,1,0:T(8,128)} fusion(f32[1,1,12,720]{3,2,1,0:T(8,128)} %collective-permute-done.7, f32[1,8,12,720]{3,2,1,0:T(8,128)S(1)} %collective-permute-done.6, f32[1,1,12,720]{3,2,1,0:T(8,128)} %collective-permute-done.5, f32[4,1,12,720]{3,2,1,0:T(8,128)} %collective-permute-done.4, ...), kind=kLoop, calls=%fused_computation.8 | loop fusion | flops 5184000 | bytes 4147200 | tf_op jit(solution)/shard_map/concatenate | solution.py:55
  39.1 2.5 %reshape.97 = f32[720,720]{1,0:T(8,128)S(1)} reshape(f32[6,10,12,720]{3,2,1,0:T(8,128)} %maximum_maximum_fusion) | data formatting | bytes 4147200 | tf_op jit(solution)/shard_map/reshape | solution.py:243
  41.6 2.6 %gather_fusion.4 = f32[512,720]{1,0:T(8,128)} fusion(f32[720,720]{1,0:T(8,128)S(1)} %reshape.97, s32[1024]{0:T(1024)S(1)} %pad_clamp_fusion.2), kind=kCustom, calls=%fused_computation.clone | custom fusion | bytes 2951168 | tf_op jit(solution)/shard_map/jit(_take)/gather | solution.py:243
  47.4 1.8 %bitcast_add_fusion.1 = f32[4,8,16,720]{3,2,1,0:T(8,128)S(1)} fusion(f32[16,16,1,1]{1,0,3,2:T(8,128)S(1)} %copy-done.11, f32[4,8,16,720]{3,2,1,0:T(8,128)S(1)} %copy-done.6, f32[4,8,720,16]{2,3,1,0:T(8,128)S(1)} %fusion.33, f32[16]{0:T(128)S(1)} %copy-done.19), kind=kOutput, calls=%fused_computation.14 | convolution fusion | flops 72990720 | bytes 4424768 | tf_op jit(solution)/shard_map/nm,rcmw->rcnw/dot_general | solution.py:239
  55.6 2.6 %collective-permute-start.13 = (f32[1,1,12,720]{3,2,1,0:T(8,128)S(1)}, f32[1,1,12,720]{3,2,1,0:T(8,128)S(1)}, u32[]{:S(2)}, u32[]{:S(2)}) collective-permute-start(f32[1,1,12,720]{3,2,1,0:T(8,128)S(1)} %get-tuple-element.14), channel_id=1, source_target_pairs={{0,97},{1,98},{2,99},{3,100},{4,101},{5,102},{6,103},{7,104},{8,10... | collective-permute-start | bytes 103688 | tf_op jit(solution)/shard_map/ppermute | solution.py:42
  58.2 5.7 %collective-permute-start.15 = (f32[1,1,12,720]{3,2,1,0:T(8,128)S(1)}, f32[1,1,12,720]{3,2,1,0:T(8,128)S(1)}, u32[]{:S(2)}, u32[]{:S(2)}) collective-permute-start(f32[1,1,12,720]{3,2,1,0:T(8,128)S(1)} %get-tuple-element.13), channel_id=1, source_target_pairs={{0,127},{1,96},{2,97},{3,98},{4,99},{5,100},{6,101},{7,102},{8,103... | collective-permute-start | bytes 103688 | tf_op jit(solution)/shard_map/ppermute | solution.py:42
  66.4 3.1 %collective-permute-start.12 = (f32[4,1,12,720]{3,2,1,0:T(8,128)}, f32[4,1,12,720]{3,2,1,0:T(8,128)}, u32[]{:S(2)}, u32[]{:S(2)}) collective-permute-start(f32[4,1,12,720]{3,2,1,0:T(8,128)} %get-tuple-element.17), channel_id=1, source_target_pairs={{0,31},{1,0},{2,1},{3,2},{4,3},{5,4},{6,5},{7,6},{8,7},{9,8},{10,9... | collective-permute-start | bytes 414728 | tf_op jit(solution)/shard_map/ppermute | solution.py:34
  70.8 6.2 %collective-permute-done.8 = f32[1,1,12,720]{3,2,1,0:T(8,128)} collective-permute-done((f32[1,1,12,720]{3,2,1,0:T(8,128)}, f32[1,1,12,720]{3,2,1,0:T(8,128)}, u32[]{:S(2)}, u32[]{:S(2)}) %collective-permute-start.8) | collective-permute-done | bytes 34592 | tf_op jit(solution)/shard_map/ppermute | solution.py:42
  77.0 2.8 %maximum_maximum_fusion.1 = f32[6,10,12,720]{3,2,1,0:T(8,128)} fusion(f32[1,1,12,720]{3,2,1,0:T(8,128)S(1)} %collective-permute-done.15, f32[1,8,12,720]{3,2,1,0:T(8,128)S(1)} %collective-permute-done.14, f32[1,1,12,720]{3,2,1,0:T(8,128)S(1)} %collective-permute-done.13, f32[4,1,12,720]{3,2,1,0:T(8,128)} %collective-permute-done.12, ...), kind=kLoop, calls=%fused_computation.9 | loop fusion | flops 5184000 | bytes 4147200 | tf_op jit(solution)/shard_map/concatenate | solution.py:55
  79.9 2.5 %reshape.99 = f32[720,720]{1,0:T(8,128)S(1)} reshape(f32[6,10,12,720]{3,2,1,0:T(8,128)} %maximum_maximum_fusion.1) | data formatting | bytes 4147200 | tf_op jit(solution)/shard_map/reshape | solution.py:243
  82.4 2.6 %gather_fusion.5 = f32[512,720]{1,0:T(8,128)} fusion(f32[720,720]{1,0:T(8,128)S(1)} %reshape.99, s32[1024]{0:T(1024)S(1)} %copy-done.14), kind=kCustom, calls=%fused_computation.1.clone | custom fusion | bytes 2951168 | tf_op jit(solution)/shard_map/jit(_take)/gather | solution.py:243
  85.1 1.7 %broadcast_select_fusion = f32[512,720]{1,0:T(8,128)S(1)} fusion(f32[512,720]{1,0:T(8,128)} %gather_fusion.5, pred[512]{0:T(512)(128)(4,1)S(1)} %copy-done.17), kind=kLoop, calls=%fused_computation.19 | loop fusion | flops 368640 | bytes 2949632 | tf_op jit(solution)/shard_map/jit(_take)/select_n | solution.py:243
  91.7 20.0 %all_to_all.10 = f32[128,1,321]{2,1,0:T(1,128)S(1)} all-to-all(f32[128,1,321]{2,1,0:T(1,128)S(1)} %copy.51), channel_id=1, replica_groups=mesh['face'=4,'col'=32] {'face','col'}, dimensions={0} | all-to-all | bytes 328704 | tf_op jit(solution)/shard_map/all_to_all | solution.py:207
  113.2 2.5 %copy-done = bf16[10,32,64,128]{3,2,1,0:T(8,128)(2,1)S(1)} copy-done((bf16[10,32,64,128]{3,2,1,0:T(8,128)(2,1)S(1)}, bf16[10,32,64,128]{3,2,1,0:T(8,128)(2,1)}, u32[]{:S(2)}) %copy-start) | copy-done | bytes 5242904
  115.7 18.4 %shard_map.121 = (bf16[10,32,64,128]{3,2,1,0:T(8,128)(2,1)}, f32[10,32,128]{2,1,0:T(8,128)S(1)}) custom-call(f32[10,32,128]{2,1,0:T(8,128)S(1)} %bitcast.60, s32[1,128]{1,0:T(1,128)S(1)} %bitcast.62, bf16[10,32,64,128]{3,2,1,0:T(8,128)(2,1)S(1)} %copy-done), custom_call_target="tpu_custom_call" | custom-call | tf_op jit(solution)/shard_map/pallas_call | solution.py:176
  135.2 14.6 %all_to_all.11 = f32[128,1,320]{2,1,0:T(1,128)S(1)} all-to-all(f32[128,1,320]{2,1,0:T(1,128)S(1)} %copy.56), channel_id=1, replica_groups=mesh['face'=4,'col'=32] {'face','col'}, dimensions={0} | all-to-all | bytes 327680 | tf_op jit(solution)/shard_map/all_to_all | solution.py:207
  (131 shorter events, 31.2 us)
Async XLA Ops:
  6.0 20.3 %collective-permute-start = (f32[1,1,12,720]{3,2,1,0:T(8,128)}, f32[1,1,12,720]{3,2,1,0:T(8,128)S(1)}, u32[]{:S(2)}, u32[]{:S(2)}) collective-permute-start(f32[1,1,12,720]{3,2,1,0:T(8,128)} %get-tuple-element.18), channel_id=1, source_target_pairs={{0,33},{1,34},{2,35},{3,36},{4,37},{5,38},{6,39},{7,40},{8,41},{9,... | collective-permute-start | bytes 103688 | tf_op jit(solution)/shard_map/ppermute | solution.py:42
  9.6 17.3 %collective-permute-start.2 = (f32[1,1,12,720]{3,2,1,0:T(8,128)}, f32[1,1,12,720]{3,2,1,0:T(8,128)}, u32[]{:S(2)}, u32[]{:S(2)}) collective-permute-start(f32[1,1,12,720]{3,2,1,0:T(8,128)} %get-tuple-element.21), channel_id=1, source_target_pairs={{0,63},{1,32},{2,33},{3,34},{4,35},{5,36},{6,37},{7,38},{8,39},{9,... | collective-permute-start | bytes 103688 | tf_op jit(solution)/shard_map/ppermute | solution.py:42
  9.7 19.0 %collective-permute-start.5 = (f32[1,1,12,720]{3,2,1,0:T(8,128)}, f32[1,1,12,720]{3,2,1,0:T(8,128)}, u32[]{:S(2)}, u32[]{:S(2)}) collective-permute-start(f32[1,1,12,720]{3,2,1,0:T(8,128)} %get-tuple-element.20), channel_id=1, source_target_pairs={{0,97},{1,98},{2,99},{3,100},{4,101},{5,102},{6,103},{7,104},{8,10... | collective-permute-start | bytes 103688 | tf_op jit(solution)/shard_map/ppermute | solution.py:42
  13.8 3.0 %copy-start.12 = (s32[4,8,4]{1,2,0:T(4,128)S(1)}, s32[4,8,4]{1,2,0:T(4,128)}, u32[]{:S(2)}) copy-start(s32[4,8,4]{1,2,0:T(4,128)} %param.13) | copy-start | bytes 1540
  13.8 3.7 %copy-start.2 = (s32[16]{0:T(128)S(1)}, s32[16]{0:T(128)}, u32[]{:S(2)}) copy-start(s32[16]{0:T(128)} %constant.153.clone) | copy-start | bytes 196
  13.9 22.3 %collective-permute-start.1 = (f32[1,8,12,720]{3,2,1,0:T(8,128)S(1)}, f32[1,8,12,720]{3,2,1,0:T(8,128)S(1)}, u32[]{:S(2)}, u32[]{:S(2)}) collective-permute-start(f32[1,8,12,720]{3,2,1,0:T(8,128)S(1)} %slice.115), channel_id=1, source_target_pairs={{0,32},{32,64},{64,96},{96,0},{1,33},{33,65},{65,97},{97,1},{2,34}... | collective-permute-start | bytes 829448 | tf_op jit(solution)/shard_map/ppermute | solution.py:34
  14.1 22.1 %collective-permute-start.6 = (f32[1,8,12,720]{3,2,1,0:T(8,128)S(1)}, f32[1,8,12,720]{3,2,1,0:T(8,128)S(1)}, u32[]{:S(2)}, u32[]{:S(2)}) collective-permute-start(f32[1,8,12,720]{3,2,1,0:T(8,128)S(1)} %pad_maximum_fusion.3), channel_id=1, source_target_pairs={{0,96},{32,0},{64,32},{96,64},{1,97},{33,1},{65,33},{97,65},{2,98}... | collective-permute-start | bytes 829448 | tf_op jit(solution)/shard_map/ppermute | solution.py:34
  25.4 10.8 %copy-start.21 = (s32[128]{0:T(128)}, s32[128]{0:T(128)S(1)}, u32[]{:S(2)}) copy-start(s32[128]{0:T(128)S(1)} %compare_select_fusion.3) | copy-start | bytes 1540
  26.9 9.3 %collective-permute-start.3 = (f32[4,1,12,720]{3,2,1,0:T(8,128)}, f32[4,1,12,720]{3,2,1,0:T(8,128)S(1)}, u32[]{:S(2)}, u32[]{:S(2)}) collective-permute-start(f32[4,1,12,720]{3,2,1,0:T(8,128)} %get-tuple-element.22), channel_id=1, source_target_pairs={{0,1},{1,2},{2,3},{3,4},{4,5},{5,6},{6,7},{7,8},{8,9},{9,10},{10,1... | collective-permute-start | bytes 414728 | tf_op jit(solution)/shard_map/ppermute | solution.py:34
  26.9 9.3 %collective-permute-start.4 = (f32[4,1,12,720]{3,2,1,0:T(8,128)}, f32[4,1,12,720]{3,2,1,0:T(8,128)}, u32[]{:S(2)}, u32[]{:S(2)}) collective-permute-start(f32[4,1,12,720]{3,2,1,0:T(8,128)} %get-tuple-element.23), channel_id=1, source_target_pairs={{0,31},{1,0},{2,1},{3,2},{4,3},{5,4},{6,5},{7,6},{8,7},{9,8},{10,9... | collective-permute-start | bytes 414728 | tf_op jit(solution)/shard_map/ppermute | solution.py:34
  28.6 13.0 %copy-start.13 = (s32[1024]{0:T(1024)}, s32[1024]{0:T(1024)S(1)}, u32[]{:S(2)}) copy-start(s32[1024]{0:T(1024)S(1)} %pad_clamp_fusion.2) | copy-start | bytes 12292
  28.6 7.6 %collective-permute-start.7 = (f32[1,1,12,720]{3,2,1,0:T(8,128)}, f32[1,1,12,720]{3,2,1,0:T(8,128)}, u32[]{:S(2)}, u32[]{:S(2)}) collective-permute-start(f32[1,1,12,720]{3,2,1,0:T(8,128)} %get-tuple-element.19), channel_id=1, source_target_pairs={{0,127},{1,96},{2,97},{3,98},{4,99},{5,100},{6,101},{7,102},{8,103... | collective-permute-start | bytes 103688 | tf_op jit(solution)/shard_map/ppermute | solution.py:42
  41.6 2.6 %copy-start.16 = (pred[512]{0:T(512)(128)(4,1)S(1)}, pred[512]{0:T(512)(128)(4,1)}, u32[]{:S(2)}) copy-start(pred[512]{0:T(512)(128)(4,1)} %compare_and_fusion) | copy-start | bytes 1540
  51.6 17.8 %copy-start.22 = (s32[128]{0:T(128)S(1)}, s32[128]{0:T(128)}, u32[]{:S(2)}) copy-start(s32[128]{0:T(128)} %gather_fusion.2) | copy-start | bytes 1540
  51.6 25.4 %collective-permute-start.9 = (f32[1,8,12,720]{3,2,1,0:T(8,128)S(1)}, f32[1,8,12,720]{3,2,1,0:T(8,128)S(1)}, u32[]{:S(2)}, u32[]{:S(2)}) collective-permute-start(f32[1,8,12,720]{3,2,1,0:T(8,128)S(1)} %slice.119), channel_id=1, source_target_pairs={{0,32},{32,64},{64,96},{96,0},{1,33},{33,65},{65,97},{97,1},{2,34}... | collective-permute-start | bytes 829448 | tf_op jit(solution)/shard_map/ppermute | solution.py:34
  53.1 23.9 %collective-permute-start.14 = (f32[1,8,12,720]{3,2,1,0:T(8,128)S(1)}, f32[1,8,12,720]{3,2,1,0:T(8,128)S(1)}, u32[]{:S(2)}, u32[]{:S(2)}) collective-permute-start(f32[1,8,12,720]{3,2,1,0:T(8,128)S(1)} %pad_maximum_fusion.2), channel_id=1, source_target_pairs={{0,96},{32,0},{64,32},{96,64},{1,97},{33,1},{65,33},{97,65},{2,98}... | collective-permute-start | bytes 829448 | tf_op jit(solution)/shard_map/ppermute | solution.py:34
  54.4 10.4 %collective-permute-start.10 = (f32[1,1,12,720]{3,2,1,0:T(8,128)S(1)}, f32[1,1,12,720]{3,2,1,0:T(8,128)S(1)}, u32[]{:S(2)}, u32[]{:S(2)}) collective-permute-start(f32[1,1,12,720]{3,2,1,0:T(8,128)S(1)} %get-tuple-element.15), channel_id=1, source_target_pairs={{0,63},{1,32},{2,33},{3,34},{4,35},{5,36},{6,37},{7,38},{8,39},{9,... | collective-permute-start | bytes 103688 | tf_op jit(solution)/shard_map/ppermute | solution.py:42
  55.6 10.7 %collective-permute-start.13 = (f32[1,1,12,720]{3,2,1,0:T(8,128)S(1)}, f32[1,1,12,720]{3,2,1,0:T(8,128)S(1)}, u32[]{:S(2)}, u32[]{:S(2)}) collective-permute-start(f32[1,1,12,720]{3,2,1,0:T(8,128)S(1)} %get-tuple-element.14), channel_id=1, source_target_pairs={{0,97},{1,98},{2,99},{3,100},{4,101},{5,102},{6,103},{7,104},{8,10... | collective-permute-start | bytes 103688 | tf_op jit(solution)/shard_map/ppermute | solution.py:42
  58.2 11.2 %collective-permute-start.15 = (f32[1,1,12,720]{3,2,1,0:T(8,128)S(1)}, f32[1,1,12,720]{3,2,1,0:T(8,128)S(1)}, u32[]{:S(2)}, u32[]{:S(2)}) collective-permute-start(f32[1,1,12,720]{3,2,1,0:T(8,128)S(1)} %get-tuple-element.13), channel_id=1, source_target_pairs={{0,127},{1,96},{2,97},{3,98},{4,99},{5,100},{6,101},{7,102},{8,103... | collective-permute-start | bytes 103688 | tf_op jit(solution)/shard_map/ppermute | solution.py:42
  64.8 12.2 %collective-permute-start.11 = (f32[4,1,12,720]{3,2,1,0:T(8,128)}, f32[4,1,12,720]{3,2,1,0:T(8,128)}, u32[]{:S(2)}, u32[]{:S(2)}) collective-permute-start(f32[4,1,12,720]{3,2,1,0:T(8,128)} %get-tuple-element.16), channel_id=1, source_target_pairs={{0,1},{1,2},{2,3},{3,4},{4,5},{5,6},{6,7},{7,8},{8,9},{9,10},{10,1... | collective-permute-start | bytes 414728 | tf_op jit(solution)/shard_map/ppermute | solution.py:34
  66.4 10.6 %collective-permute-start.12 = (f32[4,1,12,720]{3,2,1,0:T(8,128)}, f32[4,1,12,720]{3,2,1,0:T(8,128)}, u32[]{:S(2)}, u32[]{:S(2)}) collective-permute-start(f32[4,1,12,720]{3,2,1,0:T(8,128)} %get-tuple-element.17), channel_id=1, source_target_pairs={{0,31},{1,0},{2,1},{3,2},{4,3},{5,4},{6,5},{7,6},{8,7},{9,8},{10,9... | collective-permute-start | bytes 414728 | tf_op jit(solution)/shard_map/ppermute | solution.py:34
  69.4 7.6 %collective-permute-start.8 = (f32[1,1,12,720]{3,2,1,0:T(8,128)}, f32[1,1,12,720]{3,2,1,0:T(8,128)}, u32[]{:S(2)}, u32[]{:S(2)}) collective-permute-start(f32[1,1,12,720]{3,2,1,0:T(8,128)} %get-tuple-element.12), channel_id=1, source_target_pairs={{0,33},{1,34},{2,35},{3,36},{4,37},{5,38},{6,39},{7,40},{8,41},{9,... | collective-permute-start | bytes 103688 | tf_op jit(solution)/shard_map/ppermute | solution.py:42
  82.4 2.6 %copy-start.17 = (pred[512]{0:T(512)(128)(4,1)S(1)}, pred[512]{0:T(512)(128)(4,1)}, u32[]{:S(2)}) copy-start(pred[512]{0:T(512)(128)(4,1)} %compare_and_fusion) | copy-start | bytes 1540
  91.4 21.8 %copy-start.1 = (s32[128]{0:T(128)S(1)}, s32[128]{0:T(128)}, u32[]{:S(2)}) copy-start(s32[128]{0:T(128)} %param.15) | copy-start | bytes 1540
  (15 other events, 24.7 us)

commit v4 on v2

--- a/solution.py
+++ b/solution.py
@@ -19,6 +19,7 @@
 DIFF_Z = 0.1
 RELAX = 0.2
 CONVERT = 0.5
+KEEP = 1.0 - 2.0 * DIFF_X - 2.0 * DIFF_Z
 
 
 def extended_2(cells, sides, width):
@@ -73,7 +74,7 @@
 ZCHUNK = 4
 
 
-def crm_kernel(force_ref, live_ref, state_hbm, new_hbm, tend_ref, held, mid, out, in_sem, out_sem):
+def crm_kernel(force_ref, live_ref, state_hbm, new_hbm, tend_ref, held, wide, mid, out, in_sem, out_sem):
     nfld, nlev, nx, _ = held.shape
     chunks = nlev // ZCHUNK
 
@@ -92,7 +93,10 @@
     def sweep(src, z, last):
         upper_z = jnp.minimum(z + 1, nlev - 1)
         lower_z = jnp.maximum(z - 1, 0)
-        lead = src[0, z].astype(jnp.float32)
+        if last:
+            lead = ADVECT * mid[0, z]
+        else:
+            lead = ADVECT * wide[0, z]
         kept = {}
 
         def finish(f, fresh, state):
@@ -104,19 +108,25 @@
                 mid[f, z] = new
 
         for f in range(nfld):
-            state = src[f, z].astype(jnp.float32)
-            upper = src[f, upper_z].astype(jnp.float32)
-            lower = src[f, lower_z].astype(jnp.float32)
+            if last:
+                state = mid[f, z]
+                upper = mid[f, upper_z]
+                lower = mid[f, lower_z]
+            else:
+                state = wide[f, z]
+                lower = wide[f, lower_z]
+                upper = held[f, upper_z].astype(jnp.float32)
+                wide[f, upper_z] = upper
             east = pltpu.roll(state, nx - 1, 0)
             west = pltpu.roll(state, 1, 0)
             mean_x = jnp.mean(state, axis=0, keepdims=True)
             if not last:
                 tend_ref[f, pl.ds(z, 1)] = mean_x
             fresh = (
-                state
-                - ADVECT * lead * (east - west)
-                + DIFF_X * (east + west - 2.0 * state)
-                + DIFF_Z * (upper + lower - 2.0 * state)
+                KEEP * state
+                + DIFF_X * (east + west)
+                + DIFF_Z * (upper + lower)
+                - lead * (east - west)
                 + RELAX * (force_ref[f, pl.ds(z, 1)] - mean_x)
             )
             if f in (2, 3):
@@ -133,6 +143,8 @@
     for c in range(chunks):
         if c == 0:
             in_copy(0).wait()
+            for f in range(nfld):
+                wide[f, 0] = held[f, 0].astype(jnp.float32)
         if c + 1 < chunks:
             in_copy(c + 1).wait()
 
@@ -164,14 +176,15 @@
         in_specs=[
             pl.BlockSpec(memory_space=pltpu.VMEM),
             pl.BlockSpec(memory_space=pltpu.VMEM),
-            pl.BlockSpec(memory_space=pl.ANY),
+            pl.BlockSpec(memory_space=pltpu.HBM),
         ],
         out_specs=(
-            pl.BlockSpec(memory_space=pl.ANY),
+            pl.BlockSpec(memory_space=pltpu.HBM),
             pl.BlockSpec(memory_space=pltpu.VMEM),
         ),
         scratch_shapes=[
             pltpu.VMEM(state.shape, jnp.bfloat16),
+            pltpu.VMEM(state.shape, jnp.float32),
             pltpu.VMEM(state.shape, jnp.float32),
             pltpu.VMEM(state.shape, jnp.bfloat16),
             pltpu.SemaphoreType.DMA((nlev // ZCHUNK,)),
@@ -181,7 +194,7 @@
     )(forcing, active.reshape(1, ncol), state)
 
 
-TWO_STAGE = True
+TWO_STAGE = False
 
 
 def exchange(chunks):

time: 140 us -> 127 us (0.907)
  blocking collectives: 49.1 us -> 37.3 us
  Pallas kernels: 18.4 us -> 16.8 us
    all_to_all x4 -> x2, blocking collectives: 49.1 us -> 37.3 us  [exchange(): lax.all_to_all(chunks, ('face', 'col'), split_axis=0, concat_axis=0, tile...]
    pallas_call x1, Pallas kernels: 18.4 us -> 16.8 us  [crm_run(): pl.pallas_call(crm_kernel, out_shape=(jax.ShapeDtypeStruct(state.shape, j...]
where the time goes in v4:
time: 127 us
  blocking collectives  37.3 us (29%)
  waiting for transfers between devices  22.8 us (18%)
  local copies, waits for them, and re-layouts  17.1 us (13%)
  Pallas kernels  16.8 us (13%)
  starting transfers between devices  12.2 us (10%)
  other arithmetic  10 us (8%)
  matrix products  9.12 us (7%)
    all_to_all x2, blocking collectives, exchange(): lax.all_to_all(chunks, ('face', 'col'), split_axis=0, concat_axis=0, tile...  37.3 us
    ppermute x4, waiting for transfers between devices, extended_2(): lax.ppermute(tail, axis, [(i, (i + 1) % count) for i in range(count)])  18 us
    pallas_call x1, Pallas kernels, crm_run(): pl.pallas_call(crm_kernel, out_shape=(jax.ShapeDtypeStruct(state.shape, j...  16.8 us
    ppermute x4, starting transfers between devices, extended_2(): lax.ppermute(tail, axis, [(i, (i + 1) % count) for i in range(count)])  9.01 us
    gather x2, local copies, waits for them, and re-layouts, per_device(): jnp.take(extended.reshape(-1, width), index_flat, axis=0)  5.19 us
    dot_general x2, matrix products, per_device(): jnp.einsum('nm,rcmw->rcnw', laplace, state, precision=lax.Precision.HIGHEST)  5.18 us
    ppermute x4, waiting for transfers between devices, extended_2(): lax.ppermute(head, axis, [((i + 1) % count, i) for i in range(count)])  4.83 us
    concatenate x2, other arithmetic, extended_2(): jnp.concatenate([lax.ppermute(tail, axis, [(i, (i + 1) % count) for i in...  3.69 us
  transfers between devices with their start and end apart: 8, of which 6 were waited for; matrix products, arithmetic and copies ran while one was open for 4% of the time, Pallas kernels for 0%

profile of v4, /device:TPU:1, one launch (start us, length us, event | category | flops | bytes accessed | tf_op | source)
XLA Modules:
  0.0 126.6 jit_solution(9078507640623406089)
XLA Ops:
  0.6 3.4 %bitcast_add_fusion.3 = f32[4,8,16,720]{3,2,1,0:T(8,128)S(1)} fusion(f32[4,8,16,720]{3,2,1,0:T(8,128)} %param.11, f32[16,16,1,1]{1,0,3,2:T(8,128)} %constant.154), kind=kOutput, calls=%fused_computation.14 | convolution fusion | flops 71516160 | bytes 2950144 | tf_op jit(solution)/shard_map/nm,rcmw->rcnw/dot_general | solution.py:232
  4.1 2.2 %collective-permute-start = (f32[1,8,16,720]{3,2,1,0:T(8,128)S(1)}, f32[1,8,16,720]{3,2,1,0:T(8,128)S(1)}, u32[]{:S(2)}, u32[]{:S(2)}) collective-permute-start(f32[1,8,16,720]{3,2,1,0:T(8,128)S(1)} %get-tuple-element.18), channel_id=1, source_target_pairs={{0,32},{32,64},{64,96},{96,0},{1,33},{33,65},{65,97},{97,1},{2,34}... | collective-permute-start | bytes 1105928 | tf_op jit(solution)/shard_map/ppermute | solution.py:32
  6.3 1.5 %collective-permute-start.1 = (f32[1,8,16,720]{3,2,1,0:T(8,128)S(1)}, f32[1,8,16,720]{3,2,1,0:T(8,128)S(1)}, u32[]{:S(2)}, u32[]{:S(2)}) collective-permute-start(f32[1,8,16,720]{3,2,1,0:T(8,128)S(1)} %get-tuple-element.19), channel_id=1, source_target_pairs={{32,0},{64,32},{96,64},{0,96},{33,1},{65,33},{97,65},{1,97},{34,2}... | collective-permute-start | bytes 1105928 | tf_op jit(solution)/shard_map/ppermute | solution.py:34
  8.7 7.7 %collective-permute-done = f32[1,8,16,720]{3,2,1,0:T(8,128)S(1)} collective-permute-done((f32[1,8,16,720]{3,2,1,0:T(8,128)S(1)}, f32[1,8,16,720]{3,2,1,0:T(8,128)S(1)}, u32[]{:S(2)}, u32[]{:S(2)}) %collective-permute-start) | collective-permute-done | bytes 368672 | tf_op jit(solution)/shard_map/ppermute | solution.py:32
  16.5 2.5 %collective-permute-start.2 = (f32[6,1,16,720]{3,2,1,0:T(8,128)S(1)}, f32[6,1,16,720]{3,2,1,0:T(8,128)S(1)}, u32[]{:S(2)}, u32[]{:S(2)}) collective-permute-start(f32[6,1,16,720]{3,2,1,0:T(8,128)S(1)} %get-tuple-element.14), channel_id=1, source_target_pairs={{0,1},{1,2},{2,3},{3,4},{4,5},{5,6},{6,7},{7,8},{8,9},{9,10},{10,1... | collective-permute-start | bytes 829448 | tf_op jit(solution)/shard_map/ppermute | solution.py:32
  19.1 3.6 %collective-permute-done.2 = f32[6,1,16,720]{3,2,1,0:T(8,128)S(1)} collective-permute-done((f32[6,1,16,720]{3,2,1,0:T(8,128)S(1)}, f32[6,1,16,720]{3,2,1,0:T(8,128)S(1)}, u32[]{:S(2)}, u32[]{:S(2)}) %collective-permute-start.2) | collective-permute-done | bytes 276512 | tf_op jit(solution)/shard_map/ppermute | solution.py:32
  22.7 2.8 %collective-permute-done.3 = f32[6,1,16,720]{3,2,1,0:T(8,128)S(1)} collective-permute-done((f32[6,1,16,720]{3,2,1,0:T(8,128)S(1)}, f32[6,1,16,720]{3,2,1,0:T(8,128)S(1)}, u32[]{:S(2)}, u32[]{:S(2)}) %collective-permute-start.3) | collective-permute-done | bytes 276512 | tf_op jit(solution)/shard_map/ppermute | solution.py:34
  25.5 1.8 %pad_maximum_fusion = f32[6,10,16,720]{3,2,1,0:T(8,128)S(1)} fusion(f32[6,1,16,720]{3,2,1,0:T(8,128)S(1)} %collective-permute-done.3, f32[1,8,16,720]{3,2,1,0:T(8,128)} %copy-done.7, f32[4,8,16,720]{3,2,1,0:T(8,128)} %copy-done.2, f32[1,8,16,720]{3,2,1,0:T(8,128)S(1)} %collective-permute-done, f32[6,1,16,720]{3,2,1,0:T(8,128)S(1)} %collective-permute-done.2), kind=kLoop, calls=%fused_computation.7 | loop fusion | flops 2764800 | bytes 5529600 | tf_op jit(solution)/shard_map/concatenate | solution.py:30
  27.3 2.6 %gather_fusion.3 = f32[512,720]{1,0:T(8,128)} fusion(f32[960,720]{1,0:T(8,128)S(1)} %bitcast.66, s32[1024]{0:T(1024)S(1)} %pad_clamp_fusion.2), kind=kCustom, calls=%fused_computation.clone | custom fusion | bytes 2951168 | tf_op jit(solution)/shard_map/jit(_take)/gather | solution.py:236
  29.9 1.6 %broadcast_select_fusion.1 = f32[512,720]{1,0:T(8,128)S(1)} fusion(f32[512,720]{1,0:T(8,128)} %gather_fusion.3, pred[512]{0:T(512)(128)(4,1)S(1)} %compare_and_fusion), kind=kLoop, calls=%fused_computation.17 | loop fusion | flops 368640 | bytes 2949632 | tf_op jit(solution)/shard_map/jit(_take)/select_n | solution.py:236
  33.0 1.8 %bitcast_add_fusion.1 = f32[4,8,16,720]{3,2,1,0:T(8,128)S(1)} fusion(f32[16,16,1,1]{1,0,3,2:T(8,128)S(1)} %copy-done.11, f32[4,8,16,720]{3,2,1,0:T(8,128)S(1)} %copy-done.3, f32[4,8,720,16]{2,3,1,0:T(8,128)S(1)} %fusion.33, f32[16]{0:T(128)S(1)} %copy-done.15), kind=kOutput, calls=%fused_computation.11 | convolution fusion | flops 72990720 | bytes 4424768 | tf_op jit(solution)/shard_map/nm,rcmw->rcnw/dot_general | solution.py:232
  38.0 2.5 %sort.17 = (s32[128]{0:T(128)}, s32[128]{0:T(128)S(1)}) sort(s32[128]{0:T(128)S(1)} %reshape.86, s32[128]{0:T(128)S(1)} %iota.35), dimensions={0}, to_apply=%region_0.2 | sort | flops 896 | bytes 2048 | tf_op jit(solution)/shard_map/jit(argsort)/sort | solution.py:247
  40.6 4.5 %collective-permute-done.4 = f32[1,8,16,720]{3,2,1,0:T(8,128)S(1)} collective-permute-done((f32[1,8,16,720]{3,2,1,0:T(8,128)S(1)}, f32[1,8,16,720]{3,2,1,0:T(8,128)S(1)}, u32[]{:S(2)}, u32[]{:S(2)}) %collective-permute-start.4) | collective-permute-done | bytes 368672 | tf_op jit(solution)/shard_map/ppermute | solution.py:32
  45.1 2.9 %collective-permute-start.6 = (f32[6,1,16,720]{3,2,1,0:T(8,128)S(1)}, f32[6,1,16,720]{3,2,1,0:T(8,128)S(1)}, u32[]{:S(2)}, u32[]{:S(2)}) collective-permute-start(f32[6,1,16,720]{3,2,1,0:T(8,128)S(1)} %get-tuple-element.12), channel_id=1, source_target_pairs={{0,1},{1,2},{2,3},{3,4},{4,5},{5,6},{6,7},{7,8},{8,9},{9,10},{10,1... | collective-permute-start | bytes 829448 | tf_op jit(solution)/shard_map/ppermute | solution.py:32
  49.6 2.1 %collective-permute-done.6 = f32[6,1,16,720]{3,2,1,0:T(8,128)S(1)} collective-permute-done((f32[6,1,16,720]{3,2,1,0:T(8,128)S(1)}, f32[6,1,16,720]{3,2,1,0:T(8,128)S(1)}, u32[]{:S(2)}, u32[]{:S(2)}) %collective-permute-start.6) | collective-permute-done | bytes 276512 | tf_op jit(solution)/shard_map/ppermute | solution.py:32
  52.4 2.0 %collective-permute-done.7 = f32[6,1,16,720]{3,2,1,0:T(8,128)} collective-permute-done((f32[6,1,16,720]{3,2,1,0:T(8,128)S(1)}, f32[6,1,16,720]{3,2,1,0:T(8,128)}, u32[]{:S(2)}, u32[]{:S(2)}) %collective-permute-start.7) | collective-permute-done | bytes 276512 | tf_op jit(solution)/shard_map/ppermute | solution.py:34
  54.5 1.9 %pad_maximum_fusion.1 = f32[6,10,16,720]{3,2,1,0:T(8,128)S(1)} fusion(f32[6,1,16,720]{3,2,1,0:T(8,128)} %collective-permute-done.7, f32[1,8,16,720]{3,2,1,0:T(8,128)} %copy-done.8, f32[4,8,16,720]{3,2,1,0:T(8,128)} %copy-done.4, f32[1,8,16,720]{3,2,1,0:T(8,128)S(1)} %collective-permute-done.4, f32[6,1,16,720]{3,2,1,0:T(8,128)} %copy-done.9), kind=kLoop, calls=%fused_computation.8 | loop fusion | flops 2764800 | bytes 5529600 | tf_op jit(solution)/shard_map/concatenate | solution.py:30
  56.4 2.6 %gather_fusion.4 = f32[512,720]{1,0:T(8,128)} fusion(f32[960,720]{1,0:T(8,128)S(1)} %bitcast.65, s32[1024]{0:T(1024)S(1)} %pad_clamp_fusion.2), kind=kCustom, calls=%fused_computation.1.clone | custom fusion | bytes 2951168 | tf_op jit(solution)/shard_map/jit(_take)/gather | solution.py:236
  59.0 1.7 %broadcast_select_fusion = f32[512,720]{1,0:T(8,128)S(1)} fusion(f32[512,720]{1,0:T(8,128)} %gather_fusion.4, pred[512]{0:T(512)(128)(4,1)S(1)} %compare_and_fusion), kind=kLoop, calls=%fused_computation.16 | loop fusion | flops 368640 | bytes 2949632 | tf_op jit(solution)/shard_map/jit(_take)/select_n | solution.py:236
  60.9 1.5 %fusion = f32[4,8,16,720]{3,2,1,0:T(8,128)S(1)} fusion(f32[4,8,16,720]{3,2,1,0:T(8,128)S(1)} %copy-done.5, f32[4,8,16,720]{3,2,1,0:T(8,128)S(1)} %bitcast.68, f32[16,16,1,1]{1,0,3,2:T(8,128)S(1)} %copy-done.10, f32[16]{0:T(128)S(1)} %copy-done.15), kind=kOutput, calls=%fused_computation.10 | convolution fusion | flops 71516160 | bytes 4424768 | tf_op jit(solution)/shard_map/nm,rcmw->rcnw/dot_general | solution.py:239
  65.5 22.7 %all_to_all.10 = f32[128,1,321]{2,1,0:T(1,128)S(1)} all-to-all(f32[128,1,321]{2,1,0:T(1,128)S(1)} %copy.50), channel_id=1, replica_groups=mesh['face'=4,'col'=32] {'face','col'}, dimensions={0} | all-to-all | bytes 328704 | tf_op jit(solution)/shard_map/all_to_all | solution.py:202
  89.7 2.5 %copy-done = bf16[10,32,64,128]{3,2,1,0:T(8,128)(2,1)S(1)} copy-done((bf16[10,32,64,128]{3,2,1,0:T(8,128)(2,1)S(1)}, bf16[10,32,64,128]{3,2,1,0:T(8,128)(2,1)}, u32[]{:S(2)}) %copy-start) | copy-done | bytes 5242904
  92.2 16.8 %shard_map.112 = (bf16[10,32,64,128]{3,2,1,0:T(8,128)(2,1)}, f32[10,32,128]{2,1,0:T(8,128)S(1)}) custom-call(f32[10,32,128]{2,1,0:T(8,128)S(1)} %bitcast.62, s32[1,128]{1,0:T(1,128)S(1)} %bitcast.64, bf16[10,32,64,128]{3,2,1,0:T(8,128)(2,1)S(1)} %copy-done), custom_call_target="tpu_custom_call" | custom-call | tf_op jit(solution)/shard_map/pallas_call | solution.py:170
  110.1 14.6 %all_to_all.11 = f32[128,1,320]{2,1,0:T(1,128)S(1)} all-to-all(f32[128,1,320]{2,1,0:T(1,128)S(1)} %copy.55), channel_id=1, replica_groups=mesh['face'=4,'col'=32] {'face','col'}, dimensions={0} | all-to-all | bytes 327680 | tf_op jit(solution)/shard_map/all_to_all | solution.py:202
  (84 shorter events, 15.5 us)
Async XLA Ops:
  4.0 12.5 %copy-start.2 = (f32[4,8,16,720]{3,2,1,0:T(8,128)}, f32[4,8,16,720]{3,2,1,0:T(8,128)S(1)}, u32[]{:S(2)}) copy-start(f32[4,8,16,720]{3,2,1,0:T(8,128)S(1)} %bitcast_add_fusion.3) | copy-start | bytes 4423684
  4.0 3.8 %copy-start.12 = (s32[4,8,4]{1,2,0:T(4,128)S(1)}, s32[4,8,4]{1,2,0:T(4,128)}, u32[]{:S(2)}) copy-start(s32[4,8,4]{1,2,0:T(4,128)} %param.12) | copy-start | bytes 1540
  4.1 12.3 %collective-permute-start = (f32[1,8,16,720]{3,2,1,0:T(8,128)S(1)}, f32[1,8,16,720]{3,2,1,0:T(8,128)S(1)}, u32[]{:S(2)}, u32[]{:S(2)}) collective-permute-start(f32[1,8,16,720]{3,2,1,0:T(8,128)S(1)} %get-tuple-element.18), channel_id=1, source_target_pairs={{0,32},{32,64},{64,96},{96,0},{1,33},{33,65},{65,97},{97,1},{2,34}... | collective-permute-start | bytes 1105928 | tf_op jit(solution)/shard_map/ppermute | solution.py:32
  6.3 10.1 %collective-permute-start.1 = (f32[1,8,16,720]{3,2,1,0:T(8,128)S(1)}, f32[1,8,16,720]{3,2,1,0:T(8,128)S(1)}, u32[]{:S(2)}, u32[]{:S(2)}) collective-permute-start(f32[1,8,16,720]{3,2,1,0:T(8,128)S(1)} %get-tuple-element.19), channel_id=1, source_target_pairs={{32,0},{64,32},{96,64},{0,96},{33,1},{65,33},{97,65},{1,97},{34,2}... | collective-permute-start | bytes 1105928 | tf_op jit(solution)/shard_map/ppermute | solution.py:34
  16.4 6.3 %copy-start.7 = (f32[1,8,16,720]{3,2,1,0:T(8,128)}, f32[1,8,16,720]{3,2,1,0:T(8,128)S(1)}, u32[]{:S(2)}) copy-start(f32[1,8,16,720]{3,2,1,0:T(8,128)S(1)} %collective-permute-done.1) | copy-start | bytes 1105924
  16.5 6.2 %collective-permute-start.2 = (f32[6,1,16,720]{3,2,1,0:T(8,128)S(1)}, f32[6,1,16,720]{3,2,1,0:T(8,128)S(1)}, u32[]{:S(2)}, u32[]{:S(2)}) collective-permute-start(f32[6,1,16,720]{3,2,1,0:T(8,128)S(1)} %get-tuple-element.14), channel_id=1, source_target_pairs={{0,1},{1,2},{2,3},{3,4},{4,5},{5,6},{6,7},{7,8},{8,9},{9,10},{10,1... | collective-permute-start | bytes 829448 | tf_op jit(solution)/shard_map/ppermute | solution.py:32
  19.0 6.4 %collective-permute-start.3 = (f32[6,1,16,720]{3,2,1,0:T(8,128)S(1)}, f32[6,1,16,720]{3,2,1,0:T(8,128)S(1)}, u32[]{:S(2)}, u32[]{:S(2)}) collective-permute-start(f32[6,1,16,720]{3,2,1,0:T(8,128)S(1)} %get-tuple-element.15), channel_id=1, source_target_pairs={{1,0},{2,1},{3,2},{4,3},{5,4},{6,5},{7,6},{8,7},{9,8},{10,9},{11,1... | collective-permute-start | bytes 829448 | tf_op jit(solution)/shard_map/ppermute | solution.py:34
  29.9 1.6 %copy-start.10 = (f32[16,16,1,1]{1,0,3,2:T(8,128)S(1)}, f32[16,16,1,1]{1,0,3,2:T(8,128)}, u32[]{:S(2)}) copy-start(f32[16,16,1,1]{1,0,3,2:T(8,128)} %constant.155) | copy-start | bytes 3076
  31.5 1.5 %copy-start.3 = (f32[4,8,16,720]{3,2,1,0:T(8,128)S(1)}, f32[4,8,16,720]{3,2,1,0:T(8,128)}, u32[]{:S(2)}) copy-start(f32[4,8,16,720]{3,2,1,0:T(8,128)} %copy-done.2) | copy-start | bytes 4423684
  31.5 1.5 %copy-start.11 = (f32[16,16,1,1]{1,0,3,2:T(8,128)S(1)}, f32[16,16,1,1]{1,0,3,2:T(8,128)}, u32[]{:S(2)}) copy-start(f32[16,16,1,1]{1,0,3,2:T(8,128)} %constant.154) | copy-start | bytes 3076
  31.5 1.5 %copy-start.15 = (f32[16]{0:T(128)S(1)}, f32[16]{0:T(128)}, u32[]{:S(2)}) copy-start(f32[16]{0:T(128)} %constant.152) | copy-start | bytes 196
  34.8 10.3 %copy-start.4 = (f32[4,8,16,720]{3,2,1,0:T(8,128)}, f32[4,8,16,720]{3,2,1,0:T(8,128)S(1)}, u32[]{:S(2)}) copy-start(f32[4,8,16,720]{3,2,1,0:T(8,128)S(1)} %bitcast_add_fusion.1) | copy-start | bytes 4423684
  34.9 3.0 %copy-start.13 = (s32[4,8,4]{1,2,0:T(4,128)S(1)}, s32[4,8,4]{1,2,0:T(4,128)}, u32[]{:S(2)}) copy-start(s32[4,8,4]{1,2,0:T(4,128)} %param.13) | copy-start | bytes 1540
  34.9 10.1 %collective-permute-start.4 = (f32[1,8,16,720]{3,2,1,0:T(8,128)S(1)}, f32[1,8,16,720]{3,2,1,0:T(8,128)S(1)}, u32[]{:S(2)}, u32[]{:S(2)}) collective-permute-start(f32[1,8,16,720]{3,2,1,0:T(8,128)S(1)} %get-tuple-element.16), channel_id=1, source_target_pairs={{0,32},{32,64},{64,96},{96,0},{1,33},{33,65},{65,97},{97,1},{2,34}... | collective-permute-start | bytes 1105928 | tf_op jit(solution)/shard_map/ppermute | solution.py:32
  36.3 8.8 %collective-permute-start.5 = (f32[1,8,16,720]{3,2,1,0:T(8,128)S(1)}, f32[1,8,16,720]{3,2,1,0:T(8,128)S(1)}, u32[]{:S(2)}, u32[]{:S(2)}) collective-permute-start(f32[1,8,16,720]{3,2,1,0:T(8,128)S(1)} %get-tuple-element.17), channel_id=1, source_target_pairs={{32,0},{64,32},{96,64},{0,96},{33,1},{65,33},{97,65},{1,97},{34,2}... | collective-permute-start | bytes 1105928 | tf_op jit(solution)/shard_map/ppermute | solution.py:34
  45.1 4.4 %copy-start.8 = (f32[1,8,16,720]{3,2,1,0:T(8,128)}, f32[1,8,16,720]{3,2,1,0:T(8,128)S(1)}, u32[]{:S(2)}) copy-start(f32[1,8,16,720]{3,2,1,0:T(8,128)S(1)} %collective-permute-done.5) | copy-start | bytes 1105924
  45.1 6.6 %collective-permute-start.6 = (f32[6,1,16,720]{3,2,1,0:T(8,128)S(1)}, f32[6,1,16,720]{3,2,1,0:T(8,128)S(1)}, u32[]{:S(2)}, u32[]{:S(2)}) collective-permute-start(f32[6,1,16,720]{3,2,1,0:T(8,128)S(1)} %get-tuple-element.12), channel_id=1, source_target_pairs={{0,1},{1,2},{2,3},{3,4},{4,5},{5,6},{6,7},{7,8},{8,9},{9,10},{10,1... | collective-permute-start | bytes 829448 | tf_op jit(solution)/shard_map/ppermute | solution.py:32
  48.0 6.4 %collective-permute-start.7 = (f32[6,1,16,720]{3,2,1,0:T(8,128)S(1)}, f32[6,1,16,720]{3,2,1,0:T(8,128)}, u32[]{:S(2)}, u32[]{:S(2)}) collective-permute-start(f32[6,1,16,720]{3,2,1,0:T(8,128)S(1)} %get-tuple-element.13), channel_id=1, source_target_pairs={{1,0},{2,1},{3,2},{4,3},{5,4},{6,5},{7,6},{8,7},{9,8},{10,9},{11,1... | collective-permute-start | bytes 829448 | tf_op jit(solution)/shard_map/ppermute | solution.py:34
  51.7 0.7 copy-start.9
  59.0 1.9 %copy-start.5 = (f32[4,8,16,720]{3,2,1,0:T(8,128)S(1)}, f32[4,8,16,720]{3,2,1,0:T(8,128)}, u32[]{:S(2)}) copy-start(f32[4,8,16,720]{3,2,1,0:T(8,128)} %copy-done.4) | copy-start | bytes 4423684
  60.9 1.5 %copy-start.14 = (f32[4,16,1,1]{1,0,3,2:T(4,128)S(1)}, f32[4,16,1,1]{1,0,3,2:T(4,128)}, u32[]{:S(2)}) copy-start(f32[4,16,1,1]{1,0,3,2:T(4,128)} %constant.156) | copy-start | bytes 772
  62.4 1.6 %copy-start.6 = (f32[4,8,16,720]{3,2,1,0:T(8,128)}, f32[4,8,16,720]{3,2,1,0:T(8,128)S(1)}, u32[]{:S(2)}) copy-start(f32[4,8,16,720]{3,2,1,0:T(8,128)S(1)} %fusion) | copy-start | bytes 4423684
  65.2 24.5 %copy-start.1 = (s32[128]{0:T(128)S(1)}, s32[128]{0:T(128)}, u32[]{:S(2)}) copy-start(s32[128]{0:T(128)} %param.14) | copy-start | bytes 1540
  89.7 2.5 %copy-start = (bf16[10,32,64,128]{3,2,1,0:T(8,128)(2,1)S(1)}, bf16[10,32,64,128]{3,2,1,0:T(8,128)(2,1)}, u32[]{:S(2)}) copy-start(bf16[10,32,64,128]{3,2,1,0:T(8,128)(2,1)} %state_hbm.1) | copy-start | bytes 15728644

commit v5 on v2

--- a/solution.py
+++ b/solution.py
@@ -19,6 +19,7 @@
 DIFF_Z = 0.1
 RELAX = 0.2
 CONVERT = 0.5
+KEEP = 1.0 - 2.0 * DIFF_X - 2.0 * DIFF_Z
 
 
 def extended_2(cells, sides, width):
@@ -73,50 +74,103 @@
 ZCHUNK = 4
 
 
-def crm_kernel(force_ref, live_ref, state_hbm, new_hbm, tend_ref, held, mid, out, in_sem, out_sem):
+def chunk_copies(src, dst, sems, count):
+    def one(c):
+        part = pl.ds(c * ZCHUNK, ZCHUNK)
+        return pltpu.make_async_copy(src.at[:, part], dst.at[:, part], sems.at[c])
+
+    return [one(c) for c in range(count)]
+
+
+def neighbours(z, nlev):
+    return jnp.minimum(z + 1, nlev - 1), jnp.maximum(z - 1, 0)
+
+
+def crm_first_kernel(live_ref, state_hbm, part_hbm, mean_ref, held, wide, part, in_sem, out_sem):
     nfld, nlev, nx, _ = held.shape
     chunks = nlev // ZCHUNK
-
-    def in_copy(c):
-        part = pl.ds(c * ZCHUNK, ZCHUNK)
-        return pltpu.make_async_copy(state_hbm.at[:, part], held.at[:, part], in_sem.at[c])
-
-    def out_copy(c):
-        part = pl.ds(c * ZCHUNK, ZCHUNK)
-        return pltpu.make_async_copy(out.at[:, part], new_hbm.at[:, part], out_sem.at[c])
+    loads = chunk_copies(state_hbm, held, in_sem, chunks)
+    stores = chunk_copies(part, part_hbm, out_sem, chunks)
+    for copy in loads:
+        copy.start()
+    live = live_ref[...] == 1
+
+    def level(z, carry):
+        upper_z, lower_z = neighbours(z, nlev)
+        lead = ADVECT * wide[0, z]
+        for f in range(nfld):
+            state = wide[f, z]
+            lower = wide[f, lower_z]
+            upper = held[f, upper_z].astype(jnp.float32)
+            wide[f, upper_z] = upper
+            east = pltpu.roll(state, nx - 1, 0)
+            west = pltpu.roll(state, 1, 0)
+            mean_ref[f, pl.ds(z, 1)] = jnp.mean(state, axis=0, keepdims=True)
+            fresh = KEEP * state + DIFF_X * (east + west) + DIFF_Z * (upper + lower) - lead * (east - west)
+            part[f, z] = jnp.where(live, fresh, state)
+        return carry
 
     for c in range(chunks):
-        in_copy(c).start()
+        if c == 0:
+            loads[0].wait()
+            for f in range(nfld):
+                wide[f, 0] = held[f, 0].astype(jnp.float32)
+        if c + 1 < chunks:
+            loads[c + 1].wait()
+        lax.fori_loop(c * ZCHUNK, (c + 1) * ZCHUNK, level, 0)
+        stores[c].start()
+    for copy in stores:
+        copy.wait()
+
+
+def crm_second_kernel(force_ref, live_ref, mean_ref, part_hbm, new_hbm, tend_ref, mid, out, in_sem, out_sem):
+    nfld, nlev, nx, _ = mid.shape
+    chunks = nlev // ZCHUNK
+    loads = chunk_copies(part_hbm, mid, in_sem, chunks)
+    stores = chunk_copies(out, new_hbm, out_sem, chunks)
+    for copy in loads:
+        copy.start()
     live = live_ref[...] == 1
 
-    def sweep(src, z, last):
-        upper_z = jnp.minimum(z + 1, nlev - 1)
-        lower_z = jnp.maximum(z - 1, 0)
-        lead = src[0, z].astype(jnp.float32)
+    def finish_first(z, carry):
+        fresh = [
+            mid[f, z]
+            + jnp.where(live, RELAX * (force_ref[f, pl.ds(z, 1)] - mean_ref[f, pl.ds(z, 1)]), 0.0)
+            for f in range(nfld)
+        ]
+        cond = CONVERT * jnp.maximum(fresh[3] - fresh[2], 0.0)
+        fresh[3] = jnp.where(live, fresh[3] - cond, fresh[3])
+        fresh[4] = jnp.where(live, fresh[4] + cond, fresh[4])
+        for f in range(nfld):
+            mid[f, z] = fresh[f]
+        return carry
+
+    for c in range(chunks):
+        loads[c].wait()
+        lax.fori_loop(c * ZCHUNK, (c + 1) * ZCHUNK, finish_first, 0)
+
+    def level(z, carry):
+        upper_z, lower_z = neighbours(z, nlev)
+        lead = ADVECT * mid[0, z]
         kept = {}
 
         def finish(f, fresh, state):
             new = jnp.where(live, fresh, state)
-            if last:
-                out[f, z] = new.astype(out.dtype)
-                tend_ref[f, pl.ds(z, 1)] = (jnp.mean(new, axis=0, keepdims=True) - tend_ref[f, pl.ds(z, 1)]) / CSTEPS
-            else:
-                mid[f, z] = new
+            out[f, z] = new.astype(out.dtype)
+            tend_ref[f, pl.ds(z, 1)] = (jnp.mean(new, axis=0, keepdims=True) - mean_ref[f, pl.ds(z, 1)]) / CSTEPS
 
         for f in range(nfld):
-            state = src[f, z].astype(jnp.float32)
-            upper = src[f, upper_z].astype(jnp.float32)
-            lower = src[f, lower_z].astype(jnp.float32)
+            state = mid[f, z]
+            upper = mid[f, upper_z]
+            lower = mid[f, lower_z]
             east = pltpu.roll(state, nx - 1, 0)
             west = pltpu.roll(state, 1, 0)
             mean_x = jnp.mean(state, axis=0, keepdims=True)
-            if not last:
-                tend_ref[f, pl.ds(z, 1)] = mean_x
             fresh = (
-                state
-                - ADVECT * lead * (east - west)
-                + DIFF_X * (east + west - 2.0 * state)
-                + DIFF_Z * (upper + lower - 2.0 * state)
+                KEEP * state
+                + DIFF_X * (east + west)
+                + DIFF_Z * (upper + lower)
+                - lead * (east - west)
                 + RELAX * (force_ref[f, pl.ds(z, 1)] - mean_x)
             )
             if f in (2, 3):
@@ -129,59 +183,69 @@
             if f == 4:
                 fresh = fresh + cond
             finish(f, fresh, state)
+        return carry
 
     for c in range(chunks):
-        if c == 0:
-            in_copy(0).wait()
-        if c + 1 < chunks:
-            in_copy(c + 1).wait()
-
-        def first(z, carry):
-            sweep(held, z, False)
-            return carry
-
-        lax.fori_loop(c * ZCHUNK, (c + 1) * ZCHUNK, first, 0)
-    for c in range(chunks):
-
-        def second(z, carry):
-            sweep(mid, z, True)
-            return carry
-
-        lax.fori_loop(c * ZCHUNK, (c + 1) * ZCHUNK, second, 0)
-        out_copy(c).start()
-    for c in range(chunks):
-        out_copy(c).wait()
-
-
-def crm_run(state, forcing, active):
+        lax.fori_loop(c * ZCHUNK, (c + 1) * ZCHUNK, level, 0)
+        stores[c].start()
+    for copy in stores:
+        copy.wait()
+
+
+def crm_first(state, active):
     nfld, nlev, nx, ncol = state.shape
+    chunks = nlev // ZCHUNK
     return pl.pallas_call(
-        crm_kernel,
+        crm_first_kernel,
         out_shape=(
-            jax.ShapeDtypeStruct(state.shape, jnp.bfloat16),
+            jax.ShapeDtypeStruct(state.shape, jnp.float32),
+            jax.ShapeDtypeStruct((nfld, nlev, ncol), jnp.float32),
+        ),
+        in_specs=[pl.BlockSpec(memory_space=pltpu.VMEM), pl.BlockSpec(memory_space=pl.ANY)],
+        out_specs=(pl.BlockSpec(memory_space=pl.ANY), pl.BlockSpec(memory_space=pltpu.VMEM)),
+        scratch_shapes=[
+            pltpu.VMEM(state.shape, jnp.bfloat16),
+            pltpu.VMEM(state.shape, jnp.float32),
+            pltpu.VMEM(state.shape, jnp.float32),
+            pltpu.SemaphoreType.DMA((chunks,)),
+            pltpu.SemaphoreType.DMA((chunks,)),
+        ],
+        compiler_params=pltpu.CompilerParams(vmem_limit_bytes=48 * 1024 * 1024),
+    )(active.reshape(1, ncol), state)
+
+
+def crm_second(part, start_mean, forcing, active):
+    nfld, nlev, nx, ncol = part.shape
+    chunks = nlev // ZCHUNK
+    return pl.pallas_call(
+        crm_second_kernel,
+        out_shape=(
+            jax.ShapeDtypeStruct(part.shape, jnp.bfloat16),
             jax.ShapeDtypeStruct((nfld, nlev, ncol), jnp.float32),
         ),
         in_specs=[
             pl.BlockSpec(memory_space=pltpu.VMEM),
             pl.BlockSpec(memory_space=pltpu.VMEM),
+            pl.BlockSpec(memory_space=pltpu.VMEM),
             pl.BlockSpec(memory_space=pl.ANY),
         ],
-        out_specs=(
-            pl.BlockSpec(memory_space=pl.ANY),
-            pl.BlockSpec(memory_space=pltpu.VMEM),
-        ),
+        out_specs=(pl.BlockSpec(memory_space=pl.ANY), pl.BlockSpec(memory_space=pltpu.VMEM)),
         scratch_shapes=[
-            pltpu.VMEM(state.shape, jnp.bfloat16),
-            pltpu.VMEM(state.shape, jnp.float32),
-            pltpu.VMEM(state.shape, jnp.bfloat16),
-            pltpu.SemaphoreType.DMA((nlev // ZCHUNK,)),
-            pltpu.SemaphoreType.DMA((nlev // ZCHUNK,)),
+            pltpu.VMEM(part.shape, jnp.float32),
+            pltpu.VMEM(part.shape, jnp.bfloat16),
+            pltpu.SemaphoreType.DMA((chunks,)),
+            pltpu.SemaphoreType.DMA((chunks,)),
         ],
         compiler_params=pltpu.CompilerParams(vmem_limit_bytes=48 * 1024 * 1024),
-    )(forcing, active.reshape(1, ncol), state)
-
-
-TWO_STAGE = True
+    )(forcing, active.reshape(1, ncol), start_mean, part)
+
+
+def crm_run(state, forcing, active):
+    part, start_mean = crm_first(state, active)
+    return crm_second(part, start_mean, forcing, active)
+
+
+TWO_STAGE = False
 
 
 def exchange(chunks):

time: 140 us -> 127 us (0.907)
  blocking collectives: 49.1 us -> 20 us
  starting transfers between devices: 12.2 us -> 24.7 us
  Pallas kernels: 18.4 us -> 21.5 us
    all_to_all x4 -> x1, blocking collectives: 49.1 us -> 20 us  [exchange(): lax.all_to_all(chunks, ('face', 'col'), split_axis=0, concat_axis=0, tile...]
    all_to_all x0 -> x1, starting transfers between devices: none -> 12.5 us  [exchange(): lax.all_to_all(chunks, ('face', 'col'), split_axis=0, concat_axis=0, tile...]
    pallas_call x1 -> x2, Pallas kernels: 18.4 us -> 21.5 us  [the longest x1 13.1 us: crm_second(): pl.pallas_call(crm_second_kernel, out_shape=(jax.ShapeDtypeStruct(part.sh...]
  transfers between devices with their start and end apart: 8 -> 9, of which waited for: 6 -> 6; matrix products, arithmetic and copies ran while one was open for 4% -> 4% of each run, Pallas kernels for 0% -> 7%
where the time goes in v5:
time: 127 us
  starting transfers between devices  24.7 us (19%)
  waiting for transfers between devices  22.8 us (18%)
  Pallas kernels  21.5 us (17%)
  blocking collectives  20 us (16%)
  local copies, waits for them, and re-layouts  17.8 us (14%)
  other arithmetic  10 us (8%)
  matrix products  9.16 us (7%)
    all_to_all x1, blocking collectives, exchange(): lax.all_to_all(chunks, ('face', 'col'), split_axis=0, concat_axis=0, tile...  20 us
    ppermute x4, waiting for transfers between devices, extended_2(): lax.ppermute(tail, axis, [(i, (i + 1) % count) for i in range(count)])  18 us
    pallas_call x1, Pallas kernels, crm_second(): pl.pallas_call(crm_second_kernel, out_shape=(jax.ShapeDtypeStruct(part.sh...  13.1 us
    all_to_all x1, starting transfers between devices, exchange(): lax.all_to_all(chunks, ('face', 'col'), split_axis=0, concat_axis=0, tile...  12.5 us
    ppermute x4, starting transfers between devices, extended_2(): lax.ppermute(tail, axis, [(i, (i + 1) % count) for i in range(count)])  9.02 us
    pallas_call x1, Pallas kernels, crm_first(): pl.pallas_call(crm_first_kernel, out_shape=(jax.ShapeDtypeStruct(state.sh...  8.38 us
    dot_general x2, matrix products, per_device(): jnp.einsum('nm,rcmw->rcnw', laplace, state, precision=lax.Precision.HIGHEST)  5.22 us
    gather x2, local copies, waits for them, and re-layouts, per_device(): jnp.take(extended.reshape(-1, width), index_flat, axis=0)  5.19 us
  transfers between devices with their start and end apart: 9, of which 6 were waited for; matrix products, arithmetic and copies ran while one was open for 4% of the time, Pallas kernels for 7%

profile of v5, /device:TPU:1, one launch (start us, length us, event | category | flops | bytes accessed | tf_op | source)
XLA Modules:
  0.0 127.1 jit_solution(5272351872673980480)
XLA Ops:
  0.6 3.4 %bitcast_add_fusion.3 = f32[4,8,16,720]{3,2,1,0:T(8,128)S(1)} fusion(f32[4,8,16,720]{3,2,1,0:T(8,128)} %param.11, f32[16,16,1,1]{1,0,3,2:T(8,128)} %constant.154), kind=kOutput, calls=%fused_computation.14 | convolution fusion | flops 71516160 | bytes 2950144 | tf_op jit(solution)/shard_map/nm,rcmw->rcnw/dot_general | solution.py:283
  4.1 2.2 %collective-permute-start = (f32[1,8,16,720]{3,2,1,0:T(8,128)S(1)}, f32[1,8,16,720]{3,2,1,0:T(8,128)S(1)}, u32[]{:S(2)}, u32[]{:S(2)}) collective-permute-start(f32[1,8,16,720]{3,2,1,0:T(8,128)S(1)} %get-tuple-element.22), channel_id=1, source_target_pairs={{0,32},{32,64},{64,96},{96,0},{1,33},{33,65},{65,97},{97,1},{2,34}... | collective-permute-start | bytes 1105928 | tf_op jit(solution)/shard_map/ppermute | solution.py:32
  8.7 7.7 %collective-permute-done = f32[1,8,16,720]{3,2,1,0:T(8,128)S(1)} collective-permute-done((f32[1,8,16,720]{3,2,1,0:T(8,128)S(1)}, f32[1,8,16,720]{3,2,1,0:T(8,128)S(1)}, u32[]{:S(2)}, u32[]{:S(2)}) %collective-permute-start) | collective-permute-done | bytes 368672 | tf_op jit(solution)/shard_map/ppermute | solution.py:32
  16.5 2.5 %collective-permute-start.2 = (f32[6,1,16,720]{3,2,1,0:T(8,128)S(1)}, f32[6,1,16,720]{3,2,1,0:T(8,128)S(1)}, u32[]{:S(2)}, u32[]{:S(2)}) collective-permute-start(f32[6,1,16,720]{3,2,1,0:T(8,128)S(1)} %get-tuple-element.18), channel_id=1, source_target_pairs={{0,1},{1,2},{2,3},{3,4},{4,5},{5,6},{6,7},{7,8},{8,9},{9,10},{10,1... | collective-permute-start | bytes 829448 | tf_op jit(solution)/shard_map/ppermute | solution.py:32
  19.1 3.6 %collective-permute-done.2 = f32[6,1,16,720]{3,2,1,0:T(8,128)S(1)} collective-permute-done((f32[6,1,16,720]{3,2,1,0:T(8,128)S(1)}, f32[6,1,16,720]{3,2,1,0:T(8,128)S(1)}, u32[]{:S(2)}, u32[]{:S(2)}) %collective-permute-start.2) | collective-permute-done | bytes 276512 | tf_op jit(solution)/shard_map/ppermute | solution.py:32
  22.7 2.8 %collective-permute-done.3 = f32[6,1,16,720]{3,2,1,0:T(8,128)S(1)} collective-permute-done((f32[6,1,16,720]{3,2,1,0:T(8,128)S(1)}, f32[6,1,16,720]{3,2,1,0:T(8,128)S(1)}, u32[]{:S(2)}, u32[]{:S(2)}) %collective-permute-start.3) | collective-permute-done | bytes 276512 | tf_op jit(solution)/shard_map/ppermute | solution.py:34
  25.5 1.8 %pad_maximum_fusion = f32[6,10,16,720]{3,2,1,0:T(8,128)S(1)} fusion(f32[6,1,16,720]{3,2,1,0:T(8,128)S(1)} %collective-permute-done.3, f32[1,8,16,720]{3,2,1,0:T(8,128)} %copy-done.7, f32[4,8,16,720]{3,2,1,0:T(8,128)} %copy-done.2, f32[1,8,16,720]{3,2,1,0:T(8,128)S(1)} %collective-permute-done, f32[6,1,16,720]{3,2,1,0:T(8,128)S(1)} %collective-permute-done.2), kind=kLoop, calls=%fused_computation.7 | loop fusion | flops 2764800 | bytes 5529600 | tf_op jit(solution)/shard_map/concatenate | solution.py:30
  27.3 2.6 %gather_fusion.3 = f32[512,720]{1,0:T(8,128)} fusion(f32[960,720]{1,0:T(8,128)S(1)} %bitcast.65, s32[1024]{0:T(1024)S(1)} %pad_clamp_fusion.2), kind=kCustom, calls=%fused_computation.clone | custom fusion | bytes 2951168 | tf_op jit(solution)/shard_map/jit(_take)/gather | solution.py:287
  29.9 1.6 %broadcast_select_fusion.1 = f32[512,720]{1,0:T(8,128)S(1)} fusion(f32[512,720]{1,0:T(8,128)} %gather_fusion.3, pred[512]{0:T(512)(128)(4,1)S(1)} %compare_and_fusion), kind=kLoop, calls=%fused_computation.17 | loop fusion | flops 368640 | bytes 2949632 | tf_op jit(solution)/shard_map/jit(_take)/select_n | solution.py:287
  33.1 1.8 %bitcast_add_fusion.1 = f32[4,8,16,720]{3,2,1,0:T(8,128)S(1)} fusion(f32[16,16,1,1]{1,0,3,2:T(8,128)S(1)} %copy-done.11, f32[4,8,16,720]{3,2,1,0:T(8,128)S(1)} %copy-done.3, f32[4,8,720,16]{2,3,1,0:T(8,128)S(1)} %fusion.33, f32[16]{0:T(128)S(1)} %copy-done.15), kind=kOutput, calls=%fused_computation.11 | convolution fusion | flops 72990720 | bytes 4424768 | tf_op jit(solution)/shard_map/nm,rcmw->rcnw/dot_general | solution.py:283
  38.1 2.5 %sort.17 = (s32[128]{0:T(128)}, s32[128]{0:T(128)S(1)}) sort(s32[128]{0:T(128)S(1)} %reshape.87, s32[128]{0:T(128)S(1)} %iota.35), dimensions={0}, to_apply=%region_0.2 | sort | flops 896 | bytes 2048 | tf_op jit(solution)/shard_map/jit(argsort)/sort | solution.py:298
  40.6 4.5 %collective-permute-done.4 = f32[1,8,16,720]{3,2,1,0:T(8,128)S(1)} collective-permute-done((f32[1,8,16,720]{3,2,1,0:T(8,128)S(1)}, f32[1,8,16,720]{3,2,1,0:T(8,128)S(1)}, u32[]{:S(2)}, u32[]{:S(2)}) %collective-permute-start.4) | collective-permute-done | bytes 368672 | tf_op jit(solution)/shard_map/ppermute | solution.py:32
  45.2 2.9 %collective-permute-start.6 = (f32[6,1,16,720]{3,2,1,0:T(8,128)S(1)}, f32[6,1,16,720]{3,2,1,0:T(8,128)S(1)}, u32[]{:S(2)}, u32[]{:S(2)}) collective-permute-start(f32[6,1,16,720]{3,2,1,0:T(8,128)S(1)} %get-tuple-element.16), channel_id=1, source_target_pairs={{0,1},{1,2},{2,3},{3,4},{4,5},{5,6},{6,7},{7,8},{8,9},{9,10},{10,1... | collective-permute-start | bytes 829448 | tf_op jit(solution)/shard_map/ppermute | solution.py:32
  49.6 2.1 %collective-permute-done.6 = f32[6,1,16,720]{3,2,1,0:T(8,128)S(1)} collective-permute-done((f32[6,1,16,720]{3,2,1,0:T(8,128)S(1)}, f32[6,1,16,720]{3,2,1,0:T(8,128)S(1)}, u32[]{:S(2)}, u32[]{:S(2)}) %collective-permute-start.6) | collective-permute-done | bytes 276512 | tf_op jit(solution)/shard_map/ppermute | solution.py:32
  52.5 2.1 %collective-permute-done.7 = f32[6,1,16,720]{3,2,1,0:T(8,128)} collective-permute-done((f32[6,1,16,720]{3,2,1,0:T(8,128)S(1)}, f32[6,1,16,720]{3,2,1,0:T(8,128)}, u32[]{:S(2)}, u32[]{:S(2)}) %collective-permute-start.7) | collective-permute-done | bytes 276512 | tf_op jit(solution)/shard_map/ppermute | solution.py:34
  54.5 1.9 %pad_maximum_fusion.1 = f32[6,10,16,720]{3,2,1,0:T(8,128)S(1)} fusion(f32[6,1,16,720]{3,2,1,0:T(8,128)} %collective-permute-done.7, f32[1,8,16,720]{3,2,1,0:T(8,128)} %copy-done.8, f32[4,8,16,720]{3,2,1,0:T(8,128)} %copy-done.4, f32[1,8,16,720]{3,2,1,0:T(8,128)S(1)} %collective-permute-done.4, f32[6,1,16,720]{3,2,1,0:T(8,128)} %copy-done.9), kind=kLoop, calls=%fused_computation.8 | loop fusion | flops 2764800 | bytes 5529600 | tf_op jit(solution)/shard_map/concatenate | solution.py:30
  56.4 2.6 %gather_fusion.4 = f32[512,720]{1,0:T(8,128)} fusion(f32[960,720]{1,0:T(8,128)S(1)} %bitcast.64, s32[1024]{0:T(1024)S(1)} %pad_clamp_fusion.2), kind=kCustom, calls=%fused_computation.1.clone | custom fusion | bytes 2951168 | tf_op jit(solution)/shard_map/jit(_take)/gather | solution.py:287
  59.0 1.7 %broadcast_select_fusion = f32[512,720]{1,0:T(8,128)S(1)} fusion(f32[512,720]{1,0:T(8,128)} %gather_fusion.4, pred[512]{0:T(512)(128)(4,1)S(1)} %compare_and_fusion), kind=kLoop, calls=%fused_computation.16 | loop fusion | flops 368640 | bytes 2949632 | tf_op jit(solution)/shard_map/jit(_take)/select_n | solution.py:287
  60.9 1.5 %fusion = f32[4,8,16,720]{3,2,1,0:T(8,128)S(1)} fusion(f32[4,8,16,720]{3,2,1,0:T(8,128)S(1)} %copy-done.5, f32[4,8,16,720]{3,2,1,0:T(8,128)S(1)} %bitcast.67, f32[16,16,1,1]{1,0,3,2:T(8,128)S(1)} %copy-done.10, f32[16]{0:T(128)S(1)} %copy-done.15), kind=kOutput, calls=%fused_computation.10 | convolution fusion | flops 71516160 | bytes 4424768 | tf_op jit(solution)/shard_map/nm,rcmw->rcnw/dot_general | solution.py:290
  66.2 12.5 %all-to-all-start = ((f32[128,1,321]{2,1,0:T(1,128)}), f32[128,1,321]{2,1,0:T(1,128)S(1)}, u32[]{:S(2)}, u32[]{:S(2)}) async-start(f32[128,1,321]{2,1,0:T(1,128)} %copy.50), calls=%async_computation | async-start | bytes 393216 | tf_op jit(solution)/shard_map/all_to_all | solution.py:253
  78.7 2.5 %copy-done = bf16[10,32,64,128]{3,2,1,0:T(8,128)(2,1)S(1)} copy-done((bf16[10,32,64,128]{3,2,1,0:T(8,128)(2,1)S(1)}, bf16[10,32,64,128]{3,2,1,0:T(8,128)(2,1)}, u32[]{:S(2)}) %copy-start) | copy-done | bytes 5242904
  81.2 8.4 %shard_map.112 = (f32[10,32,64,128]{3,2,1,0:T(8,128)}, f32[10,32,128]{2,1,0:T(8,128)S(1)}) custom-call(s32[1,128]{1,0:T(1,128)S(1)} %bitcast.62, bf16[10,32,64,128]{3,2,1,0:T(8,128)(2,1)S(1)} %copy-done), custom_call_target="tpu_custom_call" | custom-call | tf_op jit(solution)/shard_map/pallas_call | solution.py:198
  91.1 13.1 %shard_map.113 = (bf16[10,32,64,128]{3,2,1,0:T(8,128)(2,1)}, f32[10,32,128]{2,1,0:T(8,128)S(1)}) custom-call(f32[10,32,128]{2,1,0:T(8,128)S(1)} %bitcast.60, s32[1,128]{1,0:T(1,128)S(1)} %bitcast.63, f32[10,32,128]{2,1,0:T(8,128)S(1)} %get-tuple-element.10.mean_ref, f32[10,32,64,128]{3,2,1,0:T(8,128)} %get-tuple-element.11.part_hbm), custom_call_target="tpu_custom_call" | custom-call | tf_op jit(solution)/shard_map/pallas_call | solution.py:220
  105.3 20.0 %all_to_all.10 = f32[128,1,320]{2,1,0:T(1,128)S(1)} all-to-all(f32[128,1,320]{2,1,0:T(1,128)S(1)} %copy.55), channel_id=1, replica_groups=mesh['face'=4,'col'=32] {'face','col'}, dimensions={0} | all-to-all | bytes 327680 | tf_op jit(solution)/shard_map/all_to_all | solution.py:253
  (86 shorter events, 17.6 us)
Async XLA Ops:
  4.0 12.5 %copy-start.2 = (f32[4,8,16,720]{3,2,1,0:T(8,128)}, f32[4,8,16,720]{3,2,1,0:T(8,128)S(1)}, u32[]{:S(2)}) copy-start(f32[4,8,16,720]{3,2,1,0:T(8,128)S(1)} %bitcast_add_fusion.3) | copy-start | bytes 4423684
  4.1 3.8 %copy-start.12 = (s32[4,8,4]{1,2,0:T(4,128)S(1)}, s32[4,8,4]{1,2,0:T(4,128)}, u32[]{:S(2)}) copy-start(s32[4,8,4]{1,2,0:T(4,128)} %param.12) | copy-start | bytes 1540
  4.1 12.3 %collective-permute-start = (f32[1,8,16,720]{3,2,1,0:T(8,128)S(1)}, f32[1,8,16,720]{3,2,1,0:T(8,128)S(1)}, u32[]{:S(2)}, u32[]{:S(2)}) collective-permute-start(f32[1,8,16,720]{3,2,1,0:T(8,128)S(1)} %get-tuple-element.22), channel_id=1, source_target_pairs={{0,32},{32,64},{64,96},{96,0},{1,33},{33,65},{65,97},{97,1},{2,34}... | collective-permute-start | bytes 1105928 | tf_op jit(solution)/shard_map/ppermute | solution.py:32
  6.3 10.1 %collective-permute-start.1 = (f32[1,8,16,720]{3,2,1,0:T(8,128)S(1)}, f32[1,8,16,720]{3,2,1,0:T(8,128)S(1)}, u32[]{:S(2)}, u32[]{:S(2)}) collective-permute-start(f32[1,8,16,720]{3,2,1,0:T(8,128)S(1)} %get-tuple-element.23), channel_id=1, source_target_pairs={{32,0},{64,32},{96,64},{0,96},{33,1},{65,33},{97,65},{1,97},{34,2}... | collective-permute-start | bytes 1105928 | tf_op jit(solution)/shard_map/ppermute | solution.py:34
  16.5 6.3 %copy-start.7 = (f32[1,8,16,720]{3,2,1,0:T(8,128)}, f32[1,8,16,720]{3,2,1,0:T(8,128)S(1)}, u32[]{:S(2)}) copy-start(f32[1,8,16,720]{3,2,1,0:T(8,128)S(1)} %collective-permute-done.1) | copy-start | bytes 1105924
  16.5 6.2 %collective-permute-start.2 = (f32[6,1,16,720]{3,2,1,0:T(8,128)S(1)}, f32[6,1,16,720]{3,2,1,0:T(8,128)S(1)}, u32[]{:S(2)}, u32[]{:S(2)}) collective-permute-start(f32[6,1,16,720]{3,2,1,0:T(8,128)S(1)} %get-tuple-element.18), channel_id=1, source_target_pairs={{0,1},{1,2},{2,3},{3,4},{4,5},{5,6},{6,7},{7,8},{8,9},{9,10},{10,1... | collective-permute-start | bytes 829448 | tf_op jit(solution)/shard_map/ppermute | solution.py:32
  19.1 6.4 %collective-permute-start.3 = (f32[6,1,16,720]{3,2,1,0:T(8,128)S(1)}, f32[6,1,16,720]{3,2,1,0:T(8,128)S(1)}, u32[]{:S(2)}, u32[]{:S(2)}) collective-permute-start(f32[6,1,16,720]{3,2,1,0:T(8,128)S(1)} %get-tuple-element.19), channel_id=1, source_target_pairs={{1,0},{2,1},{3,2},{4,3},{5,4},{6,5},{7,6},{8,7},{9,8},{10,9},{11,1... | collective-permute-start | bytes 829448 | tf_op jit(solution)/shard_map/ppermute | solution.py:34
  29.9 1.6 %copy-start.10 = (f32[16,16,1,1]{1,0,3,2:T(8,128)S(1)}, f32[16,16,1,1]{1,0,3,2:T(8,128)}, u32[]{:S(2)}) copy-start(f32[16,16,1,1]{1,0,3,2:T(8,128)} %constant.155) | copy-start | bytes 3076
  31.5 1.5 %copy-start.3 = (f32[4,8,16,720]{3,2,1,0:T(8,128)S(1)}, f32[4,8,16,720]{3,2,1,0:T(8,128)}, u32[]{:S(2)}) copy-start(f32[4,8,16,720]{3,2,1,0:T(8,128)} %copy-done.2) | copy-start | bytes 4423684
  31.5 1.5 %copy-start.11 = (f32[16,16,1,1]{1,0,3,2:T(8,128)S(1)}, f32[16,16,1,1]{1,0,3,2:T(8,128)}, u32[]{:S(2)}) copy-start(f32[16,16,1,1]{1,0,3,2:T(8,128)} %constant.154) | copy-start | bytes 3076
  31.5 1.5 %copy-start.15 = (f32[16]{0:T(128)S(1)}, f32[16]{0:T(128)}, u32[]{:S(2)}) copy-start(f32[16]{0:T(128)} %constant.152) | copy-start | bytes 196
  34.9 10.3 %copy-start.4 = (f32[4,8,16,720]{3,2,1,0:T(8,128)}, f32[4,8,16,720]{3,2,1,0:T(8,128)S(1)}, u32[]{:S(2)}) copy-start(f32[4,8,16,720]{3,2,1,0:T(8,128)S(1)} %bitcast_add_fusion.1) | copy-start | bytes 4423684
  34.9 3.0 %copy-start.13 = (s32[4,8,4]{1,2,0:T(4,128)S(1)}, s32[4,8,4]{1,2,0:T(4,128)}, u32[]{:S(2)}) copy-start(s32[4,8,4]{1,2,0:T(4,128)} %param.13) | copy-start | bytes 1540
  35.0 10.1 %collective-permute-start.4 = (f32[1,8,16,720]{3,2,1,0:T(8,128)S(1)}, f32[1,8,16,720]{3,2,1,0:T(8,128)S(1)}, u32[]{:S(2)}, u32[]{:S(2)}) collective-permute-start(f32[1,8,16,720]{3,2,1,0:T(8,128)S(1)} %get-tuple-element.20), channel_id=1, source_target_pairs={{0,32},{32,64},{64,96},{96,0},{1,33},{33,65},{65,97},{97,1},{2,34}... | collective-permute-start | bytes 1105928 | tf_op jit(solution)/shard_map/ppermute | solution.py:32
  36.3 8.8 %collective-permute-start.5 = (f32[1,8,16,720]{3,2,1,0:T(8,128)S(1)}, f32[1,8,16,720]{3,2,1,0:T(8,128)S(1)}, u32[]{:S(2)}, u32[]{:S(2)}) collective-permute-start(f32[1,8,16,720]{3,2,1,0:T(8,128)S(1)} %get-tuple-element.21), channel_id=1, source_target_pairs={{32,0},{64,32},{96,64},{0,96},{33,1},{65,33},{97,65},{1,97},{34,2}... | collective-permute-start | bytes 1105928 | tf_op jit(solution)/shard_map/ppermute | solution.py:34
  45.1 4.4 %copy-start.8 = (f32[1,8,16,720]{3,2,1,0:T(8,128)}, f32[1,8,16,720]{3,2,1,0:T(8,128)S(1)}, u32[]{:S(2)}) copy-start(f32[1,8,16,720]{3,2,1,0:T(8,128)S(1)} %collective-permute-done.5) | copy-start | bytes 1105924
  45.2 6.6 %collective-permute-start.6 = (f32[6,1,16,720]{3,2,1,0:T(8,128)S(1)}, f32[6,1,16,720]{3,2,1,0:T(8,128)S(1)}, u32[]{:S(2)}, u32[]{:S(2)}) collective-permute-start(f32[6,1,16,720]{3,2,1,0:T(8,128)S(1)} %get-tuple-element.16), channel_id=1, source_target_pairs={{0,1},{1,2},{2,3},{3,4},{4,5},{5,6},{6,7},{7,8},{8,9},{9,10},{10,1... | collective-permute-start | bytes 829448 | tf_op jit(solution)/shard_map/ppermute | solution.py:32
  48.1 6.4 %collective-permute-start.7 = (f32[6,1,16,720]{3,2,1,0:T(8,128)S(1)}, f32[6,1,16,720]{3,2,1,0:T(8,128)}, u32[]{:S(2)}, u32[]{:S(2)}) collective-permute-start(f32[6,1,16,720]{3,2,1,0:T(8,128)S(1)} %get-tuple-element.17), channel_id=1, source_target_pairs={{1,0},{2,1},{3,2},{4,3},{5,4},{6,5},{7,6},{8,7},{9,8},{10,9},{11,1... | collective-permute-start | bytes 829448 | tf_op jit(solution)/shard_map/ppermute | solution.py:34
  59.0 1.9 %copy-start.5 = (f32[4,8,16,720]{3,2,1,0:T(8,128)S(1)}, f32[4,8,16,720]{3,2,1,0:T(8,128)}, u32[]{:S(2)}) copy-start(f32[4,8,16,720]{3,2,1,0:T(8,128)} %copy-done.4) | copy-start | bytes 4423684
  60.9 1.5 %copy-start.14 = (f32[4,16,1,1]{1,0,3,2:T(4,128)S(1)}, f32[4,16,1,1]{1,0,3,2:T(4,128)}, u32[]{:S(2)}) copy-start(f32[4,16,1,1]{1,0,3,2:T(4,128)} %constant.156) | copy-start | bytes 772
  62.5 1.6 %copy-start.6 = (f32[4,8,16,720]{3,2,1,0:T(8,128)}, f32[4,8,16,720]{3,2,1,0:T(8,128)S(1)}, u32[]{:S(2)}) copy-start(f32[4,8,16,720]{3,2,1,0:T(8,128)S(1)} %fusion) | copy-start | bytes 4423684
  64.4 14.2 %copy-start.1 = (s32[128]{0:T(128)S(1)}, s32[128]{0:T(128)}, u32[]{:S(2)}) copy-start(s32[128]{0:T(128)} %param.14) | copy-start | bytes 1540
  66.2 23.3 %all-to-all-start = ((f32[128,1,321]{2,1,0:T(1,128)}), f32[128,1,321]{2,1,0:T(1,128)S(1)}, u32[]{:S(2)}, u32[]{:S(2)}) async-start(f32[128,1,321]{2,1,0:T(1,128)} %copy.50), calls=%async_computation | async-start | bytes 393216 | tf_op jit(solution)/shard_map/all_to_all | solution.py:253
  78.7 2.5 %copy-start = (bf16[10,32,64,128]{3,2,1,0:T(8,128)(2,1)S(1)}, bf16[10,32,64,128]{3,2,1,0:T(8,128)(2,1)}, u32[]{:S(2)}) copy-start(bf16[10,32,64,128]{3,2,1,0:T(8,128)(2,1)} %state_hbm.1) | copy-start | bytes 15728644
  (1 other events, 0.7 us)

commit v6 on v5

--- a/solution.py
+++ b/solution.py
@@ -278,12 +278,15 @@
     place = (local_row + drow + 1) * (cols_dev + 2) + (local_col + dcol + 1)
     index_flat = place[..., None] * 16 + pick
     index_flat = index_flat.reshape(-1)
+    part, start_mean = crm_first(crm_state, crm_active)
     state = dyn_state
     for step in range(DSTEPS):
         state = state + KAPPA * jnp.einsum(
             "nm,rcmw->rcnw", laplace, state, precision=lax.Precision.HIGHEST
         )
         extended = extended_2(state, (("face", 0), ("col", 1)), 1)
+        if step == 0:
+            extended, part, start_mean = lax.optimization_barrier((extended, part, start_mean))
         matched = jnp.take(extended.reshape(-1, width), index_flat, axis=0).reshape(
             rows_dev, cols_dev, 16, width
         )
@@ -304,7 +307,7 @@
     slots = arrived[:, NFLD * CLEV].astype(jnp.int32) % per_dev
     physics = jnp.zeros((per_dev, NFLD * CLEV), jnp.float32).at[slots].set(arrived[:, : NFLD * CLEV])
     forcing = physics.reshape(per_dev, NFLD, CLEV).transpose(1, 2, 0)
-    crm_new, tend = crm_run(crm_state, forcing, crm_active)
+    crm_new, tend = crm_second(part, start_mean, forcing, crm_active)
     tend_rows = tend.reshape(NFLD * CLEV, per_dev).T[slots]
     returned = exchange(tend_rows.reshape(ndev, count, NFLD * CLEV))
     placed = (

time: 127 us -> 125 us (0.984)
  blocking collectives: 20 us -> 36.3 us
  starting transfers between devices: 24.7 us -> 15.2 us
  waiting for transfers between devices: 22.8 us -> 13.8 us
    all_to_all x1 -> x2, blocking collectives: 20 us -> 36.3 us  [exchange(): lax.all_to_all(chunks, ('face', 'col'), split_axis=0, concat_axis=0, tile...]
    all_to_all x1 -> x0, starting transfers between devices: 12.5 us -> none  [exchange(): lax.all_to_all(chunks, ('face', 'col'), split_axis=0, concat_axis=0, tile...]
    ppermute x4, waiting for transfers between devices: 18 us -> 11.7 us  [extended_2(): lax.ppermute(tail, axis, [(i, (i + 1) % count) for i in range(count)])]
    ppermute x4, starting transfers between devices: 9.02 us -> 12.2 us  [extended_2(): lax.ppermute(tail, axis, [(i, (i + 1) % count) for i in range(count)])]
    ppermute x4, waiting for transfers between devices: 4.84 us -> 2.08 us  [extended_2(): lax.ppermute(head, axis, [((i + 1) % count, i) for i in range(count)])]
    unnamed x33 -> x37, local copies, waits for them, and re-layouts: 3.54 us -> 3.56 us
  transfers between devices with their start and end apart: 9 -> 8, of which waited for: 6 -> 4; matrix products, arithmetic and copies ran while one was open for 4% -> 4% of each run, Pallas kernels for 7% -> 7%
where the time goes in v6:
time: 125 us
  blocking collectives  36.3 us (29%)
  Pallas kernels  21.5 us (17%)
  local copies, waits for them, and re-layouts  17.8 us (14%)
  starting transfers between devices  15.2 us (12%)
  waiting for transfers between devices  13.8 us (11%)
  other arithmetic  9.41 us (8%)
  matrix products  9.31 us (7%)
    all_to_all x2, blocking collectives, exchange(): lax.all_to_all(chunks, ('face', 'col'), split_axis=0, concat_axis=0, tile...  36.3 us
    pallas_call x1, Pallas kernels, crm_second(): pl.pallas_call(crm_second_kernel, out_shape=(jax.ShapeDtypeStruct(part.sh...  13.1 us
    ppermute x4, starting transfers between devices, extended_2(): lax.ppermute(tail, axis, [(i, (i + 1) % count) for i in range(count)])  12.2 us
    ppermute x4, waiting for transfers between devices, extended_2(): lax.ppermute(tail, axis, [(i, (i + 1) % count) for i in range(count)])  11.7 us
    pallas_call x1, Pallas kernels, crm_first(): pl.pallas_call(crm_first_kernel, out_shape=(jax.ShapeDtypeStruct(state.sh...  8.38 us
    dot_general x2, matrix products, per_device(): jnp.einsum('nm,rcmw->rcnw', laplace, state, precision=lax.Precision.HIGHEST)  5.34 us
    gather x2, local copies, waits for them, and re-layouts, per_device(): jnp.take(extended.reshape(-1, width), index_flat, axis=0)  5.19 us
    unnamed x37, local copies, waits for them, and re-layouts  3.56 us
  transfers between devices with their start and end apart: 8, of which 4 were waited for; matrix products, arithmetic and copies ran while one was open for 4% of the time, Pallas kernels for 7%

profile of v6, /device:TPU:1, one launch (start us, length us, event | category | flops | bytes accessed | tf_op | source)
XLA Modules:
  0.0 124.5 jit_solution(6369960824932844464)
XLA Ops:
  0.6 3.4 %bitcast_add_fusion.3 = f32[4,8,16,720]{3,2,1,0:T(8,128)S(1)} fusion(f32[4,8,16,720]{3,2,1,0:T(8,128)} %param.11, f32[16,16,1,1]{1,0,3,2:T(8,128)} %constant.154), kind=kOutput, calls=%fused_computation.14 | convolution fusion | flops 71516160 | bytes 2950144 | tf_op jit(solution)/shard_map/nm,rcmw->rcnw/dot_general | solution.py:284
  4.2 2.2 %collective-permute-start = (f32[1,8,16,720]{3,2,1,0:T(8,128)S(1)}, f32[1,8,16,720]{3,2,1,0:T(8,128)S(1)}, u32[]{:S(2)}, u32[]{:S(2)}) collective-permute-start(f32[1,8,16,720]{3,2,1,0:T(8,128)S(1)} %get-tuple-element.28), channel_id=1, source_target_pairs={{0,32},{32,64},{64,96},{96,0},{1,33},{33,65},{65,97},{97,1},{2,34}... | collective-permute-start | bytes 1105928 | tf_op jit(solution)/shard_map/ppermute | solution.py:32
  6.4 1.5 %collective-permute-start.1 = (f32[1,8,16,720]{3,2,1,0:T(8,128)S(1)}, f32[1,8,16,720]{3,2,1,0:T(8,128)S(1)}, u32[]{:S(2)}, u32[]{:S(2)}) collective-permute-start(f32[1,8,16,720]{3,2,1,0:T(8,128)S(1)} %get-tuple-element.29), channel_id=1, source_target_pairs={{32,0},{64,32},{96,64},{0,96},{33,1},{65,33},{97,65},{1,97},{34,2}... | collective-permute-start | bytes 1105928 | tf_op jit(solution)/shard_map/ppermute | solution.py:34
  8.8 7.7 %collective-permute-done = f32[1,8,16,720]{3,2,1,0:T(8,128)S(1)} collective-permute-done((f32[1,8,16,720]{3,2,1,0:T(8,128)S(1)}, f32[1,8,16,720]{3,2,1,0:T(8,128)S(1)}, u32[]{:S(2)}, u32[]{:S(2)}) %collective-permute-start) | collective-permute-done | bytes 368672 | tf_op jit(solution)/shard_map/ppermute | solution.py:32
  16.6 2.5 %collective-permute-start.2 = (f32[6,1,16,720]{3,2,1,0:T(8,128)S(1)}, f32[6,1,16,720]{3,2,1,0:T(8,128)S(1)}, u32[]{:S(2)}, u32[]{:S(2)}) collective-permute-start(f32[6,1,16,720]{3,2,1,0:T(8,128)S(1)} %get-tuple-element.24), channel_id=1, source_target_pairs={{0,1},{1,2},{2,3},{3,4},{4,5},{5,6},{6,7},{7,8},{8,9},{9,10},{10,1... | collective-permute-start | bytes 829448 | tf_op jit(solution)/shard_map/ppermute | solution.py:32
  19.1 2.5 %copy-done = bf16[10,32,64,128]{3,2,1,0:T(8,128)(2,1)S(1)} copy-done((bf16[10,32,64,128]{3,2,1,0:T(8,128)(2,1)S(1)}, bf16[10,32,64,128]{3,2,1,0:T(8,128)(2,1)}, u32[]{:S(2)}) %copy-start) | copy-done | bytes 5242904
  21.6 8.4 %shard_map.112 = (f32[10,32,64,128]{3,2,1,0:T(8,128)}, f32[10,32,128]{2,1,0:T(8,128)S(1)}) custom-call(s32[1,128]{1,0:T(1,128)S(1)} %bitcast.62, bf16[10,32,64,128]{3,2,1,0:T(8,128)(2,1)S(1)} %copy-done), custom_call_target="tpu_custom_call" | custom-call | tf_op jit(solution)/shard_map/pallas_call | solution.py:198
  31.3 2.6 %gather_fusion.3 = f32[512,720]{1,0:T(8,128)} fusion(f32[960,720]{1,0:T(8,128)S(1)} %bitcast.64, s32[1024]{0:T(1024)S(1)} %pad_clamp_fusion.2), kind=kCustom, calls=%fused_computation.clone | custom fusion | bytes 2951168 | tf_op jit(solution)/shard_map/jit(_take)/gather | solution.py:290
  33.9 1.6 %broadcast_select_fusion.1 = f32[512,720]{1,0:T(8,128)S(1)} fusion(f32[512,720]{1,0:T(8,128)} %gather_fusion.3, pred[512]{0:T(512)(128)(4,1)S(1)} %compare_and_fusion), kind=kLoop, calls=%fused_computation.17 | loop fusion | flops 368640 | bytes 2949632 | tf_op jit(solution)/shard_map/jit(_take)/select_n | solution.py:290
  35.5 1.5 %fusion.33 = f32[4,8,720,16]{2,3,1,0:T(8,128)S(1)} fusion(f32[4,8,16,720]{3,2,1,0:T(8,128)S(1)} %bitcast.68, f32[16,16,1,1]{1,0,3,2:T(8,128)S(1)} %copy-done.12), kind=kOutput, calls=%fused_computation.99 | convolution fusion | flops 70778880 | bytes 2950144 | tf_op jit(solution)/shard_map/nm,rcmw->rcnw/dot_general | solution.py:293
  37.0 1.9 %bitcast_add_fusion.1 = f32[4,8,16,720]{3,2,1,0:T(8,128)S(1)} fusion(f32[16,16,1,1]{1,0,3,2:T(8,128)S(1)} %copy-done.13, f32[4,8,16,720]{3,2,1,0:T(8,128)S(1)} %copy-done.4, f32[4,8,720,16]{2,3,1,0:T(8,128)S(1)} %fusion.33, f32[16]{0:T(128)S(1)} %copy-done.17), kind=kOutput, calls=%fused_computation.11 | convolution fusion | flops 72990720 | bytes 4424768 | tf_op jit(solution)/shard_map/nm,rcmw->rcnw/dot_general | solution.py:284
  40.4 1.5 %collective-permute-start.5 = (f32[1,8,16,720]{3,2,1,0:T(8,128)S(1)}, f32[1,8,16,720]{3,2,1,0:T(8,128)S(1)}, u32[]{:S(2)}, u32[]{:S(2)}) collective-permute-start(f32[1,8,16,720]{3,2,1,0:T(8,128)S(1)} %get-tuple-element.27), channel_id=1, source_target_pairs={{32,0},{64,32},{96,64},{0,96},{33,1},{65,33},{97,65},{1,97},{34,2}... | collective-permute-start | bytes 1105928 | tf_op jit(solution)/shard_map/ppermute | solution.py:34
  42.1 2.5 %sort.17 = (s32[128]{0:T(128)}, s32[128]{0:T(128)S(1)}) sort(s32[128]{0:T(128)S(1)} %reshape.88, s32[128]{0:T(128)S(1)} %iota.35), dimensions={0}, to_apply=%region_0.2 | sort | flops 896 | bytes 2048 | tf_op jit(solution)/shard_map/jit(argsort)/sort | solution.py:301
  44.6 2.3 %collective-permute-done.4 = f32[1,8,16,720]{3,2,1,0:T(8,128)S(1)} collective-permute-done((f32[1,8,16,720]{3,2,1,0:T(8,128)S(1)}, f32[1,8,16,720]{3,2,1,0:T(8,128)S(1)}, u32[]{:S(2)}, u32[]{:S(2)}) %collective-permute-start.4) | collective-permute-done | bytes 368672 | tf_op jit(solution)/shard_map/ppermute | solution.py:32
  47.1 6.1 %collective-permute-start.6 = (f32[6,1,16,720]{3,2,1,0:T(8,128)S(1)}, f32[6,1,16,720]{3,2,1,0:T(8,128)S(1)}, u32[]{:S(2)}, u32[]{:S(2)}) collective-permute-start(f32[6,1,16,720]{3,2,1,0:T(8,128)S(1)} %get-tuple-element.22), channel_id=1, source_target_pairs={{0,1},{1,2},{2,3},{3,4},{4,5},{5,6},{6,7},{7,8},{8,9},{9,10},{10,1... | collective-permute-start | bytes 829448 | tf_op jit(solution)/shard_map/ppermute | solution.py:32
  55.1 1.7 %collective-permute-done.6 = f32[6,1,16,720]{3,2,1,0:T(8,128)S(1)} collective-permute-done((f32[6,1,16,720]{3,2,1,0:T(8,128)S(1)}, f32[6,1,16,720]{3,2,1,0:T(8,128)S(1)}, u32[]{:S(2)}, u32[]{:S(2)}) %collective-permute-start.6) | collective-permute-done | bytes 276512 | tf_op jit(solution)/shard_map/ppermute | solution.py:32
  57.5 2.0 %collective-permute-done.7 = f32[6,1,16,720]{3,2,1,0:T(8,128)} collective-permute-done((f32[6,1,16,720]{3,2,1,0:T(8,128)S(1)}, f32[6,1,16,720]{3,2,1,0:T(8,128)}, u32[]{:S(2)}, u32[]{:S(2)}) %collective-permute-start.7) | collective-permute-done | bytes 276512 | tf_op jit(solution)/shard_map/ppermute | solution.py:34
  59.6 1.8 %pad_maximum_fusion.1 = f32[6,10,16,720]{3,2,1,0:T(8,128)S(1)} fusion(f32[6,1,16,720]{3,2,1,0:T(8,128)} %collective-permute-done.7, f32[1,8,16,720]{3,2,1,0:T(8,128)} %copy-done.9, f32[4,8,16,720]{3,2,1,0:T(8,128)} %copy-done.5, f32[1,8,16,720]{3,2,1,0:T(8,128)S(1)} %collective-permute-done.4, f32[6,1,16,720]{3,2,1,0:T(8,128)} %copy-done.10), kind=kLoop, calls=%fused_computation.8 | loop fusion | flops 2764800 | bytes 5529600 | tf_op jit(solution)/shard_map/concatenate | solution.py:30
  61.4 2.6 %gather_fusion.4 = f32[512,720]{1,0:T(8,128)} fusion(f32[960,720]{1,0:T(8,128)S(1)} %bitcast.65, s32[1024]{0:T(1024)S(1)} %pad_clamp_fusion.2), kind=kCustom, calls=%fused_computation.1.clone | custom fusion | bytes 2951168 | tf_op jit(solution)/shard_map/jit(_take)/gather | solution.py:290
  64.0 1.7 %broadcast_select_fusion = f32[512,720]{1,0:T(8,128)S(1)} fusion(f32[512,720]{1,0:T(8,128)} %gather_fusion.4, pred[512]{0:T(512)(128)(4,1)S(1)} %compare_and_fusion), kind=kLoop, calls=%fused_computation.16 | loop fusion | flops 368640 | bytes 2949632 | tf_op jit(solution)/shard_map/jit(_take)/select_n | solution.py:290
  65.9 1.6 %fusion = f32[4,8,16,720]{3,2,1,0:T(8,128)S(1)} fusion(f32[4,8,16,720]{3,2,1,0:T(8,128)S(1)} %copy-done.6, f32[4,8,16,720]{3,2,1,0:T(8,128)S(1)} %bitcast.67, f32[16,16,1,1]{1,0,3,2:T(8,128)S(1)} %copy-done.12, f32[16]{0:T(128)S(1)} %copy-done.17), kind=kOutput, calls=%fused_computation.10 | convolution fusion | flops 71516160 | bytes 4424768 | tf_op jit(solution)/shard_map/nm,rcmw->rcnw/dot_general | solution.py:293
  70.6 21.7 %all_to_all.10 = f32[128,1,321]{2,1,0:T(1,128)S(1)} all-to-all(f32[128,1,321]{2,1,0:T(1,128)S(1)} %copy.50), channel_id=1, replica_groups=mesh['face'=4,'col'=32] {'face','col'}, dimensions={0} | all-to-all | bytes 328704 | tf_op jit(solution)/shard_map/all_to_all | solution.py:253
  93.8 13.1 %shard_map.113 = (bf16[10,32,64,128]{3,2,1,0:T(8,128)(2,1)}, f32[10,32,128]{2,1,0:T(8,128)S(1)}) custom-call(f32[10,32,128]{2,1,0:T(8,128)S(1)} %bitcast.60, s32[1,128]{1,0:T(1,128)S(1)} %bitcast.63, f32[10,32,128]{2,1,0:T(8,128)S(1)} %get-tuple-element.16.mean_ref, f32[10,32,64,128]{3,2,1,0:T(8,128)} %get-tuple-element.17.part_hbm), custom_call_target="tpu_custom_call" | custom-call | tf_op jit(solution)/shard_map/pallas_call | solution.py:220
  108.0 14.6 %all_to_all.11 = f32[128,1,320]{2,1,0:T(1,128)S(1)} all-to-all(f32[128,1,320]{2,1,0:T(1,128)S(1)} %copy.55), channel_id=1, replica_groups=mesh['face'=4,'col'=32] {'face','col'}, dimensions={0} | all-to-all | bytes 327680 | tf_op jit(solution)/shard_map/all_to_all | solution.py:253
  (89 shorter events, 14.2 us)
Async XLA Ops:
  4.1 12.5 %copy-start.2 = (f32[4,8,16,720]{3,2,1,0:T(8,128)}, f32[4,8,16,720]{3,2,1,0:T(8,128)S(1)}, u32[]{:S(2)}) copy-start(f32[4,8,16,720]{3,2,1,0:T(8,128)S(1)} %bitcast_add_fusion.3) | copy-start | bytes 4423684
  4.1 3.8 %copy-start.14 = (s32[4,8,4]{1,2,0:T(4,128)S(1)}, s32[4,8,4]{1,2,0:T(4,128)}, u32[]{:S(2)}) copy-start(s32[4,8,4]{1,2,0:T(4,128)} %param.12) | copy-start | bytes 1540
  4.2 12.3 %collective-permute-start = (f32[1,8,16,720]{3,2,1,0:T(8,128)S(1)}, f32[1,8,16,720]{3,2,1,0:T(8,128)S(1)}, u32[]{:S(2)}, u32[]{:S(2)}) collective-permute-start(f32[1,8,16,720]{3,2,1,0:T(8,128)S(1)} %get-tuple-element.28), channel_id=1, source_target_pairs={{0,32},{32,64},{64,96},{96,0},{1,33},{33,65},{65,97},{97,1},{2,34}... | collective-permute-start | bytes 1105928 | tf_op jit(solution)/shard_map/ppermute | solution.py:32
  6.4 10.1 %collective-permute-start.1 = (f32[1,8,16,720]{3,2,1,0:T(8,128)S(1)}, f32[1,8,16,720]{3,2,1,0:T(8,128)S(1)}, u32[]{:S(2)}, u32[]{:S(2)}) collective-permute-start(f32[1,8,16,720]{3,2,1,0:T(8,128)S(1)} %get-tuple-element.29), channel_id=1, source_target_pairs={{32,0},{64,32},{96,64},{0,96},{33,1},{65,33},{97,65},{1,97},{34,2}... | collective-permute-start | bytes 1105928 | tf_op jit(solution)/shard_map/ppermute | solution.py:34
  8.4 10.7 %copy-start.1 = (s32[128]{0:T(128)S(1)}, s32[128]{0:T(128)}, u32[]{:S(2)}) copy-start(s32[128]{0:T(128)} %param.14) | copy-start | bytes 1540
  16.5 13.5 %copy-start.8 = (f32[1,8,16,720]{3,2,1,0:T(8,128)}, f32[1,8,16,720]{3,2,1,0:T(8,128)S(1)}, u32[]{:S(2)}) copy-start(f32[1,8,16,720]{3,2,1,0:T(8,128)S(1)} %collective-permute-done.1) | copy-start | bytes 1105924
  16.6 13.5 %collective-permute-start.2 = (f32[6,1,16,720]{3,2,1,0:T(8,128)S(1)}, f32[6,1,16,720]{3,2,1,0:T(8,128)S(1)}, u32[]{:S(2)}, u32[]{:S(2)}) collective-permute-start(f32[6,1,16,720]{3,2,1,0:T(8,128)S(1)} %get-tuple-element.24), channel_id=1, source_target_pairs={{0,1},{1,2},{2,3},{3,4},{4,5},{5,6},{6,7},{7,8},{8,9},{9,10},{10,1... | collective-permute-start | bytes 829448 | tf_op jit(solution)/shard_map/ppermute | solution.py:32
  19.1 10.9 %collective-permute-start.3 = (f32[6,1,16,720]{3,2,1,0:T(8,128)S(1)}, f32[6,1,16,720]{3,2,1,0:T(8,128)S(1)}, u32[]{:S(2)}, u32[]{:S(2)}) collective-permute-start(f32[6,1,16,720]{3,2,1,0:T(8,128)S(1)} %get-tuple-element.25), channel_id=1, source_target_pairs={{1,0},{2,1},{3,2},{4,3},{5,4},{6,5},{7,6},{8,7},{9,8},{10,9},{11,1... | collective-permute-start | bytes 829448 | tf_op jit(solution)/shard_map/ppermute | solution.py:34
  19.1 2.5 %copy-start = (bf16[10,32,64,128]{3,2,1,0:T(8,128)(2,1)S(1)}, bf16[10,32,64,128]{3,2,1,0:T(8,128)(2,1)}, u32[]{:S(2)}) copy-start(bf16[10,32,64,128]{3,2,1,0:T(8,128)(2,1)} %state_hbm.1) | copy-start | bytes 15728644
  21.6 8.4 %copy-start.3 = (f32[4,8,16,720]{3,2,1,0:T(8,128)S(1)}, f32[4,8,16,720]{3,2,1,0:T(8,128)}, u32[]{:S(2)}) copy-start(f32[4,8,16,720]{3,2,1,0:T(8,128)} %copy-done.2) | copy-start | bytes 4423684
  33.9 1.6 %copy-start.12 = (f32[16,16,1,1]{1,0,3,2:T(8,128)S(1)}, f32[16,16,1,1]{1,0,3,2:T(8,128)}, u32[]{:S(2)}) copy-start(f32[16,16,1,1]{1,0,3,2:T(8,128)} %constant.155) | copy-start | bytes 3076
  35.5 1.5 %copy-start.4 = (f32[4,8,16,720]{3,2,1,0:T(8,128)S(1)}, f32[4,8,16,720]{3,2,1,0:T(8,128)}, u32[]{:S(2)}) copy-start(f32[4,8,16,720]{3,2,1,0:T(8,128)} %copy-done.2) | copy-start | bytes 4423684
  35.5 1.5 %copy-start.13 = (f32[16,16,1,1]{1,0,3,2:T(8,128)S(1)}, f32[16,16,1,1]{1,0,3,2:T(8,128)}, u32[]{:S(2)}) copy-start(f32[16,16,1,1]{1,0,3,2:T(8,128)} %constant.154) | copy-start | bytes 3076
  35.5 1.5 %copy-start.17 = (f32[16]{0:T(128)S(1)}, f32[16]{0:T(128)}, u32[]{:S(2)}) copy-start(f32[16]{0:T(128)} %constant.152) | copy-start | bytes 196
  38.9 8.1 %copy-start.5 = (f32[4,8,16,720]{3,2,1,0:T(8,128)}, f32[4,8,16,720]{3,2,1,0:T(8,128)S(1)}, u32[]{:S(2)}) copy-start(f32[4,8,16,720]{3,2,1,0:T(8,128)S(1)} %bitcast_add_fusion.1) | copy-start | bytes 4423684
  38.9 3.0 %copy-start.15 = (s32[4,8,4]{1,2,0:T(4,128)S(1)}, s32[4,8,4]{1,2,0:T(4,128)}, u32[]{:S(2)}) copy-start(s32[4,8,4]{1,2,0:T(4,128)} %param.13) | copy-start | bytes 1540
  39.0 8.0 %collective-permute-start.4 = (f32[1,8,16,720]{3,2,1,0:T(8,128)S(1)}, f32[1,8,16,720]{3,2,1,0:T(8,128)S(1)}, u32[]{:S(2)}, u32[]{:S(2)}) collective-permute-start(f32[1,8,16,720]{3,2,1,0:T(8,128)S(1)} %get-tuple-element.26), channel_id=1, source_target_pairs={{0,32},{32,64},{64,96},{96,0},{1,33},{33,65},{65,97},{97,1},{2,34}... | collective-permute-start | bytes 1105928 | tf_op jit(solution)/shard_map/ppermute | solution.py:32
  40.4 6.6 %collective-permute-start.5 = (f32[1,8,16,720]{3,2,1,0:T(8,128)S(1)}, f32[1,8,16,720]{3,2,1,0:T(8,128)S(1)}, u32[]{:S(2)}, u32[]{:S(2)}) collective-permute-start(f32[1,8,16,720]{3,2,1,0:T(8,128)S(1)} %get-tuple-element.27), channel_id=1, source_target_pairs={{32,0},{64,32},{96,64},{0,96},{33,1},{65,33},{97,65},{1,97},{34,2}... | collective-permute-start | bytes 1105928 | tf_op jit(solution)/shard_map/ppermute | solution.py:34
  47.0 7.4 %copy-start.9 = (f32[1,8,16,720]{3,2,1,0:T(8,128)}, f32[1,8,16,720]{3,2,1,0:T(8,128)S(1)}, u32[]{:S(2)}) copy-start(f32[1,8,16,720]{3,2,1,0:T(8,128)S(1)} %collective-permute-done.5) | copy-start | bytes 1105924
  47.1 9.7 %collective-permute-start.6 = (f32[6,1,16,720]{3,2,1,0:T(8,128)S(1)}, f32[6,1,16,720]{3,2,1,0:T(8,128)S(1)}, u32[]{:S(2)}, u32[]{:S(2)}) collective-permute-start(f32[6,1,16,720]{3,2,1,0:T(8,128)S(1)} %get-tuple-element.22), channel_id=1, source_target_pairs={{0,1},{1,2},{2,3},{3,4},{4,5},{5,6},{6,7},{7,8},{8,9},{9,10},{10,1... | collective-permute-start | bytes 829448 | tf_op jit(solution)/shard_map/ppermute | solution.py:32
  53.1 6.4 %collective-permute-start.7 = (f32[6,1,16,720]{3,2,1,0:T(8,128)S(1)}, f32[6,1,16,720]{3,2,1,0:T(8,128)}, u32[]{:S(2)}, u32[]{:S(2)}) collective-permute-start(f32[6,1,16,720]{3,2,1,0:T(8,128)S(1)} %get-tuple-element.23), channel_id=1, source_target_pairs={{1,0},{2,1},{3,2},{4,3},{5,4},{6,5},{7,6},{8,7},{9,8},{10,9},{11,1... | collective-permute-start | bytes 829448 | tf_op jit(solution)/shard_map/ppermute | solution.py:34
  64.0 1.9 %copy-start.6 = (f32[4,8,16,720]{3,2,1,0:T(8,128)S(1)}, f32[4,8,16,720]{3,2,1,0:T(8,128)}, u32[]{:S(2)}) copy-start(f32[4,8,16,720]{3,2,1,0:T(8,128)} %copy-done.5) | copy-start | bytes 4423684
  65.9 1.6 %copy-start.16 = (f32[4,16,1,1]{1,0,3,2:T(4,128)S(1)}, f32[4,16,1,1]{1,0,3,2:T(4,128)}, u32[]{:S(2)}) copy-start(f32[4,16,1,1]{1,0,3,2:T(4,128)} %constant.156) | copy-start | bytes 772
  67.5 1.6 %copy-start.7 = (f32[4,8,16,720]{3,2,1,0:T(8,128)}, f32[4,8,16,720]{3,2,1,0:T(8,128)S(1)}, u32[]{:S(2)}) copy-start(f32[4,8,16,720]{3,2,1,0:T(8,128)S(1)} %fusion) | copy-start | bytes 4423684
  (2 other events, 2.0 us)

commit v7 on v6

--- a/solution.py
+++ b/solution.py
@@ -144,10 +144,6 @@
         for f in range(nfld):
             mid[f, z] = fresh[f]
         return carry
-
-    for c in range(chunks):
-        loads[c].wait()
-        lax.fori_loop(c * ZCHUNK, (c + 1) * ZCHUNK, finish_first, 0)
 
     def level(z, carry):
         upper_z, lower_z = neighbours(z, nlev)
@@ -185,8 +181,19 @@
             finish(f, fresh, state)
         return carry
 
+    def ahead(z, carry):
+        @pl.when(z + 1 < nlev)
+        def _():
+            finish_first(z + 1, 0)
+
+        return level(z, carry)
+
+    loads[0].wait()
+    finish_first(0, 0)
     for c in range(chunks):
-        lax.fori_loop(c * ZCHUNK, (c + 1) * ZCHUNK, level, 0)
+        if c + 1 < chunks:
+            loads[c + 1].wait()
+        lax.fori_loop(c * ZCHUNK, (c + 1) * ZCHUNK, ahead, 0)
         stores[c].start()
     for copy in stores:
         copy.wait()
@@ -284,9 +291,12 @@
         state = state + KAPPA * jnp.einsum(
             "nm,rcmw->rcnw", laplace, state, precision=lax.Precision.HIGHEST
         )
-        extended = extended_2(state, (("face", 0), ("col", 1)), 1)
         if step == 0:
-            extended, part, start_mean = lax.optimization_barrier((extended, part, start_mean))
+            faced = extended_2(state, (("face", 0),), 1)
+            faced, part, start_mean = lax.optimization_barrier((faced, part, start_mean))
+            extended = extended_2(faced, (("col", 1),), 1)
+        else:
+            extended = extended_2(state, (("face", 0), ("col", 1)), 1)
         matched = jnp.take(extended.reshape(-1, width), index_flat, axis=0).reshape(
             rows_dev, cols_dev, 16, width
         )

time: 125 us -> 121 us (0.968)
  starting transfers between devices: 15.2 us -> 12 us
  blocking collectives: 36.3 us -> 37.8 us
    ppermute x4, starting transfers between devices: 12.2 us -> 7.18 us  [extended_2(): lax.ppermute(tail, axis, [(i, (i + 1) % count) for i in range(count)])]
    ppermute x4, waiting for transfers between devices: 11.7 us -> 8.9 us  [extended_2(): lax.ppermute(tail, axis, [(i, (i + 1) % count) for i in range(count)])]
    ppermute x4, waiting for transfers between devices: 2.08 us -> 4.84 us  [extended_2(): lax.ppermute(head, axis, [((i + 1) % count, i) for i in range(count)])]
    ppermute x4, starting transfers between devices: 3.04 us -> 4.85 us  [extended_2(): lax.ppermute(head, axis, [((i + 1) % count, i) for i in range(count)])]
    all_to_all x2, blocking collectives: 36.3 us -> 37.8 us  [exchange(): lax.all_to_all(chunks, ('face', 'col'), split_axis=0, concat_axis=0, tile...]
    pallas_call x1, Pallas kernels: 13.1 us -> 11.9 us  [crm_second(): pl.pallas_call(crm_second_kernel, out_shape=(jax.ShapeDtypeStruct(part.sh...]
    concatenate x2 -> x3, other arithmetic: 3.05 us -> 2.5 us  [extended_2(): jnp.concatenate([lax.ppermute(tail, axis, [(i, (i + 1) % count) for i in...]
    unnamed x37 -> x33, local copies, waits for them, and re-layouts: 3.56 us -> 3.55 us
  transfers between devices with their start and end apart: 8 -> 8, of which waited for: 4 -> 5; matrix products, arithmetic and copies ran while one was open for 4% -> 5% of each run, Pallas kernels for 7% -> 7%
where the time goes in v7:
time: 121 us
  blocking collectives  37.8 us (31%)
  Pallas kernels  20.6 us (17%)
  local copies, waits for them, and re-layouts  17.8 us (15%)
  waiting for transfers between devices  13.7 us (11%)
  starting transfers between devices  12 us (10%)
  matrix products  9.16 us (8%)
  other arithmetic  8.82 us (7%)
    all_to_all x2, blocking collectives, exchange(): lax.all_to_all(chunks, ('face', 'col'), split_axis=0, concat_axis=0, tile...  37.8 us
    pallas_call x1, Pallas kernels, crm_second(): pl.pallas_call(crm_second_kernel, out_shape=(jax.ShapeDtypeStruct(part.sh...  11.9 us
    ppermute x4, waiting for transfers between devices, extended_2(): lax.ppermute(tail, axis, [(i, (i + 1) % count) for i in range(count)])  8.9 us
    pallas_call x1, Pallas kernels, crm_first(): pl.pallas_call(crm_first_kernel, out_shape=(jax.ShapeDtypeStruct(state.sh...  8.76 us
    ppermute x4, starting transfers between devices, extended_2(): lax.ppermute(tail, axis, [(i, (i + 1) % count) for i in range(count)])  7.18 us
    dot_general x2, matrix products, per_device(): jnp.einsum('nm,rcmw->rcnw', laplace, state, precision=lax.Precision.HIGHEST)  5.23 us
    gather x2, local copies, waits for them, and re-layouts, per_device(): jnp.take(extended.reshape(-1, width), index_flat, axis=0)  5.19 us
    ppermute x4, starting transfers between devices, extended_2(): lax.ppermute(head, axis, [((i + 1) % count, i) for i in range(count)])  4.85 us
  transfers between devices with their start and end apart: 8, of which 5 were waited for; matrix products, arithmetic and copies ran while one was open for 5% of the time, Pallas kernels for 7%

profile of v7, /device:TPU:1, one launch (start us, length us, event | category | flops | bytes accessed | tf_op | source)
XLA Modules:
  0.0 121.2 jit_solution(10263499425922787473)
XLA Ops:
  0.6 3.4 %bitcast_add_fusion.3 = f32[4,8,16,720]{3,2,1,0:T(8,128)S(1)} fusion(f32[4,8,16,720]{3,2,1,0:T(8,128)} %param.11, f32[16,16,1,1]{1,0,3,2:T(8,128)} %constant.154), kind=kOutput, calls=%fused_computation.15 | convolution fusion | flops 71516160 | bytes 2950144 | tf_op jit(solution)/shard_map/nm,rcmw->rcnw/dot_general | solution.py:291
  4.2 2.2 %collective-permute-start = (f32[1,8,16,720]{3,2,1,0:T(8,128)S(1)}, f32[1,8,16,720]{3,2,1,0:T(8,128)S(1)}, u32[]{:S(2)}, u32[]{:S(2)}) collective-permute-start(f32[1,8,16,720]{3,2,1,0:T(8,128)S(1)} %get-tuple-element.28), channel_id=1, source_target_pairs={{0,32},{32,64},{64,96},{96,0},{1,33},{33,65},{65,97},{97,1},{2,34}... | collective-permute-start | bytes 1105928 | tf_op jit(solution)/shard_map/ppermute | solution.py:32
  6.4 1.5 %collective-permute-start.1 = (f32[1,8,16,720]{3,2,1,0:T(8,128)S(1)}, f32[1,8,16,720]{3,2,1,0:T(8,128)S(1)}, u32[]{:S(2)}, u32[]{:S(2)}) collective-permute-start(f32[1,8,16,720]{3,2,1,0:T(8,128)S(1)} %get-tuple-element.29), channel_id=1, source_target_pairs={{32,0},{64,32},{96,64},{0,96},{33,1},{65,33},{97,65},{1,97},{34,2}... | collective-permute-start | bytes 1105928 | tf_op jit(solution)/shard_map/ppermute | solution.py:34
  8.8 2.5 %copy-done = bf16[10,32,64,128]{3,2,1,0:T(8,128)(2,1)S(1)} copy-done((bf16[10,32,64,128]{3,2,1,0:T(8,128)(2,1)S(1)}, bf16[10,32,64,128]{3,2,1,0:T(8,128)(2,1)}, u32[]{:S(2)}) %copy-start) | copy-done | bytes 5242904
  11.3 8.8 %shard_map.112 = (f32[10,32,64,128]{3,2,1,0:T(8,128)}, f32[10,32,128]{2,1,0:T(8,128)S(1)}) custom-call(s32[1,128]{1,0:T(1,128)S(1)} %bitcast.62, bf16[10,32,64,128]{3,2,1,0:T(8,128)(2,1)S(1)} %copy-done), custom_call_target="tpu_custom_call" | custom-call | tf_op jit(solution)/shard_map/pallas_call | solution.py:205
  20.4 2.3 %collective-permute-start.2 = (f32[6,1,16,720]{3,2,1,0:T(8,128)S(1)}, f32[6,1,16,720]{3,2,1,0:T(8,128)S(1)}, u32[]{:S(2)}, u32[]{:S(2)}) collective-permute-start(f32[6,1,16,720]{3,2,1,0:T(8,128)S(1)} %get-tuple-element.24), channel_id=1, source_target_pairs={{0,1},{1,2},{2,3},{3,4},{4,5},{5,6},{6,7},{7,8},{8,9},{9,10},{10,1... | collective-permute-start | bytes 829448 | tf_op jit(solution)/shard_map/ppermute | solution.py:32
  22.7 3.6 %collective-permute-done.2 = f32[6,1,16,720]{3,2,1,0:T(8,128)S(1)} collective-permute-done((f32[6,1,16,720]{3,2,1,0:T(8,128)S(1)}, f32[6,1,16,720]{3,2,1,0:T(8,128)S(1)}, u32[]{:S(2)}, u32[]{:S(2)}) %collective-permute-start.2) | collective-permute-done | bytes 276512 | tf_op jit(solution)/shard_map/ppermute | solution.py:32
  26.3 2.8 %collective-permute-done.3 = f32[6,1,16,720]{3,2,1,0:T(8,128)S(1)} collective-permute-done((f32[6,1,16,720]{3,2,1,0:T(8,128)S(1)}, f32[6,1,16,720]{3,2,1,0:T(8,128)S(1)}, u32[]{:S(2)}, u32[]{:S(2)}) %collective-permute-start.3) | collective-permute-done | bytes 276512 | tf_op jit(solution)/shard_map/ppermute | solution.py:34
  29.4 2.6 %gather_fusion.3 = f32[512,720]{1,0:T(8,128)} fusion(f32[960,720]{1,0:T(8,128)S(1)} %bitcast.65, s32[1024]{0:T(1024)S(1)} %pad_clamp_fusion.2), kind=kCustom, calls=%fused_computation.clone | custom fusion | bytes 2951168 | tf_op jit(solution)/shard_map/jit(_take)/gather | solution.py:300
  32.0 1.6 %broadcast_select_fusion.1 = f32[512,720]{1,0:T(8,128)S(1)} fusion(f32[512,720]{1,0:T(8,128)} %gather_fusion.3, pred[512]{0:T(512)(128)(4,1)S(1)} %compare_and_fusion), kind=kLoop, calls=%fused_computation.18 | loop fusion | flops 368640 | bytes 2949632 | tf_op jit(solution)/shard_map/jit(_take)/select_n | solution.py:300
  33.6 1.5 %fusion.34 = f32[4,8,720,16]{2,3,1,0:T(8,128)S(1)} fusion(f32[4,8,16,720]{3,2,1,0:T(8,128)S(1)} %bitcast.68, f32[16,16,1,1]{1,0,3,2:T(8,128)S(1)} %copy-done.10), kind=kOutput, calls=%fused_computation.98 | convolution fusion | flops 70778880 | bytes 2950144 | tf_op jit(solution)/shard_map/nm,rcmw->rcnw/dot_general | solution.py:303
  35.1 1.8 %bitcast_add_fusion.1 = f32[4,8,16,720]{3,2,1,0:T(8,128)S(1)} fusion(f32[16,16,1,1]{1,0,3,2:T(8,128)S(1)} %copy-done.11, f32[4,8,16,720]{3,2,1,0:T(8,128)S(1)} %copy-done.5, f32[4,8,720,16]{2,3,1,0:T(8,128)S(1)} %fusion.34, f32[16]{0:T(128)S(1)} %copy-done.15), kind=kOutput, calls=%fused_computation.12 | convolution fusion | flops 72990720 | bytes 4424768 | tf_op jit(solution)/shard_map/nm,rcmw->rcnw/dot_general | solution.py:291
  37.2 2.6 %collective-permute-start.5 = (f32[1,8,16,720]{3,2,1,0:T(8,128)S(1)}, f32[1,8,16,720]{3,2,1,0:T(8,128)S(1)}, u32[]{:S(2)}, u32[]{:S(2)}) collective-permute-start(f32[1,8,16,720]{3,2,1,0:T(8,128)S(1)} %get-tuple-element.27), channel_id=1, source_target_pairs={{32,0},{64,32},{96,64},{0,96},{33,1},{65,33},{97,65},{1,97},{34,2}... | collective-permute-start | bytes 1105928 | tf_op jit(solution)/shard_map/ppermute | solution.py:34
  40.0 2.5 %sort.17 = (s32[128]{0:T(128)}, s32[128]{0:T(128)S(1)}) sort(s32[128]{0:T(128)S(1)} %reshape.88, s32[128]{0:T(128)S(1)} %iota.35), dimensions={0}, to_apply=%region_0.2 | sort | flops 896 | bytes 2048 | tf_op jit(solution)/shard_map/jit(argsort)/sort | solution.py:311
  42.5 4.3 %collective-permute-done.4 = f32[1,8,16,720]{3,2,1,0:T(8,128)S(1)} collective-permute-done((f32[1,8,16,720]{3,2,1,0:T(8,128)S(1)}, f32[1,8,16,720]{3,2,1,0:T(8,128)S(1)}, u32[]{:S(2)}, u32[]{:S(2)}) %collective-permute-start.4) | collective-permute-done | bytes 368672 | tf_op jit(solution)/shard_map/ppermute | solution.py:32
  46.9 2.6 %collective-permute-start.6 = (f32[6,1,16,720]{3,2,1,0:T(8,128)S(1)}, f32[6,1,16,720]{3,2,1,0:T(8,128)S(1)}, u32[]{:S(2)}, u32[]{:S(2)}) collective-permute-start(f32[6,1,16,720]{3,2,1,0:T(8,128)S(1)} %get-tuple-element.22), channel_id=1, source_target_pairs={{0,1},{1,2},{2,3},{3,4},{4,5},{5,6},{6,7},{7,8},{8,9},{9,10},{10,1... | collective-permute-start | bytes 829448 | tf_op jit(solution)/shard_map/ppermute | solution.py:32
  53.9 2.1 %collective-permute-done.7 = f32[6,1,16,720]{3,2,1,0:T(8,128)} collective-permute-done((f32[6,1,16,720]{3,2,1,0:T(8,128)S(1)}, f32[6,1,16,720]{3,2,1,0:T(8,128)}, u32[]{:S(2)}, u32[]{:S(2)}) %collective-permute-start.7) | collective-permute-done | bytes 276512 | tf_op jit(solution)/shard_map/ppermute | solution.py:34
  55.9 2.0 %pad_maximum_fusion.1 = f32[6,10,16,720]{3,2,1,0:T(8,128)S(1)} fusion(f32[6,1,16,720]{3,2,1,0:T(8,128)} %collective-permute-done.7, f32[1,8,16,720]{3,2,1,0:T(8,128)} %copy-done.7, f32[4,8,16,720]{3,2,1,0:T(8,128)} %copy-done.2, f32[1,8,16,720]{3,2,1,0:T(8,128)S(1)} %collective-permute-done.4, f32[6,1,16,720]{3,2,1,0:T(8,128)} %copy-done.8), kind=kLoop, calls=%fused_computation.8 | loop fusion | flops 2764800 | bytes 5529600 | tf_op jit(solution)/shard_map/concatenate | solution.py:30
  57.9 2.6 %gather_fusion.4 = f32[512,720]{1,0:T(8,128)} fusion(f32[960,720]{1,0:T(8,128)S(1)} %bitcast.64, s32[1024]{0:T(1024)S(1)} %pad_clamp_fusion.2), kind=kCustom, calls=%fused_computation.1.clone | custom fusion | bytes 2951168 | tf_op jit(solution)/shard_map/jit(_take)/gather | solution.py:300
  60.5 1.7 %broadcast_select_fusion = f32[512,720]{1,0:T(8,128)S(1)} fusion(f32[512,720]{1,0:T(8,128)} %gather_fusion.4, pred[512]{0:T(512)(128)(4,1)S(1)} %compare_and_fusion), kind=kLoop, calls=%fused_computation.17 | loop fusion | flops 368640 | bytes 2949632 | tf_op jit(solution)/shard_map/jit(_take)/select_n | solution.py:300
  62.4 1.5 %fusion = f32[4,8,16,720]{3,2,1,0:T(8,128)S(1)} fusion(f32[4,8,16,720]{3,2,1,0:T(8,128)S(1)} %copy-done.3, f32[4,8,16,720]{3,2,1,0:T(8,128)S(1)} %bitcast.67, f32[16,16,1,1]{1,0,3,2:T(8,128)S(1)} %copy-done.10, f32[16]{0:T(128)S(1)} %copy-done.15), kind=kOutput, calls=%fused_computation.11 | convolution fusion | flops 71516160 | bytes 4424768 | tf_op jit(solution)/shard_map/nm,rcmw->rcnw/dot_general | solution.py:303
  67.1 23.2 %all_to_all.10 = f32[128,1,321]{2,1,0:T(1,128)S(1)} all-to-all(f32[128,1,321]{2,1,0:T(1,128)S(1)} %copy.50), channel_id=1, replica_groups=mesh['face'=4,'col'=32] {'face','col'}, dimensions={0} | all-to-all | bytes 328704 | tf_op jit(solution)/shard_map/all_to_all | solution.py:260
  91.7 11.9 %shard_map.113 = (bf16[10,32,64,128]{3,2,1,0:T(8,128)(2,1)}, f32[10,32,128]{2,1,0:T(8,128)S(1)}) custom-call(f32[10,32,128]{2,1,0:T(8,128)S(1)} %bitcast.60, s32[1,128]{1,0:T(1,128)S(1)} %bitcast.63, f32[10,32,128]{2,1,0:T(8,128)S(1)} %get-tuple-element.16.mean_ref, f32[10,32,64,128]{3,2,1,0:T(8,128)} %get-tuple-element.17.part_hbm), custom_call_target="tpu_custom_call" | custom-call | tf_op jit(solution)/shard_map/pallas_call | solution.py:227
  104.7 14.6 %all_to_all.11 = f32[128,1,320]{2,1,0:T(1,128)S(1)} all-to-all(f32[128,1,320]{2,1,0:T(1,128)S(1)} %copy.55), channel_id=1, replica_groups=mesh['face'=4,'col'=32] {'face','col'}, dimensions={0} | all-to-all | bytes 327680 | tf_op jit(solution)/shard_map/all_to_all | solution.py:260
  (86 shorter events, 14.0 us)
Async XLA Ops:
  4.1 16.0 %copy-start.4 = (f32[4,8,16,720]{3,2,1,0:T(8,128)}, f32[4,8,16,720]{3,2,1,0:T(8,128)S(1)}, u32[]{:S(2)}) copy-start(f32[4,8,16,720]{3,2,1,0:T(8,128)S(1)} %bitcast_add_fusion.3) | copy-start | bytes 4423684
  4.1 3.8 %copy-start.12 = (s32[4,8,4]{1,2,0:T(4,128)S(1)}, s32[4,8,4]{1,2,0:T(4,128)}, u32[]{:S(2)}) copy-start(s32[4,8,4]{1,2,0:T(4,128)} %param.12) | copy-start | bytes 1540
  4.1 4.7 %copy-start.1 = (s32[128]{0:T(128)S(1)}, s32[128]{0:T(128)}, u32[]{:S(2)}) copy-start(s32[128]{0:T(128)} %param.14) | copy-start | bytes 1540
  4.2 15.9 %collective-permute-start = (f32[1,8,16,720]{3,2,1,0:T(8,128)S(1)}, f32[1,8,16,720]{3,2,1,0:T(8,128)S(1)}, u32[]{:S(2)}, u32[]{:S(2)}) collective-permute-start(f32[1,8,16,720]{3,2,1,0:T(8,128)S(1)} %get-tuple-element.28), channel_id=1, source_target_pairs={{0,32},{32,64},{64,96},{96,0},{1,33},{33,65},{65,97},{97,1},{2,34}... | collective-permute-start | bytes 1105928 | tf_op jit(solution)/shard_map/ppermute | solution.py:32
  6.4 13.7 %collective-permute-start.1 = (f32[1,8,16,720]{3,2,1,0:T(8,128)S(1)}, f32[1,8,16,720]{3,2,1,0:T(8,128)S(1)}, u32[]{:S(2)}, u32[]{:S(2)}) collective-permute-start(f32[1,8,16,720]{3,2,1,0:T(8,128)S(1)} %get-tuple-element.29), channel_id=1, source_target_pairs={{32,0},{64,32},{96,64},{0,96},{33,1},{65,33},{97,65},{1,97},{34,2}... | collective-permute-start | bytes 1105928 | tf_op jit(solution)/shard_map/ppermute | solution.py:34
  8.8 2.5 %copy-start = (bf16[10,32,64,128]{3,2,1,0:T(8,128)(2,1)S(1)}, bf16[10,32,64,128]{3,2,1,0:T(8,128)(2,1)}, u32[]{:S(2)}) copy-start(bf16[10,32,64,128]{3,2,1,0:T(8,128)(2,1)} %state_hbm.1) | copy-start | bytes 15728644
  20.4 5.9 %collective-permute-start.2 = (f32[6,1,16,720]{3,2,1,0:T(8,128)S(1)}, f32[6,1,16,720]{3,2,1,0:T(8,128)S(1)}, u32[]{:S(2)}, u32[]{:S(2)}) collective-permute-start(f32[6,1,16,720]{3,2,1,0:T(8,128)S(1)} %get-tuple-element.24), channel_id=1, source_target_pairs={{0,1},{1,2},{2,3},{3,4},{4,5},{5,6},{6,7},{7,8},{8,9},{9,10},{10,1... | collective-permute-start | bytes 829448 | tf_op jit(solution)/shard_map/ppermute | solution.py:32
  22.6 6.4 %collective-permute-start.3 = (f32[6,1,16,720]{3,2,1,0:T(8,128)S(1)}, f32[6,1,16,720]{3,2,1,0:T(8,128)S(1)}, u32[]{:S(2)}, u32[]{:S(2)}) collective-permute-start(f32[6,1,16,720]{3,2,1,0:T(8,128)S(1)} %get-tuple-element.25), channel_id=1, source_target_pairs={{1,0},{2,1},{3,2},{4,3},{5,4},{6,5},{7,6},{8,7},{9,8},{10,9},{11,1... | collective-permute-start | bytes 829448 | tf_op jit(solution)/shard_map/ppermute | solution.py:34
  32.0 1.6 %copy-start.10 = (f32[16,16,1,1]{1,0,3,2:T(8,128)S(1)}, f32[16,16,1,1]{1,0,3,2:T(8,128)}, u32[]{:S(2)}) copy-start(f32[16,16,1,1]{1,0,3,2:T(8,128)} %constant.155) | copy-start | bytes 3076
  33.6 1.5 %copy-start.5 = (f32[4,8,16,720]{3,2,1,0:T(8,128)S(1)}, f32[4,8,16,720]{3,2,1,0:T(8,128)}, u32[]{:S(2)}) copy-start(f32[4,8,16,720]{3,2,1,0:T(8,128)} %copy-done.4) | copy-start | bytes 4423684
  33.6 1.5 %copy-start.11 = (f32[16,16,1,1]{1,0,3,2:T(8,128)S(1)}, f32[16,16,1,1]{1,0,3,2:T(8,128)}, u32[]{:S(2)}) copy-start(f32[16,16,1,1]{1,0,3,2:T(8,128)} %constant.154) | copy-start | bytes 3076
  33.6 1.5 %copy-start.15 = (f32[16]{0:T(128)S(1)}, f32[16]{0:T(128)}, u32[]{:S(2)}) copy-start(f32[16]{0:T(128)} %constant.152) | copy-start | bytes 196
  36.9 10.0 %copy-start.2 = (f32[4,8,16,720]{3,2,1,0:T(8,128)}, f32[4,8,16,720]{3,2,1,0:T(8,128)S(1)}, u32[]{:S(2)}) copy-start(f32[4,8,16,720]{3,2,1,0:T(8,128)S(1)} %bitcast_add_fusion.1) | copy-start | bytes 4423684
  36.9 2.8 %copy-start.13 = (s32[4,8,4]{1,2,0:T(4,128)S(1)}, s32[4,8,4]{1,2,0:T(4,128)}, u32[]{:S(2)}) copy-start(s32[4,8,4]{1,2,0:T(4,128)} %param.13) | copy-start | bytes 1540
  37.0 9.8 %collective-permute-start.4 = (f32[1,8,16,720]{3,2,1,0:T(8,128)S(1)}, f32[1,8,16,720]{3,2,1,0:T(8,128)S(1)}, u32[]{:S(2)}, u32[]{:S(2)}) collective-permute-start(f32[1,8,16,720]{3,2,1,0:T(8,128)S(1)} %get-tuple-element.26), channel_id=1, source_target_pairs={{0,32},{32,64},{64,96},{96,0},{1,33},{33,65},{65,97},{97,1},{2,34}... | collective-permute-start | bytes 1105928 | tf_op jit(solution)/shard_map/ppermute | solution.py:32
  37.2 9.7 %collective-permute-start.5 = (f32[1,8,16,720]{3,2,1,0:T(8,128)S(1)}, f32[1,8,16,720]{3,2,1,0:T(8,128)S(1)}, u32[]{:S(2)}, u32[]{:S(2)}) collective-permute-start(f32[1,8,16,720]{3,2,1,0:T(8,128)S(1)} %get-tuple-element.27), channel_id=1, source_target_pairs={{32,0},{64,32},{96,64},{0,96},{33,1},{65,33},{97,65},{1,97},{34,2}... | collective-permute-start | bytes 1105928 | tf_op jit(solution)/shard_map/ppermute | solution.py:34
  46.9 4.6 %copy-start.7 = (f32[1,8,16,720]{3,2,1,0:T(8,128)}, f32[1,8,16,720]{3,2,1,0:T(8,128)S(1)}, u32[]{:S(2)}) copy-start(f32[1,8,16,720]{3,2,1,0:T(8,128)S(1)} %collective-permute-done.5) | copy-start | bytes 1105924
  46.9 6.2 %collective-permute-start.6 = (f32[6,1,16,720]{3,2,1,0:T(8,128)S(1)}, f32[6,1,16,720]{3,2,1,0:T(8,128)S(1)}, u32[]{:S(2)}, u32[]{:S(2)}) collective-permute-start(f32[6,1,16,720]{3,2,1,0:T(8,128)S(1)} %get-tuple-element.22), channel_id=1, source_target_pairs={{0,1},{1,2},{2,3},{3,4},{4,5},{5,6},{6,7},{7,8},{8,9},{9,10},{10,1... | collective-permute-start | bytes 829448 | tf_op jit(solution)/shard_map/ppermute | solution.py:32
  49.5 6.4 %collective-permute-start.7 = (f32[6,1,16,720]{3,2,1,0:T(8,128)S(1)}, f32[6,1,16,720]{3,2,1,0:T(8,128)}, u32[]{:S(2)}, u32[]{:S(2)}) collective-permute-start(f32[6,1,16,720]{3,2,1,0:T(8,128)S(1)} %get-tuple-element.23), channel_id=1, source_target_pairs={{1,0},{2,1},{3,2},{4,3},{5,4},{6,5},{7,6},{8,7},{9,8},{10,9},{11,1... | collective-permute-start | bytes 829448 | tf_op jit(solution)/shard_map/ppermute | solution.py:34
  53.2 0.7 copy-start.8
  60.5 1.9 %copy-start.3 = (f32[4,8,16,720]{3,2,1,0:T(8,128)S(1)}, f32[4,8,16,720]{3,2,1,0:T(8,128)}, u32[]{:S(2)}) copy-start(f32[4,8,16,720]{3,2,1,0:T(8,128)} %copy-done.2) | copy-start | bytes 4423684
  62.4 1.5 %copy-start.14 = (f32[4,16,1,1]{1,0,3,2:T(4,128)S(1)}, f32[4,16,1,1]{1,0,3,2:T(4,128)}, u32[]{:S(2)}) copy-start(f32[4,16,1,1]{1,0,3,2:T(4,128)} %constant.156) | copy-start | bytes 772
  63.9 1.6 %copy-start.6 = (f32[4,8,16,720]{3,2,1,0:T(8,128)}, f32[4,8,16,720]{3,2,1,0:T(8,128)S(1)}, u32[]{:S(2)}) copy-start(f32[4,8,16,720]{3,2,1,0:T(8,128)S(1)} %fusion) | copy-start | bytes 4423684
  65.5 1.2 %copy-start.9 = (f32[128,1]{1,0:T(8,128)S(1)}, f32[128,1]{1,0:T(8,128)}, u32[]{:S(2)}) copy-start(f32[128,1]{1,0:T(8,128)} %copy.49) | copy-start | bytes 1540

commit v8 on v7

--- a/solution.py
+++ b/solution.py
@@ -36,6 +36,29 @@
             axis=dim,
         )
     return cells
+
+
+def in_element_laplace(cells):
+    point = np.arange(16)
+    b_of = point % 4
+    a_of = point // 4
+
+    def shifted(step, valid):
+        if step > 0:
+            moved = jnp.concatenate([cells[:, :, step:], jnp.zeros_like(cells[:, :, :step])], axis=2)
+        else:
+            moved = jnp.concatenate([jnp.zeros_like(cells[:, :, step:]), cells[:, :, :step]], axis=2)
+        mask = jnp.asarray(valid.astype(np.float32))[None, None, :, None]
+        return moved * mask
+
+    total = (
+        shifted(1, b_of < 3)
+        + shifted(-1, b_of > 0)
+        + shifted(4, a_of < 3)
+        + shifted(-4, a_of > 0)
+    )
+    degree = (b_of < 3).astype(np.float32) + (b_of > 0) + (a_of < 3) + (a_of > 0)
+    return total - jnp.asarray(degree.astype(np.float32))[None, None, :, None] * cells
 
 
 def node_tables():
@@ -288,16 +311,14 @@
     part, start_mean = crm_first(crm_state, crm_active)
     state = dyn_state
     for step in range(DSTEPS):
-        state = state + KAPPA * jnp.einsum(
-            "nm,rcmw->rcnw", laplace, state, precision=lax.Precision.HIGHEST
-        )
+        state = state + KAPPA * in_element_laplace(state)
         if step == 0:
             faced = extended_2(state, (("face", 0),), 1)
             faced, part, start_mean = lax.optimization_barrier((faced, part, start_mean))
             extended = extended_2(faced, (("col", 1),), 1)
         else:
             extended = extended_2(state, (("face", 0), ("col", 1)), 1)
-        matched = jnp.take(extended.reshape(-1, width), index_flat, axis=0).reshape(
+        matched = jnp.take(extended.reshape(-1, width), index_flat, axis=0, mode="clip").reshape(
             rows_dev, cols_dev, 16, width
         )
         summed = jnp.einsum("nm,rcmw->rcnw", spread, matched, precision=lax.Precision.HIGHEST)

time: 121 us -> 125 us (1.033)
  local copies, waits for them, and re-layouts: 17.8 us -> 22.6 us
  matrix products: 9.16 us -> 7.76 us
    dot_general x2 -> x0, matrix products: 5.23 us -> none  [per_device(): jnp.einsum('nm,rcmw->rcnw', laplace, state, precision=lax.Precision.HIGHEST)]
    dot_general x2, matrix products: 2.99 us -> 6.82 us  [per_device(): jnp.einsum('nm,rcmw->rcnw', spread, matched, precision=lax.Precision.HIGH...]
    select_n x3 -> x0, other arithmetic: 3.29 us -> none  [per_device(): jnp.take(extended.reshape(-1, width), index_flat, axis=0)]
    slice x0 -> x4, local copies, waits for them, and re-layouts: none -> 3.04 us  [shifted(): cells[:, :, step:]]
    add x0 -> x2, other arithmetic: none -> 2.03 us  [per_device(): state = state + KAPPA * in_element_laplace(state)]
    concatenate x3, other arithmetic: 2.5 us -> 4.28 us  [extended_2(): jnp.concatenate([lax.ppermute(tail, axis, [(i, (i + 1) % count) for i in...]
    unnamed x33 -> x41, local copies, waits for them, and re-layouts: 3.55 us -> 5.26 us
  transfers between devices with their start and end apart: 8 -> 8, of which waited for: 5 -> 5; matrix products, arithmetic and copies ran while one was open for 5% -> 4% of each run, Pallas kernels for 7% -> 7%
where the time goes in v8:
time: 125 us
  blocking collectives  38.1 us (30%)
  local copies, waits for them, and re-layouts  22.6 us (18%)
  Pallas kernels  20.6 us (16%)
  waiting for transfers between devices  13.1 us (10%)
  starting transfers between devices  12 us (10%)
  other arithmetic  9.33 us (7%)
  matrix products  7.76 us (6%)
    all_to_all x2, blocking collectives, exchange(): lax.all_to_all(chunks, ('face', 'col'), split_axis=0, concat_axis=0, tile...  38.1 us
    pallas_call x1, Pallas kernels, crm_second(): pl.pallas_call(crm_second_kernel, out_shape=(jax.ShapeDtypeStruct(part.sh...  11.9 us
    pallas_call x1, Pallas kernels, crm_first(): pl.pallas_call(crm_first_kernel, out_shape=(jax.ShapeDtypeStruct(state.sh...  8.78 us
    ppermute x4, waiting for transfers between devices, extended_2(): lax.ppermute(tail, axis, [(i, (i + 1) % count) for i in range(count)])  8.49 us
    ppermute x4, starting transfers between devices, extended_2(): lax.ppermute(tail, axis, [(i, (i + 1) % count) for i in range(count)])  7.08 us
    dot_general x2, matrix products, per_device(): jnp.einsum('nm,rcmw->rcnw', spread, matched, precision=lax.Precision.HIGH...  6.82 us
    unnamed x41, local copies, waits for them, and re-layouts  5.26 us
    gather x2, local copies, waits for them, and re-layouts, per_device(): jnp.take(extended.reshape(-1, width), index_flat, axis=0, mode='clip')  5.19 us
  transfers between devices with their start and end apart: 8, of which 5 were waited for; matrix products, arithmetic and copies ran while one was open for 4% of the time, Pallas kernels for 7%

profile of v8, /device:TPU:1, one launch (start us, length us, event | category | flops | bytes accessed | tf_op | source)
XLA Modules:
  0.0 124.7 jit_solution(14960223592999881985)
XLA Ops:
  0.6 2.3 %fusion.34 = (f32[4,8,15,720]{3,2,1,0:T(8,128)S(1)}, f32[4,8,15,720]{3,2,1,0:T(8,128)S(1)}) fusion(f32[4,8,16,720]{3,2,1,0:T(8,128)} %param.18), kind=kLoop, calls=%fused_computation.95 | loop fusion | bytes 5529600 | tf_op jit(solution)/shard_map/slice | solution.py:48
  4.8 2.2 %collective-permute-start = (f32[1,8,16,720]{3,2,1,0:T(8,128)S(1)}, f32[1,8,16,720]{3,2,1,0:T(8,128)S(1)}, u32[]{:S(2)}, u32[]{:S(2)}) collective-permute-start(f32[1,8,16,720]{3,2,1,0:T(8,128)S(1)} %get-tuple-element.31), channel_id=1, source_target_pairs={{0,32},{32,64},{64,96},{96,0},{1,33},{33,65},{65,97},{97,1},{2,34}... | collective-permute-start | bytes 1105928 | tf_op jit(solution)/shard_map/ppermute | solution.py:32
  7.0 1.5 %collective-permute-start.1 = (f32[1,8,16,720]{3,2,1,0:T(8,128)S(1)}, f32[1,8,16,720]{3,2,1,0:T(8,128)S(1)}, u32[]{:S(2)}, u32[]{:S(2)}) collective-permute-start(f32[1,8,16,720]{3,2,1,0:T(8,128)S(1)} %get-tuple-element.32), channel_id=1, source_target_pairs={{32,0},{64,32},{96,64},{0,96},{33,1},{65,33},{97,65},{1,97},{34,2}... | collective-permute-start | bytes 1105928 | tf_op jit(solution)/shard_map/ppermute | solution.py:34
  9.1 2.5 %copy-done = bf16[10,32,64,128]{3,2,1,0:T(8,128)(2,1)S(1)} copy-done((bf16[10,32,64,128]{3,2,1,0:T(8,128)(2,1)S(1)}, bf16[10,32,64,128]{3,2,1,0:T(8,128)(2,1)}, u32[]{:S(2)}) %copy-start) | copy-done | bytes 5242904
  11.6 8.8 %shard_map.193 = (f32[10,32,64,128]{3,2,1,0:T(8,128)}, f32[10,32,128]{2,1,0:T(8,128)S(1)}) custom-call(s32[1,128]{1,0:T(1,128)S(1)} %bitcast.48, bf16[10,32,64,128]{3,2,1,0:T(8,128)(2,1)S(1)} %copy-done), custom_call_target="tpu_custom_call" | custom-call | tf_op jit(solution)/shard_map/pallas_call | solution.py:228
  20.7 1.4 %copy-done.5 = f32[6,8,16,720]{3,2,1,0:T(8,128)} copy-done((f32[6,8,16,720]{3,2,1,0:T(8,128)}, f32[6,8,16,720]{3,2,1,0:T(8,128)S(1)}, u32[]{:S(2)}) %copy-start.5) | copy-done | bytes 2211864
  22.1 2.3 %collective-permute-start.2 = (f32[6,1,16,720]{3,2,1,0:T(8,128)S(1)}, f32[6,1,16,720]{3,2,1,0:T(8,128)S(1)}, u32[]{:S(2)}, u32[]{:S(2)}) collective-permute-start(f32[6,1,16,720]{3,2,1,0:T(8,128)S(1)} %get-tuple-element.23), channel_id=1, source_target_pairs={{0,1},{1,2},{2,3},{3,4},{4,5},{5,6},{6,7},{7,8},{8,9},{9,10},{10,1... | collective-permute-start | bytes 829448 | tf_op jit(solution)/shard_map/ppermute | solution.py:32
  24.7 3.3 %collective-permute-done.2 = f32[6,1,16,720]{3,2,1,0:T(8,128)S(1)} collective-permute-done((f32[6,1,16,720]{3,2,1,0:T(8,128)S(1)}, f32[6,1,16,720]{3,2,1,0:T(8,128)S(1)}, u32[]{:S(2)}, u32[]{:S(2)}) %collective-permute-start.2) | collective-permute-done | bytes 276512 | tf_op jit(solution)/shard_map/ppermute | solution.py:32
  28.0 2.8 %collective-permute-done.3 = f32[6,1,16,720]{3,2,1,0:T(8,128)} collective-permute-done((f32[6,1,16,720]{3,2,1,0:T(8,128)S(1)}, f32[6,1,16,720]{3,2,1,0:T(8,128)}, u32[]{:S(2)}, u32[]{:S(2)}) %collective-permute-start.3) | collective-permute-done | bytes 276512 | tf_op jit(solution)/shard_map/ppermute | solution.py:34
  30.8 2.1 %pad_maximum_fusion = f32[6,10,16,720]{3,2,1,0:T(8,128)S(1)} fusion(f32[6,1,16,720]{3,2,1,0:T(8,128)} %collective-permute-done.3, f32[6,8,16,720]{3,2,1,0:T(8,128)} %copy-done.5, f32[6,1,16,720]{3,2,1,0:T(8,128)S(1)} %collective-permute-done.2), kind=kLoop, calls=%fused_computation.7 | loop fusion | flops 1382400 | bytes 5529600 | tf_op jit(solution)/shard_map/concatenate | solution.py:30
  32.9 2.6 %gather_fusion = f32[512,720]{1,0:T(8,128)} fusion(f32[960,720]{1,0:T(8,128)S(1)} %bitcast.51, s32[1024]{0:T(1024)S(1)} %pad_clamp_fusion.2), kind=kCustom, calls=%fused_computation | custom fusion | bytes 2951168 | tf_op jit(solution)/shard_map/jit(_take)/gather | solution.py:321
  35.5 3.4 %fusion.1 = f32[4,8,16,720]{3,2,1,0:T(8,128)S(1)} fusion(f32[4,8,16,720]{3,2,1,0:T(8,128)} %copy-done.4, f32[4,8,16,720]{3,2,1,0:T(8,128)} %bitcast.54, f32[16,16,1,1]{1,0,3,2:T(8,128)S(1)} %copy-done.10, f32[16]{0:T(128)S(1)} %copy-done.14), kind=kOutput, calls=%fused_computation.13 | convolution fusion | flops 71516160 | bytes 4424768 | tf_op jit(solution)/shard_map/nm,rcmw->rcnw/dot_general | solution.py:324
  40.7 2.6 %collective-permute-start.5 = (f32[1,8,16,720]{3,2,1,0:T(8,128)S(1)}, f32[1,8,16,720]{3,2,1,0:T(8,128)S(1)}, u32[]{:S(2)}, u32[]{:S(2)}) collective-permute-start(f32[1,8,16,720]{3,2,1,0:T(8,128)S(1)} %get-tuple-element.26), channel_id=1, source_target_pairs={{32,0},{64,32},{96,64},{0,96},{33,1},{65,33},{97,65},{1,97},{34,2}... | collective-permute-start | bytes 1105928 | tf_op jit(solution)/shard_map/ppermute | solution.py:34
  43.5 2.5 %sort.17 = (s32[128]{0:T(128)}, s32[128]{0:T(128)S(1)}) sort(s32[128]{0:T(128)S(1)} %reshape.154, s32[128]{0:T(128)S(1)} %iota.35), dimensions={0}, to_apply=%region_0.1 | sort | flops 896 | bytes 2048 | tf_op jit(solution)/shard_map/jit(argsort)/sort | solution.py:332
  46.0 4.3 %collective-permute-done.4 = f32[1,8,16,720]{3,2,1,0:T(8,128)S(1)} collective-permute-done((f32[1,8,16,720]{3,2,1,0:T(8,128)S(1)}, f32[1,8,16,720]{3,2,1,0:T(8,128)S(1)}, u32[]{:S(2)}, u32[]{:S(2)}) %collective-permute-start.4) | collective-permute-done | bytes 368672 | tf_op jit(solution)/shard_map/ppermute | solution.py:32
  50.4 2.5 %collective-permute-start.6 = (f32[6,1,16,720]{3,2,1,0:T(8,128)S(1)}, f32[6,1,16,720]{3,2,1,0:T(8,128)S(1)}, u32[]{:S(2)}, u32[]{:S(2)}) collective-permute-start(f32[6,1,16,720]{3,2,1,0:T(8,128)S(1)} %get-tuple-element.21), channel_id=1, source_target_pairs={{0,1},{1,2},{2,3},{3,4},{4,5},{5,6},{6,7},{7,8},{8,9},{9,10},{10,1... | collective-permute-start | bytes 829448 | tf_op jit(solution)/shard_map/ppermute | solution.py:32
  53.7 1.2 gather_fusion.3
  57.3 1.9 %collective-permute-done.7 = f32[6,1,16,720]{3,2,1,0:T(8,128)} collective-permute-done((f32[6,1,16,720]{3,2,1,0:T(8,128)S(1)}, f32[6,1,16,720]{3,2,1,0:T(8,128)}, u32[]{:S(2)}, u32[]{:S(2)}) %collective-permute-start.7) | collective-permute-done | bytes 276512 | tf_op jit(solution)/shard_map/ppermute | solution.py:34
  59.1 2.0 %pad_maximum_fusion.1 = f32[6,10,16,720]{3,2,1,0:T(8,128)S(1)} fusion(f32[6,1,16,720]{3,2,1,0:T(8,128)} %collective-permute-done.7, f32[1,8,16,720]{3,2,1,0:T(8,128)} %copy-done.7, f32[4,8,16,720]{3,2,1,0:T(8,128)} %copy-done.3, f32[1,8,16,720]{3,2,1,0:T(8,128)S(1)} %collective-permute-done.4, f32[6,1,16,720]{3,2,1,0:T(8,128)} %copy-done.8), kind=kLoop, calls=%fused_computation.8 | loop fusion | flops 2764800 | bytes 5529600 | tf_op jit(solution)/shard_map/concatenate | solution.py:30
  61.1 2.6 %gather_fusion.1 = f32[512,720]{1,0:T(8,128)} fusion(f32[960,720]{1,0:T(8,128)S(1)} %bitcast.50, s32[1024]{0:T(1024)S(1)} %pad_clamp_fusion.2), kind=kCustom, calls=%fused_computation.1 | custom fusion | bytes 2951168 | tf_op jit(solution)/shard_map/jit(_take)/gather | solution.py:321
  63.7 3.4 %fusion = f32[4,8,16,720]{3,2,1,0:T(8,128)S(1)} fusion(f32[4,8,16,720]{3,2,1,0:T(8,128)} %copy-done.3, f32[4,8,16,720]{3,2,1,0:T(8,128)} %bitcast.53, f32[16,16,1,1]{1,0,3,2:T(8,128)S(1)} %copy-done.10, f32[16]{0:T(128)S(1)} %copy-done.14), kind=kOutput, calls=%fused_computation.11 | convolution fusion | flops 71516160 | bytes 4424768 | tf_op jit(solution)/shard_map/nm,rcmw->rcnw/dot_general | solution.py:324
  70.3 23.5 %all_to_all.10 = f32[128,1,321]{2,1,0:T(1,128)S(1)} all-to-all(f32[128,1,321]{2,1,0:T(1,128)S(1)} %copy.59), channel_id=1, replica_groups=mesh['face'=4,'col'=32] {'face','col'}, dimensions={0} | all-to-all | bytes 328704 | tf_op jit(solution)/shard_map/all_to_all | solution.py:283
  95.3 11.9 %shard_map.194 = (bf16[10,32,64,128]{3,2,1,0:T(8,128)(2,1)}, f32[10,32,128]{2,1,0:T(8,128)S(1)}) custom-call(f32[10,32,128]{2,1,0:T(8,128)S(1)} %bitcast.46, s32[1,128]{1,0:T(1,128)S(1)} %bitcast.49, f32[10,32,128]{2,1,0:T(8,128)S(1)} %get-tuple-element.15.mean_ref, f32[10,32,64,128]{3,2,1,0:T(8,128)} %get-tuple-element.16.part_hbm), custom_call_target="tpu_custom_call" | custom-call | tf_op jit(solution)/shard_map/pallas_call | solution.py:250
  108.3 14.6 %all_to_all.11 = f32[128,1,320]{2,1,0:T(1,128)S(1)} all-to-all(f32[128,1,320]{2,1,0:T(1,128)S(1)} %copy.64), channel_id=1, replica_groups=mesh['face'=4,'col'=32] {'face','col'}, dimensions={0} | all-to-all | bytes 327680 | tf_op jit(solution)/shard_map/all_to_all | solution.py:283
  (94 shorter events, 15.6 us)
Async XLA Ops:
  0.6 2.4 %copy-start.2 = (f32[4,8,16,720]{3,2,1,0:T(8,128)S(1)}, f32[4,8,16,720]{3,2,1,0:T(8,128)}, u32[]{:S(2)}) copy-start(f32[4,8,16,720]{3,2,1,0:T(8,128)} %param.18) | copy-start | bytes 4423684
  3.0 0.7 copy-start.19
  4.7 15.7 %copy-start.4 = (f32[4,8,16,720]{3,2,1,0:T(8,128)}, f32[4,8,16,720]{3,2,1,0:T(8,128)S(1)}, u32[]{:S(2)}) copy-start(f32[4,8,16,720]{3,2,1,0:T(8,128)S(1)} %multiply_add_fusion.1) | copy-start | bytes 4423684
  4.7 3.8 %copy-start.11 = (s32[4,8,4]{1,2,0:T(4,128)S(1)}, s32[4,8,4]{1,2,0:T(4,128)}, u32[]{:S(2)}) copy-start(s32[4,8,4]{1,2,0:T(4,128)} %param.19) | copy-start | bytes 1540
  4.7 4.3 %copy-start.1 = (s32[128]{0:T(128)S(1)}, s32[128]{0:T(128)}, u32[]{:S(2)}) copy-start(s32[128]{0:T(128)} %param.21) | copy-start | bytes 1540
  4.8 15.5 %collective-permute-start = (f32[1,8,16,720]{3,2,1,0:T(8,128)S(1)}, f32[1,8,16,720]{3,2,1,0:T(8,128)S(1)}, u32[]{:S(2)}, u32[]{:S(2)}) collective-permute-start(f32[1,8,16,720]{3,2,1,0:T(8,128)S(1)} %get-tuple-element.31), channel_id=1, source_target_pairs={{0,32},{32,64},{64,96},{96,0},{1,33},{33,65},{65,97},{97,1},{2,34}... | collective-permute-start | bytes 1105928 | tf_op jit(solution)/shard_map/ppermute | solution.py:32
  7.0 13.4 %collective-permute-start.1 = (f32[1,8,16,720]{3,2,1,0:T(8,128)S(1)}, f32[1,8,16,720]{3,2,1,0:T(8,128)S(1)}, u32[]{:S(2)}, u32[]{:S(2)}) collective-permute-start(f32[1,8,16,720]{3,2,1,0:T(8,128)S(1)} %get-tuple-element.32), channel_id=1, source_target_pairs={{32,0},{64,32},{96,64},{0,96},{33,1},{65,33},{97,65},{1,97},{34,2}... | collective-permute-start | bytes 1105928 | tf_op jit(solution)/shard_map/ppermute | solution.py:34
  9.1 2.5 %copy-start = (bf16[10,32,64,128]{3,2,1,0:T(8,128)(2,1)S(1)}, bf16[10,32,64,128]{3,2,1,0:T(8,128)(2,1)}, u32[]{:S(2)}) copy-start(bf16[10,32,64,128]{3,2,1,0:T(8,128)(2,1)} %state_hbm.1) | copy-start | bytes 15728644
  20.6 1.4 %copy-start.5 = (f32[6,8,16,720]{3,2,1,0:T(8,128)}, f32[6,8,16,720]{3,2,1,0:T(8,128)S(1)}, u32[]{:S(2)}) copy-start(f32[6,8,16,720]{3,2,1,0:T(8,128)S(1)} %pad_maximum_fusion.2) | copy-start | bytes 6635524
  22.1 5.9 %collective-permute-start.2 = (f32[6,1,16,720]{3,2,1,0:T(8,128)S(1)}, f32[6,1,16,720]{3,2,1,0:T(8,128)S(1)}, u32[]{:S(2)}, u32[]{:S(2)}) collective-permute-start(f32[6,1,16,720]{3,2,1,0:T(8,128)S(1)} %get-tuple-element.23), channel_id=1, source_target_pairs={{0,1},{1,2},{2,3},{3,4},{4,5},{5,6},{6,7},{7,8},{8,9},{9,10},{10,1... | collective-permute-start | bytes 829448 | tf_op jit(solution)/shard_map/ppermute | solution.py:32
  24.4 6.4 %collective-permute-start.3 = (f32[6,1,16,720]{3,2,1,0:T(8,128)S(1)}, f32[6,1,16,720]{3,2,1,0:T(8,128)}, u32[]{:S(2)}, u32[]{:S(2)}) collective-permute-start(f32[6,1,16,720]{3,2,1,0:T(8,128)S(1)} %get-tuple-element.24), channel_id=1, source_target_pairs={{1,0},{2,1},{3,2},{4,3},{5,4},{6,5},{7,6},{8,7},{9,8},{10,9},{11,1... | collective-permute-start | bytes 829448 | tf_op jit(solution)/shard_map/ppermute | solution.py:34
  32.9 2.6 %copy-start.10 = (f32[16,16,1,1]{1,0,3,2:T(8,128)S(1)}, f32[16,16,1,1]{1,0,3,2:T(8,128)}, u32[]{:S(2)}) copy-start(f32[16,16,1,1]{1,0,3,2:T(8,128)} %constant.174) | copy-start | bytes 3076
  32.9 2.6 %copy-start.14 = (f32[16]{0:T(128)S(1)}, f32[16]{0:T(128)}, u32[]{:S(2)}) copy-start(f32[16]{0:T(128)} %constant.172) | copy-start | bytes 196
  40.4 10.0 %copy-start.3 = (f32[4,8,16,720]{3,2,1,0:T(8,128)}, f32[4,8,16,720]{3,2,1,0:T(8,128)S(1)}, u32[]{:S(2)}) copy-start(f32[4,8,16,720]{3,2,1,0:T(8,128)S(1)} %multiply_add_fusion) | copy-start | bytes 4423684
  40.4 2.8 %copy-start.12 = (s32[4,8,4]{1,2,0:T(4,128)S(1)}, s32[4,8,4]{1,2,0:T(4,128)}, u32[]{:S(2)}) copy-start(s32[4,8,4]{1,2,0:T(4,128)} %param.20) | copy-start | bytes 1540
  40.5 9.8 %collective-permute-start.4 = (f32[1,8,16,720]{3,2,1,0:T(8,128)S(1)}, f32[1,8,16,720]{3,2,1,0:T(8,128)S(1)}, u32[]{:S(2)}, u32[]{:S(2)}) collective-permute-start(f32[1,8,16,720]{3,2,1,0:T(8,128)S(1)} %get-tuple-element.25), channel_id=1, source_target_pairs={{0,32},{32,64},{64,96},{96,0},{1,33},{33,65},{65,97},{97,1},{2,34}... | collective-permute-start | bytes 1105928 | tf_op jit(solution)/shard_map/ppermute | solution.py:32
  40.7 9.7 %collective-permute-start.5 = (f32[1,8,16,720]{3,2,1,0:T(8,128)S(1)}, f32[1,8,16,720]{3,2,1,0:T(8,128)S(1)}, u32[]{:S(2)}, u32[]{:S(2)}) collective-permute-start(f32[1,8,16,720]{3,2,1,0:T(8,128)S(1)} %get-tuple-element.26), channel_id=1, source_target_pairs={{32,0},{64,32},{96,64},{0,96},{33,1},{65,33},{97,65},{1,97},{34,2}... | collective-permute-start | bytes 1105928 | tf_op jit(solution)/shard_map/ppermute | solution.py:34
  50.4 4.6 %copy-start.7 = (f32[1,8,16,720]{3,2,1,0:T(8,128)}, f32[1,8,16,720]{3,2,1,0:T(8,128)S(1)}, u32[]{:S(2)}) copy-start(f32[1,8,16,720]{3,2,1,0:T(8,128)S(1)} %collective-permute-done.5) | copy-start | bytes 1105924
  50.4 6.1 %collective-permute-start.6 = (f32[6,1,16,720]{3,2,1,0:T(8,128)S(1)}, f32[6,1,16,720]{3,2,1,0:T(8,128)S(1)}, u32[]{:S(2)}, u32[]{:S(2)}) collective-permute-start(f32[6,1,16,720]{3,2,1,0:T(8,128)S(1)} %get-tuple-element.21), channel_id=1, source_target_pairs={{0,1},{1,2},{2,3},{3,4},{4,5},{5,6},{6,7},{7,8},{8,9},{9,10},{10,1... | collective-permute-start | bytes 829448 | tf_op jit(solution)/shard_map/ppermute | solution.py:32
  52.9 6.3 %collective-permute-start.7 = (f32[6,1,16,720]{3,2,1,0:T(8,128)S(1)}, f32[6,1,16,720]{3,2,1,0:T(8,128)}, u32[]{:S(2)}, u32[]{:S(2)}) collective-permute-start(f32[6,1,16,720]{3,2,1,0:T(8,128)S(1)} %get-tuple-element.22), channel_id=1, source_target_pairs={{1,0},{2,1},{3,2},{4,3},{5,4},{6,5},{7,6},{8,7},{9,8},{10,9},{11,1... | collective-permute-start | bytes 829448 | tf_op jit(solution)/shard_map/ppermute | solution.py:34
  56.6 0.7 copy-start.8
  63.7 3.5 %copy-start.13 = (f32[4,16,1,1]{1,0,3,2:T(4,128)S(1)}, f32[4,16,1,1]{1,0,3,2:T(4,128)}, u32[]{:S(2)}) copy-start(f32[4,16,1,1]{1,0,3,2:T(4,128)} %constant.175) | copy-start | bytes 772
  67.2 1.6 %copy-start.6 = (f32[4,8,16,720]{3,2,1,0:T(8,128)}, f32[4,8,16,720]{3,2,1,0:T(8,128)S(1)}, u32[]{:S(2)}) copy-start(f32[4,8,16,720]{3,2,1,0:T(8,128)S(1)} %fusion) | copy-start | bytes 4423684
  68.7 1.2 copy-start.9
  (4 other events, 2.7 us)

commit v9 on v7

--- a/solution.py
+++ b/solution.py
@@ -320,12 +320,8 @@
     crm_new, tend = crm_second(part, start_mean, forcing, crm_active)
     tend_rows = tend.reshape(NFLD * CLEV, per_dev).T[slots]
     returned = exchange(tend_rows.reshape(ndev, count, NFLD * CLEV))
-    placed = (
-        jnp.zeros((per_dev, NFLD * CLEV), jnp.float32)
-        .at[order]
-        .set(returned.reshape(per_dev, NFLD * CLEV))
-    )
-    column_tend = placed.reshape(rows_dev, cols_dev, 4, NFLD * CLEV)
+    rank = jnp.zeros((per_dev,), jnp.int32).at[order].set(jnp.arange(per_dev, dtype=jnp.int32))
+    column_tend = returned.reshape(per_dev, NFLD * CLEV)[rank.reshape(rows_dev, cols_dev, 4)]
     return (state, column_tend, crm_new)
 
 

time: 121 us -> 123 us (1.017)
  blocking collectives: 37.8 us -> 0 us
  waiting for transfers between devices: 13.7 us -> 33.3 us
  starting transfers between devices: 12 us -> 29.4 us
  local copies, waits for them, and re-layouts: 17.8 us -> 20.1 us
    all_to_all x2 -> x0, blocking collectives: 37.8 us -> none  [exchange(): lax.all_to_all(chunks, ('face', 'col'), split_axis=0, concat_axis=0, tile...]
    all_to_all x0 -> x2, waiting for transfers between devices: none -> 19.5 us  [exchange(): lax.all_to_all(chunks, ('face', 'col'), split_axis=0, concat_axis=0, tile...]
    all_to_all x0 -> x2, starting transfers between devices: none -> 17.4 us  [exchange(): lax.all_to_all(chunks, ('face', 'col'), split_axis=0, concat_axis=0, tile...]
    gather x0 -> x2, local copies, waits for them, and re-layouts: none -> 1.5 us  [per_device(): returned.reshape(per_dev, NFLD * CLEV)[rank.reshape(rows_dev, cols_dev, 4)]]
  transfers between devices with their start and end apart: 8 -> 10, of which waited for: 5 -> 7; matrix products, arithmetic and copies ran while one was open for 5% -> 6% of each run, Pallas kernels for 7% -> 7%
where the time goes in v9:
time: 123 us
  waiting for transfers between devices  33.3 us (27%)
  starting transfers between devices  29.4 us (24%)
  Pallas kernels  20.6 us (17%)
  local copies, waits for them, and re-layouts  20.1 us (16%)
  matrix products  9.17 us (7%)
  other arithmetic  8.84 us (7%)
    all_to_all x2, waiting for transfers between devices, exchange(): lax.all_to_all(chunks, ('face', 'col'), split_axis=0, concat_axis=0, tile...  19.5 us
    all_to_all x2, starting transfers between devices, exchange(): lax.all_to_all(chunks, ('face', 'col'), split_axis=0, concat_axis=0, tile...  17.4 us
    pallas_call x1, Pallas kernels, crm_second(): pl.pallas_call(crm_second_kernel, out_shape=(jax.ShapeDtypeStruct(part.sh...  11.9 us
    ppermute x4, waiting for transfers between devices, extended_2(): lax.ppermute(tail, axis, [(i, (i + 1) % count) for i in range(count)])  8.91 us
    pallas_call x1, Pallas kernels, crm_first(): pl.pallas_call(crm_first_kernel, out_shape=(jax.ShapeDtypeStruct(state.sh...  8.78 us
    ppermute x4, starting transfers between devices, extended_2(): lax.ppermute(tail, axis, [(i, (i + 1) % count) for i in range(count)])  7.18 us
    dot_general x2, matrix products, per_device(): jnp.einsum('nm,rcmw->rcnw', laplace, state, precision=lax.Precision.HIGHEST)  5.23 us
    gather x2, local copies, waits for them, and re-layouts, per_device(): jnp.take(extended.reshape(-1, width), index_flat, axis=0)  5.19 us
  transfers between devices with their start and end apart: 10, of which 7 were waited for; matrix products, arithmetic and copies ran while one was open for 6% of the time, Pallas kernels for 7%

profile of v9, /device:TPU:1, one launch (start us, length us, event | category | flops | bytes accessed | tf_op | source)
XLA Modules:
  0.0 122.6 jit_solution(4462471129990657265)
XLA Ops:
  0.6 3.4 %bitcast_add_fusion.3 = f32[4,8,16,720]{3,2,1,0:T(8,128)S(1)} fusion(f32[4,8,16,720]{3,2,1,0:T(8,128)} %param.11, f32[16,16,1,1]{1,0,3,2:T(8,128)} %constant.156), kind=kOutput, calls=%fused_computation.16 | convolution fusion | flops 71516160 | bytes 2950144 | tf_op jit(solution)/shard_map/nm,rcmw->rcnw/dot_general | solution.py:291
  4.2 2.2 %collective-permute-start = (f32[1,8,16,720]{3,2,1,0:T(8,128)S(1)}, f32[1,8,16,720]{3,2,1,0:T(8,128)S(1)}, u32[]{:S(2)}, u32[]{:S(2)}) collective-permute-start(f32[1,8,16,720]{3,2,1,0:T(8,128)S(1)} %get-tuple-element.28), channel_id=1, source_target_pairs={{0,32},{32,64},{64,96},{96,0},{1,33},{33,65},{65,97},{97,1},{2,34}... | collective-permute-start | bytes 1105928 | tf_op jit(solution)/shard_map/ppermute | solution.py:32
  8.8 2.5 %copy-done = bf16[10,32,64,128]{3,2,1,0:T(8,128)(2,1)S(1)} copy-done((bf16[10,32,64,128]{3,2,1,0:T(8,128)(2,1)S(1)}, bf16[10,32,64,128]{3,2,1,0:T(8,128)(2,1)}, u32[]{:S(2)}) %copy-start) | copy-done | bytes 5242904
  11.3 8.8 %shard_map.112 = (f32[10,32,64,128]{3,2,1,0:T(8,128)}, f32[10,32,128]{2,1,0:T(8,128)S(1)}) custom-call(s32[1,128]{1,0:T(1,128)S(1)} %bitcast.66, bf16[10,32,64,128]{3,2,1,0:T(8,128)(2,1)S(1)} %copy-done), custom_call_target="tpu_custom_call" | custom-call | tf_op jit(solution)/shard_map/pallas_call | solution.py:205
  20.4 2.3 %collective-permute-start.2 = (f32[6,1,16,720]{3,2,1,0:T(8,128)S(1)}, f32[6,1,16,720]{3,2,1,0:T(8,128)S(1)}, u32[]{:S(2)}, u32[]{:S(2)}) collective-permute-start(f32[6,1,16,720]{3,2,1,0:T(8,128)S(1)} %get-tuple-element.24), channel_id=1, source_target_pairs={{0,1},{1,2},{2,3},{3,4},{4,5},{5,6},{6,7},{7,8},{8,9},{9,10},{10,1... | collective-permute-start | bytes 829448 | tf_op jit(solution)/shard_map/ppermute | solution.py:32
  22.7 3.6 %collective-permute-done.2 = f32[6,1,16,720]{3,2,1,0:T(8,128)S(1)} collective-permute-done((f32[6,1,16,720]{3,2,1,0:T(8,128)S(1)}, f32[6,1,16,720]{3,2,1,0:T(8,128)S(1)}, u32[]{:S(2)}, u32[]{:S(2)}) %collective-permute-start.2) | collective-permute-done | bytes 276512 | tf_op jit(solution)/shard_map/ppermute | solution.py:32
  26.3 2.8 %collective-permute-done.3 = f32[6,1,16,720]{3,2,1,0:T(8,128)S(1)} collective-permute-done((f32[6,1,16,720]{3,2,1,0:T(8,128)S(1)}, f32[6,1,16,720]{3,2,1,0:T(8,128)S(1)}, u32[]{:S(2)}, u32[]{:S(2)}) %collective-permute-start.3) | collective-permute-done | bytes 276512 | tf_op jit(solution)/shard_map/ppermute | solution.py:34
  29.4 2.6 %gather_fusion.4 = f32[512,720]{1,0:T(8,128)} fusion(f32[960,720]{1,0:T(8,128)S(1)} %bitcast.69, s32[1024]{0:T(1024)S(1)} %pad_clamp_fusion.3), kind=kCustom, calls=%fused_computation.clone | custom fusion | bytes 2951168 | tf_op jit(solution)/shard_map/jit(_take)/gather | solution.py:300
  32.0 1.6 %broadcast_select_fusion.1 = f32[512,720]{1,0:T(8,128)S(1)} fusion(f32[512,720]{1,0:T(8,128)} %gather_fusion.4, pred[512]{0:T(512)(128)(4,1)S(1)} %compare_and_fusion), kind=kLoop, calls=%fused_computation.19 | loop fusion | flops 368640 | bytes 2949632 | tf_op jit(solution)/shard_map/jit(_take)/select_n | solution.py:300
  35.1 1.8 %bitcast_add_fusion.1 = f32[4,8,16,720]{3,2,1,0:T(8,128)S(1)} fusion(f32[16,16,1,1]{1,0,3,2:T(8,128)S(1)} %copy-done.11, f32[4,8,16,720]{3,2,1,0:T(8,128)S(1)} %copy-done.5, f32[4,8,720,16]{2,3,1,0:T(8,128)S(1)} %fusion.32, f32[16]{0:T(128)S(1)} %copy-done.15), kind=kOutput, calls=%fused_computation.13 | convolution fusion | flops 72990720 | bytes 4424768 | tf_op jit(solution)/shard_map/nm,rcmw->rcnw/dot_general | solution.py:291
  37.2 2.6 %collective-permute-start.5 = (f32[1,8,16,720]{3,2,1,0:T(8,128)S(1)}, f32[1,8,16,720]{3,2,1,0:T(8,128)S(1)}, u32[]{:S(2)}, u32[]{:S(2)}) collective-permute-start(f32[1,8,16,720]{3,2,1,0:T(8,128)S(1)} %get-tuple-element.27), channel_id=1, source_target_pairs={{32,0},{64,32},{96,64},{0,96},{33,1},{65,33},{97,65},{1,97},{34,2}... | collective-permute-start | bytes 1105928 | tf_op jit(solution)/shard_map/ppermute | solution.py:34
  40.0 2.5 %sort.17 = (s32[128]{0:T(128)}, s32[128]{0:T(128)S(1)}) sort(s32[128]{0:T(128)S(1)} %reshape.118, s32[128]{0:T(128)S(1)} %iota.38), dimensions={0}, to_apply=%region_0.2 | sort | flops 896 | bytes 2048 | tf_op jit(solution)/shard_map/jit(argsort)/sort | solution.py:311
  42.5 4.3 %collective-permute-done.4 = f32[1,8,16,720]{3,2,1,0:T(8,128)S(1)} collective-permute-done((f32[1,8,16,720]{3,2,1,0:T(8,128)S(1)}, f32[1,8,16,720]{3,2,1,0:T(8,128)S(1)}, u32[]{:S(2)}, u32[]{:S(2)}) %collective-permute-start.4) | collective-permute-done | bytes 368672 | tf_op jit(solution)/shard_map/ppermute | solution.py:32
  46.9 2.6 %collective-permute-start.6 = (f32[6,1,16,720]{3,2,1,0:T(8,128)S(1)}, f32[6,1,16,720]{3,2,1,0:T(8,128)S(1)}, u32[]{:S(2)}, u32[]{:S(2)}) collective-permute-start(f32[6,1,16,720]{3,2,1,0:T(8,128)S(1)} %get-tuple-element.22), channel_id=1, source_target_pairs={{0,1},{1,2},{2,3},{3,4},{4,5},{5,6},{6,7},{7,8},{8,9},{9,10},{10,1... | collective-permute-start | bytes 829448 | tf_op jit(solution)/shard_map/ppermute | solution.py:32
  53.9 2.0 %collective-permute-done.7 = f32[6,1,16,720]{3,2,1,0:T(8,128)} collective-permute-done((f32[6,1,16,720]{3,2,1,0:T(8,128)S(1)}, f32[6,1,16,720]{3,2,1,0:T(8,128)}, u32[]{:S(2)}, u32[]{:S(2)}) %collective-permute-start.7) | collective-permute-done | bytes 276512 | tf_op jit(solution)/shard_map/ppermute | solution.py:34
  55.9 2.0 %pad_maximum_fusion.1 = f32[6,10,16,720]{3,2,1,0:T(8,128)S(1)} fusion(f32[6,1,16,720]{3,2,1,0:T(8,128)} %collective-permute-done.7, f32[1,8,16,720]{3,2,1,0:T(8,128)} %copy-done.7, f32[4,8,16,720]{3,2,1,0:T(8,128)} %copy-done.2, f32[1,8,16,720]{3,2,1,0:T(8,128)S(1)} %collective-permute-done.4, f32[6,1,16,720]{3,2,1,0:T(8,128)} %copy-done.8), kind=kLoop, calls=%fused_computation.9 | loop fusion | flops 2764800 | bytes 5529600 | tf_op jit(solution)/shard_map/concatenate | solution.py:30
  57.9 2.6 %gather_fusion.5 = f32[512,720]{1,0:T(8,128)} fusion(f32[960,720]{1,0:T(8,128)S(1)} %bitcast.68, s32[1024]{0:T(1024)S(1)} %pad_clamp_fusion.3), kind=kCustom, calls=%fused_computation.1.clone | custom fusion | bytes 2951168 | tf_op jit(solution)/shard_map/jit(_take)/gather | solution.py:300
  60.5 1.7 %broadcast_select_fusion = f32[512,720]{1,0:T(8,128)S(1)} fusion(f32[512,720]{1,0:T(8,128)} %gather_fusion.5, pred[512]{0:T(512)(128)(4,1)S(1)} %compare_and_fusion), kind=kLoop, calls=%fused_computation.18 | loop fusion | flops 368640 | bytes 2949632 | tf_op jit(solution)/shard_map/jit(_take)/select_n | solution.py:300
  62.4 1.5 %fusion = f32[4,8,16,720]{3,2,1,0:T(8,128)S(1)} fusion(f32[4,8,16,720]{3,2,1,0:T(8,128)S(1)} %copy-done.3, f32[4,8,16,720]{3,2,1,0:T(8,128)S(1)} %bitcast.72, f32[16,16,1,1]{1,0,3,2:T(8,128)S(1)} %copy-done.10, f32[16]{0:T(128)S(1)} %copy-done.15), kind=kOutput, calls=%fused_computation.12 | convolution fusion | flops 71516160 | bytes 4424768 | tf_op jit(solution)/shard_map/nm,rcmw->rcnw/dot_general | solution.py:303
  67.7 13.0 %all-to-all-start = ((f32[128,1,321]{2,1,0:T(1,128)}), f32[128,1,321]{2,1,0:T(1,128)S(1)}, u32[]{:S(2)}, u32[]{:S(2)}) async-start(f32[128,1,321]{2,1,0:T(1,128)} %copy.49), calls=%async_computation | async-start | bytes 393216 | tf_op jit(solution)/shard_map/all_to_all | solution.py:260
  81.8 9.3 %all-to-all-done = f32[128,1,321]{2,1,0:T(1,128)S(1)} async-done(((f32[128,1,321]{2,1,0:T(1,128)}), f32[128,1,321]{2,1,0:T(1,128)S(1)}, u32[]{:S(2)}, u32[]{:S(2)}) %all-to-all-start) | async-done | bytes 164384 | tf_op jit(solution)/shard_map/all_to_all | solution.py:260
  92.6 11.9 %shard_map.113 = (bf16[10,32,64,128]{3,2,1,0:T(8,128)(2,1)}, f32[10,32,128]{2,1,0:T(8,128)S(1)}) custom-call(f32[10,32,128]{2,1,0:T(8,128)S(1)} %bitcast.64, s32[1,128]{1,0:T(1,128)S(1)} %bitcast.67, f32[10,32,128]{2,1,0:T(8,128)S(1)} %get-tuple-element.16.mean_ref, f32[10,32,64,128]{3,2,1,0:T(8,128)} %get-tuple-element.17.part_hbm), custom_call_target="tpu_custom_call" | custom-call | tf_op jit(solution)/shard_map/pallas_call | solution.py:227
  106.3 4.4 %all-to-all-start.1 = ((f32[128,1,320]{2,1,0:T(1,128)}), f32[128,1,320]{2,1,0:T(1,128)S(1)}, u32[]{:S(2)}, u32[]{:S(2)}) async-start(f32[128,1,320]{2,1,0:T(1,128)} %copy.54), calls=%async_computation.1 | async-start | bytes 393216 | tf_op jit(solution)/shard_map/all_to_all | solution.py:260
  110.8 10.3 %all-to-all-done.1 = f32[128,1,320]{2,1,0:T(1,128)S(1)} async-done(((f32[128,1,320]{2,1,0:T(1,128)}), f32[128,1,320]{2,1,0:T(1,128)S(1)}, u32[]{:S(2)}, u32[]{:S(2)}) %all-to-all-start.1) | async-done | bytes 163872 | tf_op jit(solution)/shard_map/all_to_all | solution.py:260
  (95 shorter events, 19.2 us)
Async XLA Ops:
  4.1 16.0 %copy-start.4 = (f32[4,8,16,720]{3,2,1,0:T(8,128)}, f32[4,8,16,720]{3,2,1,0:T(8,128)S(1)}, u32[]{:S(2)}) copy-start(f32[4,8,16,720]{3,2,1,0:T(8,128)S(1)} %bitcast_add_fusion.3) | copy-start | bytes 4423684
  4.1 3.8 %copy-start.12 = (s32[4,8,4]{1,2,0:T(4,128)S(1)}, s32[4,8,4]{1,2,0:T(4,128)}, u32[]{:S(2)}) copy-start(s32[4,8,4]{1,2,0:T(4,128)} %param.12) | copy-start | bytes 1540
  4.1 4.7 %copy-start.1 = (s32[128]{0:T(128)S(1)}, s32[128]{0:T(128)}, u32[]{:S(2)}) copy-start(s32[128]{0:T(128)} %param.14) | copy-start | bytes 1540
  4.2 15.9 %collective-permute-start = (f32[1,8,16,720]{3,2,1,0:T(8,128)S(1)}, f32[1,8,16,720]{3,2,1,0:T(8,128)S(1)}, u32[]{:S(2)}, u32[]{:S(2)}) collective-permute-start(f32[1,8,16,720]{3,2,1,0:T(8,128)S(1)} %get-tuple-element.28), channel_id=1, source_target_pairs={{0,32},{32,64},{64,96},{96,0},{1,33},{33,65},{65,97},{97,1},{2,34}... | collective-permute-start | bytes 1105928 | tf_op jit(solution)/shard_map/ppermute | solution.py:32
  6.4 13.7 %collective-permute-start.1 = (f32[1,8,16,720]{3,2,1,0:T(8,128)S(1)}, f32[1,8,16,720]{3,2,1,0:T(8,128)S(1)}, u32[]{:S(2)}, u32[]{:S(2)}) collective-permute-start(f32[1,8,16,720]{3,2,1,0:T(8,128)S(1)} %get-tuple-element.29), channel_id=1, source_target_pairs={{32,0},{64,32},{96,64},{0,96},{33,1},{65,33},{97,65},{1,97},{34,2}... | collective-permute-start | bytes 1105928 | tf_op jit(solution)/shard_map/ppermute | solution.py:34
  8.8 2.5 %copy-start = (bf16[10,32,64,128]{3,2,1,0:T(8,128)(2,1)S(1)}, bf16[10,32,64,128]{3,2,1,0:T(8,128)(2,1)}, u32[]{:S(2)}) copy-start(bf16[10,32,64,128]{3,2,1,0:T(8,128)(2,1)} %state_hbm.1) | copy-start | bytes 15728644
  20.4 5.9 %collective-permute-start.2 = (f32[6,1,16,720]{3,2,1,0:T(8,128)S(1)}, f32[6,1,16,720]{3,2,1,0:T(8,128)S(1)}, u32[]{:S(2)}, u32[]{:S(2)}) collective-permute-start(f32[6,1,16,720]{3,2,1,0:T(8,128)S(1)} %get-tuple-element.24), channel_id=1, source_target_pairs={{0,1},{1,2},{2,3},{3,4},{4,5},{5,6},{6,7},{7,8},{8,9},{9,10},{10,1... | collective-permute-start | bytes 829448 | tf_op jit(solution)/shard_map/ppermute | solution.py:32
  22.7 6.4 %collective-permute-start.3 = (f32[6,1,16,720]{3,2,1,0:T(8,128)S(1)}, f32[6,1,16,720]{3,2,1,0:T(8,128)S(1)}, u32[]{:S(2)}, u32[]{:S(2)}) collective-permute-start(f32[6,1,16,720]{3,2,1,0:T(8,128)S(1)} %get-tuple-element.25), channel_id=1, source_target_pairs={{1,0},{2,1},{3,2},{4,3},{5,4},{6,5},{7,6},{8,7},{9,8},{10,9},{11,1... | collective-permute-start | bytes 829448 | tf_op jit(solution)/shard_map/ppermute | solution.py:34
  32.0 1.6 %copy-start.10 = (f32[16,16,1,1]{1,0,3,2:T(8,128)S(1)}, f32[16,16,1,1]{1,0,3,2:T(8,128)}, u32[]{:S(2)}) copy-start(f32[16,16,1,1]{1,0,3,2:T(8,128)} %constant.157) | copy-start | bytes 3076
  33.6 1.5 %copy-start.5 = (f32[4,8,16,720]{3,2,1,0:T(8,128)S(1)}, f32[4,8,16,720]{3,2,1,0:T(8,128)}, u32[]{:S(2)}) copy-start(f32[4,8,16,720]{3,2,1,0:T(8,128)} %copy-done.4) | copy-start | bytes 4423684
  33.6 1.5 %copy-start.11 = (f32[16,16,1,1]{1,0,3,2:T(8,128)S(1)}, f32[16,16,1,1]{1,0,3,2:T(8,128)}, u32[]{:S(2)}) copy-start(f32[16,16,1,1]{1,0,3,2:T(8,128)} %constant.156) | copy-start | bytes 3076
  33.6 1.5 %copy-start.15 = (f32[16]{0:T(128)S(1)}, f32[16]{0:T(128)}, u32[]{:S(2)}) copy-start(f32[16]{0:T(128)} %constant.154) | copy-start | bytes 196
  36.9 10.0 %copy-start.2 = (f32[4,8,16,720]{3,2,1,0:T(8,128)}, f32[4,8,16,720]{3,2,1,0:T(8,128)S(1)}, u32[]{:S(2)}) copy-start(f32[4,8,16,720]{3,2,1,0:T(8,128)S(1)} %bitcast_add_fusion.1) | copy-start | bytes 4423684
  37.0 2.8 %copy-start.13 = (s32[4,8,4]{1,2,0:T(4,128)S(1)}, s32[4,8,4]{1,2,0:T(4,128)}, u32[]{:S(2)}) copy-start(s32[4,8,4]{1,2,0:T(4,128)} %param.13) | copy-start | bytes 1540
  37.0 9.8 %collective-permute-start.4 = (f32[1,8,16,720]{3,2,1,0:T(8,128)S(1)}, f32[1,8,16,720]{3,2,1,0:T(8,128)S(1)}, u32[]{:S(2)}, u32[]{:S(2)}) collective-permute-start(f32[1,8,16,720]{3,2,1,0:T(8,128)S(1)} %get-tuple-element.26), channel_id=1, source_target_pairs={{0,32},{32,64},{64,96},{96,0},{1,33},{33,65},{65,97},{97,1},{2,34}... | collective-permute-start | bytes 1105928 | tf_op jit(solution)/shard_map/ppermute | solution.py:32
  37.2 9.7 %collective-permute-start.5 = (f32[1,8,16,720]{3,2,1,0:T(8,128)S(1)}, f32[1,8,16,720]{3,2,1,0:T(8,128)S(1)}, u32[]{:S(2)}, u32[]{:S(2)}) collective-permute-start(f32[1,8,16,720]{3,2,1,0:T(8,128)S(1)} %get-tuple-element.27), channel_id=1, source_target_pairs={{32,0},{64,32},{96,64},{0,96},{33,1},{65,33},{97,65},{1,97},{34,2}... | collective-permute-start | bytes 1105928 | tf_op jit(solution)/shard_map/ppermute | solution.py:34
  46.9 4.6 %copy-start.7 = (f32[1,8,16,720]{3,2,1,0:T(8,128)}, f32[1,8,16,720]{3,2,1,0:T(8,128)S(1)}, u32[]{:S(2)}) copy-start(f32[1,8,16,720]{3,2,1,0:T(8,128)S(1)} %collective-permute-done.5) | copy-start | bytes 1105924
  46.9 6.2 %collective-permute-start.6 = (f32[6,1,16,720]{3,2,1,0:T(8,128)S(1)}, f32[6,1,16,720]{3,2,1,0:T(8,128)S(1)}, u32[]{:S(2)}, u32[]{:S(2)}) collective-permute-start(f32[6,1,16,720]{3,2,1,0:T(8,128)S(1)} %get-tuple-element.22), channel_id=1, source_target_pairs={{0,1},{1,2},{2,3},{3,4},{4,5},{5,6},{6,7},{7,8},{8,9},{9,10},{10,1... | collective-permute-start | bytes 829448 | tf_op jit(solution)/shard_map/ppermute | solution.py:32
  49.5 6.4 %collective-permute-start.7 = (f32[6,1,16,720]{3,2,1,0:T(8,128)S(1)}, f32[6,1,16,720]{3,2,1,0:T(8,128)}, u32[]{:S(2)}, u32[]{:S(2)}) collective-permute-start(f32[6,1,16,720]{3,2,1,0:T(8,128)S(1)} %get-tuple-element.23), channel_id=1, source_target_pairs={{1,0},{2,1},{3,2},{4,3},{5,4},{6,5},{7,6},{8,7},{9,8},{10,9},{11,1... | collective-permute-start | bytes 829448 | tf_op jit(solution)/shard_map/ppermute | solution.py:34
  60.5 1.9 %copy-start.3 = (f32[4,8,16,720]{3,2,1,0:T(8,128)S(1)}, f32[4,8,16,720]{3,2,1,0:T(8,128)}, u32[]{:S(2)}) copy-start(f32[4,8,16,720]{3,2,1,0:T(8,128)} %copy-done.2) | copy-start | bytes 4423684
  62.4 1.5 %copy-start.14 = (f32[4,16,1,1]{1,0,3,2:T(4,128)S(1)}, f32[4,16,1,1]{1,0,3,2:T(4,128)}, u32[]{:S(2)}) copy-start(f32[4,16,1,1]{1,0,3,2:T(4,128)} %constant.158) | copy-start | bytes 772
  63.9 1.6 %copy-start.6 = (f32[4,8,16,720]{3,2,1,0:T(8,128)}, f32[4,8,16,720]{3,2,1,0:T(8,128)S(1)}, u32[]{:S(2)}) copy-start(f32[4,8,16,720]{3,2,1,0:T(8,128)S(1)} %fusion) | copy-start | bytes 4423684
  67.7 23.4 %all-to-all-start = ((f32[128,1,321]{2,1,0:T(1,128)}), f32[128,1,321]{2,1,0:T(1,128)S(1)}, u32[]{:S(2)}, u32[]{:S(2)}) async-start(f32[128,1,321]{2,1,0:T(1,128)} %copy.49), calls=%async_computation | async-start | bytes 393216 | tf_op jit(solution)/shard_map/all_to_all | solution.py:260
  106.3 14.8 %all-to-all-start.1 = ((f32[128,1,320]{2,1,0:T(1,128)}), f32[128,1,320]{2,1,0:T(1,128)S(1)}, u32[]{:S(2)}, u32[]{:S(2)}) async-start(f32[128,1,320]{2,1,0:T(1,128)} %copy.54), calls=%async_computation.1 | async-start | bytes 393216 | tf_op jit(solution)/shard_map/all_to_all | solution.py:260
  (2 other events, 2.0 us)

commit v10 on v7

--- a/solution.py
+++ b/solution.py
@@ -1,3 +1,5 @@
+import functools
+
 import jax
 import jax.numpy as jnp
 import numpy as np
@@ -86,13 +88,26 @@
     return jnp.minimum(z + 1, nlev - 1), jnp.maximum(z - 1, 0)
 
 
-def crm_first_kernel(live_ref, state_hbm, part_hbm, mean_ref, held, wide, part, in_sem, out_sem):
+def crm_first_kernel(first, last, live_ref, state_hbm, part_hbm, mean_ref, held, wide, part, in_sem, out_sem):
     nfld, nlev, nx, _ = held.shape
-    chunks = nlev // ZCHUNK
-    loads = chunk_copies(state_hbm, held, in_sem, chunks)
-    stores = chunk_copies(part, part_hbm, out_sem, chunks)
-    for copy in loads:
-        copy.start()
+    lo_chunk = max(first - 1, 0) // ZCHUNK
+    hi_chunk = (min(last + 1, nlev) + ZCHUNK - 1) // ZCHUNK
+    loads = {
+        c: pltpu.make_async_copy(
+            state_hbm.at[:, pl.ds(c * ZCHUNK, ZCHUNK)], held.at[:, pl.ds(c * ZCHUNK, ZCHUNK)], in_sem.at[c]
+        )
+        for c in range(lo_chunk, hi_chunk)
+    }
+    own = (last - first) // ZCHUNK
+
+    def store(c):
+        return pltpu.make_async_copy(
+            part.at[:, pl.ds(c * ZCHUNK, ZCHUNK)], part_hbm.at[:, pl.ds(c * ZCHUNK, ZCHUNK)], out_sem.at[c]
+        )
+
+    stores = [store(c) for c in range(own)]
+    for c in range(lo_chunk, hi_chunk):
+        loads[c].start()
     live = live_ref[...] == 1
 
     def level(z, carry):
@@ -105,28 +120,47 @@
             wide[f, upper_z] = upper
             east = pltpu.roll(state, nx - 1, 0)
             west = pltpu.roll(state, 1, 0)
-            mean_ref[f, pl.ds(z, 1)] = jnp.mean(state, axis=0, keepdims=True)
+            mean_ref[f, pl.ds(z - first, 1)] = jnp.mean(state, axis=0, keepdims=True)
             fresh = KEEP * state + DIFF_X * (east + west) + DIFF_Z * (upper + lower) - lead * (east - west)
-            part[f, z] = jnp.where(live, fresh, state)
+            part[f, z - first] = jnp.where(live, fresh, state)
         return carry
 
-    for c in range(chunks):
+    waited = set()
+
+    def need(c):
+        if c < hi_chunk and c not in waited:
+            loads[c].wait()
+            waited.add(c)
+
+    for c in range(own):
+        base = first + c * ZCHUNK
         if c == 0:
-            loads[0].wait()
+            need(max(first - 1, 0) // ZCHUNK)
+            need(first // ZCHUNK)
             for f in range(nfld):
-                wide[f, 0] = held[f, 0].astype(jnp.float32)
-        if c + 1 < chunks:
-            loads[c + 1].wait()
-        lax.fori_loop(c * ZCHUNK, (c + 1) * ZCHUNK, level, 0)
+                for z in sorted({max(first - 1, 0), first}):
+                    wide[f, z] = held[f, z].astype(jnp.float32)
+        need((base + ZCHUNK) // ZCHUNK)
+        lax.fori_loop(base, base + ZCHUNK, level, 0)
         stores[c].start()
+    for c in range(lo_chunk, hi_chunk):
+        need(c)
     for copy in stores:
         copy.wait()
 
 
-def crm_second_kernel(force_ref, live_ref, mean_ref, part_hbm, new_hbm, tend_ref, mid, out, in_sem, out_sem):
+def crm_second_kernel(force_ref, live_ref, mean_ref, low_hbm, high_hbm, new_hbm, tend_ref, mid, out, in_sem, out_sem):
     nfld, nlev, nx, _ = mid.shape
     chunks = nlev // ZCHUNK
-    loads = chunk_copies(part_hbm, mid, in_sem, chunks)
+    half = low_hbm.shape[1] // ZCHUNK
+
+    def load(c):
+        src_ref, at = (low_hbm, c) if c < half else (high_hbm, c - half)
+        return pltpu.make_async_copy(
+            src_ref.at[:, pl.ds(at * ZCHUNK, ZCHUNK)], mid.at[:, pl.ds(c * ZCHUNK, ZCHUNK)], in_sem.at[c]
+        )
+
+    loads = [load(c) for c in range(chunks)]
     stores = chunk_copies(out, new_hbm, out_sem, chunks)
     for copy in loads:
         copy.start()
@@ -199,21 +233,22 @@
         copy.wait()
 
 
-def crm_first(state, active):
+def crm_first(state, active, first, last):
     nfld, nlev, nx, ncol = state.shape
     chunks = nlev // ZCHUNK
+    span = (nfld, last - first, nx, ncol)
     return pl.pallas_call(
-        crm_first_kernel,
+        functools.partial(crm_first_kernel, first, last),
         out_shape=(
-            jax.ShapeDtypeStruct(state.shape, jnp.float32),
-            jax.ShapeDtypeStruct((nfld, nlev, ncol), jnp.float32),
+            jax.ShapeDtypeStruct(span, jnp.float32),
+            jax.ShapeDtypeStruct((nfld, last - first, ncol), jnp.float32),
         ),
         in_specs=[pl.BlockSpec(memory_space=pltpu.VMEM), pl.BlockSpec(memory_space=pl.ANY)],
         out_specs=(pl.BlockSpec(memory_space=pl.ANY), pl.BlockSpec(memory_space=pltpu.VMEM)),
         scratch_shapes=[
             pltpu.VMEM(state.shape, jnp.bfloat16),
             pltpu.VMEM(state.shape, jnp.float32),
-            pltpu.VMEM(state.shape, jnp.float32),
+            pltpu.VMEM(span, jnp.float32),
             pltpu.SemaphoreType.DMA((chunks,)),
             pltpu.SemaphoreType.DMA((chunks,)),
         ],
@@ -221,13 +256,15 @@
     )(active.reshape(1, ncol), state)
 
 
-def crm_second(part, start_mean, forcing, active):
-    nfld, nlev, nx, ncol = part.shape
+def crm_second(low, high, start_mean, forcing, active):
+    nfld, nlev, ncol = start_mean.shape
+    nx = low.shape[2]
     chunks = nlev // ZCHUNK
+    shape = (nfld, nlev, nx, ncol)
     return pl.pallas_call(
         crm_second_kernel,
         out_shape=(
-            jax.ShapeDtypeStruct(part.shape, jnp.bfloat16),
+            jax.ShapeDtypeStruct(shape, jnp.bfloat16),
             jax.ShapeDtypeStruct((nfld, nlev, ncol), jnp.float32),
         ),
         in_specs=[
@@ -235,21 +272,17 @@
             pl.BlockSpec(memory_space=pltpu.VMEM),
             pl.BlockSpec(memory_space=pltpu.VMEM),
             pl.BlockSpec(memory_space=pl.ANY),
+            pl.BlockSpec(memory_space=pl.ANY),
         ],
         out_specs=(pl.BlockSpec(memory_space=pl.ANY), pl.BlockSpec(memory_space=pltpu.VMEM)),
         scratch_shapes=[
-            pltpu.VMEM(part.shape, jnp.float32),
-            pltpu.VMEM(part.shape, jnp.bfloat16),
+            pltpu.VMEM(shape, jnp.float32),
+            pltpu.VMEM(shape, jnp.bfloat16),
             pltpu.SemaphoreType.DMA((chunks,)),
             pltpu.SemaphoreType.DMA((chunks,)),
         ],
         compiler_params=pltpu.CompilerParams(vmem_limit_bytes=48 * 1024 * 1024),
-    )(forcing, active.reshape(1, ncol), start_mean, part)
-
-
-def crm_run(state, forcing, active):
-    part, start_mean = crm_first(state, active)
-    return crm_second(part, start_mean, forcing, active)
+    )(forcing, active.reshape(1, ncol), start_mean, low, high)
 
 
 TWO_STAGE = False
@@ -285,18 +318,20 @@
     place = (local_row + drow + 1) * (cols_dev + 2) + (local_col + dcol + 1)
     index_flat = place[..., None] * 16 + pick
     index_flat = index_flat.reshape(-1)
-    part, start_mean = crm_first(crm_state, crm_active)
+    split = crm_state.shape[1] // 2
+    low, low_mean = crm_first(crm_state, crm_active, 0, split)
+    high, high_mean = crm_first(crm_state, crm_active, split, crm_state.shape[1])
     state = dyn_state
     for step in range(DSTEPS):
         state = state + KAPPA * jnp.einsum(
             "nm,rcmw->rcnw", laplace, state, precision=lax.Precision.HIGHEST
         )
+        faced = extended_2(state, (("face", 0),), 1)
         if step == 0:
-            faced = extended_2(state, (("face", 0),), 1)
-            faced, part, start_mean = lax.optimization_barrier((faced, part, start_mean))
-            extended = extended_2(faced, (("col", 1),), 1)
+            faced, low, low_mean = lax.optimization_barrier((faced, low, low_mean))
         else:
-            extended = extended_2(state, (("face", 0), ("col", 1)), 1)
+            faced, high, high_mean = lax.optimization_barrier((faced, high, high_mean))
+        extended = extended_2(faced, (("col", 1),), 1)
         matched = jnp.take(extended.reshape(-1, width), index_flat, axis=0).reshape(
             rows_dev, cols_dev, 16, width
         )
@@ -317,7 +352,8 @@
     slots = arrived[:, NFLD * CLEV].astype(jnp.int32) % per_dev
     physics = jnp.zeros((per_dev, NFLD * CLEV), jnp.float32).at[slots].set(arrived[:, : NFLD * CLEV])
     forcing = physics.reshape(per_dev, NFLD, CLEV).transpose(1, 2, 0)
-    crm_new, tend = crm_second(part, start_mean, forcing, crm_active)
+    start_mean = jnp.concatenate([low_mean, high_mean], axis=1)
+    crm_new, tend = crm_second(low, high, start_mean, forcing, crm_active)
     tend_rows = tend.reshape(NFLD * CLEV, per_dev).T[slots]
     returned = exchange(tend_rows.reshape(ndev, count, NFLD * CLEV))
     placed = (

time: 121 us -> 123 us (1.017)
  blocking collectives: 37.8 us -> 14.6 us
  starting transfers between devices: 12 us -> 24.5 us
  waiting for transfers between devices: 13.7 us -> 19.4 us
  local copies, waits for them, and re-layouts: 17.8 us -> 23.3 us
    all_to_all x2 -> x1, blocking collectives: 37.8 us -> 14.6 us  [exchange(): lax.all_to_all(chunks, ('face', 'col'), split_axis=0, concat_axis=0, tile...]
    all_to_all x0 -> x1, starting transfers between devices: none -> 12.7 us  [exchange(): lax.all_to_all(chunks, ('face', 'col'), split_axis=0, concat_axis=0, tile...]
    all_to_all x0 -> x1, waiting for transfers between devices: none -> 10.4 us  [exchange(): lax.all_to_all(chunks, ('face', 'col'), split_axis=0, concat_axis=0, tile...]
    unnamed x33, local copies, waits for them, and re-layouts: 3.55 us -> 8.88 us
    ppermute x4, waiting for transfers between devices: 8.9 us -> 3.65 us  [extended_2(): lax.ppermute(tail, axis, [(i, (i + 1) % count) for i in range(count)])]
    pallas_call x2 -> x3, Pallas kernels: 20.6 us -> 21.6 us  [the longest x2 11 us: crm_first(): pl.pallas_call(functools.partial(crm_first_kernel, first, last), out_shap...]
    concatenate x3 -> x4, other arithmetic: 2.5 us -> 2.79 us  [extended_2(): jnp.concatenate([lax.ppermute(tail, axis, [(i, (i + 1) % count) for i in...]
  transfers between devices with their start and end apart: 8 -> 9, of which waited for: 5 -> 4; matrix products, arithmetic and copies ran while one was open for 5% -> 4% of each run, Pallas kernels for 7% -> 9%
where the time goes in v10:
time: 123 us
  starting transfers between devices  24.5 us (20%)
  local copies, waits for them, and re-layouts  23.3 us (19%)
  Pallas kernels  21.6 us (18%)
  waiting for transfers between devices  19.4 us (16%)
  blocking collectives  14.6 us (12%)
  matrix products  9.25 us (8%)
  other arithmetic  9.09 us (7%)
    all_to_all x1, blocking collectives, exchange(): lax.all_to_all(chunks, ('face', 'col'), split_axis=0, concat_axis=0, tile...  14.6 us
    all_to_all x1, starting transfers between devices, exchange(): lax.all_to_all(chunks, ('face', 'col'), split_axis=0, concat_axis=0, tile...  12.7 us
    pallas_call x2, Pallas kernels, crm_first(): pl.pallas_call(functools.partial(crm_first_kernel, first, last), out_shap...  11 us
    pallas_call x1, Pallas kernels, crm_second(): pl.pallas_call(crm_second_kernel, out_shape=(jax.ShapeDtypeStruct(shape,...  10.5 us
    all_to_all x1, waiting for transfers between devices, exchange(): lax.all_to_all(chunks, ('face', 'col'), split_axis=0, concat_axis=0, tile...  10.4 us
    unnamed x33, local copies, waits for them, and re-layouts  8.88 us
    ppermute x4, starting transfers between devices, extended_2(): lax.ppermute(tail, axis, [(i, (i + 1) % count) for i in range(count)])  6.4 us
    ppermute x4, waiting for transfers between devices, extended_2(): lax.ppermute(head, axis, [((i + 1) % count, i) for i in range(count)])  5.36 us
  transfers between devices with their start and end apart: 9, of which 4 were waited for; matrix products, arithmetic and copies ran while one was open for 4% of the time, Pallas kernels for 9%

profile of v10, /device:TPU:1, one launch (start us, length us, event | category | flops | bytes accessed | tf_op | source)
XLA Modules:
  0.0 122.8 jit_solution(13529620909764628955)
XLA Ops:
  0.6 3.4 %bitcast_add_fusion.3 = f32[4,8,16,720]{3,2,1,0:T(8,128)S(1)} fusion(f32[4,8,16,720]{3,2,1,0:T(8,128)} %param.11, f32[16,16,1,1]{1,0,3,2:T(8,128)} %constant.154), kind=kOutput, calls=%fused_computation.16 | convolution fusion | flops 71516160 | bytes 2950144 | tf_op jit(solution)/shard_map/nm,rcmw->rcnw/dot_general | solution.py:326
  4.2 2.2 %collective-permute-start = (f32[1,8,16,720]{3,2,1,0:T(8,128)S(1)}, f32[1,8,16,720]{3,2,1,0:T(8,128)S(1)}, u32[]{:S(2)}, u32[]{:S(2)}) collective-permute-start(f32[1,8,16,720]{3,2,1,0:T(8,128)S(1)} %get-tuple-element.38), channel_id=1, source_target_pairs={{0,32},{32,64},{64,96},{96,0},{1,33},{33,65},{65,97},{97,1},{2,34}... | collective-permute-start | bytes 1105928 | tf_op jit(solution)/shard_map/ppermute | solution.py:34
  8.8 5.4 %shard_map.112 = (f32[10,16,64,128]{3,2,1,0:T(8,128)S(1)}, f32[10,16,128]{2,1,0:T(8,128)S(1)}) custom-call(s32[1,128]{1,0:T(1,128)S(1)} %bitcast.62, bf16[10,32,64,128]{3,2,1,0:T(8,128)(2,1)} %state_hbm.3), custom_call_target="tpu_custom_call" | custom-call | tf_op jit(solution)/shard_map/pallas_call | solution.py:240
  14.2 2.3 %copy-done = f32[10,16,64,128]{3,2,1,0:T(8,128)} copy-done((f32[10,16,64,128]{3,2,1,0:T(8,128)}, f32[10,16,64,128]{3,2,1,0:T(8,128)S(1)}, u32[]{:S(2)}) %copy-start) | copy-done | bytes 5242904
  16.9 2.5 %collective-permute-start.2 = (f32[6,1,16,720]{3,2,1,0:T(8,128)S(1)}, f32[6,1,16,720]{3,2,1,0:T(8,128)S(1)}, u32[]{:S(2)}, u32[]{:S(2)}) collective-permute-start(f32[6,1,16,720]{3,2,1,0:T(8,128)S(1)} %get-tuple-element.34), channel_id=1, source_target_pairs={{0,1},{1,2},{2,3},{3,4},{4,5},{5,6},{6,7},{7,8},{8,9},{9,10},{10,1... | collective-permute-start | bytes 829448 | tf_op jit(solution)/shard_map/ppermute | solution.py:34
  19.4 3.6 %collective-permute-done.2 = f32[6,1,16,720]{3,2,1,0:T(8,128)S(1)} collective-permute-done((f32[6,1,16,720]{3,2,1,0:T(8,128)S(1)}, f32[6,1,16,720]{3,2,1,0:T(8,128)S(1)}, u32[]{:S(2)}, u32[]{:S(2)}) %collective-permute-start.2) | collective-permute-done | bytes 276512 | tf_op jit(solution)/shard_map/ppermute | solution.py:34
  23.0 2.8 %collective-permute-done.3 = f32[6,1,16,720]{3,2,1,0:T(8,128)S(1)} collective-permute-done((f32[6,1,16,720]{3,2,1,0:T(8,128)S(1)}, f32[6,1,16,720]{3,2,1,0:T(8,128)S(1)}, u32[]{:S(2)}, u32[]{:S(2)}) %collective-permute-start.3) | collective-permute-done | bytes 276512 | tf_op jit(solution)/shard_map/ppermute | solution.py:36
  26.1 2.6 %gather_fusion.3 = f32[512,720]{1,0:T(8,128)} fusion(f32[960,720]{1,0:T(8,128)S(1)} %bitcast.66, s32[1024]{0:T(1024)S(1)} %pad_clamp_fusion.2), kind=kCustom, calls=%fused_computation.clone | custom fusion | bytes 2951168 | tf_op jit(solution)/shard_map/jit(_take)/gather | solution.py:335
  28.8 1.6 %broadcast_select_fusion.1 = f32[512,720]{1,0:T(8,128)S(1)} fusion(f32[512,720]{1,0:T(8,128)} %gather_fusion.3, pred[512]{0:T(512)(128)(4,1)S(1)} %compare_and_fusion), kind=kLoop, calls=%fused_computation.19 | loop fusion | flops 368640 | bytes 2949632 | tf_op jit(solution)/shard_map/jit(_take)/select_n | solution.py:335
  31.9 1.9 %bitcast_add_fusion.1 = f32[4,8,16,720]{3,2,1,0:T(8,128)S(1)} fusion(f32[16,16,1,1]{1,0,3,2:T(8,128)S(1)} %copy-done.11, f32[4,8,16,720]{3,2,1,0:T(8,128)S(1)} %copy-done.7, f32[4,8,720,16]{2,3,1,0:T(8,128)S(1)} %fusion.35, f32[16]{0:T(128)S(1)} %copy-done.15), kind=kOutput, calls=%fused_computation.13 | convolution fusion | flops 72990720 | bytes 4424768 | tf_op jit(solution)/shard_map/nm,rcmw->rcnw/dot_general | solution.py:326
  36.7 5.6 %shard_map.113 = (f32[10,16,64,128]{3,2,1,0:T(8,128)S(1)}, f32[10,16,128]{2,1,0:T(8,128)S(1)}) custom-call(s32[1,128]{1,0:T(1,128)S(1)} %bitcast.63, bf16[10,32,64,128]{3,2,1,0:T(8,128)(2,1)} %state_hbm.3), custom_call_target="tpu_custom_call" | custom-call | tf_op jit(solution)/shard_map/pallas_call | solution.py:240
  42.4 2.3 %copy-done.2 = f32[10,16,64,128]{3,2,1,0:T(8,128)} copy-done((f32[10,16,64,128]{3,2,1,0:T(8,128)}, f32[10,16,64,128]{3,2,1,0:T(8,128)S(1)}, u32[]{:S(2)}) %copy-start.2) | copy-done | bytes 5242904
  44.9 2.5 %sort.17 = (s32[128]{0:T(128)}, s32[128]{0:T(128)S(1)}) sort(s32[128]{0:T(128)S(1)} %reshape.89, s32[128]{0:T(128)S(1)} %iota.35), dimensions={0}, to_apply=%region_0.2 | sort | flops 896 | bytes 2048 | tf_op jit(solution)/shard_map/jit(argsort)/sort | solution.py:346
  49.5 2.3 %collective-permute-start.7 = (f32[6,1,16,720]{3,2,1,0:T(8,128)S(1)}, f32[6,1,16,720]{3,2,1,0:T(8,128)}, u32[]{:S(2)}, u32[]{:S(2)}) collective-permute-start(f32[6,1,16,720]{3,2,1,0:T(8,128)S(1)} %get-tuple-element.33), channel_id=1, source_target_pairs={{1,0},{2,1},{3,2},{4,3},{5,4},{6,5},{7,6},{8,7},{9,8},{10,9},{11,1... | collective-permute-start | bytes 829448 | tf_op jit(solution)/shard_map/ppermute | solution.py:36
  53.1 2.6 %collective-permute-done.7 = f32[6,1,16,720]{3,2,1,0:T(8,128)} collective-permute-done((f32[6,1,16,720]{3,2,1,0:T(8,128)S(1)}, f32[6,1,16,720]{3,2,1,0:T(8,128)}, u32[]{:S(2)}, u32[]{:S(2)}) %collective-permute-start.7) | collective-permute-done | bytes 276512 | tf_op jit(solution)/shard_map/ppermute | solution.py:36
  55.7 2.1 %pad_maximum_fusion.1 = f32[6,10,16,720]{3,2,1,0:T(8,128)S(1)} fusion(f32[6,1,16,720]{3,2,1,0:T(8,128)} %collective-permute-done.7, f32[6,8,16,720]{3,2,1,0:T(8,128)} %copy-done.8, f32[6,1,16,720]{3,2,1,0:T(8,128)S(1)} %collective-permute-done.6), kind=kLoop, calls=%fused_computation.8 | loop fusion | flops 1382400 | bytes 5529600 | tf_op jit(solution)/shard_map/concatenate | solution.py:32
  57.8 2.6 %gather_fusion.4 = f32[512,720]{1,0:T(8,128)} fusion(f32[960,720]{1,0:T(8,128)S(1)} %bitcast.65, s32[1024]{0:T(1024)S(1)} %pad_clamp_fusion.2), kind=kCustom, calls=%fused_computation.1.clone | custom fusion | bytes 2951168 | tf_op jit(solution)/shard_map/jit(_take)/gather | solution.py:335
  60.4 1.7 %broadcast_select_fusion = f32[512,720]{1,0:T(8,128)S(1)} fusion(f32[512,720]{1,0:T(8,128)} %gather_fusion.4, pred[512]{0:T(512)(128)(4,1)S(1)} %compare_and_fusion), kind=kLoop, calls=%fused_computation.18 | loop fusion | flops 368640 | bytes 2949632 | tf_op jit(solution)/shard_map/jit(_take)/select_n | solution.py:335
  62.3 1.5 %fusion = f32[4,8,16,720]{3,2,1,0:T(8,128)S(1)} fusion(f32[4,8,16,720]{3,2,1,0:T(8,128)S(1)} %copy-done.5, f32[4,8,16,720]{3,2,1,0:T(8,128)S(1)} %bitcast.68, f32[16,16,1,1]{1,0,3,2:T(8,128)S(1)} %copy-done.10, f32[16]{0:T(128)S(1)} %copy-done.15), kind=kOutput, calls=%fused_computation.12 | convolution fusion | flops 71516160 | bytes 4424768 | tf_op jit(solution)/shard_map/nm,rcmw->rcnw/dot_general | solution.py:338
  67.6 12.7 %all-to-all-start = ((f32[128,1,321]{2,1,0:T(1,128)}), f32[128,1,321]{2,1,0:T(1,128)S(1)}, u32[]{:S(2)}, u32[]{:S(2)}) async-start(f32[128,1,321]{2,1,0:T(1,128)} %copy.50), calls=%async_computation | async-start | bytes 393216 | tf_op jit(solution)/shard_map/all_to_all | solution.py:293
  80.3 10.4 %all-to-all-done = f32[128,1,321]{2,1,0:T(1,128)S(1)} async-done(((f32[128,1,321]{2,1,0:T(1,128)}), f32[128,1,321]{2,1,0:T(1,128)S(1)}, u32[]{:S(2)}, u32[]{:S(2)}) %all-to-all-start) | async-done | bytes 164384 | tf_op jit(solution)/shard_map/all_to_all | solution.py:293
  92.2 2.5 %copy-done.1 = f32[10,16,64,128]{3,2,1,0:T(8,128)S(1)} copy-done((f32[10,16,64,128]{3,2,1,0:T(8,128)S(1)}, f32[10,16,64,128]{3,2,1,0:T(8,128)}, u32[]{:S(2)}) %copy-start.1) | copy-done | bytes 5242904
  94.7 10.5 %shard_map.114 = (bf16[10,32,64,128]{3,2,1,0:T(8,128)(2,1)}, f32[10,32,128]{2,1,0:T(8,128)S(1)}) custom-call(f32[10,32,128]{2,1,0:T(8,128)S(1)} %bitcast.60, s32[1,128]{1,0:T(1,128)S(1)} %bitcast.64, f32[10,32,128]{2,1,0:T(8,128)S(1)} %pad_maximum_fusion.4.mean_ref, f32[10,16,64,128]{3,2,1,0:T(8,128)S(1)} %copy-done.1, f32[10,16,64,128]{3,2,1,0:T(8,128)} %copy-done.2), custom_call_target="tpu_custom_call" | custom-call | tf_op jit(solution)/shard_map/pallas_call | solution.py:264
  106.4 14.6 %all_to_all.10 = f32[128,1,320]{2,1,0:T(1,128)S(1)} all-to-all(f32[128,1,320]{2,1,0:T(1,128)S(1)} %copy.55), channel_id=1, replica_groups=mesh['face'=4,'col'=32] {'face','col'}, dimensions={0} | all-to-all | bytes 327680 | tf_op jit(solution)/shard_map/all_to_all | solution.py:293
  (90 shorter events, 19.3 us)
Async XLA Ops:
  4.1 12.5 %copy-start.6 = (f32[4,8,16,720]{3,2,1,0:T(8,128)}, f32[4,8,16,720]{3,2,1,0:T(8,128)S(1)}, u32[]{:S(2)}) copy-start(f32[4,8,16,720]{3,2,1,0:T(8,128)S(1)} %bitcast_add_fusion.3) | copy-start | bytes 4423684
  4.1 3.8 %copy-start.12 = (s32[4,8,4]{1,2,0:T(4,128)S(1)}, s32[4,8,4]{1,2,0:T(4,128)}, u32[]{:S(2)}) copy-start(s32[4,8,4]{1,2,0:T(4,128)} %param.12) | copy-start | bytes 1540
  4.1 4.7 %copy-start.3 = (s32[128]{0:T(128)S(1)}, s32[128]{0:T(128)}, u32[]{:S(2)}) copy-start(s32[128]{0:T(128)} %param.14) | copy-start | bytes 1540
  4.2 12.4 %collective-permute-start = (f32[1,8,16,720]{3,2,1,0:T(8,128)S(1)}, f32[1,8,16,720]{3,2,1,0:T(8,128)S(1)}, u32[]{:S(2)}, u32[]{:S(2)}) collective-permute-start(f32[1,8,16,720]{3,2,1,0:T(8,128)S(1)} %get-tuple-element.38), channel_id=1, source_target_pairs={{0,32},{32,64},{64,96},{96,0},{1,33},{33,65},{65,97},{97,1},{2,34}... | collective-permute-start | bytes 1105928 | tf_op jit(solution)/shard_map/ppermute | solution.py:34
  6.4 10.2 %collective-permute-start.1 = (f32[1,8,16,720]{3,2,1,0:T(8,128)S(1)}, f32[1,8,16,720]{3,2,1,0:T(8,128)S(1)}, u32[]{:S(2)}, u32[]{:S(2)}) collective-permute-start(f32[1,8,16,720]{3,2,1,0:T(8,128)S(1)} %get-tuple-element.39), channel_id=1, source_target_pairs={{32,0},{64,32},{96,64},{0,96},{33,1},{65,33},{97,65},{1,97},{34,2}... | collective-permute-start | bytes 1105928 | tf_op jit(solution)/shard_map/ppermute | solution.py:36
  14.2 2.4 %copy-start = (f32[10,16,64,128]{3,2,1,0:T(8,128)}, f32[10,16,64,128]{3,2,1,0:T(8,128)S(1)}, u32[]{:S(2)}) copy-start(f32[10,16,64,128]{3,2,1,0:T(8,128)S(1)} %get-tuple-element.26.low_hbm) | copy-start | bytes 15728644
  16.9 6.1 %collective-permute-start.2 = (f32[6,1,16,720]{3,2,1,0:T(8,128)S(1)}, f32[6,1,16,720]{3,2,1,0:T(8,128)S(1)}, u32[]{:S(2)}, u32[]{:S(2)}) collective-permute-start(f32[6,1,16,720]{3,2,1,0:T(8,128)S(1)} %get-tuple-element.34), channel_id=1, source_target_pairs={{0,1},{1,2},{2,3},{3,4},{4,5},{5,6},{6,7},{7,8},{8,9},{9,10},{10,1... | collective-permute-start | bytes 829448 | tf_op jit(solution)/shard_map/ppermute | solution.py:34
  19.4 6.4 %collective-permute-start.3 = (f32[6,1,16,720]{3,2,1,0:T(8,128)S(1)}, f32[6,1,16,720]{3,2,1,0:T(8,128)S(1)}, u32[]{:S(2)}, u32[]{:S(2)}) collective-permute-start(f32[6,1,16,720]{3,2,1,0:T(8,128)S(1)} %get-tuple-element.35), channel_id=1, source_target_pairs={{1,0},{2,1},{3,2},{4,3},{5,4},{6,5},{7,6},{8,7},{9,8},{10,9},{11,1... | collective-permute-start | bytes 829448 | tf_op jit(solution)/shard_map/ppermute | solution.py:36
  28.7 1.6 %copy-start.10 = (f32[16,16,1,1]{1,0,3,2:T(8,128)S(1)}, f32[16,16,1,1]{1,0,3,2:T(8,128)}, u32[]{:S(2)}) copy-start(f32[16,16,1,1]{1,0,3,2:T(8,128)} %constant.155) | copy-start | bytes 3076
  30.4 1.5 %copy-start.7 = (f32[4,8,16,720]{3,2,1,0:T(8,128)S(1)}, f32[4,8,16,720]{3,2,1,0:T(8,128)}, u32[]{:S(2)}) copy-start(f32[4,8,16,720]{3,2,1,0:T(8,128)} %copy-done.6) | copy-start | bytes 4423684
  30.4 1.5 %copy-start.11 = (f32[16,16,1,1]{1,0,3,2:T(8,128)S(1)}, f32[16,16,1,1]{1,0,3,2:T(8,128)}, u32[]{:S(2)}) copy-start(f32[16,16,1,1]{1,0,3,2:T(8,128)} %constant.154) | copy-start | bytes 3076
  30.4 1.5 %copy-start.15 = (f32[16]{0:T(128)S(1)}, f32[16]{0:T(128)}, u32[]{:S(2)}) copy-start(f32[16]{0:T(128)} %constant.152) | copy-start | bytes 196
  33.8 13.7 %copy-start.4 = (f32[4,8,16,720]{3,2,1,0:T(8,128)}, f32[4,8,16,720]{3,2,1,0:T(8,128)S(1)}, u32[]{:S(2)}) copy-start(f32[4,8,16,720]{3,2,1,0:T(8,128)S(1)} %bitcast_add_fusion.1) | copy-start | bytes 4423684
  33.9 13.6 %collective-permute-start.4 = (f32[1,8,16,720]{3,2,1,0:T(8,128)S(1)}, f32[1,8,16,720]{3,2,1,0:T(8,128)S(1)}, u32[]{:S(2)}, u32[]{:S(2)}) collective-permute-start(f32[1,8,16,720]{3,2,1,0:T(8,128)S(1)} %get-tuple-element.36), channel_id=1, source_target_pairs={{0,32},{32,64},{64,96},{96,0},{1,33},{33,65},{65,97},{97,1},{2,34}... | collective-permute-start | bytes 1105928 | tf_op jit(solution)/shard_map/ppermute | solution.py:34
  35.2 9.5 %copy-start.13 = (s32[4,8,4]{1,2,0:T(4,128)S(1)}, s32[4,8,4]{1,2,0:T(4,128)}, u32[]{:S(2)}) copy-start(s32[4,8,4]{1,2,0:T(4,128)} %param.13) | copy-start | bytes 1540
  35.2 12.2 %collective-permute-start.5 = (f32[1,8,16,720]{3,2,1,0:T(8,128)S(1)}, f32[1,8,16,720]{3,2,1,0:T(8,128)S(1)}, u32[]{:S(2)}, u32[]{:S(2)}) collective-permute-start(f32[1,8,16,720]{3,2,1,0:T(8,128)S(1)} %get-tuple-element.37), channel_id=1, source_target_pairs={{32,0},{64,32},{96,64},{0,96},{33,1},{65,33},{97,65},{1,97},{34,2}... | collective-permute-start | bytes 1105928 | tf_op jit(solution)/shard_map/ppermute | solution.py:36
  42.4 2.3 %copy-start.2 = (f32[10,16,64,128]{3,2,1,0:T(8,128)}, f32[10,16,64,128]{3,2,1,0:T(8,128)S(1)}, u32[]{:S(2)}) copy-start(f32[10,16,64,128]{3,2,1,0:T(8,128)S(1)} %get-tuple-element.27.high_hbm) | copy-start | bytes 15728644
  49.1 4.0 %collective-permute-start.6 = (f32[6,1,16,720]{3,2,1,0:T(8,128)S(1)}, f32[6,1,16,720]{3,2,1,0:T(8,128)S(1)}, u32[]{:S(2)}, u32[]{:S(2)}) collective-permute-start(f32[6,1,16,720]{3,2,1,0:T(8,128)S(1)} %get-tuple-element.32), channel_id=1, source_target_pairs={{0,1},{1,2},{2,3},{3,4},{4,5},{5,6},{6,7},{7,8},{8,9},{9,10},{10,1... | collective-permute-start | bytes 829448 | tf_op jit(solution)/shard_map/ppermute | solution.py:34
  49.5 6.3 %collective-permute-start.7 = (f32[6,1,16,720]{3,2,1,0:T(8,128)S(1)}, f32[6,1,16,720]{3,2,1,0:T(8,128)}, u32[]{:S(2)}, u32[]{:S(2)}) collective-permute-start(f32[6,1,16,720]{3,2,1,0:T(8,128)S(1)} %get-tuple-element.33), channel_id=1, source_target_pairs={{1,0},{2,1},{3,2},{4,3},{5,4},{6,5},{7,6},{8,7},{9,8},{10,9},{11,1... | collective-permute-start | bytes 829448 | tf_op jit(solution)/shard_map/ppermute | solution.py:36
  60.4 1.9 %copy-start.5 = (f32[4,8,16,720]{3,2,1,0:T(8,128)S(1)}, f32[4,8,16,720]{3,2,1,0:T(8,128)}, u32[]{:S(2)}) copy-start(f32[4,8,16,720]{3,2,1,0:T(8,128)} %copy-done.4) | copy-start | bytes 4423684
  62.3 1.5 %copy-start.14 = (f32[4,16,1,1]{1,0,3,2:T(4,128)S(1)}, f32[4,16,1,1]{1,0,3,2:T(4,128)}, u32[]{:S(2)}) copy-start(f32[4,16,1,1]{1,0,3,2:T(4,128)} %constant.156) | copy-start | bytes 772
  63.8 1.6 %copy-start.9 = (f32[4,8,16,720]{3,2,1,0:T(8,128)}, f32[4,8,16,720]{3,2,1,0:T(8,128)S(1)}, u32[]{:S(2)}) copy-start(f32[4,8,16,720]{3,2,1,0:T(8,128)S(1)} %fusion) | copy-start | bytes 4423684
  67.6 23.1 %all-to-all-start = ((f32[128,1,321]{2,1,0:T(1,128)}), f32[128,1,321]{2,1,0:T(1,128)S(1)}, u32[]{:S(2)}, u32[]{:S(2)}) async-start(f32[128,1,321]{2,1,0:T(1,128)} %copy.50), calls=%async_computation | async-start | bytes 393216 | tf_op jit(solution)/shard_map/all_to_all | solution.py:293
  92.2 2.5 %copy-start.1 = (f32[10,16,64,128]{3,2,1,0:T(8,128)S(1)}, f32[10,16,64,128]{3,2,1,0:T(8,128)}, u32[]{:S(2)}) copy-start(f32[10,16,64,128]{3,2,1,0:T(8,128)} %copy-done) | copy-start | bytes 15728644
  (1 other events, 1.4 us)

commit v11 on v7

--- a/solution.py
+++ b/solution.py
@@ -193,7 +193,7 @@
     for c in range(chunks):
         if c + 1 < chunks:
             loads[c + 1].wait()
-        lax.fori_loop(c * ZCHUNK, (c + 1) * ZCHUNK, ahead, 0)
+        lax.fori_loop(c * ZCHUNK, (c + 1) * ZCHUNK, ahead, 0, unroll=2)
         stores[c].start()
     for copy in stores:
         copy.wait()

time: 121 us -> 121 us (level)
  no operation moved by 1% of the time
where the time goes in v11:
time: 121 us
  blocking collectives  37.8 us (31%)
  Pallas kernels  20.5 us (17%)
  local copies, waits for them, and re-layouts  18.1 us (15%)
  waiting for transfers between devices  13.7 us (11%)
  starting transfers between devices  12 us (10%)
  matrix products  9.16 us (8%)
  other arithmetic  8.82 us (7%)
    all_to_all x2, blocking collectives, exchange(): lax.all_to_all(chunks, ('face', 'col'), split_axis=0, concat_axis=0, tile...  37.8 us
    pallas_call x1, Pallas kernels, crm_second(): pl.pallas_call(crm_second_kernel, out_shape=(jax.ShapeDtypeStruct(part.sh...  11.7 us
    ppermute x4, waiting for transfers between devices, extended_2(): lax.ppermute(tail, axis, [(i, (i + 1) % count) for i in range(count)])  8.9 us
    pallas_call x1, Pallas kernels, crm_first(): pl.pallas_call(crm_first_kernel, out_shape=(jax.ShapeDtypeStruct(state.sh...  8.76 us
    ppermute x4, starting transfers between devices, extended_2(): lax.ppermute(tail, axis, [(i, (i + 1) % count) for i in range(count)])  7.18 us
    dot_general x2, matrix products, per_device(): jnp.einsum('nm,rcmw->rcnw', laplace, state, precision=lax.Precision.HIGHEST)  5.23 us
    gather x2, local copies, waits for them, and re-layouts, per_device(): jnp.take(extended.reshape(-1, width), index_flat, axis=0)  5.19 us
    ppermute x4, starting transfers between devices, extended_2(): lax.ppermute(head, axis, [((i + 1) % count, i) for i in range(count)])  4.85 us
  transfers between devices with their start and end apart: 8, of which 5 were waited for; matrix products, arithmetic and copies ran while one was open for 5% of the time, Pallas kernels for 7%

profile of v11, /device:TPU:1, one launch (start us, length us, event | category | flops | bytes accessed | tf_op | source)
XLA Modules:
  0.0 121.2 jit_solution(17277474031221414779)
XLA Ops:
  0.6 3.4 %bitcast_add_fusion.3 = f32[4,8,16,720]{3,2,1,0:T(8,128)S(1)} fusion(f32[4,8,16,720]{3,2,1,0:T(8,128)} %param.11, f32[16,16,1,1]{1,0,3,2:T(8,128)} %constant.154), kind=kOutput, calls=%fused_computation.15 | convolution fusion | flops 71516160 | bytes 2950144 | tf_op jit(solution)/shard_map/nm,rcmw->rcnw/dot_general | solution.py:291
  4.2 2.2 %collective-permute-start = (f32[1,8,16,720]{3,2,1,0:T(8,128)S(1)}, f32[1,8,16,720]{3,2,1,0:T(8,128)S(1)}, u32[]{:S(2)}, u32[]{:S(2)}) collective-permute-start(f32[1,8,16,720]{3,2,1,0:T(8,128)S(1)} %get-tuple-element.28), channel_id=1, source_target_pairs={{0,32},{32,64},{64,96},{96,0},{1,33},{33,65},{65,97},{97,1},{2,34}... | collective-permute-start | bytes 1105928 | tf_op jit(solution)/shard_map/ppermute | solution.py:32
  6.4 1.5 %collective-permute-start.1 = (f32[1,8,16,720]{3,2,1,0:T(8,128)S(1)}, f32[1,8,16,720]{3,2,1,0:T(8,128)S(1)}, u32[]{:S(2)}, u32[]{:S(2)}) collective-permute-start(f32[1,8,16,720]{3,2,1,0:T(8,128)S(1)} %get-tuple-element.29), channel_id=1, source_target_pairs={{32,0},{64,32},{96,64},{0,96},{33,1},{65,33},{97,65},{1,97},{34,2}... | collective-permute-start | bytes 1105928 | tf_op jit(solution)/shard_map/ppermute | solution.py:34
  8.8 2.5 %copy-done = bf16[10,32,64,128]{3,2,1,0:T(8,128)(2,1)S(1)} copy-done((bf16[10,32,64,128]{3,2,1,0:T(8,128)(2,1)S(1)}, bf16[10,32,64,128]{3,2,1,0:T(8,128)(2,1)}, u32[]{:S(2)}) %copy-start) | copy-done | bytes 5242904
  11.3 8.8 %shard_map.112 = (f32[10,32,64,128]{3,2,1,0:T(8,128)}, f32[10,32,128]{2,1,0:T(8,128)S(1)}) custom-call(s32[1,128]{1,0:T(1,128)S(1)} %bitcast.62, bf16[10,32,64,128]{3,2,1,0:T(8,128)(2,1)S(1)} %copy-done), custom_call_target="tpu_custom_call" | custom-call | tf_op jit(solution)/shard_map/pallas_call | solution.py:205
  20.4 2.3 %collective-permute-start.2 = (f32[6,1,16,720]{3,2,1,0:T(8,128)S(1)}, f32[6,1,16,720]{3,2,1,0:T(8,128)S(1)}, u32[]{:S(2)}, u32[]{:S(2)}) collective-permute-start(f32[6,1,16,720]{3,2,1,0:T(8,128)S(1)} %get-tuple-element.24), channel_id=1, source_target_pairs={{0,1},{1,2},{2,3},{3,4},{4,5},{5,6},{6,7},{7,8},{8,9},{9,10},{10,1... | collective-permute-start | bytes 829448 | tf_op jit(solution)/shard_map/ppermute | solution.py:32
  22.7 3.6 %collective-permute-done.2 = f32[6,1,16,720]{3,2,1,0:T(8,128)S(1)} collective-permute-done((f32[6,1,16,720]{3,2,1,0:T(8,128)S(1)}, f32[6,1,16,720]{3,2,1,0:T(8,128)S(1)}, u32[]{:S(2)}, u32[]{:S(2)}) %collective-permute-start.2) | collective-permute-done | bytes 276512 | tf_op jit(solution)/shard_map/ppermute | solution.py:32
  26.3 2.8 %collective-permute-done.3 = f32[6,1,16,720]{3,2,1,0:T(8,128)S(1)} collective-permute-done((f32[6,1,16,720]{3,2,1,0:T(8,128)S(1)}, f32[6,1,16,720]{3,2,1,0:T(8,128)S(1)}, u32[]{:S(2)}, u32[]{:S(2)}) %collective-permute-start.3) | collective-permute-done | bytes 276512 | tf_op jit(solution)/shard_map/ppermute | solution.py:34
  29.4 2.6 %gather_fusion.3 = f32[512,720]{1,0:T(8,128)} fusion(f32[960,720]{1,0:T(8,128)S(1)} %bitcast.65, s32[1024]{0:T(1024)S(1)} %pad_clamp_fusion.2), kind=kCustom, calls=%fused_computation.clone | custom fusion | bytes 2951168 | tf_op jit(solution)/shard_map/jit(_take)/gather | solution.py:300
  32.0 1.6 %broadcast_select_fusion.1 = f32[512,720]{1,0:T(8,128)S(1)} fusion(f32[512,720]{1,0:T(8,128)} %gather_fusion.3, pred[512]{0:T(512)(128)(4,1)S(1)} %compare_and_fusion), kind=kLoop, calls=%fused_computation.18 | loop fusion | flops 368640 | bytes 2949632 | tf_op jit(solution)/shard_map/jit(_take)/select_n | solution.py:300
  33.6 1.5 %fusion.34 = f32[4,8,720,16]{2,3,1,0:T(8,128)S(1)} fusion(f32[4,8,16,720]{3,2,1,0:T(8,128)S(1)} %bitcast.68, f32[16,16,1,1]{1,0,3,2:T(8,128)S(1)} %copy-done.10), kind=kOutput, calls=%fused_computation.98 | convolution fusion | flops 70778880 | bytes 2950144 | tf_op jit(solution)/shard_map/nm,rcmw->rcnw/dot_general | solution.py:303
  35.1 1.8 %bitcast_add_fusion.1 = f32[4,8,16,720]{3,2,1,0:T(8,128)S(1)} fusion(f32[16,16,1,1]{1,0,3,2:T(8,128)S(1)} %copy-done.11, f32[4,8,16,720]{3,2,1,0:T(8,128)S(1)} %copy-done.5, f32[4,8,720,16]{2,3,1,0:T(8,128)S(1)} %fusion.34, f32[16]{0:T(128)S(1)} %copy-done.15), kind=kOutput, calls=%fused_computation.12 | convolution fusion | flops 72990720 | bytes 4424768 | tf_op jit(solution)/shard_map/nm,rcmw->rcnw/dot_general | solution.py:291
  37.2 2.6 %collective-permute-start.5 = (f32[1,8,16,720]{3,2,1,0:T(8,128)S(1)}, f32[1,8,16,720]{3,2,1,0:T(8,128)S(1)}, u32[]{:S(2)}, u32[]{:S(2)}) collective-permute-start(f32[1,8,16,720]{3,2,1,0:T(8,128)S(1)} %get-tuple-element.27), channel_id=1, source_target_pairs={{32,0},{64,32},{96,64},{0,96},{33,1},{65,33},{97,65},{1,97},{34,2}... | collective-permute-start | bytes 1105928 | tf_op jit(solution)/shard_map/ppermute | solution.py:34
  40.0 2.5 %sort.17 = (s32[128]{0:T(128)}, s32[128]{0:T(128)S(1)}) sort(s32[128]{0:T(128)S(1)} %reshape.88, s32[128]{0:T(128)S(1)} %iota.35), dimensions={0}, to_apply=%region_0.2 | sort | flops 896 | bytes 2048 | tf_op jit(solution)/shard_map/jit(argsort)/sort | solution.py:311
  42.5 4.3 %collective-permute-done.4 = f32[1,8,16,720]{3,2,1,0:T(8,128)S(1)} collective-permute-done((f32[1,8,16,720]{3,2,1,0:T(8,128)S(1)}, f32[1,8,16,720]{3,2,1,0:T(8,128)S(1)}, u32[]{:S(2)}, u32[]{:S(2)}) %collective-permute-start.4) | collective-permute-done | bytes 368672 | tf_op jit(solution)/shard_map/ppermute | solution.py:32
  46.9 2.6 %collective-permute-start.6 = (f32[6,1,16,720]{3,2,1,0:T(8,128)S(1)}, f32[6,1,16,720]{3,2,1,0:T(8,128)S(1)}, u32[]{:S(2)}, u32[]{:S(2)}) collective-permute-start(f32[6,1,16,720]{3,2,1,0:T(8,128)S(1)} %get-tuple-element.22), channel_id=1, source_target_pairs={{0,1},{1,2},{2,3},{3,4},{4,5},{5,6},{6,7},{7,8},{8,9},{9,10},{10,1... | collective-permute-start | bytes 829448 | tf_op jit(solution)/shard_map/ppermute | solution.py:32
  53.9 2.1 %collective-permute-done.7 = f32[6,1,16,720]{3,2,1,0:T(8,128)} collective-permute-done((f32[6,1,16,720]{3,2,1,0:T(8,128)S(1)}, f32[6,1,16,720]{3,2,1,0:T(8,128)}, u32[]{:S(2)}, u32[]{:S(2)}) %collective-permute-start.7) | collective-permute-done | bytes 276512 | tf_op jit(solution)/shard_map/ppermute | solution.py:34
  55.9 2.0 %pad_maximum_fusion.1 = f32[6,10,16,720]{3,2,1,0:T(8,128)S(1)} fusion(f32[6,1,16,720]{3,2,1,0:T(8,128)} %collective-permute-done.7, f32[1,8,16,720]{3,2,1,0:T(8,128)} %copy-done.7, f32[4,8,16,720]{3,2,1,0:T(8,128)} %copy-done.2, f32[1,8,16,720]{3,2,1,0:T(8,128)S(1)} %collective-permute-done.4, f32[6,1,16,720]{3,2,1,0:T(8,128)} %copy-done.8), kind=kLoop, calls=%fused_computation.8 | loop fusion | flops 2764800 | bytes 5529600 | tf_op jit(solution)/shard_map/concatenate | solution.py:30
  57.9 2.6 %gather_fusion.4 = f32[512,720]{1,0:T(8,128)} fusion(f32[960,720]{1,0:T(8,128)S(1)} %bitcast.64, s32[1024]{0:T(1024)S(1)} %pad_clamp_fusion.2), kind=kCustom, calls=%fused_computation.1.clone | custom fusion | bytes 2951168 | tf_op jit(solution)/shard_map/jit(_take)/gather | solution.py:300
  60.5 1.7 %broadcast_select_fusion = f32[512,720]{1,0:T(8,128)S(1)} fusion(f32[512,720]{1,0:T(8,128)} %gather_fusion.4, pred[512]{0:T(512)(128)(4,1)S(1)} %compare_and_fusion), kind=kLoop, calls=%fused_computation.17 | loop fusion | flops 368640 | bytes 2949632 | tf_op jit(solution)/shard_map/jit(_take)/select_n | solution.py:300
  62.4 1.5 %fusion = f32[4,8,16,720]{3,2,1,0:T(8,128)S(1)} fusion(f32[4,8,16,720]{3,2,1,0:T(8,128)S(1)} %copy-done.3, f32[4,8,16,720]{3,2,1,0:T(8,128)S(1)} %bitcast.67, f32[16,16,1,1]{1,0,3,2:T(8,128)S(1)} %copy-done.10, f32[16]{0:T(128)S(1)} %copy-done.15), kind=kOutput, calls=%fused_computation.11 | convolution fusion | flops 71516160 | bytes 4424768 | tf_op jit(solution)/shard_map/nm,rcmw->rcnw/dot_general | solution.py:303
  67.1 23.2 %all_to_all.10 = f32[128,1,321]{2,1,0:T(1,128)S(1)} all-to-all(f32[128,1,321]{2,1,0:T(1,128)S(1)} %copy.50), channel_id=1, replica_groups=mesh['face'=4,'col'=32] {'face','col'}, dimensions={0} | all-to-all | bytes 328704 | tf_op jit(solution)/shard_map/all_to_all | solution.py:260
  92.0 11.7 %shard_map.113 = (bf16[10,32,64,128]{3,2,1,0:T(8,128)(2,1)}, f32[10,32,128]{2,1,0:T(8,128)S(1)}) custom-call(f32[10,32,128]{2,1,0:T(8,128)S(1)} %bitcast.60, s32[1,128]{1,0:T(1,128)S(1)} %bitcast.63, f32[10,32,128]{2,1,0:T(8,128)S(1)} %get-tuple-element.16.mean_ref, f32[10,32,64,128]{3,2,1,0:T(8,128)} %get-tuple-element.17.part_hbm), custom_call_target="tpu_custom_call" | custom-call | tf_op jit(solution)/shard_map/pallas_call | solution.py:227
  104.8 14.6 %all_to_all.11 = f32[128,1,320]{2,1,0:T(1,128)S(1)} all-to-all(f32[128,1,320]{2,1,0:T(1,128)S(1)} %copy.55), channel_id=1, replica_groups=mesh['face'=4,'col'=32] {'face','col'}, dimensions={0} | all-to-all | bytes 327680 | tf_op jit(solution)/shard_map/all_to_all | solution.py:260
  (86 shorter events, 14.2 us)
Async XLA Ops:
  4.1 16.0 %copy-start.4 = (f32[4,8,16,720]{3,2,1,0:T(8,128)}, f32[4,8,16,720]{3,2,1,0:T(8,128)S(1)}, u32[]{:S(2)}) copy-start(f32[4,8,16,720]{3,2,1,0:T(8,128)S(1)} %bitcast_add_fusion.3) | copy-start | bytes 4423684
  4.1 3.8 %copy-start.12 = (s32[4,8,4]{1,2,0:T(4,128)S(1)}, s32[4,8,4]{1,2,0:T(4,128)}, u32[]{:S(2)}) copy-start(s32[4,8,4]{1,2,0:T(4,128)} %param.12) | copy-start | bytes 1540
  4.1 4.7 %copy-start.1 = (s32[128]{0:T(128)S(1)}, s32[128]{0:T(128)}, u32[]{:S(2)}) copy-start(s32[128]{0:T(128)} %param.14) | copy-start | bytes 1540
  4.2 15.9 %collective-permute-start = (f32[1,8,16,720]{3,2,1,0:T(8,128)S(1)}, f32[1,8,16,720]{3,2,1,0:T(8,128)S(1)}, u32[]{:S(2)}, u32[]{:S(2)}) collective-permute-start(f32[1,8,16,720]{3,2,1,0:T(8,128)S(1)} %get-tuple-element.28), channel_id=1, source_target_pairs={{0,32},{32,64},{64,96},{96,0},{1,33},{33,65},{65,97},{97,1},{2,34}... | collective-permute-start | bytes 1105928 | tf_op jit(solution)/shard_map/ppermute | solution.py:32
  6.4 13.7 %collective-permute-start.1 = (f32[1,8,16,720]{3,2,1,0:T(8,128)S(1)}, f32[1,8,16,720]{3,2,1,0:T(8,128)S(1)}, u32[]{:S(2)}, u32[]{:S(2)}) collective-permute-start(f32[1,8,16,720]{3,2,1,0:T(8,128)S(1)} %get-tuple-element.29), channel_id=1, source_target_pairs={{32,0},{64,32},{96,64},{0,96},{33,1},{65,33},{97,65},{1,97},{34,2}... | collective-permute-start | bytes 1105928 | tf_op jit(solution)/shard_map/ppermute | solution.py:34
  8.8 2.5 %copy-start = (bf16[10,32,64,128]{3,2,1,0:T(8,128)(2,1)S(1)}, bf16[10,32,64,128]{3,2,1,0:T(8,128)(2,1)}, u32[]{:S(2)}) copy-start(bf16[10,32,64,128]{3,2,1,0:T(8,128)(2,1)} %state_hbm.1) | copy-start | bytes 15728644
  20.4 5.9 %collective-permute-start.2 = (f32[6,1,16,720]{3,2,1,0:T(8,128)S(1)}, f32[6,1,16,720]{3,2,1,0:T(8,128)S(1)}, u32[]{:S(2)}, u32[]{:S(2)}) collective-permute-start(f32[6,1,16,720]{3,2,1,0:T(8,128)S(1)} %get-tuple-element.24), channel_id=1, source_target_pairs={{0,1},{1,2},{2,3},{3,4},{4,5},{5,6},{6,7},{7,8},{8,9},{9,10},{10,1... | collective-permute-start | bytes 829448 | tf_op jit(solution)/shard_map/ppermute | solution.py:32
  22.6 6.4 %collective-permute-start.3 = (f32[6,1,16,720]{3,2,1,0:T(8,128)S(1)}, f32[6,1,16,720]{3,2,1,0:T(8,128)S(1)}, u32[]{:S(2)}, u32[]{:S(2)}) collective-permute-start(f32[6,1,16,720]{3,2,1,0:T(8,128)S(1)} %get-tuple-element.25), channel_id=1, source_target_pairs={{1,0},{2,1},{3,2},{4,3},{5,4},{6,5},{7,6},{8,7},{9,8},{10,9},{11,1... | collective-permute-start | bytes 829448 | tf_op jit(solution)/shard_map/ppermute | solution.py:34
  32.0 1.6 %copy-start.10 = (f32[16,16,1,1]{1,0,3,2:T(8,128)S(1)}, f32[16,16,1,1]{1,0,3,2:T(8,128)}, u32[]{:S(2)}) copy-start(f32[16,16,1,1]{1,0,3,2:T(8,128)} %constant.155) | copy-start | bytes 3076
  33.6 1.5 %copy-start.5 = (f32[4,8,16,720]{3,2,1,0:T(8,128)S(1)}, f32[4,8,16,720]{3,2,1,0:T(8,128)}, u32[]{:S(2)}) copy-start(f32[4,8,16,720]{3,2,1,0:T(8,128)} %copy-done.4) | copy-start | bytes 4423684
  33.6 1.5 %copy-start.11 = (f32[16,16,1,1]{1,0,3,2:T(8,128)S(1)}, f32[16,16,1,1]{1,0,3,2:T(8,128)}, u32[]{:S(2)}) copy-start(f32[16,16,1,1]{1,0,3,2:T(8,128)} %constant.154) | copy-start | bytes 3076
  33.6 1.5 %copy-start.15 = (f32[16]{0:T(128)S(1)}, f32[16]{0:T(128)}, u32[]{:S(2)}) copy-start(f32[16]{0:T(128)} %constant.152) | copy-start | bytes 196
  36.9 10.0 %copy-start.2 = (f32[4,8,16,720]{3,2,1,0:T(8,128)}, f32[4,8,16,720]{3,2,1,0:T(8,128)S(1)}, u32[]{:S(2)}) copy-start(f32[4,8,16,720]{3,2,1,0:T(8,128)S(1)} %bitcast_add_fusion.1) | copy-start | bytes 4423684
  36.9 2.8 %copy-start.13 = (s32[4,8,4]{1,2,0:T(4,128)S(1)}, s32[4,8,4]{1,2,0:T(4,128)}, u32[]{:S(2)}) copy-start(s32[4,8,4]{1,2,0:T(4,128)} %param.13) | copy-start | bytes 1540
  37.0 9.8 %collective-permute-start.4 = (f32[1,8,16,720]{3,2,1,0:T(8,128)S(1)}, f32[1,8,16,720]{3,2,1,0:T(8,128)S(1)}, u32[]{:S(2)}, u32[]{:S(2)}) collective-permute-start(f32[1,8,16,720]{3,2,1,0:T(8,128)S(1)} %get-tuple-element.26), channel_id=1, source_target_pairs={{0,32},{32,64},{64,96},{96,0},{1,33},{33,65},{65,97},{97,1},{2,34}... | collective-permute-start | bytes 1105928 | tf_op jit(solution)/shard_map/ppermute | solution.py:32
  37.2 9.7 %collective-permute-start.5 = (f32[1,8,16,720]{3,2,1,0:T(8,128)S(1)}, f32[1,8,16,720]{3,2,1,0:T(8,128)S(1)}, u32[]{:S(2)}, u32[]{:S(2)}) collective-permute-start(f32[1,8,16,720]{3,2,1,0:T(8,128)S(1)} %get-tuple-element.27), channel_id=1, source_target_pairs={{32,0},{64,32},{96,64},{0,96},{33,1},{65,33},{97,65},{1,97},{34,2}... | collective-permute-start | bytes 1105928 | tf_op jit(solution)/shard_map/ppermute | solution.py:34
  46.9 4.6 %copy-start.7 = (f32[1,8,16,720]{3,2,1,0:T(8,128)}, f32[1,8,16,720]{3,2,1,0:T(8,128)S(1)}, u32[]{:S(2)}) copy-start(f32[1,8,16,720]{3,2,1,0:T(8,128)S(1)} %collective-permute-done.5) | copy-start | bytes 1105924
  46.9 6.2 %collective-permute-start.6 = (f32[6,1,16,720]{3,2,1,0:T(8,128)S(1)}, f32[6,1,16,720]{3,2,1,0:T(8,128)S(1)}, u32[]{:S(2)}, u32[]{:S(2)}) collective-permute-start(f32[6,1,16,720]{3,2,1,0:T(8,128)S(1)} %get-tuple-element.22), channel_id=1, source_target_pairs={{0,1},{1,2},{2,3},{3,4},{4,5},{5,6},{6,7},{7,8},{8,9},{9,10},{10,1... | collective-permute-start | bytes 829448 | tf_op jit(solution)/shard_map/ppermute | solution.py:32
  49.5 6.4 %collective-permute-start.7 = (f32[6,1,16,720]{3,2,1,0:T(8,128)S(1)}, f32[6,1,16,720]{3,2,1,0:T(8,128)}, u32[]{:S(2)}, u32[]{:S(2)}) collective-permute-start(f32[6,1,16,720]{3,2,1,0:T(8,128)S(1)} %get-tuple-element.23), channel_id=1, source_target_pairs={{1,0},{2,1},{3,2},{4,3},{5,4},{6,5},{7,6},{8,7},{9,8},{10,9},{11,1... | collective-permute-start | bytes 829448 | tf_op jit(solution)/shard_map/ppermute | solution.py:34
  53.2 0.7 copy-start.8
  60.5 1.9 %copy-start.3 = (f32[4,8,16,720]{3,2,1,0:T(8,128)S(1)}, f32[4,8,16,720]{3,2,1,0:T(8,128)}, u32[]{:S(2)}) copy-start(f32[4,8,16,720]{3,2,1,0:T(8,128)} %copy-done.2) | copy-start | bytes 4423684
  62.4 1.5 %copy-start.14 = (f32[4,16,1,1]{1,0,3,2:T(4,128)S(1)}, f32[4,16,1,1]{1,0,3,2:T(4,128)}, u32[]{:S(2)}) copy-start(f32[4,16,1,1]{1,0,3,2:T(4,128)} %constant.156) | copy-start | bytes 772
  63.9 1.6 %copy-start.6 = (f32[4,8,16,720]{3,2,1,0:T(8,128)}, f32[4,8,16,720]{3,2,1,0:T(8,128)S(1)}, u32[]{:S(2)}) copy-start(f32[4,8,16,720]{3,2,1,0:T(8,128)S(1)} %fusion) | copy-start | bytes 4423684
  65.5 1.2 %copy-start.9 = (f32[128,1]{1,0:T(8,128)S(1)}, f32[128,1]{1,0:T(8,128)}, u32[]{:S(2)}) copy-start(f32[128,1]{1,0:T(8,128)} %copy.49) | copy-start | bytes 1540

commit v12 on v11

--- a/solution.py
+++ b/solution.py
@@ -296,7 +296,7 @@
             faced, part, start_mean = lax.optimization_barrier((faced, part, start_mean))
             extended = extended_2(faced, (("col", 1),), 1)
         else:
-            extended = extended_2(state, (("face", 0), ("col", 1)), 1)
+            extended = extended_2(state, (("col", 1), ("face", 0)), 1)
         matched = jnp.take(extended.reshape(-1, width), index_flat, axis=0).reshape(
             rows_dev, cols_dev, 16, width
         )

time: 121 us -> 120 us (level)
  waiting for transfers between devices: 13.7 us -> 10.9 us
  blocking collectives: 37.8 us -> 40 us
    ppermute x4, starting transfers between devices: 7.18 us -> 4.67 us  [extended_2(): lax.ppermute(tail, axis, [(i, (i + 1) % count) for i in range(count)])]
    all_to_all x2, blocking collectives: 37.8 us -> 40 us  [exchange(): lax.all_to_all(chunks, ('face', 'col'), split_axis=0, concat_axis=0, tile...]
    ppermute x4, waiting for transfers between devices: 4.84 us -> 3 us  [extended_2(): lax.ppermute(head, axis, [((i + 1) % count, i) for i in range(count)])]
    ppermute x4, starting transfers between devices: 4.85 us -> 6.3 us  [extended_2(): lax.ppermute(head, axis, [((i + 1) % count, i) for i in range(count)])]
    unnamed x33 -> x31, local copies, waits for them, and re-layouts: 3.55 us -> 3.6 us
  transfers between devices with their start and end apart: 8 -> 8, of which waited for: 5 -> 4; matrix products, arithmetic and copies ran while one was open for 5% -> 5% of each run, Pallas kernels for 7% -> 7%
where the time goes in v12:
time: 120 us
  blocking collectives  40 us (33%)
  Pallas kernels  20.5 us (17%)
  local copies, waits for them, and re-layouts  18.1 us (15%)
  starting transfers between devices  11 us (9%)
  waiting for transfers between devices  10.9 us (9%)
  matrix products  9.16 us (8%)
  other arithmetic  8.83 us (7%)
    all_to_all x2, blocking collectives, exchange(): lax.all_to_all(chunks, ('face', 'col'), split_axis=0, concat_axis=0, tile...  40 us
    pallas_call x1, Pallas kernels, crm_second(): pl.pallas_call(crm_second_kernel, out_shape=(jax.ShapeDtypeStruct(part.sh...  11.7 us
    pallas_call x1, Pallas kernels, crm_first(): pl.pallas_call(crm_first_kernel, out_shape=(jax.ShapeDtypeStruct(state.sh...  8.8 us
    ppermute x4, waiting for transfers between devices, extended_2(): lax.ppermute(tail, axis, [(i, (i + 1) % count) for i in range(count)])  7.86 us
    ppermute x4, starting transfers between devices, extended_2(): lax.ppermute(head, axis, [((i + 1) % count, i) for i in range(count)])  6.3 us
    dot_general x2, matrix products, per_device(): jnp.einsum('nm,rcmw->rcnw', laplace, state, precision=lax.Precision.HIGHEST)  5.23 us
    gather x2, local copies, waits for them, and re-layouts, per_device(): jnp.take(extended.reshape(-1, width), index_flat, axis=0)  5.19 us
    ppermute x4, starting transfers between devices, extended_2(): lax.ppermute(tail, axis, [(i, (i + 1) % count) for i in range(count)])  4.67 us
  transfers between devices with their start and end apart: 8, of which 4 were waited for; matrix products, arithmetic and copies ran while one was open for 5% of the time, Pallas kernels for 7%

profile of v12, /device:TPU:1, one launch (start us, length us, event | category | flops | bytes accessed | tf_op | source)
XLA Modules:
  0.0 119.6 jit_solution(5026836822544077315)
XLA Ops:
  0.6 3.4 %bitcast_add_fusion.3 = f32[4,8,16,720]{3,2,1,0:T(8,128)S(1)} fusion(f32[4,8,16,720]{3,2,1,0:T(8,128)} %param.11, f32[16,16,1,1]{1,0,3,2:T(8,128)} %constant.154), kind=kOutput, calls=%fused_computation.15 | convolution fusion | flops 71516160 | bytes 2950144 | tf_op jit(solution)/shard_map/nm,rcmw->rcnw/dot_general | solution.py:291
  4.2 2.2 %collective-permute-start = (f32[1,8,16,720]{3,2,1,0:T(8,128)S(1)}, f32[1,8,16,720]{3,2,1,0:T(8,128)S(1)}, u32[]{:S(2)}, u32[]{:S(2)}) collective-permute-start(f32[1,8,16,720]{3,2,1,0:T(8,128)S(1)} %get-tuple-element.28), channel_id=1, source_target_pairs={{0,32},{32,64},{64,96},{96,0},{1,33},{33,65},{65,97},{97,1},{2,34}... | collective-permute-start | bytes 1105928 | tf_op jit(solution)/shard_map/ppermute | solution.py:32
  6.4 1.5 %collective-permute-start.1 = (f32[1,8,16,720]{3,2,1,0:T(8,128)S(1)}, f32[1,8,16,720]{3,2,1,0:T(8,128)S(1)}, u32[]{:S(2)}, u32[]{:S(2)}) collective-permute-start(f32[1,8,16,720]{3,2,1,0:T(8,128)S(1)} %get-tuple-element.29), channel_id=1, source_target_pairs={{32,0},{64,32},{96,64},{0,96},{33,1},{65,33},{97,65},{1,97},{34,2}... | collective-permute-start | bytes 1105928 | tf_op jit(solution)/shard_map/ppermute | solution.py:34
  8.8 2.5 %copy-done = bf16[10,32,64,128]{3,2,1,0:T(8,128)(2,1)S(1)} copy-done((bf16[10,32,64,128]{3,2,1,0:T(8,128)(2,1)S(1)}, bf16[10,32,64,128]{3,2,1,0:T(8,128)(2,1)}, u32[]{:S(2)}) %copy-start) | copy-done | bytes 5242904
  11.3 8.8 %shard_map.112 = (f32[10,32,64,128]{3,2,1,0:T(8,128)}, f32[10,32,128]{2,1,0:T(8,128)S(1)}) custom-call(s32[1,128]{1,0:T(1,128)S(1)} %bitcast.62, bf16[10,32,64,128]{3,2,1,0:T(8,128)(2,1)S(1)} %copy-done), custom_call_target="tpu_custom_call" | custom-call | tf_op jit(solution)/shard_map/pallas_call | solution.py:205
  20.4 2.3 %collective-permute-start.2 = (f32[6,1,16,720]{3,2,1,0:T(8,128)S(1)}, f32[6,1,16,720]{3,2,1,0:T(8,128)S(1)}, u32[]{:S(2)}, u32[]{:S(2)}) collective-permute-start(f32[6,1,16,720]{3,2,1,0:T(8,128)S(1)} %get-tuple-element.22), channel_id=1, source_target_pairs={{0,1},{1,2},{2,3},{3,4},{4,5},{5,6},{6,7},{7,8},{8,9},{9,10},{10,1... | collective-permute-start | bytes 829448 | tf_op jit(solution)/shard_map/ppermute | solution.py:32
  22.7 3.6 %collective-permute-done.2 = f32[6,1,16,720]{3,2,1,0:T(8,128)S(1)} collective-permute-done((f32[6,1,16,720]{3,2,1,0:T(8,128)S(1)}, f32[6,1,16,720]{3,2,1,0:T(8,128)S(1)}, u32[]{:S(2)}, u32[]{:S(2)}) %collective-permute-start.2) | collective-permute-done | bytes 276512 | tf_op jit(solution)/shard_map/ppermute | solution.py:32
  26.3 2.8 %collective-permute-done.3 = f32[6,1,16,720]{3,2,1,0:T(8,128)S(1)} collective-permute-done((f32[6,1,16,720]{3,2,1,0:T(8,128)S(1)}, f32[6,1,16,720]{3,2,1,0:T(8,128)S(1)}, u32[]{:S(2)}, u32[]{:S(2)}) %collective-permute-start.3) | collective-permute-done | bytes 276512 | tf_op jit(solution)/shard_map/ppermute | solution.py:34
  29.4 2.6 %gather_fusion.3 = f32[512,720]{1,0:T(8,128)} fusion(f32[960,720]{1,0:T(8,128)S(1)} %bitcast.65, s32[1024]{0:T(1024)S(1)} %pad_clamp_fusion.2), kind=kCustom, calls=%fused_computation.clone | custom fusion | bytes 2951168 | tf_op jit(solution)/shard_map/jit(_take)/gather | solution.py:300
  32.0 1.6 %broadcast_select_fusion.1 = f32[512,720]{1,0:T(8,128)S(1)} fusion(f32[512,720]{1,0:T(8,128)} %gather_fusion.3, pred[512]{0:T(512)(128)(4,1)S(1)} %compare_and_fusion), kind=kLoop, calls=%fused_computation.18 | loop fusion | flops 368640 | bytes 2949632 | tf_op jit(solution)/shard_map/jit(_take)/select_n | solution.py:300
  33.7 1.5 %fusion.34 = f32[4,8,720,16]{2,3,1,0:T(8,128)S(1)} fusion(f32[4,8,16,720]{3,2,1,0:T(8,128)S(1)} %bitcast.68, f32[16,16,1,1]{1,0,3,2:T(8,128)S(1)} %copy-done.9), kind=kOutput, calls=%fused_computation.98 | convolution fusion | flops 70778880 | bytes 2950144 | tf_op jit(solution)/shard_map/nm,rcmw->rcnw/dot_general | solution.py:303
  35.2 1.8 %bitcast_add_fusion.1 = f32[4,8,16,720]{3,2,1,0:T(8,128)S(1)} fusion(f32[16,16,1,1]{1,0,3,2:T(8,128)S(1)} %copy-done.10, f32[4,8,16,720]{3,2,1,0:T(8,128)S(1)} %copy-done.5, f32[4,8,720,16]{2,3,1,0:T(8,128)S(1)} %fusion.34, f32[16]{0:T(128)S(1)} %copy-done.14), kind=kOutput, calls=%fused_computation.12 | convolution fusion | flops 72990720 | bytes 4424768 | tf_op jit(solution)/shard_map/nm,rcmw->rcnw/dot_general | solution.py:291
  37.1 2.2 %collective-permute-start.5 = (f32[4,1,16,720]{3,2,1,0:T(8,128)S(1)}, f32[4,1,16,720]{3,2,1,0:T(8,128)S(1)}, u32[]{:S(2)}, u32[]{:S(2)}) collective-permute-start(f32[4,1,16,720]{3,2,1,0:T(8,128)S(1)} %get-tuple-element.27), channel_id=1, source_target_pairs={{1,0},{2,1},{3,2},{4,3},{5,4},{6,5},{7,6},{8,7},{9,8},{10,9},{11,1... | collective-permute-start | bytes 552968 | tf_op jit(solution)/shard_map/ppermute | solution.py:34
  39.5 2.5 %sort.17 = (s32[128]{0:T(128)}, s32[128]{0:T(128)S(1)}) sort(s32[128]{0:T(128)S(1)} %reshape.88, s32[128]{0:T(128)S(1)} %iota.35), dimensions={0}, to_apply=%region_0.2 | sort | flops 896 | bytes 2048 | tf_op jit(solution)/shard_map/jit(argsort)/sort | solution.py:311
  42.5 2.6 %collective-permute-start.7 = (f32[1,10,16,720]{3,2,1,0:T(8,128)S(1)}, f32[1,10,16,720]{3,2,1,0:T(8,128)}, u32[]{:S(2)}, u32[]{:S(2)}) collective-permute-start(f32[1,10,16,720]{3,2,1,0:T(8,128)S(1)} %get-tuple-element.25), channel_id=1, source_target_pairs={{32,0},{64,32},{96,64},{0,96},{33,1},{65,33},{97,65},{1,97},{34,2}... | collective-permute-start | bytes 1382408 | tf_op jit(solution)/shard_map/ppermute | solution.py:34
  47.1 4.2 %collective-permute-done.6 = f32[1,10,16,720]{3,2,1,0:T(8,128)S(1)} collective-permute-done((f32[1,10,16,720]{3,2,1,0:T(8,128)S(1)}, f32[1,10,16,720]{3,2,1,0:T(8,128)S(1)}, u32[]{:S(2)}, u32[]{:S(2)}) %collective-permute-start.6) | collective-permute-done | bytes 460832 | tf_op jit(solution)/shard_map/ppermute | solution.py:32
  52.1 1.9 %pad_maximum_fusion.1 = f32[6,10,16,720]{3,2,1,0:T(8,128)S(1)} fusion(f32[1,10,16,720]{3,2,1,0:T(8,128)} %collective-permute-done.7, f32[4,1,16,720]{3,2,1,0:T(8,128)S(1)} %collective-permute-done.5, f32[4,8,16,720]{3,2,1,0:T(8,128)} %copy-done.2, f32[4,1,16,720]{3,2,1,0:T(8,128)S(1)} %collective-permute-done.4, f32[1,10,16,720]{3,2,1,0:T(8,128)} %copy-done.7), kind=kLoop, calls=%fused_computation.8 | loop fusion | flops 2764800 | bytes 5529600 | tf_op jit(solution)/shard_map/concatenate | solution.py:30
  54.0 2.6 %gather_fusion.4 = f32[512,720]{1,0:T(8,128)} fusion(f32[960,720]{1,0:T(8,128)S(1)} %bitcast.64, s32[1024]{0:T(1024)S(1)} %pad_clamp_fusion.2), kind=kCustom, calls=%fused_computation.1.clone | custom fusion | bytes 2951168 | tf_op jit(solution)/shard_map/jit(_take)/gather | solution.py:300
  56.6 1.7 %broadcast_select_fusion = f32[512,720]{1,0:T(8,128)S(1)} fusion(f32[512,720]{1,0:T(8,128)} %gather_fusion.4, pred[512]{0:T(512)(128)(4,1)S(1)} %compare_and_fusion), kind=kLoop, calls=%fused_computation.17 | loop fusion | flops 368640 | bytes 2949632 | tf_op jit(solution)/shard_map/jit(_take)/select_n | solution.py:300
  58.5 1.5 %fusion = f32[4,8,16,720]{3,2,1,0:T(8,128)S(1)} fusion(f32[4,8,16,720]{3,2,1,0:T(8,128)S(1)} %copy-done.3, f32[4,8,16,720]{3,2,1,0:T(8,128)S(1)} %bitcast.67, f32[16,16,1,1]{1,0,3,2:T(8,128)S(1)} %copy-done.9, f32[16]{0:T(128)S(1)} %copy-done.14), kind=kOutput, calls=%fused_computation.11 | convolution fusion | flops 71516160 | bytes 4424768 | tf_op jit(solution)/shard_map/nm,rcmw->rcnw/dot_general | solution.py:303
  63.2 25.4 %all_to_all.10 = f32[128,1,321]{2,1,0:T(1,128)S(1)} all-to-all(f32[128,1,321]{2,1,0:T(1,128)S(1)} %copy.50), channel_id=1, replica_groups=mesh['face'=4,'col'=32] {'face','col'}, dimensions={0} | all-to-all | bytes 328704 | tf_op jit(solution)/shard_map/all_to_all | solution.py:260
  88.9 1.3 %scatter_custom_fusion = f32[128,320]{1,0:T(8,128)S(1)} fusion(s32[128]{0:T(128)S(1)} %fusion.30, f32[128,320]{1,0:T(8,128)S(1)} %copy.52, f32[]{:T(128)} %constant.142.clone.1), kind=kCustom, calls=%fused_computation.28 | custom fusion | bytes 163844 | tf_op jit(solution)/shard_map/scatter | solution.py:318
  90.3 11.7 %shard_map.113 = (bf16[10,32,64,128]{3,2,1,0:T(8,128)(2,1)}, f32[10,32,128]{2,1,0:T(8,128)S(1)}) custom-call(f32[10,32,128]{2,1,0:T(8,128)S(1)} %bitcast.60, s32[1,128]{1,0:T(1,128)S(1)} %bitcast.63, f32[10,32,128]{2,1,0:T(8,128)S(1)} %get-tuple-element.16.mean_ref, f32[10,32,64,128]{3,2,1,0:T(8,128)} %get-tuple-element.17.part_hbm), custom_call_target="tpu_custom_call" | custom-call | tf_op jit(solution)/shard_map/pallas_call | solution.py:227
  103.1 14.6 %all_to_all.11 = f32[128,1,320]{2,1,0:T(1,128)S(1)} all-to-all(f32[128,1,320]{2,1,0:T(1,128)S(1)} %copy.55), channel_id=1, replica_groups=mesh['face'=4,'col'=32] {'face','col'}, dimensions={0} | all-to-all | bytes 327680 | tf_op jit(solution)/shard_map/all_to_all | solution.py:260
  (84 shorter events, 11.6 us)
Async XLA Ops:
  4.1 16.0 %copy-start.4 = (f32[4,8,16,720]{3,2,1,0:T(8,128)}, f32[4,8,16,720]{3,2,1,0:T(8,128)S(1)}, u32[]{:S(2)}) copy-start(f32[4,8,16,720]{3,2,1,0:T(8,128)S(1)} %bitcast_add_fusion.3) | copy-start | bytes 4423684
  4.1 3.8 %copy-start.11 = (s32[4,8,4]{1,2,0:T(4,128)S(1)}, s32[4,8,4]{1,2,0:T(4,128)}, u32[]{:S(2)}) copy-start(s32[4,8,4]{1,2,0:T(4,128)} %param.12) | copy-start | bytes 1540
  4.1 4.7 %copy-start.1 = (s32[128]{0:T(128)S(1)}, s32[128]{0:T(128)}, u32[]{:S(2)}) copy-start(s32[128]{0:T(128)} %param.14) | copy-start | bytes 1540
  4.2 15.9 %collective-permute-start = (f32[1,8,16,720]{3,2,1,0:T(8,128)S(1)}, f32[1,8,16,720]{3,2,1,0:T(8,128)S(1)}, u32[]{:S(2)}, u32[]{:S(2)}) collective-permute-start(f32[1,8,16,720]{3,2,1,0:T(8,128)S(1)} %get-tuple-element.28), channel_id=1, source_target_pairs={{0,32},{32,64},{64,96},{96,0},{1,33},{33,65},{65,97},{97,1},{2,34}... | collective-permute-start | bytes 1105928 | tf_op jit(solution)/shard_map/ppermute | solution.py:32
  6.4 13.7 %collective-permute-start.1 = (f32[1,8,16,720]{3,2,1,0:T(8,128)S(1)}, f32[1,8,16,720]{3,2,1,0:T(8,128)S(1)}, u32[]{:S(2)}, u32[]{:S(2)}) collective-permute-start(f32[1,8,16,720]{3,2,1,0:T(8,128)S(1)} %get-tuple-element.29), channel_id=1, source_target_pairs={{32,0},{64,32},{96,64},{0,96},{33,1},{65,33},{97,65},{1,97},{34,2}... | collective-permute-start | bytes 1105928 | tf_op jit(solution)/shard_map/ppermute | solution.py:34
  8.8 2.5 %copy-start = (bf16[10,32,64,128]{3,2,1,0:T(8,128)(2,1)S(1)}, bf16[10,32,64,128]{3,2,1,0:T(8,128)(2,1)}, u32[]{:S(2)}) copy-start(bf16[10,32,64,128]{3,2,1,0:T(8,128)(2,1)} %state_hbm.1) | copy-start | bytes 15728644
  20.4 5.9 %collective-permute-start.2 = (f32[6,1,16,720]{3,2,1,0:T(8,128)S(1)}, f32[6,1,16,720]{3,2,1,0:T(8,128)S(1)}, u32[]{:S(2)}, u32[]{:S(2)}) collective-permute-start(f32[6,1,16,720]{3,2,1,0:T(8,128)S(1)} %get-tuple-element.22), channel_id=1, source_target_pairs={{0,1},{1,2},{2,3},{3,4},{4,5},{5,6},{6,7},{7,8},{8,9},{9,10},{10,1... | collective-permute-start | bytes 829448 | tf_op jit(solution)/shard_map/ppermute | solution.py:32
  22.7 6.4 %collective-permute-start.3 = (f32[6,1,16,720]{3,2,1,0:T(8,128)S(1)}, f32[6,1,16,720]{3,2,1,0:T(8,128)S(1)}, u32[]{:S(2)}, u32[]{:S(2)}) collective-permute-start(f32[6,1,16,720]{3,2,1,0:T(8,128)S(1)} %get-tuple-element.23), channel_id=1, source_target_pairs={{1,0},{2,1},{3,2},{4,3},{5,4},{6,5},{7,6},{8,7},{9,8},{10,9},{11,1... | collective-permute-start | bytes 829448 | tf_op jit(solution)/shard_map/ppermute | solution.py:34
  32.0 1.6 %copy-start.9 = (f32[16,16,1,1]{1,0,3,2:T(8,128)S(1)}, f32[16,16,1,1]{1,0,3,2:T(8,128)}, u32[]{:S(2)}) copy-start(f32[16,16,1,1]{1,0,3,2:T(8,128)} %constant.155) | copy-start | bytes 3076
  33.6 1.5 %copy-start.5 = (f32[4,8,16,720]{3,2,1,0:T(8,128)S(1)}, f32[4,8,16,720]{3,2,1,0:T(8,128)}, u32[]{:S(2)}) copy-start(f32[4,8,16,720]{3,2,1,0:T(8,128)} %copy-done.4) | copy-start | bytes 4423684
  33.6 1.5 %copy-start.10 = (f32[16,16,1,1]{1,0,3,2:T(8,128)S(1)}, f32[16,16,1,1]{1,0,3,2:T(8,128)}, u32[]{:S(2)}) copy-start(f32[16,16,1,1]{1,0,3,2:T(8,128)} %constant.154) | copy-start | bytes 3076
  33.7 1.5 %copy-start.14 = (f32[16]{0:T(128)S(1)}, f32[16]{0:T(128)}, u32[]{:S(2)}) copy-start(f32[16]{0:T(128)} %constant.152) | copy-start | bytes 196
  35.2 4.1 %copy-start.12 = (s32[4,8,4]{1,2,0:T(4,128)S(1)}, s32[4,8,4]{1,2,0:T(4,128)}, u32[]{:S(2)}) copy-start(s32[4,8,4]{1,2,0:T(4,128)} %param.13) | copy-start | bytes 1540
  37.0 5.4 %copy-start.2 = (f32[4,8,16,720]{3,2,1,0:T(8,128)}, f32[4,8,16,720]{3,2,1,0:T(8,128)S(1)}, u32[]{:S(2)}) copy-start(f32[4,8,16,720]{3,2,1,0:T(8,128)S(1)} %bitcast_add_fusion.1) | copy-start | bytes 4423684
  37.0 5.0 %collective-permute-start.4 = (f32[4,1,16,720]{3,2,1,0:T(8,128)S(1)}, f32[4,1,16,720]{3,2,1,0:T(8,128)S(1)}, u32[]{:S(2)}, u32[]{:S(2)}) collective-permute-start(f32[4,1,16,720]{3,2,1,0:T(8,128)S(1)} %get-tuple-element.26), channel_id=1, source_target_pairs={{0,1},{1,2},{2,3},{3,4},{4,5},{5,6},{6,7},{7,8},{8,9},{9,10},{10,1... | collective-permute-start | bytes 552968 | tf_op jit(solution)/shard_map/ppermute | solution.py:32
  37.1 5.2 %collective-permute-start.5 = (f32[4,1,16,720]{3,2,1,0:T(8,128)S(1)}, f32[4,1,16,720]{3,2,1,0:T(8,128)S(1)}, u32[]{:S(2)}, u32[]{:S(2)}) collective-permute-start(f32[4,1,16,720]{3,2,1,0:T(8,128)S(1)} %get-tuple-element.27), channel_id=1, source_target_pairs={{1,0},{2,1},{3,2},{4,3},{5,4},{6,5},{7,6},{8,7},{9,8},{10,9},{11,1... | collective-permute-start | bytes 552968 | tf_op jit(solution)/shard_map/ppermute | solution.py:34
  42.4 9.0 %collective-permute-start.6 = (f32[1,10,16,720]{3,2,1,0:T(8,128)S(1)}, f32[1,10,16,720]{3,2,1,0:T(8,128)S(1)}, u32[]{:S(2)}, u32[]{:S(2)}) collective-permute-start(f32[1,10,16,720]{3,2,1,0:T(8,128)S(1)} %get-tuple-element.24), channel_id=1, source_target_pairs={{0,32},{32,64},{64,96},{96,0},{1,33},{33,65},{65,97},{97,1},{2,34}... | collective-permute-start | bytes 1382408 | tf_op jit(solution)/shard_map/ppermute | solution.py:32
  42.5 9.6 %collective-permute-start.7 = (f32[1,10,16,720]{3,2,1,0:T(8,128)S(1)}, f32[1,10,16,720]{3,2,1,0:T(8,128)}, u32[]{:S(2)}, u32[]{:S(2)}) collective-permute-start(f32[1,10,16,720]{3,2,1,0:T(8,128)S(1)} %get-tuple-element.25), channel_id=1, source_target_pairs={{32,0},{64,32},{96,64},{0,96},{33,1},{65,33},{97,65},{1,97},{34,2}... | collective-permute-start | bytes 1382408 | tf_op jit(solution)/shard_map/ppermute | solution.py:34
  51.3 0.8 copy-start.7
  56.6 1.9 %copy-start.3 = (f32[4,8,16,720]{3,2,1,0:T(8,128)S(1)}, f32[4,8,16,720]{3,2,1,0:T(8,128)}, u32[]{:S(2)}) copy-start(f32[4,8,16,720]{3,2,1,0:T(8,128)} %copy-done.2) | copy-start | bytes 4423684
  58.5 1.5 %copy-start.13 = (f32[4,16,1,1]{1,0,3,2:T(4,128)S(1)}, f32[4,16,1,1]{1,0,3,2:T(4,128)}, u32[]{:S(2)}) copy-start(f32[4,16,1,1]{1,0,3,2:T(4,128)} %constant.156) | copy-start | bytes 772
  60.1 1.6 %copy-start.6 = (f32[4,8,16,720]{3,2,1,0:T(8,128)}, f32[4,8,16,720]{3,2,1,0:T(8,128)S(1)}, u32[]{:S(2)}) copy-start(f32[4,8,16,720]{3,2,1,0:T(8,128)S(1)} %fusion) | copy-start | bytes 4423684
  61.6 1.2 %copy-start.8 = (f32[128,1]{1,0:T(8,128)S(1)}, f32[128,1]{1,0:T(8,128)}, u32[]{:S(2)}) copy-start(f32[128,1]{1,0:T(8,128)} %copy.49) | copy-start | bytes 1540

commit v13 on v12

--- a/solution.py
+++ b/solution.py
@@ -292,9 +292,9 @@
             "nm,rcmw->rcnw", laplace, state, precision=lax.Precision.HIGHEST
         )
         if step == 0:
-            faced = extended_2(state, (("face", 0),), 1)
-            faced, part, start_mean = lax.optimization_barrier((faced, part, start_mean))
-            extended = extended_2(faced, (("col", 1),), 1)
+            sided = extended_2(state, (("col", 1),), 1)
+            sided, part, start_mean = lax.optimization_barrier((sided, part, start_mean))
+            extended = extended_2(sided, (("face", 0),), 1)
         else:
             extended = extended_2(state, (("col", 1), ("face", 0)), 1)
         matched = jnp.take(extended.reshape(-1, width), index_flat, axis=0).reshape(

time: 120 us -> 125 us (1.042)
  waiting for transfers between devices: 10.9 us -> 16.3 us
  blocking collectives: 40 us -> 35.4 us
  starting transfers between devices: 11 us -> 15.2 us
    ppermute x4, starting transfers between devices: 4.67 us -> 12 us  [extended_2(): lax.ppermute(tail, axis, [(i, (i + 1) % count) for i in range(count)])]
    ppermute x4, waiting for transfers between devices: 7.86 us -> 13.7 us  [extended_2(): lax.ppermute(tail, axis, [(i, (i + 1) % count) for i in range(count)])]
    all_to_all x2, blocking collectives: 40 us -> 35.4 us  [exchange(): lax.all_to_all(chunks, ('face', 'col'), split_axis=0, concat_axis=0, tile...]
    ppermute x4, starting transfers between devices: 6.3 us -> 3.22 us  [extended_2(): lax.ppermute(head, axis, [((i + 1) % count, i) for i in range(count)])]
  transfers between devices with their start and end apart: 8 -> 8, of which waited for: 4 -> 3; matrix products, arithmetic and copies ran while one was open for 5% -> 4% of each run, Pallas kernels for 7% -> 7%
where the time goes in v13:
time: 125 us; the launch traced here: 124 us
  blocking collectives  35.4 us (28%)
  Pallas kernels  20.5 us (16%)
  local copies, waits for them, and re-layouts  18.1 us (14%)
  waiting for transfers between devices  16.3 us (13%)
  starting transfers between devices  15.2 us (12%)
  matrix products  9.16 us (7%)
  other arithmetic  8.63 us (7%)
    all_to_all x2, blocking collectives, exchange(): lax.all_to_all(chunks, ('face', 'col'), split_axis=0, concat_axis=0, tile...  35.4 us
    ppermute x4, waiting for transfers between devices, extended_2(): lax.ppermute(tail, axis, [(i, (i + 1) % count) for i in range(count)])  13.7 us
    ppermute x4, starting transfers between devices, extended_2(): lax.ppermute(tail, axis, [(i, (i + 1) % count) for i in range(count)])  12 us
    pallas_call x1, Pallas kernels, crm_second(): pl.pallas_call(crm_second_kernel, out_shape=(jax.ShapeDtypeStruct(part.sh...  11.7 us
    pallas_call x1, Pallas kernels, crm_first(): pl.pallas_call(crm_first_kernel, out_shape=(jax.ShapeDtypeStruct(state.sh...  8.8 us
    dot_general x2, matrix products, per_device(): jnp.einsum('nm,rcmw->rcnw', laplace, state, precision=lax.Precision.HIGHEST)  5.23 us
    gather x2, local copies, waits for them, and re-layouts, per_device(): jnp.take(extended.reshape(-1, width), index_flat, axis=0)  5.19 us
    unnamed x31, local copies, waits for them, and re-layouts  3.6 us
  transfers between devices with their start and end apart: 8, of which 3 were waited for; matrix products, arithmetic and copies ran while one was open for 4% of the time, Pallas kernels for 7%

profile of v13, /device:TPU:1, one launch (start us, length us, event | category | flops | bytes accessed | tf_op | source)
XLA Modules:
  0.0 124.5 jit_solution(1182078445439047232)
XLA Ops:
  0.7 3.4 %bitcast_add_fusion.3 = f32[4,8,16,720]{3,2,1,0:T(8,128)S(1)} fusion(f32[4,8,16,720]{3,2,1,0:T(8,128)} %param.11, f32[16,16,1,1]{1,0,3,2:T(8,128)} %constant.154), kind=kOutput, calls=%fused_computation.15 | convolution fusion | flops 71516160 | bytes 2950144 | tf_op jit(solution)/shard_map/nm,rcmw->rcnw/dot_general | solution.py:291
  4.1 2.7 %collective-permute-start = (f32[4,1,16,720]{3,2,1,0:T(8,128)S(1)}, f32[4,1,16,720]{3,2,1,0:T(8,128)S(1)}, u32[]{:S(2)}, u32[]{:S(2)}) collective-permute-start(f32[4,1,16,720]{3,2,1,0:T(8,128)S(1)} %get-tuple-element.28), channel_id=1, source_target_pairs={{0,1},{1,2},{2,3},{3,4},{4,5},{5,6},{6,7},{7,8},{8,9},{9,10},{10,1... | collective-permute-start | bytes 552968 | tf_op jit(solution)/shard_map/ppermute | solution.py:32
  7.7 2.5 %copy-done = bf16[10,32,64,128]{3,2,1,0:T(8,128)(2,1)S(1)} copy-done((bf16[10,32,64,128]{3,2,1,0:T(8,128)(2,1)S(1)}, bf16[10,32,64,128]{3,2,1,0:T(8,128)(2,1)}, u32[]{:S(2)}) %copy-start) | copy-done | bytes 5242904
  10.2 8.8 %shard_map.112 = (f32[10,32,64,128]{3,2,1,0:T(8,128)}, f32[10,32,128]{2,1,0:T(8,128)S(1)}) custom-call(s32[1,128]{1,0:T(1,128)S(1)} %bitcast.62, bf16[10,32,64,128]{3,2,1,0:T(8,128)(2,1)S(1)} %copy-done), custom_call_target="tpu_custom_call" | custom-call | tf_op jit(solution)/shard_map/pallas_call | solution.py:205
  19.3 1.4 %collective-permute-start.2 = (f32[1,10,16,720]{3,2,1,0:T(8,128)S(1)}, f32[1,10,16,720]{3,2,1,0:T(8,128)S(1)}, u32[]{:S(2)}, u32[]{:S(2)}) collective-permute-start(f32[1,10,16,720]{3,2,1,0:T(8,128)S(1)} %get-tuple-element.24), channel_id=1, source_target_pairs={{0,32},{32,64},{64,96},{96,0},{1,33},{33,65},{65,97},{97,1},{2,34}... | collective-permute-start | bytes 1382408 | tf_op jit(solution)/shard_map/ppermute | solution.py:32
  20.6 1.5 %collective-permute-start.3 = (f32[1,10,16,720]{3,2,1,0:T(8,128)S(1)}, f32[1,10,16,720]{3,2,1,0:T(8,128)S(1)}, u32[]{:S(2)}, u32[]{:S(2)}) collective-permute-start(f32[1,10,16,720]{3,2,1,0:T(8,128)S(1)} %get-tuple-element.25), channel_id=1, source_target_pairs={{32,0},{64,32},{96,64},{0,96},{33,1},{65,33},{97,65},{1,97},{34,2}... | collective-permute-start | bytes 1382408 | tf_op jit(solution)/shard_map/ppermute | solution.py:34
  22.2 6.6 %collective-permute-done.2 = f32[1,10,16,720]{3,2,1,0:T(8,128)S(1)} collective-permute-done((f32[1,10,16,720]{3,2,1,0:T(8,128)S(1)}, f32[1,10,16,720]{3,2,1,0:T(8,128)S(1)}, u32[]{:S(2)}, u32[]{:S(2)}) %collective-permute-start.2) | collective-permute-done | bytes 460832 | tf_op jit(solution)/shard_map/ppermute | solution.py:32
  29.0 2.6 %gather_fusion.3 = f32[512,720]{1,0:T(8,128)} fusion(f32[960,720]{1,0:T(8,128)S(1)} %bitcast.65, s32[1024]{0:T(1024)S(1)} %pad_clamp_fusion.2), kind=kCustom, calls=%fused_computation.clone | custom fusion | bytes 2951168 | tf_op jit(solution)/shard_map/jit(_take)/gather | solution.py:300
  31.6 1.6 %broadcast_select_fusion.1 = f32[512,720]{1,0:T(8,128)S(1)} fusion(f32[512,720]{1,0:T(8,128)} %gather_fusion.3, pred[512]{0:T(512)(128)(4,1)S(1)} %compare_and_fusion), kind=kLoop, calls=%fused_computation.18 | loop fusion | flops 368640 | bytes 2949632 | tf_op jit(solution)/shard_map/jit(_take)/select_n | solution.py:300
  33.3 1.5 %fusion.34 = f32[4,8,720,16]{2,3,1,0:T(8,128)S(1)} fusion(f32[4,8,16,720]{3,2,1,0:T(8,128)S(1)} %bitcast.68, f32[16,16,1,1]{1,0,3,2:T(8,128)S(1)} %copy-done.9), kind=kOutput, calls=%fused_computation.98 | convolution fusion | flops 70778880 | bytes 2950144 | tf_op jit(solution)/shard_map/nm,rcmw->rcnw/dot_general | solution.py:303
  34.8 1.8 %bitcast_add_fusion.1 = f32[4,8,16,720]{3,2,1,0:T(8,128)S(1)} fusion(f32[16,16,1,1]{1,0,3,2:T(8,128)S(1)} %copy-done.10, f32[4,8,16,720]{3,2,1,0:T(8,128)S(1)} %copy-done.5, f32[4,8,720,16]{2,3,1,0:T(8,128)S(1)} %fusion.34, f32[16]{0:T(128)S(1)} %copy-done.14), kind=kOutput, calls=%fused_computation.12 | convolution fusion | flops 72990720 | bytes 4424768 | tf_op jit(solution)/shard_map/nm,rcmw->rcnw/dot_general | solution.py:291
  36.6 6.6 %collective-permute-start.4 = (f32[4,1,16,720]{3,2,1,0:T(8,128)S(1)}, f32[4,1,16,720]{3,2,1,0:T(8,128)S(1)}, u32[]{:S(2)}, u32[]{:S(2)}) collective-permute-start(f32[4,1,16,720]{3,2,1,0:T(8,128)S(1)} %get-tuple-element.26), channel_id=1, source_target_pairs={{0,1},{1,2},{2,3},{3,4},{4,5},{5,6},{6,7},{7,8},{8,9},{9,10},{10,1... | collective-permute-start | bytes 552968 | tf_op jit(solution)/shard_map/ppermute | solution.py:32
  43.5 2.5 %sort.17 = (s32[128]{0:T(128)}, s32[128]{0:T(128)S(1)}) sort(s32[128]{0:T(128)S(1)} %reshape.88, s32[128]{0:T(128)S(1)} %iota.35), dimensions={0}, to_apply=%region_0.2 | sort | flops 896 | bytes 2048 | tf_op jit(solution)/shard_map/jit(argsort)/sort | solution.py:311
  46.0 2.6 %collective-permute-done.5 = f32[4,1,16,720]{3,2,1,0:T(8,128)S(1)} collective-permute-done((f32[4,1,16,720]{3,2,1,0:T(8,128)S(1)}, f32[4,1,16,720]{3,2,1,0:T(8,128)S(1)}, u32[]{:S(2)}, u32[]{:S(2)}) %collective-permute-start.5) | collective-permute-done | bytes 184352 | tf_op jit(solution)/shard_map/ppermute | solution.py:34
  48.7 1.4 %collective-permute-start.6 = (f32[1,10,16,720]{3,2,1,0:T(8,128)S(1)}, f32[1,10,16,720]{3,2,1,0:T(8,128)S(1)}, u32[]{:S(2)}, u32[]{:S(2)}) collective-permute-start(f32[1,10,16,720]{3,2,1,0:T(8,128)S(1)} %get-tuple-element.22), channel_id=1, source_target_pairs={{0,32},{32,64},{64,96},{96,0},{1,33},{33,65},{65,97},{97,1},{2,34}... | collective-permute-start | bytes 1382408 | tf_op jit(solution)/shard_map/ppermute | solution.py:32
  50.1 1.7 %collective-permute-start.7 = (f32[1,10,16,720]{3,2,1,0:T(8,128)S(1)}, f32[1,10,16,720]{3,2,1,0:T(8,128)}, u32[]{:S(2)}, u32[]{:S(2)}) collective-permute-start(f32[1,10,16,720]{3,2,1,0:T(8,128)S(1)} %get-tuple-element.23), channel_id=1, source_target_pairs={{32,0},{64,32},{96,64},{0,96},{33,1},{65,33},{97,65},{1,97},{34,2}... | collective-permute-start | bytes 1382408 | tf_op jit(solution)/shard_map/ppermute | solution.py:34
  53.8 7.1 %collective-permute-done.6 = f32[1,10,16,720]{3,2,1,0:T(8,128)S(1)} collective-permute-done((f32[1,10,16,720]{3,2,1,0:T(8,128)S(1)}, f32[1,10,16,720]{3,2,1,0:T(8,128)S(1)}, u32[]{:S(2)}, u32[]{:S(2)}) %collective-permute-start.6) | collective-permute-done | bytes 460832 | tf_op jit(solution)/shard_map/ppermute | solution.py:32
  61.6 1.9 %pad_maximum_fusion.1 = f32[6,10,16,720]{3,2,1,0:T(8,128)S(1)} fusion(f32[1,10,16,720]{3,2,1,0:T(8,128)} %collective-permute-done.7, f32[4,1,16,720]{3,2,1,0:T(8,128)S(1)} %collective-permute-done.5, f32[4,8,16,720]{3,2,1,0:T(8,128)} %copy-done.2, f32[4,1,16,720]{3,2,1,0:T(8,128)S(1)} %collective-permute-done.4, f32[1,10,16,720]{3,2,1,0:T(8,128)} %copy-done.7), kind=kLoop, calls=%fused_computation.8 | loop fusion | flops 2764800 | bytes 5529600 | tf_op jit(solution)/shard_map/concatenate | solution.py:30
  63.6 2.6 %gather_fusion.4 = f32[512,720]{1,0:T(8,128)} fusion(f32[960,720]{1,0:T(8,128)S(1)} %bitcast.64, s32[1024]{0:T(1024)S(1)} %pad_clamp_fusion.2), kind=kCustom, calls=%fused_computation.1.clone | custom fusion | bytes 2951168 | tf_op jit(solution)/shard_map/jit(_take)/gather | solution.py:300
  66.2 1.7 %broadcast_select_fusion = f32[512,720]{1,0:T(8,128)S(1)} fusion(f32[512,720]{1,0:T(8,128)} %gather_fusion.4, pred[512]{0:T(512)(128)(4,1)S(1)} %compare_and_fusion), kind=kLoop, calls=%fused_computation.17 | loop fusion | flops 368640 | bytes 2949632 | tf_op jit(solution)/shard_map/jit(_take)/select_n | solution.py:300
  68.0 1.5 %fusion = f32[4,8,16,720]{3,2,1,0:T(8,128)S(1)} fusion(f32[4,8,16,720]{3,2,1,0:T(8,128)S(1)} %copy-done.3, f32[4,8,16,720]{3,2,1,0:T(8,128)S(1)} %bitcast.67, f32[16,16,1,1]{1,0,3,2:T(8,128)S(1)} %copy-done.9, f32[16]{0:T(128)S(1)} %copy-done.14), kind=kOutput, calls=%fused_computation.11 | convolution fusion | flops 71516160 | bytes 4424768 | tf_op jit(solution)/shard_map/nm,rcmw->rcnw/dot_general | solution.py:303
  72.7 20.8 %all_to_all.10 = f32[128,1,321]{2,1,0:T(1,128)S(1)} all-to-all(f32[128,1,321]{2,1,0:T(1,128)S(1)} %copy.50), channel_id=1, replica_groups=mesh['face'=4,'col'=32] {'face','col'}, dimensions={0} | all-to-all | bytes 328704 | tf_op jit(solution)/shard_map/all_to_all | solution.py:260
  95.2 11.7 %shard_map.113 = (bf16[10,32,64,128]{3,2,1,0:T(8,128)(2,1)}, f32[10,32,128]{2,1,0:T(8,128)S(1)}) custom-call(f32[10,32,128]{2,1,0:T(8,128)S(1)} %bitcast.60, s32[1,128]{1,0:T(1,128)S(1)} %bitcast.63, f32[10,32,128]{2,1,0:T(8,128)S(1)} %get-tuple-element.16.mean_ref, f32[10,32,64,128]{3,2,1,0:T(8,128)} %get-tuple-element.17.part_hbm), custom_call_target="tpu_custom_call" | custom-call | tf_op jit(solution)/shard_map/pallas_call | solution.py:227
  108.0 14.6 %all_to_all.11 = f32[128,1,320]{2,1,0:T(1,128)S(1)} all-to-all(f32[128,1,320]{2,1,0:T(1,128)S(1)} %copy.55), channel_id=1, replica_groups=mesh['face'=4,'col'=32] {'face','col'}, dimensions={0} | all-to-all | bytes 327680 | tf_op jit(solution)/shard_map/all_to_all | solution.py:260
  (84 shorter events, 12.3 us)
Async XLA Ops:
  0.6 6.2 %copy-start.11 = (s32[4,8,4]{1,2,0:T(4,128)S(1)}, s32[4,8,4]{1,2,0:T(4,128)}, u32[]{:S(2)}) copy-start(s32[4,8,4]{1,2,0:T(4,128)} %param.12) | copy-start | bytes 1540
  0.6 7.1 %copy-start.1 = (s32[128]{0:T(128)S(1)}, s32[128]{0:T(128)}, u32[]{:S(2)}) copy-start(s32[128]{0:T(128)} %param.14) | copy-start | bytes 1540
  4.1 14.9 %copy-start.4 = (f32[4,8,16,720]{3,2,1,0:T(8,128)}, f32[4,8,16,720]{3,2,1,0:T(8,128)S(1)}, u32[]{:S(2)}) copy-start(f32[4,8,16,720]{3,2,1,0:T(8,128)S(1)} %bitcast_add_fusion.3) | copy-start | bytes 4423684
  4.1 14.9 %collective-permute-start = (f32[4,1,16,720]{3,2,1,0:T(8,128)S(1)}, f32[4,1,16,720]{3,2,1,0:T(8,128)S(1)}, u32[]{:S(2)}, u32[]{:S(2)}) collective-permute-start(f32[4,1,16,720]{3,2,1,0:T(8,128)S(1)} %get-tuple-element.28), channel_id=1, source_target_pairs={{0,1},{1,2},{2,3},{3,4},{4,5},{5,6},{6,7},{7,8},{8,9},{9,10},{10,1... | collective-permute-start | bytes 552968 | tf_op jit(solution)/shard_map/ppermute | solution.py:32
  6.8 12.2 %collective-permute-start.1 = (f32[4,1,16,720]{3,2,1,0:T(8,128)S(1)}, f32[4,1,16,720]{3,2,1,0:T(8,128)S(1)}, u32[]{:S(2)}, u32[]{:S(2)}) collective-permute-start(f32[4,1,16,720]{3,2,1,0:T(8,128)S(1)} %get-tuple-element.29), channel_id=1, source_target_pairs={{1,0},{2,1},{3,2},{4,3},{5,4},{6,5},{7,6},{8,7},{9,8},{10,9},{11,1... | collective-permute-start | bytes 552968 | tf_op jit(solution)/shard_map/ppermute | solution.py:34
  7.7 2.5 %copy-start = (bf16[10,32,64,128]{3,2,1,0:T(8,128)(2,1)S(1)}, bf16[10,32,64,128]{3,2,1,0:T(8,128)(2,1)}, u32[]{:S(2)}) copy-start(bf16[10,32,64,128]{3,2,1,0:T(8,128)(2,1)} %state_hbm.1) | copy-start | bytes 15728644
  19.3 9.5 %collective-permute-start.2 = (f32[1,10,16,720]{3,2,1,0:T(8,128)S(1)}, f32[1,10,16,720]{3,2,1,0:T(8,128)S(1)}, u32[]{:S(2)}, u32[]{:S(2)}) collective-permute-start(f32[1,10,16,720]{3,2,1,0:T(8,128)S(1)} %get-tuple-element.24), channel_id=1, source_target_pairs={{0,32},{32,64},{64,96},{96,0},{1,33},{33,65},{65,97},{97,1},{2,34}... | collective-permute-start | bytes 1382408 | tf_op jit(solution)/shard_map/ppermute | solution.py:32
  20.6 8.2 %collective-permute-start.3 = (f32[1,10,16,720]{3,2,1,0:T(8,128)S(1)}, f32[1,10,16,720]{3,2,1,0:T(8,128)S(1)}, u32[]{:S(2)}, u32[]{:S(2)}) collective-permute-start(f32[1,10,16,720]{3,2,1,0:T(8,128)S(1)} %get-tuple-element.25), channel_id=1, source_target_pairs={{32,0},{64,32},{96,64},{0,96},{33,1},{65,33},{97,65},{1,97},{34,2}... | collective-permute-start | bytes 1382408 | tf_op jit(solution)/shard_map/ppermute | solution.py:34
  31.6 1.6 %copy-start.9 = (f32[16,16,1,1]{1,0,3,2:T(8,128)S(1)}, f32[16,16,1,1]{1,0,3,2:T(8,128)}, u32[]{:S(2)}) copy-start(f32[16,16,1,1]{1,0,3,2:T(8,128)} %constant.155) | copy-start | bytes 3076
  33.2 1.5 %copy-start.5 = (f32[4,8,16,720]{3,2,1,0:T(8,128)S(1)}, f32[4,8,16,720]{3,2,1,0:T(8,128)}, u32[]{:S(2)}) copy-start(f32[4,8,16,720]{3,2,1,0:T(8,128)} %copy-done.4) | copy-start | bytes 4423684
  33.2 1.5 %copy-start.10 = (f32[16,16,1,1]{1,0,3,2:T(8,128)S(1)}, f32[16,16,1,1]{1,0,3,2:T(8,128)}, u32[]{:S(2)}) copy-start(f32[16,16,1,1]{1,0,3,2:T(8,128)} %constant.154) | copy-start | bytes 3076
  33.2 1.5 %copy-start.14 = (f32[16]{0:T(128)S(1)}, f32[16]{0:T(128)}, u32[]{:S(2)}) copy-start(f32[16]{0:T(128)} %constant.152) | copy-start | bytes 196
  34.8 8.5 %copy-start.12 = (s32[4,8,4]{1,2,0:T(4,128)S(1)}, s32[4,8,4]{1,2,0:T(4,128)}, u32[]{:S(2)}) copy-start(s32[4,8,4]{1,2,0:T(4,128)} %param.13) | copy-start | bytes 1540
  36.6 12.1 %copy-start.2 = (f32[4,8,16,720]{3,2,1,0:T(8,128)}, f32[4,8,16,720]{3,2,1,0:T(8,128)S(1)}, u32[]{:S(2)}) copy-start(f32[4,8,16,720]{3,2,1,0:T(8,128)S(1)} %bitcast_add_fusion.1) | copy-start | bytes 4423684
  36.6 9.4 %collective-permute-start.4 = (f32[4,1,16,720]{3,2,1,0:T(8,128)S(1)}, f32[4,1,16,720]{3,2,1,0:T(8,128)S(1)}, u32[]{:S(2)}, u32[]{:S(2)}) collective-permute-start(f32[4,1,16,720]{3,2,1,0:T(8,128)S(1)} %get-tuple-element.26), channel_id=1, source_target_pairs={{0,1},{1,2},{2,3},{3,4},{4,5},{5,6},{6,7},{7,8},{8,9},{9,10},{10,1... | collective-permute-start | bytes 552968 | tf_op jit(solution)/shard_map/ppermute | solution.py:32
  43.2 5.4 %collective-permute-start.5 = (f32[4,1,16,720]{3,2,1,0:T(8,128)S(1)}, f32[4,1,16,720]{3,2,1,0:T(8,128)S(1)}, u32[]{:S(2)}, u32[]{:S(2)}) collective-permute-start(f32[4,1,16,720]{3,2,1,0:T(8,128)S(1)} %get-tuple-element.27), channel_id=1, source_target_pairs={{1,0},{2,1},{3,2},{4,3},{5,4},{6,5},{7,6},{8,7},{9,8},{10,9},{11,1... | collective-permute-start | bytes 552968 | tf_op jit(solution)/shard_map/ppermute | solution.py:34
  48.7 12.1 %collective-permute-start.6 = (f32[1,10,16,720]{3,2,1,0:T(8,128)S(1)}, f32[1,10,16,720]{3,2,1,0:T(8,128)S(1)}, u32[]{:S(2)}, u32[]{:S(2)}) collective-permute-start(f32[1,10,16,720]{3,2,1,0:T(8,128)S(1)} %get-tuple-element.22), channel_id=1, source_target_pairs={{0,32},{32,64},{64,96},{96,0},{1,33},{33,65},{65,97},{97,1},{2,34}... | collective-permute-start | bytes 1382408 | tf_op jit(solution)/shard_map/ppermute | solution.py:32
  50.1 11.5 %collective-permute-start.7 = (f32[1,10,16,720]{3,2,1,0:T(8,128)S(1)}, f32[1,10,16,720]{3,2,1,0:T(8,128)}, u32[]{:S(2)}, u32[]{:S(2)}) collective-permute-start(f32[1,10,16,720]{3,2,1,0:T(8,128)S(1)} %get-tuple-element.23), channel_id=1, source_target_pairs={{32,0},{64,32},{96,64},{0,96},{33,1},{65,33},{97,65},{1,97},{34,2}... | collective-permute-start | bytes 1382408 | tf_op jit(solution)/shard_map/ppermute | solution.py:34
  60.8 0.8 copy-start.7
  66.2 1.9 %copy-start.3 = (f32[4,8,16,720]{3,2,1,0:T(8,128)S(1)}, f32[4,8,16,720]{3,2,1,0:T(8,128)}, u32[]{:S(2)}) copy-start(f32[4,8,16,720]{3,2,1,0:T(8,128)} %copy-done.2) | copy-start | bytes 4423684
  68.0 1.5 %copy-start.13 = (f32[4,16,1,1]{1,0,3,2:T(4,128)S(1)}, f32[4,16,1,1]{1,0,3,2:T(4,128)}, u32[]{:S(2)}) copy-start(f32[4,16,1,1]{1,0,3,2:T(4,128)} %constant.156) | copy-start | bytes 772
  69.6 1.6 %copy-start.6 = (f32[4,8,16,720]{3,2,1,0:T(8,128)}, f32[4,8,16,720]{3,2,1,0:T(8,128)S(1)}, u32[]{:S(2)}) copy-start(f32[4,8,16,720]{3,2,1,0:T(8,128)S(1)} %fusion) | copy-start | bytes 4423684
  71.2 1.2 copy-start.8

commit v14 on v12

--- a/solution.py
+++ b/solution.py
@@ -72,11 +72,12 @@
 
 
 ZCHUNK = 4
-
-
-def chunk_copies(src, dst, sems, count):
+BCHUNK = 2
+
+
+def chunk_copies(src, dst, sems, count, size=ZCHUNK):
     def one(c):
-        part = pl.ds(c * ZCHUNK, ZCHUNK)
+        part = pl.ds(c * size, size)
         return pltpu.make_async_copy(src.at[:, part], dst.at[:, part], sems.at[c])
 
     return [one(c) for c in range(count)]
@@ -125,9 +126,9 @@
 
 def crm_second_kernel(force_ref, live_ref, mean_ref, part_hbm, new_hbm, tend_ref, mid, out, in_sem, out_sem):
     nfld, nlev, nx, _ = mid.shape
-    chunks = nlev // ZCHUNK
-    loads = chunk_copies(part_hbm, mid, in_sem, chunks)
-    stores = chunk_copies(out, new_hbm, out_sem, chunks)
+    chunks = nlev // BCHUNK
+    loads = chunk_copies(part_hbm, mid, in_sem, chunks, BCHUNK)
+    stores = chunk_copies(out, new_hbm, out_sem, chunks, BCHUNK)
     for copy in loads:
         copy.start()
     live = live_ref[...] == 1
@@ -193,7 +194,7 @@
     for c in range(chunks):
         if c + 1 < chunks:
             loads[c + 1].wait()
-        lax.fori_loop(c * ZCHUNK, (c + 1) * ZCHUNK, ahead, 0, unroll=2)
+        lax.fori_loop(c * BCHUNK, (c + 1) * BCHUNK, ahead, 0, unroll=2)
         stores[c].start()
     for copy in stores:
         copy.wait()
@@ -223,7 +224,7 @@
 
 def crm_second(part, start_mean, forcing, active):
     nfld, nlev, nx, ncol = part.shape
-    chunks = nlev // ZCHUNK
+    chunks = nlev // BCHUNK
     return pl.pallas_call(
         crm_second_kernel,
         out_shape=(

time: 120 us -> 119 us (level)
  no operation moved by 1% of the time
where the time goes in v14:
time: 119 us
  blocking collectives  40 us (34%)
  Pallas kernels  19.9 us (17%)
  local copies, waits for them, and re-layouts  18.1 us (15%)
  starting transfers between devices  11 us (9%)
  waiting for transfers between devices  10.9 us (9%)
  matrix products  9.16 us (8%)
  other arithmetic  8.83 us (7%)
    all_to_all x2, blocking collectives, exchange(): lax.all_to_all(chunks, ('face', 'col'), split_axis=0, concat_axis=0, tile...  40 us
    pallas_call x1, Pallas kernels, crm_second(): pl.pallas_call(crm_second_kernel, out_shape=(jax.ShapeDtypeStruct(part.sh...  11.1 us
    pallas_call x1, Pallas kernels, crm_first(): pl.pallas_call(crm_first_kernel, out_shape=(jax.ShapeDtypeStruct(state.sh...  8.8 us
    ppermute x4, waiting for transfers between devices, extended_2(): lax.ppermute(tail, axis, [(i, (i + 1) % count) for i in range(count)])  7.86 us
    ppermute x4, starting transfers between devices, extended_2(): lax.ppermute(head, axis, [((i + 1) % count, i) for i in range(count)])  6.3 us
    dot_general x2, matrix products, per_device(): jnp.einsum('nm,rcmw->rcnw', laplace, state, precision=lax.Precision.HIGHEST)  5.23 us
    gather x2, local copies, waits for them, and re-layouts, per_device(): jnp.take(extended.reshape(-1, width), index_flat, axis=0)  5.19 us
    ppermute x4, starting transfers between devices, extended_2(): lax.ppermute(tail, axis, [(i, (i + 1) % count) for i in range(count)])  4.67 us
  transfers between devices with their start and end apart: 8, of which 4 were waited for; matrix products, arithmetic and copies ran while one was open for 5% of the time, Pallas kernels for 7%

profile of v14, /device:TPU:1, one launch (start us, length us, event | category | flops | bytes accessed | tf_op | source)
XLA Modules:
  0.0 119.0 jit_solution(8498210886784530396)
XLA Ops:
  0.6 3.4 %bitcast_add_fusion.3 = f32[4,8,16,720]{3,2,1,0:T(8,128)S(1)} fusion(f32[4,8,16,720]{3,2,1,0:T(8,128)} %param.11, f32[16,16,1,1]{1,0,3,2:T(8,128)} %constant.154), kind=kOutput, calls=%fused_computation.15 | convolution fusion | flops 71516160 | bytes 2950144 | tf_op jit(solution)/shard_map/nm,rcmw->rcnw/dot_general | solution.py:292
  4.2 2.2 %collective-permute-start = (f32[1,8,16,720]{3,2,1,0:T(8,128)S(1)}, f32[1,8,16,720]{3,2,1,0:T(8,128)S(1)}, u32[]{:S(2)}, u32[]{:S(2)}) collective-permute-start(f32[1,8,16,720]{3,2,1,0:T(8,128)S(1)} %get-tuple-element.28), channel_id=1, source_target_pairs={{0,32},{32,64},{64,96},{96,0},{1,33},{33,65},{65,97},{97,1},{2,34}... | collective-permute-start | bytes 1105928 | tf_op jit(solution)/shard_map/ppermute | solution.py:32
  6.4 1.5 %collective-permute-start.1 = (f32[1,8,16,720]{3,2,1,0:T(8,128)S(1)}, f32[1,8,16,720]{3,2,1,0:T(8,128)S(1)}, u32[]{:S(2)}, u32[]{:S(2)}) collective-permute-start(f32[1,8,16,720]{3,2,1,0:T(8,128)S(1)} %get-tuple-element.29), channel_id=1, source_target_pairs={{32,0},{64,32},{96,64},{0,96},{33,1},{65,33},{97,65},{1,97},{34,2}... | collective-permute-start | bytes 1105928 | tf_op jit(solution)/shard_map/ppermute | solution.py:34
  8.8 2.5 %copy-done = bf16[10,32,64,128]{3,2,1,0:T(8,128)(2,1)S(1)} copy-done((bf16[10,32,64,128]{3,2,1,0:T(8,128)(2,1)S(1)}, bf16[10,32,64,128]{3,2,1,0:T(8,128)(2,1)}, u32[]{:S(2)}) %copy-start) | copy-done | bytes 5242904
  11.3 8.8 %shard_map.112 = (f32[10,32,64,128]{3,2,1,0:T(8,128)}, f32[10,32,128]{2,1,0:T(8,128)S(1)}) custom-call(s32[1,128]{1,0:T(1,128)S(1)} %bitcast.62, bf16[10,32,64,128]{3,2,1,0:T(8,128)(2,1)S(1)} %copy-done), custom_call_target="tpu_custom_call" | custom-call | tf_op jit(solution)/shard_map/pallas_call | solution.py:206
  20.4 2.3 %collective-permute-start.2 = (f32[6,1,16,720]{3,2,1,0:T(8,128)S(1)}, f32[6,1,16,720]{3,2,1,0:T(8,128)S(1)}, u32[]{:S(2)}, u32[]{:S(2)}) collective-permute-start(f32[6,1,16,720]{3,2,1,0:T(8,128)S(1)} %get-tuple-element.22), channel_id=1, source_target_pairs={{0,1},{1,2},{2,3},{3,4},{4,5},{5,6},{6,7},{7,8},{8,9},{9,10},{10,1... | collective-permute-start | bytes 829448 | tf_op jit(solution)/shard_map/ppermute | solution.py:32
  22.7 3.6 %collective-permute-done.2 = f32[6,1,16,720]{3,2,1,0:T(8,128)S(1)} collective-permute-done((f32[6,1,16,720]{3,2,1,0:T(8,128)S(1)}, f32[6,1,16,720]{3,2,1,0:T(8,128)S(1)}, u32[]{:S(2)}, u32[]{:S(2)}) %collective-permute-start.2) | collective-permute-done | bytes 276512 | tf_op jit(solution)/shard_map/ppermute | solution.py:32
  26.3 2.8 %collective-permute-done.3 = f32[6,1,16,720]{3,2,1,0:T(8,128)S(1)} collective-permute-done((f32[6,1,16,720]{3,2,1,0:T(8,128)S(1)}, f32[6,1,16,720]{3,2,1,0:T(8,128)S(1)}, u32[]{:S(2)}, u32[]{:S(2)}) %collective-permute-start.3) | collective-permute-done | bytes 276512 | tf_op jit(solution)/shard_map/ppermute | solution.py:34
  29.4 2.6 %gather_fusion.3 = f32[512,720]{1,0:T(8,128)} fusion(f32[960,720]{1,0:T(8,128)S(1)} %bitcast.65, s32[1024]{0:T(1024)S(1)} %pad_clamp_fusion.2), kind=kCustom, calls=%fused_computation.clone | custom fusion | bytes 2951168 | tf_op jit(solution)/shard_map/jit(_take)/gather | solution.py:301
  32.0 1.6 %broadcast_select_fusion.1 = f32[512,720]{1,0:T(8,128)S(1)} fusion(f32[512,720]{1,0:T(8,128)} %gather_fusion.3, pred[512]{0:T(512)(128)(4,1)S(1)} %compare_and_fusion), kind=kLoop, calls=%fused_computation.18 | loop fusion | flops 368640 | bytes 2949632 | tf_op jit(solution)/shard_map/jit(_take)/select_n | solution.py:301
  33.7 1.5 %fusion.34 = f32[4,8,720,16]{2,3,1,0:T(8,128)S(1)} fusion(f32[4,8,16,720]{3,2,1,0:T(8,128)S(1)} %bitcast.68, f32[16,16,1,1]{1,0,3,2:T(8,128)S(1)} %copy-done.9), kind=kOutput, calls=%fused_computation.98 | convolution fusion | flops 70778880 | bytes 2950144 | tf_op jit(solution)/shard_map/nm,rcmw->rcnw/dot_general | solution.py:304
  35.2 1.8 %bitcast_add_fusion.1 = f32[4,8,16,720]{3,2,1,0:T(8,128)S(1)} fusion(f32[16,16,1,1]{1,0,3,2:T(8,128)S(1)} %copy-done.10, f32[4,8,16,720]{3,2,1,0:T(8,128)S(1)} %copy-done.5, f32[4,8,720,16]{2,3,1,0:T(8,128)S(1)} %fusion.34, f32[16]{0:T(128)S(1)} %copy-done.14), kind=kOutput, calls=%fused_computation.12 | convolution fusion | flops 72990720 | bytes 4424768 | tf_op jit(solution)/shard_map/nm,rcmw->rcnw/dot_general | solution.py:292
  37.1 2.2 %collective-permute-start.5 = (f32[4,1,16,720]{3,2,1,0:T(8,128)S(1)}, f32[4,1,16,720]{3,2,1,0:T(8,128)S(1)}, u32[]{:S(2)}, u32[]{:S(2)}) collective-permute-start(f32[4,1,16,720]{3,2,1,0:T(8,128)S(1)} %get-tuple-element.27), channel_id=1, source_target_pairs={{1,0},{2,1},{3,2},{4,3},{5,4},{6,5},{7,6},{8,7},{9,8},{10,9},{11,1... | collective-permute-start | bytes 552968 | tf_op jit(solution)/shard_map/ppermute | solution.py:34
  39.5 2.5 %sort.17 = (s32[128]{0:T(128)}, s32[128]{0:T(128)S(1)}) sort(s32[128]{0:T(128)S(1)} %reshape.88, s32[128]{0:T(128)S(1)} %iota.35), dimensions={0}, to_apply=%region_0.2 | sort | flops 896 | bytes 2048 | tf_op jit(solution)/shard_map/jit(argsort)/sort | solution.py:312
  42.5 2.6 %collective-permute-start.7 = (f32[1,10,16,720]{3,2,1,0:T(8,128)S(1)}, f32[1,10,16,720]{3,2,1,0:T(8,128)}, u32[]{:S(2)}, u32[]{:S(2)}) collective-permute-start(f32[1,10,16,720]{3,2,1,0:T(8,128)S(1)} %get-tuple-element.25), channel_id=1, source_target_pairs={{32,0},{64,32},{96,64},{0,96},{33,1},{65,33},{97,65},{1,97},{34,2}... | collective-permute-start | bytes 1382408 | tf_op jit(solution)/shard_map/ppermute | solution.py:34
  47.1 4.2 %collective-permute-done.6 = f32[1,10,16,720]{3,2,1,0:T(8,128)S(1)} collective-permute-done((f32[1,10,16,720]{3,2,1,0:T(8,128)S(1)}, f32[1,10,16,720]{3,2,1,0:T(8,128)S(1)}, u32[]{:S(2)}, u32[]{:S(2)}) %collective-permute-start.6) | collective-permute-done | bytes 460832 | tf_op jit(solution)/shard_map/ppermute | solution.py:32
  52.1 1.9 %pad_maximum_fusion.1 = f32[6,10,16,720]{3,2,1,0:T(8,128)S(1)} fusion(f32[1,10,16,720]{3,2,1,0:T(8,128)} %collective-permute-done.7, f32[4,1,16,720]{3,2,1,0:T(8,128)S(1)} %collective-permute-done.5, f32[4,8,16,720]{3,2,1,0:T(8,128)} %copy-done.2, f32[4,1,16,720]{3,2,1,0:T(8,128)S(1)} %collective-permute-done.4, f32[1,10,16,720]{3,2,1,0:T(8,128)} %copy-done.7), kind=kLoop, calls=%fused_computation.8 | loop fusion | flops 2764800 | bytes 5529600 | tf_op jit(solution)/shard_map/concatenate | solution.py:30
  54.0 2.6 %gather_fusion.4 = f32[512,720]{1,0:T(8,128)} fusion(f32[960,720]{1,0:T(8,128)S(1)} %bitcast.64, s32[1024]{0:T(1024)S(1)} %pad_clamp_fusion.2), kind=kCustom, calls=%fused_computation.1.clone | custom fusion | bytes 2951168 | tf_op jit(solution)/shard_map/jit(_take)/gather | solution.py:301
  56.6 1.7 %broadcast_select_fusion = f32[512,720]{1,0:T(8,128)S(1)} fusion(f32[512,720]{1,0:T(8,128)} %gather_fusion.4, pred[512]{0:T(512)(128)(4,1)S(1)} %compare_and_fusion), kind=kLoop, calls=%fused_computation.17 | loop fusion | flops 368640 | bytes 2949632 | tf_op jit(solution)/shard_map/jit(_take)/select_n | solution.py:301
  58.5 1.5 %fusion = f32[4,8,16,720]{3,2,1,0:T(8,128)S(1)} fusion(f32[4,8,16,720]{3,2,1,0:T(8,128)S(1)} %copy-done.3, f32[4,8,16,720]{3,2,1,0:T(8,128)S(1)} %bitcast.67, f32[16,16,1,1]{1,0,3,2:T(8,128)S(1)} %copy-done.9, f32[16]{0:T(128)S(1)} %copy-done.14), kind=kOutput, calls=%fused_computation.11 | convolution fusion | flops 71516160 | bytes 4424768 | tf_op jit(solution)/shard_map/nm,rcmw->rcnw/dot_general | solution.py:304
  63.2 25.4 %all_to_all.10 = f32[128,1,321]{2,1,0:T(1,128)S(1)} all-to-all(f32[128,1,321]{2,1,0:T(1,128)S(1)} %copy.50), channel_id=1, replica_groups=mesh['face'=4,'col'=32] {'face','col'}, dimensions={0} | all-to-all | bytes 328704 | tf_op jit(solution)/shard_map/all_to_all | solution.py:261
  88.9 1.3 %scatter_custom_fusion = f32[128,320]{1,0:T(8,128)S(1)} fusion(s32[128]{0:T(128)S(1)} %fusion.30, f32[128,320]{1,0:T(8,128)S(1)} %copy.52, f32[]{:T(128)} %constant.142.clone.1), kind=kCustom, calls=%fused_computation.28 | custom fusion | bytes 163844 | tf_op jit(solution)/shard_map/scatter | solution.py:319
  90.3 11.1 %shard_map.113 = (bf16[10,32,64,128]{3,2,1,0:T(8,128)(2,1)}, f32[10,32,128]{2,1,0:T(8,128)S(1)}) custom-call(f32[10,32,128]{2,1,0:T(8,128)S(1)} %bitcast.60, s32[1,128]{1,0:T(1,128)S(1)} %bitcast.63, f32[10,32,128]{2,1,0:T(8,128)S(1)} %get-tuple-element.16.mean_ref, f32[10,32,64,128]{3,2,1,0:T(8,128)} %get-tuple-element.17.part_hbm), custom_call_target="tpu_custom_call" | custom-call | tf_op jit(solution)/shard_map/pallas_call | solution.py:228
  102.5 14.6 %all_to_all.11 = f32[128,1,320]{2,1,0:T(1,128)S(1)} all-to-all(f32[128,1,320]{2,1,0:T(1,128)S(1)} %copy.55), channel_id=1, replica_groups=mesh['face'=4,'col'=32] {'face','col'}, dimensions={0} | all-to-all | bytes 327680 | tf_op jit(solution)/shard_map/all_to_all | solution.py:261
  (84 shorter events, 11.6 us)
Async XLA Ops:
  4.1 16.0 %copy-start.4 = (f32[4,8,16,720]{3,2,1,0:T(8,128)}, f32[4,8,16,720]{3,2,1,0:T(8,128)S(1)}, u32[]{:S(2)}) copy-start(f32[4,8,16,720]{3,2,1,0:T(8,128)S(1)} %bitcast_add_fusion.3) | copy-start | bytes 4423684
  4.1 3.8 %copy-start.11 = (s32[4,8,4]{1,2,0:T(4,128)S(1)}, s32[4,8,4]{1,2,0:T(4,128)}, u32[]{:S(2)}) copy-start(s32[4,8,4]{1,2,0:T(4,128)} %param.12) | copy-start | bytes 1540
  4.1 4.7 %copy-start.1 = (s32[128]{0:T(128)S(1)}, s32[128]{0:T(128)}, u32[]{:S(2)}) copy-start(s32[128]{0:T(128)} %param.14) | copy-start | bytes 1540
  4.2 15.9 %collective-permute-start = (f32[1,8,16,720]{3,2,1,0:T(8,128)S(1)}, f32[1,8,16,720]{3,2,1,0:T(8,128)S(1)}, u32[]{:S(2)}, u32[]{:S(2)}) collective-permute-start(f32[1,8,16,720]{3,2,1,0:T(8,128)S(1)} %get-tuple-element.28), channel_id=1, source_target_pairs={{0,32},{32,64},{64,96},{96,0},{1,33},{33,65},{65,97},{97,1},{2,34}... | collective-permute-start | bytes 1105928 | tf_op jit(solution)/shard_map/ppermute | solution.py:32
  6.4 13.7 %collective-permute-start.1 = (f32[1,8,16,720]{3,2,1,0:T(8,128)S(1)}, f32[1,8,16,720]{3,2,1,0:T(8,128)S(1)}, u32[]{:S(2)}, u32[]{:S(2)}) collective-permute-start(f32[1,8,16,720]{3,2,1,0:T(8,128)S(1)} %get-tuple-element.29), channel_id=1, source_target_pairs={{32,0},{64,32},{96,64},{0,96},{33,1},{65,33},{97,65},{1,97},{34,2}... | collective-permute-start | bytes 1105928 | tf_op jit(solution)/shard_map/ppermute | solution.py:34
  8.8 2.5 %copy-start = (bf16[10,32,64,128]{3,2,1,0:T(8,128)(2,1)S(1)}, bf16[10,32,64,128]{3,2,1,0:T(8,128)(2,1)}, u32[]{:S(2)}) copy-start(bf16[10,32,64,128]{3,2,1,0:T(8,128)(2,1)} %state_hbm.1) | copy-start | bytes 15728644
  20.4 5.9 %collective-permute-start.2 = (f32[6,1,16,720]{3,2,1,0:T(8,128)S(1)}, f32[6,1,16,720]{3,2,1,0:T(8,128)S(1)}, u32[]{:S(2)}, u32[]{:S(2)}) collective-permute-start(f32[6,1,16,720]{3,2,1,0:T(8,128)S(1)} %get-tuple-element.22), channel_id=1, source_target_pairs={{0,1},{1,2},{2,3},{3,4},{4,5},{5,6},{6,7},{7,8},{8,9},{9,10},{10,1... | collective-permute-start | bytes 829448 | tf_op jit(solution)/shard_map/ppermute | solution.py:32
  22.7 6.4 %collective-permute-start.3 = (f32[6,1,16,720]{3,2,1,0:T(8,128)S(1)}, f32[6,1,16,720]{3,2,1,0:T(8,128)S(1)}, u32[]{:S(2)}, u32[]{:S(2)}) collective-permute-start(f32[6,1,16,720]{3,2,1,0:T(8,128)S(1)} %get-tuple-element.23), channel_id=1, source_target_pairs={{1,0},{2,1},{3,2},{4,3},{5,4},{6,5},{7,6},{8,7},{9,8},{10,9},{11,1... | collective-permute-start | bytes 829448 | tf_op jit(solution)/shard_map/ppermute | solution.py:34
  32.0 1.6 %copy-start.9 = (f32[16,16,1,1]{1,0,3,2:T(8,128)S(1)}, f32[16,16,1,1]{1,0,3,2:T(8,128)}, u32[]{:S(2)}) copy-start(f32[16,16,1,1]{1,0,3,2:T(8,128)} %constant.155) | copy-start | bytes 3076
  33.6 1.5 %copy-start.5 = (f32[4,8,16,720]{3,2,1,0:T(8,128)S(1)}, f32[4,8,16,720]{3,2,1,0:T(8,128)}, u32[]{:S(2)}) copy-start(f32[4,8,16,720]{3,2,1,0:T(8,128)} %copy-done.4) | copy-start | bytes 4423684
  33.6 1.5 %copy-start.10 = (f32[16,16,1,1]{1,0,3,2:T(8,128)S(1)}, f32[16,16,1,1]{1,0,3,2:T(8,128)}, u32[]{:S(2)}) copy-start(f32[16,16,1,1]{1,0,3,2:T(8,128)} %constant.154) | copy-start | bytes 3076
  33.7 1.5 %copy-start.14 = (f32[16]{0:T(128)S(1)}, f32[16]{0:T(128)}, u32[]{:S(2)}) copy-start(f32[16]{0:T(128)} %constant.152) | copy-start | bytes 196
  35.2 4.1 %copy-start.12 = (s32[4,8,4]{1,2,0:T(4,128)S(1)}, s32[4,8,4]{1,2,0:T(4,128)}, u32[]{:S(2)}) copy-start(s32[4,8,4]{1,2,0:T(4,128)} %param.13) | copy-start | bytes 1540
  37.0 5.4 %copy-start.2 = (f32[4,8,16,720]{3,2,1,0:T(8,128)}, f32[4,8,16,720]{3,2,1,0:T(8,128)S(1)}, u32[]{:S(2)}) copy-start(f32[4,8,16,720]{3,2,1,0:T(8,128)S(1)} %bitcast_add_fusion.1) | copy-start | bytes 4423684
  37.0 5.0 %collective-permute-start.4 = (f32[4,1,16,720]{3,2,1,0:T(8,128)S(1)}, f32[4,1,16,720]{3,2,1,0:T(8,128)S(1)}, u32[]{:S(2)}, u32[]{:S(2)}) collective-permute-start(f32[4,1,16,720]{3,2,1,0:T(8,128)S(1)} %get-tuple-element.26), channel_id=1, source_target_pairs={{0,1},{1,2},{2,3},{3,4},{4,5},{5,6},{6,7},{7,8},{8,9},{9,10},{10,1... | collective-permute-start | bytes 552968 | tf_op jit(solution)/shard_map/ppermute | solution.py:32
  37.1 5.2 %collective-permute-start.5 = (f32[4,1,16,720]{3,2,1,0:T(8,128)S(1)}, f32[4,1,16,720]{3,2,1,0:T(8,128)S(1)}, u32[]{:S(2)}, u32[]{:S(2)}) collective-permute-start(f32[4,1,16,720]{3,2,1,0:T(8,128)S(1)} %get-tuple-element.27), channel_id=1, source_target_pairs={{1,0},{2,1},{3,2},{4,3},{5,4},{6,5},{7,6},{8,7},{9,8},{10,9},{11,1... | collective-permute-start | bytes 552968 | tf_op jit(solution)/shard_map/ppermute | solution.py:34
  42.4 9.0 %collective-permute-start.6 = (f32[1,10,16,720]{3,2,1,0:T(8,128)S(1)}, f32[1,10,16,720]{3,2,1,0:T(8,128)S(1)}, u32[]{:S(2)}, u32[]{:S(2)}) collective-permute-start(f32[1,10,16,720]{3,2,1,0:T(8,128)S(1)} %get-tuple-element.24), channel_id=1, source_target_pairs={{0,32},{32,64},{64,96},{96,0},{1,33},{33,65},{65,97},{97,1},{2,34}... | collective-permute-start | bytes 1382408 | tf_op jit(solution)/shard_map/ppermute | solution.py:32
  42.5 9.6 %collective-permute-start.7 = (f32[1,10,16,720]{3,2,1,0:T(8,128)S(1)}, f32[1,10,16,720]{3,2,1,0:T(8,128)}, u32[]{:S(2)}, u32[]{:S(2)}) collective-permute-start(f32[1,10,16,720]{3,2,1,0:T(8,128)S(1)} %get-tuple-element.25), channel_id=1, source_target_pairs={{32,0},{64,32},{96,64},{0,96},{33,1},{65,33},{97,65},{1,97},{34,2}... | collective-permute-start | bytes 1382408 | tf_op jit(solution)/shard_map/ppermute | solution.py:34
  51.3 0.8 copy-start.7
  56.6 1.9 %copy-start.3 = (f32[4,8,16,720]{3,2,1,0:T(8,128)S(1)}, f32[4,8,16,720]{3,2,1,0:T(8,128)}, u32[]{:S(2)}) copy-start(f32[4,8,16,720]{3,2,1,0:T(8,128)} %copy-done.2) | copy-start | bytes 4423684
  58.5 1.5 %copy-start.13 = (f32[4,16,1,1]{1,0,3,2:T(4,128)S(1)}, f32[4,16,1,1]{1,0,3,2:T(4,128)}, u32[]{:S(2)}) copy-start(f32[4,16,1,1]{1,0,3,2:T(4,128)} %constant.156) | copy-start | bytes 772
  60.1 1.6 %copy-start.6 = (f32[4,8,16,720]{3,2,1,0:T(8,128)}, f32[4,8,16,720]{3,2,1,0:T(8,128)S(1)}, u32[]{:S(2)}) copy-start(f32[4,8,16,720]{3,2,1,0:T(8,128)S(1)} %fusion) | copy-start | bytes 4423684
  61.6 1.2 %copy-start.8 = (f32[128,1]{1,0:T(8,128)S(1)}, f32[128,1]{1,0:T(8,128)}, u32[]{:S(2)}) copy-start(f32[128,1]{1,0:T(8,128)} %copy.49) | copy-start | bytes 1540

commit v15 on v14

--- a/solution.py
+++ b/solution.py
@@ -71,7 +71,7 @@
     return base[..., None] + stride[..., None] * along
 
 
-ZCHUNK = 4
+ZCHUNK = 2
 BCHUNK = 2
 
 

time: 119 us -> 119 us (level)
  no operation moved by 1% of the time
where the time goes in v15:
time: 119 us
  blocking collectives  40 us (34%)
  Pallas kernels  19.8 us (17%)
  local copies, waits for them, and re-layouts  17.9 us (15%)
  starting transfers between devices  11.1 us (9%)
  waiting for transfers between devices  10.8 us (9%)
  matrix products  9.16 us (8%)
  other arithmetic  8.83 us (7%)
    all_to_all x2, blocking collectives, exchange(): lax.all_to_all(chunks, ('face', 'col'), split_axis=0, concat_axis=0, tile...  40 us
    pallas_call x1, Pallas kernels, crm_second(): pl.pallas_call(crm_second_kernel, out_shape=(jax.ShapeDtypeStruct(part.sh...  11.1 us
    pallas_call x1, Pallas kernels, crm_first(): pl.pallas_call(crm_first_kernel, out_shape=(jax.ShapeDtypeStruct(state.sh...  8.72 us
    ppermute x4, waiting for transfers between devices, extended_2(): lax.ppermute(tail, axis, [(i, (i + 1) % count) for i in range(count)])  7.86 us
    ppermute x4, starting transfers between devices, extended_2(): lax.ppermute(head, axis, [((i + 1) % count, i) for i in range(count)])  6.4 us
    dot_general x2, matrix products, per_device(): jnp.einsum('nm,rcmw->rcnw', laplace, state, precision=lax.Precision.HIGHEST)  5.23 us
    gather x2, local copies, waits for them, and re-layouts, per_device(): jnp.take(extended.reshape(-1, width), index_flat, axis=0)  5.19 us
    ppermute x4, starting transfers between devices, extended_2(): lax.ppermute(tail, axis, [(i, (i + 1) % count) for i in range(count)])  4.67 us
  transfers between devices with their start and end apart: 8, of which 4 were waited for; matrix products, arithmetic and copies ran while one was open for 5% of the time, Pallas kernels for 7%

profile of v15, /device:TPU:1, one launch (start us, length us, event | category | flops | bytes accessed | tf_op | source)
XLA Modules:
  0.0 118.7 jit_solution(4192094751522614263)
XLA Ops:
  0.6 3.4 %bitcast_add_fusion.3 = f32[4,8,16,720]{3,2,1,0:T(8,128)S(1)} fusion(f32[4,8,16,720]{3,2,1,0:T(8,128)} %param.11, f32[16,16,1,1]{1,0,3,2:T(8,128)} %constant.154), kind=kOutput, calls=%fused_computation.15 | convolution fusion | flops 71516160 | bytes 2950144 | tf_op jit(solution)/shard_map/nm,rcmw->rcnw/dot_general | solution.py:292
  4.2 2.2 %collective-permute-start = (f32[1,8,16,720]{3,2,1,0:T(8,128)S(1)}, f32[1,8,16,720]{3,2,1,0:T(8,128)S(1)}, u32[]{:S(2)}, u32[]{:S(2)}) collective-permute-start(f32[1,8,16,720]{3,2,1,0:T(8,128)S(1)} %get-tuple-element.28), channel_id=1, source_target_pairs={{0,32},{32,64},{64,96},{96,0},{1,33},{33,65},{65,97},{97,1},{2,34}... | collective-permute-start | bytes 1105928 | tf_op jit(solution)/shard_map/ppermute | solution.py:32
  6.4 1.5 %collective-permute-start.1 = (f32[1,8,16,720]{3,2,1,0:T(8,128)S(1)}, f32[1,8,16,720]{3,2,1,0:T(8,128)S(1)}, u32[]{:S(2)}, u32[]{:S(2)}) collective-permute-start(f32[1,8,16,720]{3,2,1,0:T(8,128)S(1)} %get-tuple-element.29), channel_id=1, source_target_pairs={{32,0},{64,32},{96,64},{0,96},{33,1},{65,33},{97,65},{1,97},{34,2}... | collective-permute-start | bytes 1105928 | tf_op jit(solution)/shard_map/ppermute | solution.py:34
  8.8 2.5 %copy-done = bf16[10,32,64,128]{3,2,1,0:T(8,128)(2,1)S(1)} copy-done((bf16[10,32,64,128]{3,2,1,0:T(8,128)(2,1)S(1)}, bf16[10,32,64,128]{3,2,1,0:T(8,128)(2,1)}, u32[]{:S(2)}) %copy-start) | copy-done | bytes 5242904
  11.3 8.7 %shard_map.112 = (f32[10,32,64,128]{3,2,1,0:T(8,128)}, f32[10,32,128]{2,1,0:T(8,128)S(1)}) custom-call(s32[1,128]{1,0:T(1,128)S(1)} %bitcast.62, bf16[10,32,64,128]{3,2,1,0:T(8,128)(2,1)S(1)} %copy-done), custom_call_target="tpu_custom_call" | custom-call | tf_op jit(solution)/shard_map/pallas_call | solution.py:206
  20.3 2.3 %collective-permute-start.2 = (f32[6,1,16,720]{3,2,1,0:T(8,128)S(1)}, f32[6,1,16,720]{3,2,1,0:T(8,128)S(1)}, u32[]{:S(2)}, u32[]{:S(2)}) collective-permute-start(f32[6,1,16,720]{3,2,1,0:T(8,128)S(1)} %get-tuple-element.22), channel_id=1, source_target_pairs={{0,1},{1,2},{2,3},{3,4},{4,5},{5,6},{6,7},{7,8},{8,9},{9,10},{10,1... | collective-permute-start | bytes 829448 | tf_op jit(solution)/shard_map/ppermute | solution.py:32
  22.6 3.6 %collective-permute-done.2 = f32[6,1,16,720]{3,2,1,0:T(8,128)S(1)} collective-permute-done((f32[6,1,16,720]{3,2,1,0:T(8,128)S(1)}, f32[6,1,16,720]{3,2,1,0:T(8,128)S(1)}, u32[]{:S(2)}, u32[]{:S(2)}) %collective-permute-start.2) | collective-permute-done | bytes 276512 | tf_op jit(solution)/shard_map/ppermute | solution.py:32
  26.3 2.8 %collective-permute-done.3 = f32[6,1,16,720]{3,2,1,0:T(8,128)S(1)} collective-permute-done((f32[6,1,16,720]{3,2,1,0:T(8,128)S(1)}, f32[6,1,16,720]{3,2,1,0:T(8,128)S(1)}, u32[]{:S(2)}, u32[]{:S(2)}) %collective-permute-start.3) | collective-permute-done | bytes 276512 | tf_op jit(solution)/shard_map/ppermute | solution.py:34
  29.3 2.6 %gather_fusion.3 = f32[512,720]{1,0:T(8,128)} fusion(f32[960,720]{1,0:T(8,128)S(1)} %bitcast.65, s32[1024]{0:T(1024)S(1)} %pad_clamp_fusion.2), kind=kCustom, calls=%fused_computation.clone | custom fusion | bytes 2951168 | tf_op jit(solution)/shard_map/jit(_take)/gather | solution.py:301
  31.9 1.6 %broadcast_select_fusion.1 = f32[512,720]{1,0:T(8,128)S(1)} fusion(f32[512,720]{1,0:T(8,128)} %gather_fusion.3, pred[512]{0:T(512)(128)(4,1)S(1)} %compare_and_fusion), kind=kLoop, calls=%fused_computation.18 | loop fusion | flops 368640 | bytes 2949632 | tf_op jit(solution)/shard_map/jit(_take)/select_n | solution.py:301
  33.6 1.5 %fusion.34 = f32[4,8,720,16]{2,3,1,0:T(8,128)S(1)} fusion(f32[4,8,16,720]{3,2,1,0:T(8,128)S(1)} %bitcast.68, f32[16,16,1,1]{1,0,3,2:T(8,128)S(1)} %copy-done.9), kind=kOutput, calls=%fused_computation.98 | convolution fusion | flops 70778880 | bytes 2950144 | tf_op jit(solution)/shard_map/nm,rcmw->rcnw/dot_general | solution.py:304
  35.1 1.8 %bitcast_add_fusion.1 = f32[4,8,16,720]{3,2,1,0:T(8,128)S(1)} fusion(f32[16,16,1,1]{1,0,3,2:T(8,128)S(1)} %copy-done.10, f32[4,8,16,720]{3,2,1,0:T(8,128)S(1)} %copy-done.5, f32[4,8,720,16]{2,3,1,0:T(8,128)S(1)} %fusion.34, f32[16]{0:T(128)S(1)} %copy-done.14), kind=kOutput, calls=%fused_computation.12 | convolution fusion | flops 72990720 | bytes 4424768 | tf_op jit(solution)/shard_map/nm,rcmw->rcnw/dot_general | solution.py:292
  37.0 2.3 %collective-permute-start.5 = (f32[4,1,16,720]{3,2,1,0:T(8,128)S(1)}, f32[4,1,16,720]{3,2,1,0:T(8,128)S(1)}, u32[]{:S(2)}, u32[]{:S(2)}) collective-permute-start(f32[4,1,16,720]{3,2,1,0:T(8,128)S(1)} %get-tuple-element.27), channel_id=1, source_target_pairs={{1,0},{2,1},{3,2},{4,3},{5,4},{6,5},{7,6},{8,7},{9,8},{10,9},{11,1... | collective-permute-start | bytes 552968 | tf_op jit(solution)/shard_map/ppermute | solution.py:34
  39.5 2.5 %sort.17 = (s32[128]{0:T(128)}, s32[128]{0:T(128)S(1)}) sort(s32[128]{0:T(128)S(1)} %reshape.88, s32[128]{0:T(128)S(1)} %iota.35), dimensions={0}, to_apply=%region_0.2 | sort | flops 896 | bytes 2048 | tf_op jit(solution)/shard_map/jit(argsort)/sort | solution.py:312
  42.4 2.6 %collective-permute-start.7 = (f32[1,10,16,720]{3,2,1,0:T(8,128)S(1)}, f32[1,10,16,720]{3,2,1,0:T(8,128)}, u32[]{:S(2)}, u32[]{:S(2)}) collective-permute-start(f32[1,10,16,720]{3,2,1,0:T(8,128)S(1)} %get-tuple-element.25), channel_id=1, source_target_pairs={{32,0},{64,32},{96,64},{0,96},{33,1},{65,33},{97,65},{1,97},{34,2}... | collective-permute-start | bytes 1382408 | tf_op jit(solution)/shard_map/ppermute | solution.py:34
  45.0 1.2 %gather_fusion.1 = s32[128]{0:T(128)S(1)} fusion(s32[128]{0:T(128)S(1)} %reshape.88, s32[1024]{0:T(1024)S(1)} %pad_clamp_fusion.1), kind=kCustom, calls=%fused_computation.3 | custom fusion | bytes 1536 | tf_op jit(solution)/shard_map/gather | solution.py:313
  47.0 4.2 %collective-permute-done.6 = f32[1,10,16,720]{3,2,1,0:T(8,128)S(1)} collective-permute-done((f32[1,10,16,720]{3,2,1,0:T(8,128)S(1)}, f32[1,10,16,720]{3,2,1,0:T(8,128)S(1)}, u32[]{:S(2)}, u32[]{:S(2)}) %collective-permute-start.6) | collective-permute-done | bytes 460832 | tf_op jit(solution)/shard_map/ppermute | solution.py:32
  52.0 1.9 %pad_maximum_fusion.1 = f32[6,10,16,720]{3,2,1,0:T(8,128)S(1)} fusion(f32[1,10,16,720]{3,2,1,0:T(8,128)} %collective-permute-done.7, f32[4,1,16,720]{3,2,1,0:T(8,128)S(1)} %collective-permute-done.5, f32[4,8,16,720]{3,2,1,0:T(8,128)} %copy-done.2, f32[4,1,16,720]{3,2,1,0:T(8,128)S(1)} %collective-permute-done.4, f32[1,10,16,720]{3,2,1,0:T(8,128)} %copy-done.7), kind=kLoop, calls=%fused_computation.8 | loop fusion | flops 2764800 | bytes 5529600 | tf_op jit(solution)/shard_map/concatenate | solution.py:30
  54.0 2.6 %gather_fusion.4 = f32[512,720]{1,0:T(8,128)} fusion(f32[960,720]{1,0:T(8,128)S(1)} %bitcast.64, s32[1024]{0:T(1024)S(1)} %pad_clamp_fusion.2), kind=kCustom, calls=%fused_computation.1.clone | custom fusion | bytes 2951168 | tf_op jit(solution)/shard_map/jit(_take)/gather | solution.py:301
  56.6 1.7 %broadcast_select_fusion = f32[512,720]{1,0:T(8,128)S(1)} fusion(f32[512,720]{1,0:T(8,128)} %gather_fusion.4, pred[512]{0:T(512)(128)(4,1)S(1)} %compare_and_fusion), kind=kLoop, calls=%fused_computation.17 | loop fusion | flops 368640 | bytes 2949632 | tf_op jit(solution)/shard_map/jit(_take)/select_n | solution.py:301
  58.4 1.5 %fusion = f32[4,8,16,720]{3,2,1,0:T(8,128)S(1)} fusion(f32[4,8,16,720]{3,2,1,0:T(8,128)S(1)} %copy-done.3, f32[4,8,16,720]{3,2,1,0:T(8,128)S(1)} %bitcast.67, f32[16,16,1,1]{1,0,3,2:T(8,128)S(1)} %copy-done.9, f32[16]{0:T(128)S(1)} %copy-done.14), kind=kOutput, calls=%fused_computation.11 | convolution fusion | flops 71516160 | bytes 4424768 | tf_op jit(solution)/shard_map/nm,rcmw->rcnw/dot_general | solution.py:304
  63.1 25.4 %all_to_all.10 = f32[128,1,321]{2,1,0:T(1,128)S(1)} all-to-all(f32[128,1,321]{2,1,0:T(1,128)S(1)} %copy.50), channel_id=1, replica_groups=mesh['face'=4,'col'=32] {'face','col'}, dimensions={0} | all-to-all | bytes 328704 | tf_op jit(solution)/shard_map/all_to_all | solution.py:261
  90.0 11.1 %shard_map.113 = (bf16[10,32,64,128]{3,2,1,0:T(8,128)(2,1)}, f32[10,32,128]{2,1,0:T(8,128)S(1)}) custom-call(f32[10,32,128]{2,1,0:T(8,128)S(1)} %bitcast.60, s32[1,128]{1,0:T(1,128)S(1)} %bitcast.63, f32[10,32,128]{2,1,0:T(8,128)S(1)} %get-tuple-element.16.mean_ref, f32[10,32,64,128]{3,2,1,0:T(8,128)} %get-tuple-element.17.part_hbm), custom_call_target="tpu_custom_call" | custom-call | tf_op jit(solution)/shard_map/pallas_call | solution.py:228
  102.2 14.6 %all_to_all.11 = f32[128,1,320]{2,1,0:T(1,128)S(1)} all-to-all(f32[128,1,320]{2,1,0:T(1,128)S(1)} %copy.55), channel_id=1, replica_groups=mesh['face'=4,'col'=32] {'face','col'}, dimensions={0} | all-to-all | bytes 327680 | tf_op jit(solution)/shard_map/all_to_all | solution.py:261
  (84 shorter events, 11.4 us)
Async XLA Ops:
  4.1 15.9 %copy-start.4 = (f32[4,8,16,720]{3,2,1,0:T(8,128)}, f32[4,8,16,720]{3,2,1,0:T(8,128)S(1)}, u32[]{:S(2)}) copy-start(f32[4,8,16,720]{3,2,1,0:T(8,128)S(1)} %bitcast_add_fusion.3) | copy-start | bytes 4423684
  4.1 3.8 %copy-start.11 = (s32[4,8,4]{1,2,0:T(4,128)S(1)}, s32[4,8,4]{1,2,0:T(4,128)}, u32[]{:S(2)}) copy-start(s32[4,8,4]{1,2,0:T(4,128)} %param.12) | copy-start | bytes 1540
  4.1 4.7 %copy-start.1 = (s32[128]{0:T(128)S(1)}, s32[128]{0:T(128)}, u32[]{:S(2)}) copy-start(s32[128]{0:T(128)} %param.14) | copy-start | bytes 1540
  4.2 15.8 %collective-permute-start = (f32[1,8,16,720]{3,2,1,0:T(8,128)S(1)}, f32[1,8,16,720]{3,2,1,0:T(8,128)S(1)}, u32[]{:S(2)}, u32[]{:S(2)}) collective-permute-start(f32[1,8,16,720]{3,2,1,0:T(8,128)S(1)} %get-tuple-element.28), channel_id=1, source_target_pairs={{0,32},{32,64},{64,96},{96,0},{1,33},{33,65},{65,97},{97,1},{2,34}... | collective-permute-start | bytes 1105928 | tf_op jit(solution)/shard_map/ppermute | solution.py:32
  6.4 13.7 %collective-permute-start.1 = (f32[1,8,16,720]{3,2,1,0:T(8,128)S(1)}, f32[1,8,16,720]{3,2,1,0:T(8,128)S(1)}, u32[]{:S(2)}, u32[]{:S(2)}) collective-permute-start(f32[1,8,16,720]{3,2,1,0:T(8,128)S(1)} %get-tuple-element.29), channel_id=1, source_target_pairs={{32,0},{64,32},{96,64},{0,96},{33,1},{65,33},{97,65},{1,97},{34,2}... | collective-permute-start | bytes 1105928 | tf_op jit(solution)/shard_map/ppermute | solution.py:34
  8.8 2.5 %copy-start = (bf16[10,32,64,128]{3,2,1,0:T(8,128)(2,1)S(1)}, bf16[10,32,64,128]{3,2,1,0:T(8,128)(2,1)}, u32[]{:S(2)}) copy-start(bf16[10,32,64,128]{3,2,1,0:T(8,128)(2,1)} %state_hbm.1) | copy-start | bytes 15728644
  20.3 5.9 %collective-permute-start.2 = (f32[6,1,16,720]{3,2,1,0:T(8,128)S(1)}, f32[6,1,16,720]{3,2,1,0:T(8,128)S(1)}, u32[]{:S(2)}, u32[]{:S(2)}) collective-permute-start(f32[6,1,16,720]{3,2,1,0:T(8,128)S(1)} %get-tuple-element.22), channel_id=1, source_target_pairs={{0,1},{1,2},{2,3},{3,4},{4,5},{5,6},{6,7},{7,8},{8,9},{9,10},{10,1... | collective-permute-start | bytes 829448 | tf_op jit(solution)/shard_map/ppermute | solution.py:32
  22.6 6.4 %collective-permute-start.3 = (f32[6,1,16,720]{3,2,1,0:T(8,128)S(1)}, f32[6,1,16,720]{3,2,1,0:T(8,128)S(1)}, u32[]{:S(2)}, u32[]{:S(2)}) collective-permute-start(f32[6,1,16,720]{3,2,1,0:T(8,128)S(1)} %get-tuple-element.23), channel_id=1, source_target_pairs={{1,0},{2,1},{3,2},{4,3},{5,4},{6,5},{7,6},{8,7},{9,8},{10,9},{11,1... | collective-permute-start | bytes 829448 | tf_op jit(solution)/shard_map/ppermute | solution.py:34
  31.9 1.6 %copy-start.9 = (f32[16,16,1,1]{1,0,3,2:T(8,128)S(1)}, f32[16,16,1,1]{1,0,3,2:T(8,128)}, u32[]{:S(2)}) copy-start(f32[16,16,1,1]{1,0,3,2:T(8,128)} %constant.155) | copy-start | bytes 3076
  33.6 1.5 %copy-start.5 = (f32[4,8,16,720]{3,2,1,0:T(8,128)S(1)}, f32[4,8,16,720]{3,2,1,0:T(8,128)}, u32[]{:S(2)}) copy-start(f32[4,8,16,720]{3,2,1,0:T(8,128)} %copy-done.4) | copy-start | bytes 4423684
  33.6 1.5 %copy-start.10 = (f32[16,16,1,1]{1,0,3,2:T(8,128)S(1)}, f32[16,16,1,1]{1,0,3,2:T(8,128)}, u32[]{:S(2)}) copy-start(f32[16,16,1,1]{1,0,3,2:T(8,128)} %constant.154) | copy-start | bytes 3076
  33.6 1.5 %copy-start.14 = (f32[16]{0:T(128)S(1)}, f32[16]{0:T(128)}, u32[]{:S(2)}) copy-start(f32[16]{0:T(128)} %constant.152) | copy-start | bytes 196
  35.1 4.2 %copy-start.12 = (s32[4,8,4]{1,2,0:T(4,128)S(1)}, s32[4,8,4]{1,2,0:T(4,128)}, u32[]{:S(2)}) copy-start(s32[4,8,4]{1,2,0:T(4,128)} %param.13) | copy-start | bytes 1540
  36.9 5.4 %copy-start.2 = (f32[4,8,16,720]{3,2,1,0:T(8,128)}, f32[4,8,16,720]{3,2,1,0:T(8,128)S(1)}, u32[]{:S(2)}) copy-start(f32[4,8,16,720]{3,2,1,0:T(8,128)S(1)} %bitcast_add_fusion.1) | copy-start | bytes 4423684
  36.9 5.1 %collective-permute-start.4 = (f32[4,1,16,720]{3,2,1,0:T(8,128)S(1)}, f32[4,1,16,720]{3,2,1,0:T(8,128)S(1)}, u32[]{:S(2)}, u32[]{:S(2)}) collective-permute-start(f32[4,1,16,720]{3,2,1,0:T(8,128)S(1)} %get-tuple-element.26), channel_id=1, source_target_pairs={{0,1},{1,2},{2,3},{3,4},{4,5},{5,6},{6,7},{7,8},{8,9},{9,10},{10,1... | collective-permute-start | bytes 552968 | tf_op jit(solution)/shard_map/ppermute | solution.py:32
  37.0 5.2 %collective-permute-start.5 = (f32[4,1,16,720]{3,2,1,0:T(8,128)S(1)}, f32[4,1,16,720]{3,2,1,0:T(8,128)S(1)}, u32[]{:S(2)}, u32[]{:S(2)}) collective-permute-start(f32[4,1,16,720]{3,2,1,0:T(8,128)S(1)} %get-tuple-element.27), channel_id=1, source_target_pairs={{1,0},{2,1},{3,2},{4,3},{5,4},{6,5},{7,6},{8,7},{9,8},{10,9},{11,1... | collective-permute-start | bytes 552968 | tf_op jit(solution)/shard_map/ppermute | solution.py:34
  42.3 9.0 %collective-permute-start.6 = (f32[1,10,16,720]{3,2,1,0:T(8,128)S(1)}, f32[1,10,16,720]{3,2,1,0:T(8,128)S(1)}, u32[]{:S(2)}, u32[]{:S(2)}) collective-permute-start(f32[1,10,16,720]{3,2,1,0:T(8,128)S(1)} %get-tuple-element.24), channel_id=1, source_target_pairs={{0,32},{32,64},{64,96},{96,0},{1,33},{33,65},{65,97},{97,1},{2,34}... | collective-permute-start | bytes 1382408 | tf_op jit(solution)/shard_map/ppermute | solution.py:32
  42.4 9.6 %collective-permute-start.7 = (f32[1,10,16,720]{3,2,1,0:T(8,128)S(1)}, f32[1,10,16,720]{3,2,1,0:T(8,128)}, u32[]{:S(2)}, u32[]{:S(2)}) collective-permute-start(f32[1,10,16,720]{3,2,1,0:T(8,128)S(1)} %get-tuple-element.25), channel_id=1, source_target_pairs={{32,0},{64,32},{96,64},{0,96},{33,1},{65,33},{97,65},{1,97},{34,2}... | collective-permute-start | bytes 1382408 | tf_op jit(solution)/shard_map/ppermute | solution.py:34
  51.2 0.8 copy-start.7
  56.6 1.9 %copy-start.3 = (f32[4,8,16,720]{3,2,1,0:T(8,128)S(1)}, f32[4,8,16,720]{3,2,1,0:T(8,128)}, u32[]{:S(2)}) copy-start(f32[4,8,16,720]{3,2,1,0:T(8,128)} %copy-done.2) | copy-start | bytes 4423684
  58.4 1.5 %copy-start.13 = (f32[4,16,1,1]{1,0,3,2:T(4,128)S(1)}, f32[4,16,1,1]{1,0,3,2:T(4,128)}, u32[]{:S(2)}) copy-start(f32[4,16,1,1]{1,0,3,2:T(4,128)} %constant.156) | copy-start | bytes 772
  60.0 1.6 %copy-start.6 = (f32[4,8,16,720]{3,2,1,0:T(8,128)}, f32[4,8,16,720]{3,2,1,0:T(8,128)S(1)}, u32[]{:S(2)}) copy-start(f32[4,8,16,720]{3,2,1,0:T(8,128)S(1)} %fusion) | copy-start | bytes 4423684
  61.6 1.2 %copy-start.8 = (f32[128,1]{1,0:T(8,128)S(1)}, f32[128,1]{1,0:T(8,128)}, u32[]{:S(2)}) copy-start(f32[128,1]{1,0:T(8,128)} %copy.49) | copy-start | bytes 1540
